TPU v7x, 32 devices: a whole 2x2x4 slice. The times are simulated.
32 devices in a mesh: row: 8 (over z, y), col: 4 (over x, core).
Axes of the slice: x: 2, y: 2, z: 4, core: 2. Of those that a mesh axis runs over, the one named last changes fastest.
Arguments:
- x_scan: float32 [16384, 256], P(('row', 'col')), may hold values from -6 to 6
- owner_slot: int32 [16384], P(('row', 'col')), may hold values from 0 to 16383, as said below
- weight: float32 [256, 256], replicated, may hold values from -0.375 to 0.375
- norm_gain: float32 [256], replicated, may hold values from 0.1 to 1.9
- tile_values: float32 [32, 8, 128, 128], P(('row', 'col')), may hold values from -0.375 to 0.375
- tile_coords: int32 [32, 8, 2], P(('row', 'col')), may hold values from 0 to 3
- counts: int32 [32, 3], P(('row', 'col')), may hold values from 2 to 128, as said below
- boundary_rows: int32 [32, 2, 128], P(('row', 'col')), may hold values from 0 to 511
- coupling: float32 [32, 2, 128, 128], P(('row', 'col')), may hold values from -0.5 to 0.5
- cotangent: float32 [16384, 256], P(('row', 'col')), may hold values from -6 to 6
Outputs:
- output: float32 [16384, 256], P(('row', 'col'))
- x_grad: float32 [16384, 256], P(('row', 'col'))
- weight_grad: float32 [256, 256], replicated
- gain_grad: float32 [256], replicated
Inputs may be any that keep to these rules, and one draw needn't show every extreme that they name: Each value appears once. The scan rows of one partition go to partition owner_slot // 512: exactly 32 of them to one partition, none to another, and 16 to each of the rest. `counts`: column 0 lies between 2 and 8 and equals 8 on some partition; every other column lies between 32 and 128 and equals 128 on some partition.
All inputs are finite; a program needn't handle non-finite values.
Results may differ from a plain program's by a relative error of at most 0.0003.
Values sent between devices are 32-bit elements; how exact they have to be, the bound alone decides.
No kernel may reach another device: no remote copies, remote signals or barrier semaphores. Data moves between devices by JAX's collectives and lax.ppermute only.
A program may use at most 64 MiB of HBM per device.

v0:
```python
import math

import jax
import jax.numpy as jnp
from jax import lax
from jax.sharding import PartitionSpec as P

BLOCK = 128
ROUNDS = 2


EPS = 1e-05
PRECISE = lax.Precision.HIGHEST


def swapped(array, axis, apart):
    return lax.ppermute(array, axis, [(i, i ^ 1 << apart) for i in range(lax.axis_size(axis))])


def layer_piece(aggregate, weight, norm_gain):
    inv_scale = lax.rsqrt(jnp.mean(aggregate * aggregate, axis=-1, keepdims=True) + EPS)
    normed = aggregate * inv_scale * norm_gain
    return jax.nn.silu(
        jnp.dot(normed, weight, precision=PRECISE, preferred_element_type=jnp.float32)
    )


def interior(hidden, tile_values, tile_coords, live_count, transpose):
    feat_count = hidden.shape[1]
    blocks = hidden.reshape(-1, BLOCK, feat_count)
    if transpose:
        source_col, target_col, form = (0, 1, "tji,tjf->tif")
    else:
        source_col, target_col, form = (1, 0, "tij,tjf->tif")
    live_mask = (jnp.arange(tile_values.shape[0]) < live_count).astype(jnp.float32)
    source = blocks[tile_coords[:, source_col]]
    product = jnp.einsum(form, tile_values * live_mask[:, None, None], source, precision=PRECISE)
    result = jnp.zeros_like(blocks).at[tile_coords[:, target_col]].add(product)
    return result.reshape(hidden.shape)


def boundary_forward(total, hidden, boundary_rows, coupling, counts):
    for round_index in range(ROUNDS):
        picked = boundary_rows[0, round_index]
        own_mask = (jnp.arange(BLOCK) < counts[0, 1 + round_index]).astype(jnp.float32)[:, None]
        outgoing = hidden[picked] * own_mask
        received = swapped(outgoing, "col", round_index)
        contrib = (
            jnp.dot(
                coupling[0, round_index],
                received,
                precision=PRECISE,
                preferred_element_type=jnp.float32,
            )
            * own_mask
        )
        total = total.at[picked].add(contrib)
    return total


def boundary_backward(total, grad_agg, boundary_rows, coupling, counts):
    for round_index in range(ROUNDS):
        picked = boundary_rows[0, round_index]
        own_mask = (jnp.arange(BLOCK) < counts[0, 1 + round_index]).astype(jnp.float32)[:, None]
        outgoing = grad_agg[picked] * own_mask
        carried = jnp.dot(
            coupling[0, round_index].T,
            outgoing,
            precision=PRECISE,
            preferred_element_type=jnp.float32,
        )
        received = swapped(carried, "col", round_index)
        total = total.at[picked].add(received * own_mask)
    return total


def on_device(
    x_scan,
    owner_slot,
    weight,
    norm_gain,
    tile_values,
    tile_coords,
    counts,
    boundary_rows,
    coupling,
    cotangent,
):
    row_count, feat_count = x_scan.shape
    grid_rows = lax.axis_size("row")
    grid_cols = lax.axis_size("col")
    devices = grid_rows * grid_cols
    capacity = 2 * row_count // devices
    target = owner_slot // row_count
    within = owner_slot % row_count
    sorting = jnp.argsort(target, stable=True)
    sorted_target = target[sorting]
    per_peer = jnp.sum(
        (target[:, None] == jnp.arange(devices, dtype=jnp.int32)[None, :]).astype(jnp.int32), axis=0
    )
    starts = jnp.cumsum(per_peer) - per_peer
    ranked = (
        jnp.zeros((row_count,), jnp.int32)
        .at[sorting]
        .set(jnp.arange(row_count, dtype=jnp.int32) - starts[sorted_target])
    )
    bucket = target * capacity + ranked
    outbox = jnp.zeros((devices * capacity, feat_count), jnp.float32).at[bucket].set(x_scan)
    places = jnp.full((devices * capacity,), row_count, jnp.int32).at[bucket].set(within)
    inbox, place_in = (
        lax.all_to_all(
            outbox.reshape(devices, capacity, feat_count),
            ("row", "col"),
            split_axis=0,
            concat_axis=0,
            tiled=True,
        ),
        lax.all_to_all(
            places.reshape(devices, capacity),
            ("row", "col"),
            split_axis=0,
            concat_axis=0,
            tiled=True,
        ),
    )
    inbox = inbox.reshape(-1, feat_count)
    place_in = place_in.reshape(-1)
    hidden = jnp.zeros((row_count, feat_count), jnp.float32).at[place_in].set(inbox, mode="drop")
    aggregate = hidden + interior(hidden, tile_values[0], tile_coords[0], counts[0, 0], False)
    aggregate = boundary_forward(aggregate, hidden, boundary_rows, coupling, counts)
    activation, pullback = jax.vjp(layer_piece, aggregate, weight, norm_gain)
    output = hidden + activation
    grad_agg, grad_weight, grad_gain = pullback(cotangent)
    weight_sum, gain_sum = lax.psum((grad_weight, grad_gain), ("row", "col"))
    grad_nodes = (
        cotangent
        + grad_agg
        + interior(grad_agg, tile_values[0], tile_coords[0], counts[0, 0], True)
    )
    grad_nodes = boundary_backward(grad_nodes, grad_agg, boundary_rows, coupling, counts)
    valid = (place_in < row_count).astype(jnp.float32)[:, None]
    reply = grad_nodes[jnp.minimum(place_in, row_count - 1)] * valid
    returned = lax.all_to_all(
        reply.reshape(devices, capacity, feat_count),
        ("row", "col"),
        split_axis=0,
        concat_axis=0,
        tiled=True,
    )
    x_grad = returned.reshape(-1, feat_count)[bucket]
    node_scale = 1.0 / math.sqrt(row_count * devices)
    return (output, x_grad, weight_sum * node_scale, gain_sum * node_scale)


def solution(mesh):
    in_specs = (
        P(("row", "col"), None),
        P(("row", "col")),
        P(),
        P(),
        P(("row", "col"), None, None, None),
        P(("row", "col"), None, None),
        P(("row", "col"), None),
        P(("row", "col"), None, None),
        P(("row", "col"), None, None, None),
        P(("row", "col"), None),
    )
    out_specs = (P(("row", "col"), None), P(("row", "col"), None), P(), P())
    return jax.shard_map(
        on_device, mesh=mesh, in_specs=in_specs, out_specs=out_specs, check_vma=False
    )
```

profile of v0, /device:TPU:0, one launch (start us, length us, event | category | flops | bytes accessed | tf_op | source)
XLA Modules:
  0.0 280.3 jit_solution(10291379477697038767)
XLA Ops:
  7.2 0.7 add_select_fusion
  7.9 0.1 convert_reduce_fusion
  8.3 0.7 fusion.49
  9.0 0.7 fusion.48
  9.8 3.8 %sort.17 = (s32[512]{0:T(512)}, s32[512]{0:T(512)S(1)}) sort(s32[512]{0:T(512)S(1)} %get-tuple-element.38, s32[512]{0:T(512)S(1)} %iota.29), dimensions={0}, to_apply=%region_0.1 | sort | flops 4608 | bytes 8192 | tf_op jit(solution)/shard_map/jit(argsort)/sort | solution.py:96
  13.5 3.5 %gather_fusion = s32[512]{0:T(512)S(1)} fusion(s32[512]{0:T(512)S(1)} %get-tuple-element.38, s32[1024]{0:T(1024)S(1)} %pad_clamp_fusion.5), kind=kCustom, calls=%fused_computation | custom fusion | bytes 6144 | tf_op jit(solution)/shard_map/gather | solution.py:97
  17.0 4.3 %compare_select_fusion.3 = (s32[512,1]{0,1:T(1,128)S(1)}, s32[512,1]{0,1:T(1,128)S(1)}) fusion(s32[]{:T(128)} %bitcast.27, s32[]{:T(128)} %bitcast.28, s32[]{:T(128)} %bitcast.29, s32[]{:T(128)} %bitcast.30, s32[]{:T(128)} %bitcast.31, s32[]{:T(128)} %bitcast.33, s32[]{:T(128)} %bitcast.32, s32[512,1]{0,1:T(1,128)S(1)} %bitcast.100), kind=kLoop, calls=%fused_computation.104 | loop fusion | flops 7680 | bytes 6172 | tf_op jit(solution)/shard_map/gather | solution.py:105
  21.3 0.2 compare_reduce_fusion.24
  21.5 15.8 %select_subtract_fusion = s32[512]{0:T(512)S(1)} fusion(pred[512]{0:T(512)(128)(4,1)S(1)} %get-tuple-element.32, pred[512]{0:T(512)(128)(4,1)S(1)} %get-tuple-element.31, pred[512]{0:T(512)(128)(4,1)S(1)} %get-tuple-element.30, pred[512]{0:T(512)(128)(4,1)S(1)} %get-tuple-element.29, pred[512]{0:T(512)(128)(4,1)S(1)} %get-tuple-element.28, ...), kind=kLoop, calls=%fused_computation.128 | loop fusion | flops 13312 | bytes 16996 | tf_op jit(solution)/shard_map/sub | solution.py:105
  37.3 2.4 scatter_custom_fusion
  39.7 2.4 scatter_custom_fusion.1
  42.2 0.7 all_to_all.12
  42.9 7.3 %all-to-all-start = ((s32[32,1,32]{2,1,0:T(1,128)}), s32[32,1,32]{2,1,0:T(1,128)S(1)}, u32[]{:S(2)}, u32[]{:S(2)}) async-start(s32[32,1,32]{2,1,0:T(1,128)} %all_to_all.12), calls=%async_computation | async-start | bytes 32768 | tf_op jit(solution)/shard_map/all_to_all | solution.py:118
  50.2 3.7 %scatter_custom_fusion.2 = f32[1024,256]{1,0:T(8,128)} fusion(s32[512]{0:T(512)S(1)} %compare_select_fusion.9, f32[512,256]{1,0:T(8,128)} %param.10, f32[]{:T(128)} %constant.21.clone.1), kind=kCustom, calls=%fused_computation.38 | custom fusion | bytes 1049088 | tf_op jit(solution)/shard_map/scatter | solution.py:108
  53.9 3.3 %all-to-all-done = s32[32,1,32]{2,1,0:T(1,128)S(1)} async-done(((s32[32,1,32]{2,1,0:T(1,128)}), s32[32,1,32]{2,1,0:T(1,128)S(1)}, u32[]{:S(2)}, u32[]{:S(2)}) %all-to-all-start) | async-done | bytes 4128 | tf_op jit(solution)/shard_map/all_to_all | solution.py:118
  57.3 2.8 all-to-all-start.1
  60.0 0.6 fusion.47
  60.6 0.6 compare_convert_fusion.3
  61.3 0.7 compare_convert_fusion.2
  61.9 0.7 compare_convert_fusion.1
  62.6 0.7 copy-done.7
  63.3 0.7 copy-done.8
  64.0 0.5 broadcast.497
  64.5 0.7 reduce.54
  65.3 20.9 %all-to-all-done.1 = f32[32,32,256]{2,1,0:T(8,128)S(1)} async-done(((f32[32,32,256]{2,1,0:T(8,128)}), f32[32,32,256]{2,1,0:T(8,128)S(1)}, u32[]{:S(2)}, u32[]{:S(2)}) %all-to-all-start.1) | async-done | bytes 1048608 | tf_op jit(solution)/shard_map/all_to_all | solution.py:111
  86.3 4.9 %scatter_custom_fusion.3 = f32[512,256]{1,0:T(8,128)S(1)} fusion(s32[1024]{0:T(1024)S(1)} %bitcast.101, f32[1024,256]{1,0:T(8,128)S(1)} %bitcast.96, f32[]{:T(128)} %constant.21.clone.1), kind=kCustom, calls=%fused_computation.54 | custom fusion | bytes 524292 | tf_op jit(solution)/shard_map/scatter | solution.py:128
  91.2 0.6 gather_fusion.1
  91.8 0.4 copy-done.1
  92.2 1.1 fusion.7
  93.4 1.3 scatter_fusion
  94.7 0.8 gather_fusion.2
  95.7 0.8 gather_fusion.3
  96.6 1.5 collective-permute-start.1
  98.1 0.3 fusion.1
  98.5 4.0 %collective-permute-done.1 = f32[128,256]{0,1:T(8,128)S(1)} collective-permute-done((f32[128,256]{0,1:T(8,128)S(1)}, f32[128,256]{0,1:T(8,128)S(1)}, u32[]{:S(2)}, u32[]{:S(2)}) %collective-permute-start.1) | collective-permute-done | bytes 131104 | tf_op jit(solution)/shard_map/ppermute | solution.py:17
  102.6 0.3 fusion
  102.9 1.7 scatter_fusion.1
  104.6 1.5 scatter_fusion.2
  106.1 0.1 multiply_reduce_fusion.2
  106.3 0.6 copy-done.9
  107.0 1.5 multiply_add_fusion
  108.4 0.8 multiply_reduce_fusion
  109.3 0.2 add_add_fusion
  109.5 0.8 gather_fusion.5
  110.3 0.8 gather_fusion.6
  111.0 0.6 gather_fusion.4
  111.7 0.4 copy-done.2
  112.1 2.1 fusion.6
  114.2 2.5 scatter_fusion.3
  116.9 0.3 convolution_bitcast_fusion.1
  117.4 0.3 convolution_bitcast_fusion
  117.6 1.5 collective-permute-start.3
  119.3 4.3 %collective-permute-done.3 = f32[128,256]{0,1:T(8,128)S(1)} collective-permute-done((f32[128,256]{0,1:T(8,128)S(1)}, f32[128,256]{0,1:T(8,128)S(1)}, u32[]{:S(2)}, u32[]{:S(2)}) %collective-permute-start.3) | collective-permute-done | bytes 131104 | tf_op jit(solution)/shard_map/ppermute | solution.py:17
  123.7 1.5 scatter_fusion.4
  125.2 1.5 scatter_fusion.5
  126.7 3.5 %gather_fusion.7 = f32[1024,256]{1,0:T(8,128)S(1)} fusion(f32[512,256]{1,0:T(8,128)S(1)} %scatter_fusion.5, s32[1024]{0:T(1024)S(1)} %broadcast_clamp_fusion), kind=kCustom, calls=%fused_computation.7 | custom fusion | bytes 2101248 | tf_op jit(solution)/shard_map/gather | solution.py:142
  130.2 1.2 broadcast_multiply_fusion
  131.4 3.6 %all-to-all-start.2 = ((f32[32,32,256]{2,1,0:T(8,128)}), f32[32,32,256]{2,1,0:T(8,128)S(1)}, u32[]{:S(2)}, u32[]{:S(2)}) async-start(f32[32,32,256]{2,1,0:T(8,128)} %broadcast_multiply_fusion), calls=%async_computation.2 | async-start | bytes 2097152 | tf_op jit(solution)/shard_map/all_to_all | solution.py:143
  135.0 1.9 fusion.8
  136.9 45.2 %psum.15 = f32[256]{0:T(256)S(1)} all-reduce(f32[256]{0:T(256)S(1)} %get-tuple-element.6), channel_id=1, replica_groups=mesh['row'=8,'col'=4] {'row','col'}, use_global_device_ids=true, to_apply=%region_17.18 | all-reduce | flops 256 | bytes 2048 | tf_op jit(solution)/shard_map/psum | solution.py:134
  182.1 0.6 broadcast_multiply_fusion.6
  182.6 86.9 %all-reduce.2.cloned.1.call-done = f32[256,256]{1,0:T(8,128)} async-done(((f32[256,256]{1,0:T(8,128)}), f32[256,256]{1,0:T(8,128)}) %all-reduce.2.cloned.1.call-update) | async-done | bytes 262160 | tf_op jit(solution)/shard_map/psum | solution.py:134
  269.5 1.7 broadcast_multiply_fusion.1
  271.2 2.2 gather_fusion.8
  (61 shorter events, 1.7 us)
Async XLA Ops:
  7.2 99.1 %copy-start = (f32[256,256]{1,0:T(8,128)S(1)}, f32[256,256]{1,0:T(8,128)}, u32[]{:S(2)}) copy-start(f32[256,256]{1,0:T(8,128)} %param.12) | copy-start | bytes 786436
  42.9 14.4 %all-to-all-start = ((s32[32,1,32]{2,1,0:T(1,128)}), s32[32,1,32]{2,1,0:T(1,128)S(1)}, u32[]{:S(2)}, u32[]{:S(2)}) async-start(s32[32,1,32]{2,1,0:T(1,128)} %all_to_all.12), calls=%async_computation | async-start | bytes 32768 | tf_op jit(solution)/shard_map/all_to_all | solution.py:118
  57.2 2.8 copy-start.6
  57.3 29.0 %all-to-all-start.1 = ((f32[32,32,256]{2,1,0:T(8,128)}), f32[32,32,256]{2,1,0:T(8,128)S(1)}, u32[]{:S(2)}, u32[]{:S(2)}) async-start(f32[32,32,256]{2,1,0:T(8,128)} %bitcast.36), calls=%async_computation.1 | async-start | bytes 2097152 | tf_op jit(solution)/shard_map/all_to_all | solution.py:111
  62.6 0.7 copy-start.7
  63.3 0.7 copy-start.8
  91.2 1.0 copy-start.1
  95.6 2.5 collective-permute-start
  96.6 1.6 copy-start.3
  96.6 6.0 %collective-permute-start.1 = (f32[128,256]{0,1:T(8,128)S(1)}, f32[128,256]{0,1:T(8,128)S(1)}, u32[]{:S(2)}, u32[]{:S(2)}) collective-permute-start(f32[128,256]{0,1:T(8,128)S(1)} %broadcast_multiply_fusion.3), channel_id=1, source_target_pairs={{0,2},{1,3},{2,0},{3,1},{4,6},{5,7},{6,4},{7,5},{8,10},{9,11},{10,... | collective-permute-start | bytes 393224 | tf_op jit(solution)/shard_map/ppermute | solution.py:17
  106.3 0.7 copy-start.9
  107.0 1.5 copy-start.4
  108.4 0.9 copy-start.10
  111.0 1.0 copy-start.2
  114.2 2.5 copy-start.5
  117.2 2.0 collective-permute-start.2
  117.6 6.0 %collective-permute-start.3 = (f32[128,256]{0,1:T(8,128)S(1)}, f32[128,256]{0,1:T(8,128)S(1)}, u32[]{:S(2)}, u32[]{:S(2)}) collective-permute-start(f32[128,256]{0,1:T(8,128)S(1)} %convolution_bitcast_fusion), channel_id=1, source_target_pairs={{0,2},{1,3},{2,0},{3,1},{4,6},{5,7},{6,4},{7,5},{8,10},{9,11},{10,... | collective-permute-start | bytes 393224 | tf_op jit(solution)/shard_map/ppermute | solution.py:17
  131.4 3.6 %copy-start.11 = (f32[512,256]{1,0:T(8,128)S(1)}, f32[512,256]{1,0:T(8,128)}, u32[]{:S(2)}) copy-start(f32[512,256]{1,0:T(8,128)} %copy-done.10) | copy-start | bytes 1572868
  131.4 139.8 %all-to-all-start.2 = ((f32[32,32,256]{2,1,0:T(8,128)}), f32[32,32,256]{2,1,0:T(8,128)S(1)}, u32[]{:S(2)}, u32[]{:S(2)}) async-start(f32[32,32,256]{2,1,0:T(8,128)} %broadcast_multiply_fusion), calls=%async_computation.2 | async-start | bytes 2097152 | tf_op jit(solution)/shard_map/all_to_all | solution.py:143
  135.0 134.6 %all-reduce.2.cloned.1.call-start = ((), (), s32[]{:S(2)}) async-start(), calls=%async_computation.3 | async-start | bytes 524288 | tf_op jit(solution)/shard_map/psum | solution.py:134
Sparse Core Ops, SparseCore 0:
  141.9 127.6 all-reduce.1
where the time goes:
time: 281 us; the launch traced here: 280 us
  waiting for transfers between devices  119 us (42%)
  blocking collectives  45.2 us (16%)
  other arithmetic  41.7 us (15%)
  local copies, waits for them, and re-layouts  34 us (12%)
  starting transfers between devices  16.9 us (6%)
  between operations  14.6 us (5%)
  matrix products  8.46 us (3%)
    psum x1, waiting for transfers between devices, on_device(): weight_sum, gain_sum = lax.psum((grad_weight, grad_gain), ('row', 'col'))  86.9 us
    psum x1, blocking collectives, on_device(): weight_sum, gain_sum = lax.psum((grad_weight, grad_gain), ('row', 'col'))  45.2 us
    all_to_all x1, waiting for transfers between devices, on_device(): lax.all_to_all(outbox.reshape(devices, capacity, feat_count), ('row', 'co...  20.9 us
    sub x1, other arithmetic, on_device(): jnp.arange(row_count, dtype=jnp.int32) - starts[sorted_target]  15.8 us
    ppermute x4, waiting for transfers between devices, swapped(): lax.ppermute(array, axis, [(i, i ^ 1 << apart) for i in range(lax.axis_si...  8.33 us
    all_to_all x1, starting transfers between devices, on_device(): lax.all_to_all(places.reshape(devices, capacity), ('row', 'col'), split_a...  7.3 us
  transfers between devices with their start and end apart: 8, of which 5 were waited for; matrix products, arithmetic and copies ran while one was open for 5% of the time, Pallas kernels for 0%

commit v1 on v0

--- a/solution.py
+++ b/solution.py
@@ -74,6 +74,19 @@
     return total
 
 
+def summed_everywhere(grad_weight, grad_gain, devices):
+    packed = jnp.concatenate([grad_weight, grad_gain[None]], 0)
+    rows, width = packed.shape
+    pieces = packed.reshape(devices, -1)
+    gathered = lax.all_to_all(pieces, ("row", "col"), 0, 0, tiled=True)
+    chunk = jnp.sum(gathered, axis=0, keepdims=True)
+    spread = lax.all_to_all(
+        jnp.broadcast_to(chunk, pieces.shape), ("row", "col"), 0, 0, tiled=True
+    )
+    total = spread.reshape(rows, width)
+    return total[:-1], total[-1]
+
+
 def on_device(
     x_scan,
     owner_slot,
@@ -131,7 +144,7 @@
     activation, pullback = jax.vjp(layer_piece, aggregate, weight, norm_gain)
     output = hidden + activation
     grad_agg, grad_weight, grad_gain = pullback(cotangent)
-    weight_sum, gain_sum = lax.psum((grad_weight, grad_gain), ("row", "col"))
+    weight_sum, gain_sum = summed_everywhere(grad_weight, grad_gain, devices)
     grad_nodes = (
         cotangent
         + grad_agg

time: 281 us -> 173 us (0.62)
  waiting for transfers between devices: 119 us -> 51.7 us
  blocking collectives: 45.2 us -> 0 us
  between operations: 14.6 us -> 1.35 us
  starting transfers between devices: 16.9 us -> 26.1 us
  local copies, waits for them, and re-layouts: 34 us -> 40.8 us
  other arithmetic: 41.7 us -> 45.1 us
    psum x1 -> x0, waiting for transfers between devices: 86.9 us -> none  [on_device(): weight_sum, gain_sum = lax.psum((grad_weight, grad_gain), ('row', 'col'))]
    psum x1 -> x0, blocking collectives: 45.2 us -> none  [on_device(): weight_sum, gain_sum = lax.psum((grad_weight, grad_gain), ('row', 'col'))]
    all_to_all x1, waiting for transfers between devices: 0.01 us -> 24 us  [on_device(): lax.all_to_all(reply.reshape(devices, capacity, feat_count), ('row', 'col...]
    all_to_all x0 -> x2, starting transfers between devices: none -> 8.31 us  [the longest x1 4.64 us: summed_everywhere(): lax.all_to_all(jnp.broadcast_to(chunk, pieces.shape), ('row', 'col'), 0,...]
    ppermute x4, waiting for transfers between devices: 8.33 us -> 4.02 us  [swapped(): lax.ppermute(array, axis, [(i, i ^ 1 << apart) for i in range(lax.axis_si...]
  transfers between devices with their start and end apart: 8 -> 9, of which waited for: 5 -> 5; matrix products, arithmetic and copies ran while one was open for 5% -> 19% of each run, Pallas kernels for 0% -> 0%
where the time goes in v1:
time: 173 us; the launch traced here: 172 us
  waiting for transfers between devices  51.7 us (30%)
  other arithmetic  45.1 us (26%)
  local copies, waits for them, and re-layouts  40.8 us (24%)
  starting transfers between devices  26.1 us (15%)
  matrix products  7.4 us (4%)
    all_to_all x1, waiting for transfers between devices, on_device(): lax.all_to_all(reply.reshape(devices, capacity, feat_count), ('row', 'col...  24 us
    all_to_all x1, waiting for transfers between devices, on_device(): lax.all_to_all(outbox.reshape(devices, capacity, feat_count), ('row', 'co...  18.6 us
    sub x1, other arithmetic, on_device(): jnp.arange(row_count, dtype=jnp.int32) - starts[sorted_target]  15.8 us
    all_to_all x1, starting transfers between devices, on_device(): lax.all_to_all(places.reshape(devices, capacity), ('row', 'col'), split_a...  7.3 us
    unnamed x56, local copies, waits for them, and re-layouts  5.4 us
    scatter x1, local copies, waits for them, and re-layouts, on_device(): jnp.zeros((row_count, feat_count), jnp.float32).at[place_in]  4.92 us
    all_to_all x1, starting transfers between devices, summed_everywhere(): lax.all_to_all(jnp.broadcast_to(chunk, pieces.shape), ('row', 'col'), 0,...  4.64 us
    gather x2, other arithmetic, on_device(): starts[sorted_target]  4.46 us
  transfers between devices with their start and end apart: 9, of which 5 were waited for; matrix products, arithmetic and copies ran while one was open for 19% of the time, Pallas kernels for 0%

profile of v1, /device:TPU:0, one launch (start us, length us, event | category | flops | bytes accessed | tf_op | source)
XLA Modules:
  0.0 172.4 jit_solution(17476175733284755296)
XLA Ops:
  0.6 0.7 add_select_fusion
  1.8 0.7 fusion.49
  2.5 0.7 fusion.48
  3.2 3.8 %sort.17 = (s32[512]{0:T(512)}, s32[512]{0:T(512)S(1)}) sort(s32[512]{0:T(512)S(1)} %get-tuple-element.38, s32[512]{0:T(512)S(1)} %iota.29), dimensions={0}, to_apply=%region_0.1 | sort | flops 4608 | bytes 8192 | tf_op jit(solution)/shard_map/jit(argsort)/sort | solution.py:109
  7.0 3.5 %gather_fusion = s32[512]{0:T(512)S(1)} fusion(s32[512]{0:T(512)S(1)} %get-tuple-element.38, s32[1024]{0:T(1024)S(1)} %pad_clamp_fusion.5), kind=kCustom, calls=%fused_computation | custom fusion | bytes 6144 | tf_op jit(solution)/shard_map/gather | solution.py:110
  10.5 4.3 %compare_select_fusion.3 = (s32[512,1]{0,1:T(1,128)S(1)}, s32[512,1]{0,1:T(1,128)S(1)}) fusion(s32[]{:T(128)} %bitcast.27, s32[]{:T(128)} %bitcast.28, s32[]{:T(128)} %bitcast.29, s32[]{:T(128)} %bitcast.30, s32[]{:T(128)} %bitcast.31, s32[]{:T(128)} %bitcast.33, s32[]{:T(128)} %bitcast.32, s32[512,1]{0,1:T(1,128)S(1)} %bitcast.102), kind=kLoop, calls=%fused_computation.105 | loop fusion | flops 7680 | bytes 6172 | tf_op jit(solution)/shard_map/gather | solution.py:118
  15.0 15.8 %select_subtract_fusion = s32[512]{0:T(512)S(1)} fusion(pred[512]{0:T(512)(128)(4,1)S(1)} %get-tuple-element.32, pred[512]{0:T(512)(128)(4,1)S(1)} %get-tuple-element.31, pred[512]{0:T(512)(128)(4,1)S(1)} %get-tuple-element.30, pred[512]{0:T(512)(128)(4,1)S(1)} %get-tuple-element.29, pred[512]{0:T(512)(128)(4,1)S(1)} %get-tuple-element.28, ...), kind=kLoop, calls=%fused_computation.129 | loop fusion | flops 13312 | bytes 16996 | tf_op jit(solution)/shard_map/sub | solution.py:118
  30.7 2.4 %scatter_custom_fusion = s32[512]{0:T(512)S(1)} fusion(s32[512]{0:T(512)S(1)} %compare_select_fusion.10, s32[512]{0:T(512)S(1)} %select_subtract_fusion, s32[]{:T(128)} %constant.26.clone.1), kind=kCustom, calls=%fused_computation.141 | custom fusion | bytes 2052 | tf_op jit(solution)/shard_map/scatter | solution.py:118
  33.2 2.4 %scatter_custom_fusion.1 = s32[1024]{0:T(1024)S(1)} fusion(s32[512]{0:T(512)S(1)} %compare_select_fusion.9, s32[512]{0:T(512)S(1)} %get-tuple-element.37, s32[]{:T(128)} %constant.22.clone.1), kind=kCustom, calls=%fused_computation.133 | custom fusion | bytes 4100 | tf_op jit(solution)/shard_map/scatter | solution.py:122
  35.7 0.7 all_to_all.22
  36.3 7.3 %all-to-all-start = ((s32[32,1,32]{2,1,0:T(1,128)}), s32[32,1,32]{2,1,0:T(1,128)S(1)}, u32[]{:S(2)}, u32[]{:S(2)}) async-start(s32[32,1,32]{2,1,0:T(1,128)} %all_to_all.22), calls=%async_computation | async-start | bytes 32768 | tf_op jit(solution)/shard_map/all_to_all | solution.py:131
  43.7 3.7 %scatter_custom_fusion.2 = f32[1024,256]{1,0:T(8,128)} fusion(s32[512]{0:T(512)S(1)} %compare_select_fusion.9, f32[512,256]{1,0:T(8,128)} %param.10, f32[]{:T(128)} %constant.21.clone.1), kind=kCustom, calls=%fused_computation.38 | custom fusion | bytes 1049088 | tf_op jit(solution)/shard_map/scatter | solution.py:121
  47.4 3.3 %all-to-all-done = s32[32,1,32]{2,1,0:T(1,128)S(1)} async-done(((s32[32,1,32]{2,1,0:T(1,128)}), s32[32,1,32]{2,1,0:T(1,128)S(1)}, u32[]{:S(2)}, u32[]{:S(2)}) %all-to-all-start) | async-done | bytes 4128 | tf_op jit(solution)/shard_map/all_to_all | solution.py:131
  50.7 2.8 %all-to-all-start.1 = ((f32[32,32,256]{2,1,0:T(8,128)}), f32[32,32,256]{2,1,0:T(8,128)S(1)}, u32[]{:S(2)}, u32[]{:S(2)}) async-start(f32[32,32,256]{2,1,0:T(8,128)} %bitcast.36), calls=%async_computation.1 | async-start | bytes 2097152 | tf_op jit(solution)/shard_map/all_to_all | solution.py:124
  53.5 0.6 fusion.47
  54.1 0.6 compare_convert_fusion.3
  54.8 0.7 compare_convert_fusion.2
  55.4 1.2 compare_convert_fusion.1
  56.7 0.7 copy-done.25
  57.3 0.6 copy-done.22
  57.9 0.6 pad_clamp_fusion.1
  58.6 0.6 copy-done.11
  59.7 0.7 reduce.56
  60.5 0.6 broadcast_clamp_fusion
  61.1 18.6 %all-to-all-done.1 = f32[32,32,256]{2,1,0:T(8,128)S(1)} async-done(((f32[32,32,256]{2,1,0:T(8,128)}), f32[32,32,256]{2,1,0:T(8,128)S(1)}, u32[]{:S(2)}, u32[]{:S(2)}) %all-to-all-start.1) | async-done | bytes 1048608 | tf_op jit(solution)/shard_map/all_to_all | solution.py:124
  79.7 4.9 %scatter_custom_fusion.3 = f32[512,256]{1,0:T(8,128)S(1)} fusion(s32[1024]{0:T(1024)S(1)} %bitcast.103, f32[1024,256]{1,0:T(8,128)S(1)} %bitcast.98, f32[]{:T(128)} %constant.21.clone.1), kind=kCustom, calls=%fused_computation.56 | custom fusion | bytes 524292 | tf_op jit(solution)/shard_map/scatter | solution.py:141
  84.7 0.6 gather_fusion.1
  85.7 1.1 fusion.7
  86.8 1.3 scatter_fusion
  88.2 0.8 gather_fusion.2
  89.2 0.8 gather_fusion.3
  90.7 1.6 collective-permute-start.1
  92.6 4.0 %collective-permute-done.1 = f32[128,256]{0,1:T(8,128)S(1)} collective-permute-done((f32[128,256]{0,1:T(8,128)S(1)}, f32[128,256]{0,1:T(8,128)S(1)}, u32[]{:S(2)}, u32[]{:S(2)}) %collective-permute-start.1) | collective-permute-done | bytes 131104 | tf_op jit(solution)/shard_map/ppermute | solution.py:17
  97.5 1.7 scatter_fusion.1
  99.2 1.5 scatter_fusion.2
  100.9 0.6 copy-done.27
  101.5 1.5 multiply_add_fusion
  103.0 1.2 fusion.8
  104.2 0.8 multiply_reduce_fusion
  105.0 1.1 all_to_all.29
  106.2 3.7 %all-to-all-start.3 = ((f32[32,1,2056]{2,1,0:T(1,128)}), f32[32,1,2056]{2,1,0:T(1,128)}, u32[]{:S(2)}, u32[]{:S(2)}) async-start(f32[32,1,2056]{2,1,0:T(1,128)} %all_to_all.29), calls=%async_computation.3 | async-start | bytes 557056 | tf_op jit(solution)/shard_map/all_to_all | solution.py:81
  110.1 1.5 gather_fusion.5
  111.6 0.9 gather_fusion.4
  112.6 1.8 %fusion.6 = f32[8,128,256]{2,1,0:T(8,128)S(1)} fusion(f32[8,128,256]{2,1,0:T(8,128)S(1)} %gather_fusion.4, f32[1,8,128,128]{3,2,1,0:T(8,128)S(1)} %copy-done.2, f32[8]{0:T(128)} %copy-done.24), kind=kOutput, calls=%fused_computation.40 | convolution fusion | flops 402784256 | bytes 2621472 | tf_op jit(solution)/shard_map/tji,tjf->tif/dot_general | solution.py:37
  114.4 1.0 copy.51
  115.7 0.9 gather_fusion.6
  117.0 0.6 copy-done.23
  117.6 1.3 scatter_fusion.3
  118.9 1.1 bitcast_add_fusion
  120.3 1.7 %collective-permute-start.3 = (f32[128,256]{0,1:T(8,128)S(1)}, f32[128,256]{0,1:T(8,128)S(1)}, u32[]{:S(2)}, u32[]{:S(2)}) collective-permute-start(f32[128,256]{0,1:T(8,128)S(1)} %convolution_bitcast_fusion), channel_id=1, source_target_pairs={{0,2},{1,3},{2,0},{3,1},{4,6},{5,7},{6,4},{7,5},{8,10},{9,11},{10,... | collective-permute-start | bytes 393224 | tf_op jit(solution)/shard_map/ppermute | solution.py:17
  122.1 1.1 reduce_sum.57
  123.2 0.9 broadcast_in_dim.17
  124.1 4.6 %all-to-all-start.4 = ((f32[32,1,2056]{2,1,0:T(1,128)}), f32[32,1,2056]{2,1,0:T(1,128)S(1)}, u32[]{:S(2)}, u32[]{:S(2)}) async-start(f32[32,1,2056]{2,1,0:T(1,128)} %broadcast_in_dim.17), calls=%async_computation.4 | async-start | bytes 557056 | tf_op jit(solution)/shard_map/all_to_all | solution.py:83
  128.7 0.9 broadcast_multiply_fusion.3
  130.4 1.5 scatter_fusion.4
  131.9 1.5 scatter_fusion.5
  133.4 3.5 %gather_fusion.7 = f32[1024,256]{1,0:T(8,128)S(1)} fusion(f32[512,256]{1,0:T(8,128)S(1)} %scatter_fusion.5, s32[1024]{0:T(1024)S(1)} %copy-done.5), kind=kCustom, calls=%fused_computation.7 | custom fusion | bytes 2101248 | tf_op jit(solution)/shard_map/gather | solution.py:155
  136.9 1.2 broadcast_multiply_fusion
  138.1 1.7 all-to-all-done.4
  139.8 4.1 %all-to-all-start.2 = ((f32[32,32,256]{2,1,0:T(8,128)}), f32[32,32,256]{2,1,0:T(8,128)S(1)}, u32[]{:S(2)}, u32[]{:S(2)}) async-start(f32[32,32,256]{2,1,0:T(8,128)} %broadcast_multiply_fusion), calls=%async_computation.2 | async-start | bytes 2097152 | tf_op jit(solution)/shard_map/all_to_all | solution.py:156
  144.0 0.7 reduce.28
  145.4 0.7 slice_multiply_fusion
  146.1 24.0 %all-to-all-done.2 = f32[32,32,256]{2,1,0:T(8,128)S(1)} async-done(((f32[32,32,256]{2,1,0:T(8,128)}), f32[32,32,256]{2,1,0:T(8,128)S(1)}, u32[]{:S(2)}, u32[]{:S(2)}) %all-to-all-start.2) | async-done | bytes 1048608 | tf_op jit(solution)/shard_map/all_to_all | solution.py:156
  170.2 2.2 %gather_fusion.8 = f32[512,256]{1,0:T(8,128)} fusion(f32[1024,256]{1,0:T(8,128)S(1)} %bitcast.96, s32[1024]{0:T(1024)S(1)} %pad_clamp_fusion), kind=kCustom, calls=%fused_computation.8 | custom fusion | bytes 1050624 | tf_op jit(solution)/shard_map/gather | solution.py:163
  (99 shorter events, 6.9 us)
Async XLA Ops:
  0.6 100.2 %copy-start = (f32[256,256]{1,0:T(8,128)S(1)}, f32[256,256]{1,0:T(8,128)}, u32[]{:S(2)}) copy-start(f32[256,256]{1,0:T(8,128)} %param.12) | copy-start | bytes 786436
  33.2 10.5 %copy-start.17 = (s32[512]{0:T(512)}, s32[512]{0:T(512)S(1)}, u32[]{:S(2)}) copy-start(s32[512]{0:T(512)S(1)} %compare_select_fusion.9) | copy-start | bytes 6148
  36.3 14.4 %all-to-all-start = ((s32[32,1,32]{2,1,0:T(1,128)}), s32[32,1,32]{2,1,0:T(1,128)S(1)}, u32[]{:S(2)}, u32[]{:S(2)}) async-start(s32[32,1,32]{2,1,0:T(1,128)} %all_to_all.22), calls=%async_computation | async-start | bytes 32768 | tf_op jit(solution)/shard_map/all_to_all | solution.py:131
  50.7 2.8 %copy-start.21 = (s32[1,3]{1,0:T(1,128)S(1)}, s32[1,3]{1,0:T(1,128)}, u32[]{:S(2)}) copy-start(s32[1,3]{1,0:T(1,128)} %param.16) | copy-start | bytes 40
  50.7 29.0 %all-to-all-start.1 = ((f32[32,32,256]{2,1,0:T(8,128)}), f32[32,32,256]{2,1,0:T(8,128)S(1)}, u32[]{:S(2)}, u32[]{:S(2)}) async-start(f32[32,32,256]{2,1,0:T(8,128)} %bitcast.36), calls=%async_computation.1 | async-start | bytes 2097152 | tf_op jit(solution)/shard_map/all_to_all | solution.py:124
  54.8 30.5 %copy-start.24 = (f32[8]{0:T(128)}, f32[8]{0:T(128)S(1)}, u32[]{:S(2)}) copy-start(f32[8]{0:T(128)S(1)} %compare_convert_fusion.3) | copy-start | bytes 100
  55.4 33.7 %copy-start.8 = (f32[128]{0:T(128)}, f32[128]{0:T(128)S(1)}, u32[]{:S(2)}) copy-start(f32[128]{0:T(128)S(1)} %compare_convert_fusion.2) | copy-start | bytes 1540
  56.7 0.7 copy-start.25
  57.3 0.6 copy-start.22
  57.9 0.7 copy-start.26
  58.6 0.6 copy-start.11
  58.6 0.6 copy-start.14
  59.2 29.0 %copy-start.20 = (s32[1024]{0:T(1024)}, s32[1024]{0:T(1024)S(1)}, u32[]{:S(2)}) copy-start(s32[1024]{0:T(1024)S(1)} %get-tuple-element.84) | copy-start | bytes 12292
  59.2 30.0 %copy-start.19 = (s32[1024]{0:T(1024)}, s32[1024]{0:T(1024)S(1)}, u32[]{:S(2)}) copy-start(s32[1024]{0:T(1024)S(1)} %get-tuple-element.83) | copy-start | bytes 12292
  84.7 1.0 copy-start.1
  89.1 3.1 %collective-permute-start = (f32[128,256]{0,1:T(8,128)S(1)}, f32[128,256]{0,1:T(8,128)S(1)}, u32[]{:S(2)}, u32[]{:S(2)}) collective-permute-start(f32[128,256]{0,1:T(8,128)S(1)} %broadcast_multiply_fusion.4), channel_id=1, source_target_pairs={{0,1},{1,0},{2,3},{3,2},{4,5},{5,4},{6,7},{7,6},{8,9},{9,8},{10,11... | collective-permute-start | bytes 393224 | tf_op jit(solution)/shard_map/ppermute | solution.py:17
  90.0 0.7 copy-start.6
  90.6 1.6 copy-start.3
  90.6 1.6 copy-start.9
  90.7 6.0 %collective-permute-start.1 = (f32[128,256]{0,1:T(8,128)S(1)}, f32[128,256]{0,1:T(8,128)S(1)}, u32[]{:S(2)}, u32[]{:S(2)}) collective-permute-start(f32[128,256]{0,1:T(8,128)S(1)} %broadcast_multiply_fusion.2), channel_id=1, source_target_pairs={{0,2},{1,3},{2,0},{3,1},{4,6},{5,7},{6,4},{7,5},{8,10},{9,11},{10,... | collective-permute-start | bytes 393224 | tf_op jit(solution)/shard_map/ppermute | solution.py:17
  96.9 0.6 copy-start.15
  97.5 1.7 copy-start.12
  100.8 0.7 copy-start.27
  101.5 1.5 copy-start.4
  106.2 15.9 %all-to-all-start.3 = ((f32[32,1,2056]{2,1,0:T(1,128)}), f32[32,1,2056]{2,1,0:T(1,128)}, u32[]{:S(2)}, u32[]{:S(2)}) async-start(f32[32,1,2056]{2,1,0:T(1,128)} %all_to_all.29), calls=%async_computation.3 | async-start | bytes 557056 | tf_op jit(solution)/shard_map/all_to_all | solution.py:81
  111.6 1.0 copy-start.2
  114.4 1.0 copy-start.10
  116.6 12.2 %collective-permute-start.2 = (f32[128,256]{0,1:T(8,128)S(1)}, f32[128,256]{0,1:T(8,128)}, u32[]{:S(2)}, u32[]{:S(2)}) collective-permute-start(f32[128,256]{0,1:T(8,128)S(1)} %convolution_bitcast_fusion.1), channel_id=1, source_target_pairs={{0,1},{1,0},{2,3},{3,2},{4,5},{5,4},{6,7},{7,6},{8,9},{9,8},{10,11... | collective-permute-start | bytes 393224 | tf_op jit(solution)/shard_map/ppermute | solution.py:17
  116.9 0.7 copy-start.23
  118.9 1.2 copy-start.7
  120.3 9.4 %collective-permute-start.3 = (f32[128,256]{0,1:T(8,128)S(1)}, f32[128,256]{0,1:T(8,128)S(1)}, u32[]{:S(2)}, u32[]{:S(2)}) collective-permute-start(f32[128,256]{0,1:T(8,128)S(1)} %convolution_bitcast_fusion), channel_id=1, source_target_pairs={{0,2},{1,3},{2,0},{3,1},{4,6},{5,7},{6,4},{7,5},{8,10},{9,11},{10,... | collective-permute-start | bytes 393224 | tf_op jit(solution)/shard_map/ppermute | solution.py:17
  124.1 15.7 %all-to-all-start.4 = ((f32[32,1,2056]{2,1,0:T(1,128)}), f32[32,1,2056]{2,1,0:T(1,128)S(1)}, u32[]{:S(2)}, u32[]{:S(2)}) async-start(f32[32,1,2056]{2,1,0:T(1,128)} %broadcast_in_dim.17), calls=%async_computation.4 | async-start | bytes 557056 | tf_op jit(solution)/shard_map/all_to_all | solution.py:83
  129.8 0.6 copy-start.16
  130.4 1.5 copy-start.13
  131.9 1.5 copy-start.5
  138.1 5.8 %copy-start.18 = (s32[512]{0:T(512)S(1)}, s32[512]{0:T(512)}, u32[]{:S(2)}) copy-start(s32[512]{0:T(512)} %copy-done.17) | copy-start | bytes 6148
  139.8 30.4 %all-to-all-start.2 = ((f32[32,32,256]{2,1,0:T(8,128)}), f32[32,32,256]{2,1,0:T(8,128)S(1)}, u32[]{:S(2)}, u32[]{:S(2)}) async-start(f32[32,32,256]{2,1,0:T(8,128)} %broadcast_multiply_fusion), calls=%async_computation.2 | async-start | bytes 2097152 | tf_op jit(solution)/shard_map/all_to_all | solution.py:156

commit v2 on v1

--- a/solution.py
+++ b/solution.py
@@ -106,39 +106,27 @@
     capacity = 2 * row_count // devices
     target = owner_slot // row_count
     within = owner_slot % row_count
-    sorting = jnp.argsort(target, stable=True)
-    sorted_target = target[sorting]
-    per_peer = jnp.sum(
-        (target[:, None] == jnp.arange(devices, dtype=jnp.int32)[None, :]).astype(jnp.int32), axis=0
-    )
-    starts = jnp.cumsum(per_peer) - per_peer
-    ranked = (
-        jnp.zeros((row_count,), jnp.int32)
-        .at[sorting]
-        .set(jnp.arange(row_count, dtype=jnp.int32) - starts[sorted_target])
-    )
+    hit = target[:, None] == jnp.arange(devices, dtype=jnp.int32)[None, :]
+    order = jnp.arange(row_count, dtype=jnp.int32)
+    earlier = (order[:, None] > order[None, :]).astype(jnp.bfloat16)
+    before = jnp.dot(earlier, hit.astype(jnp.bfloat16), preferred_element_type=jnp.float32)
+    ranked = jnp.sum(jnp.where(hit, before, 0.0), axis=1).astype(jnp.int32)
     bucket = target * capacity + ranked
-    outbox = jnp.zeros((devices * capacity, feat_count), jnp.float32).at[bucket].set(x_scan)
-    places = jnp.full((devices * capacity,), row_count, jnp.int32).at[bucket].set(within)
-    inbox, place_in = (
-        lax.all_to_all(
-            outbox.reshape(devices, capacity, feat_count),
-            ("row", "col"),
-            split_axis=0,
-            concat_axis=0,
-            tiled=True,
-        ),
-        lax.all_to_all(
-            places.reshape(devices, capacity),
-            ("row", "col"),
-            split_axis=0,
-            concat_axis=0,
-            tiled=True,
-        ),
-    )
-    inbox = inbox.reshape(-1, feat_count)
-    place_in = place_in.reshape(-1)
-    hidden = jnp.zeros((row_count, feat_count), jnp.float32).at[place_in].set(inbox, mode="drop")
+    slots = jnp.arange(devices * capacity, dtype=jnp.int32)
+    chosen = bucket[None, :] == slots[:, None]
+    source = jnp.sum(jnp.where(chosen, order[None, :] + 1, 0), axis=1) - 1
+    filled = source >= 0
+    places = jnp.where(filled, within[jnp.maximum(source, 0)], row_count)
+    place_in = lax.all_to_all(
+        places.reshape(devices, capacity), ("row", "col"), 0, 0, tiled=True
+    ).reshape(-1)
+    outbox = x_scan[jnp.maximum(source, 0)]
+    inbox = lax.all_to_all(
+        outbox.reshape(devices, capacity, feat_count), ("row", "col"), 0, 0, tiled=True
+    ).reshape(-1, feat_count)
+    landing = place_in[None, :] == order[:, None]
+    arrival = jnp.sum(jnp.where(landing, slots[None, :], 0), axis=1)
+    hidden = inbox[arrival]
     aggregate = hidden + interior(hidden, tile_values[0], tile_coords[0], counts[0, 0], False)
     aggregate = boundary_forward(aggregate, hidden, boundary_rows, coupling, counts)
     activation, pullback = jax.vjp(layer_piece, aggregate, weight, norm_gain)
@@ -151,8 +139,7 @@
         + interior(grad_agg, tile_values[0], tile_coords[0], counts[0, 0], True)
     )
     grad_nodes = boundary_backward(grad_nodes, grad_agg, boundary_rows, coupling, counts)
-    valid = (place_in < row_count).astype(jnp.float32)[:, None]
-    reply = grad_nodes[jnp.minimum(place_in, row_count - 1)] * valid
+    reply = grad_nodes[jnp.minimum(place_in, row_count - 1)]
     returned = lax.all_to_all(
         reply.reshape(devices, capacity, feat_count),
         ("row", "col"),

time: 173 us -> 146 us (0.84)
  other arithmetic: 45.1 us -> 16.6 us
  local copies, waits for them, and re-layouts: 40.8 us -> 29.6 us
  waiting for transfers between devices: 51.7 us -> 62.6 us
    sub x2 -> x0, other arithmetic: 15.8 us -> none  [the longest x1 15.8 us: on_device(): jnp.arange(row_count, dtype=jnp.int32) - starts[sorted_target]]
    scatter x4 -> x0, local copies, waits for them, and re-layouts: 13.5 us -> none  [the longest x1 4.92 us: on_device(): jnp.zeros((row_count, feat_count), jnp.float32).at[place_in]]
    gather x4, local copies, waits for them, and re-layouts: 8.4 us -> 17.8 us  [the longest x1 6.87 us: on_device(): places = jnp.where(filled, within[jnp.maximum(source, 0)], row_count)]
    ppermute x4, waiting for transfers between devices: 4.02 us -> 9.81 us  [swapped(): lax.ppermute(array, axis, [(i, i ^ 1 << apart) for i in range(lax.axis_si...]
    gather x4 -> x3, other arithmetic: 5.06 us -> 0.02 us  [the longest x1 0.01 us: on_device(): outbox = x_scan[jnp.maximum(source, 0)]]
    unnamed x56 -> x20, local copies, waits for them, and re-layouts: 5.4 us -> 0.47 us
    all_to_all x1, waiting for transfers between devices: 0.01 us -> 4.49 us  [summed_everywhere(): gathered = lax.all_to_all(pieces, ('row', 'col'), 0, 0, tiled=True)]
    all_to_all x1, waiting for transfers between devices: 18.6 us -> 22.4 us  [on_device(): lax.all_to_all(outbox.reshape(devices, capacity, feat_count), ('row', 'co...]
  transfers between devices with their start and end apart: 9 -> 9, of which waited for: 5 -> 6; matrix products, arithmetic and copies ran while one was open for 19% -> 19% of each run, Pallas kernels for 0% -> 0%
where the time goes in v2:
time: 146 us
  waiting for transfers between devices  62.6 us (43%)
  local copies, waits for them, and re-layouts  29.6 us (20%)
  starting transfers between devices  26.6 us (18%)
  other arithmetic  16.6 us (11%)
  matrix products  9.09 us (6%)
    all_to_all x1, waiting for transfers between devices, on_device(): lax.all_to_all(reply.reshape(devices, capacity, feat_count), ('row', 'col...  24.1 us
    all_to_all x1, waiting for transfers between devices, on_device(): lax.all_to_all(outbox.reshape(devices, capacity, feat_count), ('row', 'co...  22.4 us
    ppermute x4, waiting for transfers between devices, swapped(): lax.ppermute(array, axis, [(i, i ^ 1 << apart) for i in range(lax.axis_si...  9.81 us
    all_to_all x1, starting transfers between devices, on_device(): lax.all_to_all(places.reshape(devices, capacity), ('row', 'col'), 0, 0, t...  7.3 us
    gather x1, local copies, waits for them, and re-layouts, on_device(): places = jnp.where(filled, within[jnp.maximum(source, 0)], row_count)  6.87 us
    all_to_all x1, starting transfers between devices, on_device(): lax.all_to_all(reply.reshape(devices, capacity, feat_count), ('row', 'col...  5.41 us
    gather x1, local copies, waits for them, and re-layouts, on_device(): reply = grad_nodes[jnp.minimum(place_in, row_count - 1)]  4.67 us
    gather x1, local copies, waits for them, and re-layouts, on_device(): outbox = x_scan[jnp.maximum(source, 0)]  4.66 us
  transfers between devices with their start and end apart: 9, of which 6 were waited for; matrix products, arithmetic and copies ran while one was open for 19% of the time, Pallas kernels for 0%

profile of v2, /device:TPU:0, one launch (start us, length us, event | category | flops | bytes accessed | tf_op | source)
XLA Modules:
  0.0 145.7 jit_solution(13988202358943078924)
XLA Ops:
  0.6 0.7 add_select_fusion
  1.4 0.3 fusion.2
  1.7 0.3 select_reduce_fusion.1
  2.0 6.9 %gather_fusion.1 = s32[1024]{0:T(1024)S(1)} fusion(s32[512]{0:T(512)S(1)} %get-tuple-element.10, s32[1024]{0:T(1024)S(1)} %maximum_clamp_fusion), kind=kCustom, calls=%fused_computation.1 | custom fusion | bytes 12288 | tf_op jit(solution)/shard_map/gather | solution.py:119
  8.9 0.7 select_n.105
  9.6 7.3 %all-to-all-start.1 = ((s32[32,1,32]{2,1,0:T(1,128)}), s32[32,1,32]{2,1,0:T(1,128)S(1)}, u32[]{:S(2)}, u32[]{:S(2)}) async-start(s32[32,1,32]{2,1,0:T(1,128)} %select_n.105), calls=%async_computation.1 | async-start | bytes 32768 | tf_op jit(solution)/shard_map/all_to_all | solution.py:120
  16.9 0.6 fusion.41
  17.5 4.7 %gather_fusion = f32[1024,256]{1,0:T(8,128)} fusion(f32[512,256]{1,0:T(8,128)S(1)} %copy-done, s32[1024]{0:T(1024)S(1)} %maximum_clamp_fusion), kind=kCustom, calls=%fused_computation | custom fusion | bytes 2101248 | tf_op jit(solution)/shard_map/gather | solution.py:123
  22.2 1.8 %all-to-all-done.1 = s32[32,1,32]{2,1,0:T(1,128)S(1)} async-done(((s32[32,1,32]{2,1,0:T(1,128)}), s32[32,1,32]{2,1,0:T(1,128)S(1)}, u32[]{:S(2)}, u32[]{:S(2)}) %all-to-all-start.1) | async-done | bytes 4128 | tf_op jit(solution)/shard_map/all_to_all | solution.py:120
  24.0 4.0 %all-to-all-start = ((f32[32,32,256]{2,1,0:T(8,128)}), f32[32,32,256]{2,1,0:T(8,128)S(1)}, u32[]{:S(2)}, u32[]{:S(2)}) async-start(f32[32,32,256]{2,1,0:T(8,128)} %bitcast), calls=%async_computation | async-start | bytes 2097152 | tf_op jit(solution)/shard_map/all_to_all | solution.py:124
  28.0 0.7 compare_convert_fusion.2
  28.7 0.7 compare_convert_fusion.1
  29.3 0.7 compare_convert_fusion
  30.1 0.5 broadcast.314
  30.6 0.7 minimum_reduce_fusion
  31.5 0.3 select_reduce_fusion
  31.8 22.4 %all-to-all-done = f32[32,32,256]{2,1,0:T(8,128)S(1)} async-done(((f32[32,32,256]{2,1,0:T(8,128)}), f32[32,32,256]{2,1,0:T(8,128)S(1)}, u32[]{:S(2)}, u32[]{:S(2)}) %all-to-all-start) | async-done | bytes 1048608 | tf_op jit(solution)/shard_map/all_to_all | solution.py:124
  54.2 1.6 %gather_fusion.2 = f32[512,256]{1,0:T(8,128)S(1)} fusion(f32[1024,256]{1,0:T(8,128)S(1)} %bitcast.61, s32[1024]{0:T(1024)S(1)} %pad_clamp_fusion.5), kind=kCustom, calls=%fused_computation.2 | custom fusion | bytes 1050624 | tf_op jit(solution)/shard_map/gather | solution.py:129
  55.8 0.6 gather_fusion.3
  56.4 2.1 %fusion.6 = f32[8,128,256]{2,1,0:T(8,128)S(1)} fusion(f32[8,128,256]{2,1,0:T(8,128)S(1)} %gather_fusion.3, f32[1,8,128,128]{3,2,1,0:T(8,128)} %param.14, f32[8]{0:T(128)S(1)} %compare_convert_fusion.2), kind=kOutput, calls=%fused_computation.43 | convolution fusion | flops 402784256 | bytes 2621472 | tf_op jit(solution)/shard_map/tij,tjf->tif/dot_general | solution.py:37
  58.6 1.3 scatter_fusion
  60.0 0.8 gather_fusion.4
  61.0 0.8 gather_fusion.5
  61.9 1.5 %collective-permute-start.1 = (f32[128,256]{0,1:T(8,128)S(1)}, f32[128,256]{0,1:T(8,128)S(1)}, u32[]{:S(2)}, u32[]{:S(2)}) collective-permute-start(f32[128,256]{0,1:T(8,128)S(1)} %broadcast_multiply_fusion.1), channel_id=1, source_target_pairs={{0,2},{1,3},{2,0},{3,1},{4,6},{5,7},{6,4},{7,5},{8,10},{9,11},{10,... | collective-permute-start | bytes 393224 | tf_op jit(solution)/shard_map/ppermute | solution.py:17
  63.4 0.3 fusion.1
  63.7 0.1 copy.43
  63.8 4.0 %collective-permute-done.1 = f32[128,256]{0,1:T(8,128)S(1)} collective-permute-done((f32[128,256]{0,1:T(8,128)S(1)}, f32[128,256]{0,1:T(8,128)S(1)}, u32[]{:S(2)}, u32[]{:S(2)}) %collective-permute-start.1) | collective-permute-done | bytes 131104 | tf_op jit(solution)/shard_map/ppermute | solution.py:17
  67.8 0.3 fusion
  68.2 1.5 %scatter_fusion.1 = f32[512,256]{1,0:T(8,128)S(1)} fusion(f32[512,256]{1,0:T(8,128)S(1)} %bitcast_add_fusion.1, s32[128]{0:T(128)S(1)} %get-tuple-element.13, f32[128,256]{1,0:T(8,128)S(1)} %copy.43), kind=kCustom, calls=%fused_computation.12 | custom fusion | flops 32768 | bytes 393728 | tf_op jit(solution)/shard_map/scatter-add | solution.py:57
  69.7 1.5 %scatter_fusion.2 = f32[512,256]{1,0:T(8,128)S(1)} fusion(f32[512,256]{1,0:T(8,128)S(1)} %scatter_fusion.1, s32[128]{0:T(128)S(1)} %get-tuple-element.12, f32[128,256]{1,0:T(8,128)S(1)} %copy.45), kind=kCustom, calls=%fused_computation.13 | custom fusion | flops 32768 | bytes 393728 | tf_op jit(solution)/shard_map/scatter-add | solution.py:57
  71.2 0.1 multiply_reduce_fusion.2
  71.4 1.5 %multiply_add_fusion = (f32[512,256]{1,0:T(8,128)}, f32[512,256]{1,0:T(8,128)S(1)}) fusion(f32[512,256]{1,0:T(8,128)S(1)} %gather_fusion.2, f32[256,256]{1,0:T(8,128)S(1)} %copy-done.9, f32[512,256]{1,0:T(8,128)S(1)} %scatter_fusion.2, f32[256]{0:T(256)S(1)} %copy-done.8, f32[512]{0:T(512)S(1)} %fusion.33), kind=kOutput, calls=%fused_computation.39 | convolution fusion | flops 403570688 | bytes 2362368 | tf_op jit(solution)/shard_map/jvp()/dot_general | solution.py:24
  72.9 1.2 fusion.7
  74.1 0.8 multiply_reduce_fusion
  74.9 0.2 add_add_fusion
  75.2 0.8 gather_fusion.7
  75.9 0.8 gather_fusion.8
  76.7 1.1 all_to_all.26
  77.8 3.8 %all-to-all-start.3 = ((f32[32,1,2056]{2,1,0:T(1,128)}), f32[32,1,2056]{2,1,0:T(1,128)S(1)}, u32[]{:S(2)}, u32[]{:S(2)}) async-start(f32[32,1,2056]{2,1,0:T(1,128)} %all_to_all.26), calls=%async_computation.3 | async-start | bytes 557056 | tf_op jit(solution)/shard_map/all_to_all | solution.py:81
  81.7 0.3 convolution_bitcast_fusion.1
  82.0 0.1 collective-permute-start.2
  82.2 0.6 gather_fusion.6
  82.9 0.4 copy-done.1
  83.3 2.1 %fusion.5 = f32[8,128,256]{2,1,0:T(8,128)} fusion(f32[8,128,256]{2,1,0:T(8,128)S(1)} %gather_fusion.6, f32[1,8,128,128]{3,2,1,0:T(8,128)S(1)} %copy-done.1, f32[8]{0:T(128)S(1)} %compare_convert_fusion.2), kind=kOutput, calls=%fused_computation.42 | convolution fusion | flops 402784256 | bytes 2621472 | tf_op jit(solution)/shard_map/tji,tjf->tif/dot_general | solution.py:37
  85.5 2.5 %scatter_fusion.3 = f32[4,128,256]{2,1,0:T(8,128)S(1)} fusion(f32[4,128,256]{2,1,0:T(8,128)S(1)} %broadcast.225, s32[8]{0:T(128)S(1)} %get-tuple-element.14, f32[8,128,256]{2,1,0:T(8,128)} %fusion.5), kind=kCustom, calls=%fused_computation.14 | custom fusion | flops 262144 | bytes 3145760 | tf_op jit(solution)/shard_map/scatter-add | solution.py:38
  87.9 0.1 bitcast_add_fusion
  88.0 4.5 %all-to-all-done.3 = f32[32,1,2056]{2,1,0:T(1,128)S(1)} async-done(((f32[32,1,2056]{2,1,0:T(1,128)}), f32[32,1,2056]{2,1,0:T(1,128)S(1)}, u32[]{:S(2)}, u32[]{:S(2)}) %all-to-all-start.3) | async-done | bytes 263200 | tf_op jit(solution)/shard_map/all_to_all | solution.py:81
  92.5 0.2 reduce_sum.80
  92.7 0.9 broadcast_in_dim.43
  93.6 2.6 %all-to-all-start.4 = ((f32[32,1,2056]{2,1,0:T(1,128)}), f32[32,1,2056]{2,1,0:T(1,128)S(1)}, u32[]{:S(2)}, u32[]{:S(2)}) async-start(f32[32,1,2056]{2,1,0:T(1,128)} %broadcast_in_dim.43), calls=%async_computation.4 | async-start | bytes 557056 | tf_op jit(solution)/shard_map/all_to_all | solution.py:83
  96.2 0.3 convolution_bitcast_fusion
  96.4 1.7 %collective-permute-start.3 = (f32[128,256]{0,1:T(8,128)S(1)}, f32[128,256]{0,1:T(8,128)S(1)}, u32[]{:S(2)}, u32[]{:S(2)}) collective-permute-start(f32[128,256]{0,1:T(8,128)S(1)} %convolution_bitcast_fusion), channel_id=1, source_target_pairs={{0,2},{1,3},{2,0},{3,1},{4,6},{5,7},{6,4},{7,5},{8,10},{9,11},{10,... | collective-permute-start | bytes 393224 | tf_op jit(solution)/shard_map/ppermute | solution.py:17
  98.1 0.1 copy.48
  98.2 5.8 %collective-permute-done.3 = f32[128,256]{0,1:T(8,128)S(1)} collective-permute-done((f32[128,256]{0,1:T(8,128)S(1)}, f32[128,256]{0,1:T(8,128)S(1)}, u32[]{:S(2)}, u32[]{:S(2)}) %collective-permute-start.3) | collective-permute-done | bytes 131104 | tf_op jit(solution)/shard_map/ppermute | solution.py:17
  104.1 1.5 %scatter_fusion.4 = f32[512,256]{1,0:T(8,128)S(1)} fusion(f32[512,256]{1,0:T(8,128)S(1)} %bitcast_add_fusion, s32[128]{0:T(128)S(1)} %get-tuple-element.13, f32[128,256]{1,0:T(8,128)S(1)} %copy.48), kind=kCustom, calls=%fused_computation.15 | custom fusion | flops 32768 | bytes 393728 | tf_op jit(solution)/shard_map/scatter-add | solution.py:73
  105.6 1.5 %scatter_fusion.5 = f32[512,256]{1,0:T(8,128)S(1)} fusion(f32[512,256]{1,0:T(8,128)S(1)} %scatter_fusion.4, s32[128]{0:T(128)S(1)} %get-tuple-element.12, f32[128,256]{1,0:T(8,128)S(1)} %copy.50), kind=kCustom, calls=%fused_computation.16 | custom fusion | flops 32768 | bytes 393728 | tf_op jit(solution)/shard_map/scatter-add | solution.py:73
  107.1 4.7 %gather_fusion.9 = f32[1024,256]{1,0:T(8,128)} fusion(f32[512,256]{1,0:T(8,128)S(1)} %scatter_fusion.5, s32[1024]{0:T(1024)S(1)} %broadcast_clamp_fusion), kind=kCustom, calls=%fused_computation.9 | custom fusion | bytes 2101248 | tf_op jit(solution)/shard_map/gather | solution.py:142
  111.8 5.4 %all-to-all-start.2 = ((f32[32,32,256]{2,1,0:T(8,128)}), f32[32,32,256]{2,1,0:T(8,128)S(1)}, u32[]{:S(2)}, u32[]{:S(2)}) async-start(f32[32,32,256]{2,1,0:T(8,128)} %bitcast.26), calls=%async_computation.2 | async-start | bytes 2097152 | tf_op jit(solution)/shard_map/all_to_all | solution.py:143
  117.2 0.7 reduce.3
  117.9 0.2 reshape.243
  118.1 0.6 slice_multiply_fusion.1
  118.7 0.7 slice_multiply_fusion
  119.4 24.1 %all-to-all-done.2 = f32[32,32,256]{2,1,0:T(8,128)S(1)} async-done(((f32[32,32,256]{2,1,0:T(8,128)}), f32[32,32,256]{2,1,0:T(8,128)S(1)}, u32[]{:S(2)}, u32[]{:S(2)}) %all-to-all-start.2) | async-done | bytes 1048608 | tf_op jit(solution)/shard_map/all_to_all | solution.py:143
  143.5 2.2 %gather_fusion.10 = f32[512,256]{1,0:T(8,128)} fusion(f32[1024,256]{1,0:T(8,128)S(1)} %bitcast.62, s32[1024]{0:T(1024)S(1)} %pad_clamp_fusion), kind=kCustom, calls=%fused_computation.10 | custom fusion | bytes 1050624 | tf_op jit(solution)/shard_map/gather | solution.py:150
  (53 shorter events, 1.1 us)
Async XLA Ops:
  0.6 16.9 %copy-start = (f32[512,256]{1,0:T(8,128)S(1)}, f32[512,256]{1,0:T(8,128)}, u32[]{:S(2)}) copy-start(f32[512,256]{1,0:T(8,128)} %param.10) | copy-start | bytes 1572868
  2.0 14.9 %copy-start.5 = (s32[1,3]{1,0:T(1,128)S(1)}, s32[1,3]{1,0:T(1,128)}, u32[]{:S(2)}) copy-start(s32[1,3]{1,0:T(1,128)} %param.16) | copy-start | bytes 40
  9.6 14.4 %all-to-all-start.1 = ((s32[32,1,32]{2,1,0:T(1,128)}), s32[32,1,32]{2,1,0:T(1,128)S(1)}, u32[]{:S(2)}, u32[]{:S(2)}) async-start(s32[32,1,32]{2,1,0:T(1,128)} %select_n.105), calls=%async_computation.1 | async-start | bytes 32768 | tf_op jit(solution)/shard_map/all_to_all | solution.py:120
  24.0 6.0 %copy-start.6 = (s32[1,8,2]{1,2,0:T(2,128)S(1)}, s32[1,8,2]{1,2,0:T(2,128)}, u32[]{:S(2)}) copy-start(s32[1,8,2]{1,2,0:T(2,128)} %param.15) | copy-start | bytes 196
  24.0 6.1 %copy-start.7 = (s32[1,2,128]{2,1,0:T(2,128)S(1)}, s32[1,2,128]{2,1,0:T(2,128)}, u32[]{:S(2)}) copy-start(s32[1,2,128]{2,1,0:T(2,128)} %param.17) | copy-start | bytes 3076
  24.0 30.3 %all-to-all-start = ((f32[32,32,256]{2,1,0:T(8,128)}), f32[32,32,256]{2,1,0:T(8,128)S(1)}, u32[]{:S(2)}, u32[]{:S(2)}) async-start(f32[32,32,256]{2,1,0:T(8,128)} %bitcast), calls=%async_computation | async-start | bytes 2097152 | tf_op jit(solution)/shard_map/all_to_all | solution.py:124
  60.9 2.5 %copy-start.2 = (f32[1,2,128,128]{3,2,1,0:T(8,128)S(1)}, f32[1,2,128,128]{3,2,1,0:T(8,128)}, u32[]{:S(2)}) copy-start(f32[1,2,128,128]{3,2,1,0:T(8,128)} %param.18) | copy-start | bytes 393220
  60.9 2.5 %collective-permute-start = (f32[128,256]{0,1:T(8,128)S(1)}, f32[128,256]{0,1:T(8,128)S(1)}, u32[]{:S(2)}, u32[]{:S(2)}) collective-permute-start(f32[128,256]{0,1:T(8,128)S(1)} %broadcast_multiply_fusion.3), channel_id=1, source_target_pairs={{0,1},{1,0},{2,3},{3,2},{4,5},{5,4},{6,7},{7,6},{8,9},{9,8},{10,11... | collective-permute-start | bytes 393224 | tf_op jit(solution)/shard_map/ppermute | solution.py:17
  61.9 6.0 %collective-permute-start.1 = (f32[128,256]{0,1:T(8,128)S(1)}, f32[128,256]{0,1:T(8,128)S(1)}, u32[]{:S(2)}, u32[]{:S(2)}) collective-permute-start(f32[128,256]{0,1:T(8,128)S(1)} %broadcast_multiply_fusion.1), channel_id=1, source_target_pairs={{0,2},{1,3},{2,0},{3,1},{4,6},{5,7},{6,4},{7,5},{8,10},{9,11},{10,... | collective-permute-start | bytes 393224 | tf_op jit(solution)/shard_map/ppermute | solution.py:17
  69.7 1.7 %copy-start.8 = (f32[256]{0:T(256)S(1)}, f32[256]{0:T(256)}, u32[]{:S(2)}) copy-start(f32[256]{0:T(256)} %param.13) | copy-start | bytes 3076
  69.7 1.7 %copy-start.9 = (f32[256,256]{1,0:T(8,128)S(1)}, f32[256,256]{1,0:T(8,128)}, u32[]{:S(2)}) copy-start(f32[256,256]{1,0:T(8,128)} %param.12) | copy-start | bytes 786436
  71.4 1.5 %copy-start.3 = (f32[512,256]{1,0:T(8,128)S(1)}, f32[512,256]{1,0:T(8,128)}, u32[]{:S(2)}) copy-start(f32[512,256]{1,0:T(8,128)} %param.19) | copy-start | bytes 1572868
  77.8 14.7 %all-to-all-start.3 = ((f32[32,1,2056]{2,1,0:T(1,128)}), f32[32,1,2056]{2,1,0:T(1,128)S(1)}, u32[]{:S(2)}, u32[]{:S(2)}) async-start(f32[32,1,2056]{2,1,0:T(1,128)} %all_to_all.26), calls=%async_computation.3 | async-start | bytes 557056 | tf_op jit(solution)/shard_map/all_to_all | solution.py:81
  82.0 16.1 %collective-permute-start.2 = (f32[128,256]{0,1:T(8,128)S(1)}, f32[128,256]{0,1:T(8,128)S(1)}, u32[]{:S(2)}, u32[]{:S(2)}) collective-permute-start(f32[128,256]{0,1:T(8,128)S(1)} %convolution_bitcast_fusion.1), channel_id=1, source_target_pairs={{0,1},{1,0},{2,3},{3,2},{4,5},{5,4},{6,7},{7,6},{8,9},{9,8},{10,11... | collective-permute-start | bytes 393224 | tf_op jit(solution)/shard_map/ppermute | solution.py:17
  82.2 1.0 copy-start.1
  85.4 2.5 %copy-start.4 = (f32[512,256]{1,0:T(8,128)S(1)}, f32[512,256]{1,0:T(8,128)}, u32[]{:S(2)}) copy-start(f32[512,256]{1,0:T(8,128)} %param.19) | copy-start | bytes 1572868
  93.6 18.3 %all-to-all-start.4 = ((f32[32,1,2056]{2,1,0:T(1,128)}), f32[32,1,2056]{2,1,0:T(1,128)S(1)}, u32[]{:S(2)}, u32[]{:S(2)}) async-start(f32[32,1,2056]{2,1,0:T(1,128)} %broadcast_in_dim.43), calls=%async_computation.4 | async-start | bytes 557056 | tf_op jit(solution)/shard_map/all_to_all | solution.py:83
  96.4 7.6 %collective-permute-start.3 = (f32[128,256]{0,1:T(8,128)S(1)}, f32[128,256]{0,1:T(8,128)S(1)}, u32[]{:S(2)}, u32[]{:S(2)}) collective-permute-start(f32[128,256]{0,1:T(8,128)S(1)} %convolution_bitcast_fusion), channel_id=1, source_target_pairs={{0,2},{1,3},{2,0},{3,1},{4,6},{5,7},{6,4},{7,5},{8,10},{9,11},{10,... | collective-permute-start | bytes 393224 | tf_op jit(solution)/shard_map/ppermute | solution.py:17
  111.8 31.7 %all-to-all-start.2 = ((f32[32,32,256]{2,1,0:T(8,128)}), f32[32,32,256]{2,1,0:T(8,128)S(1)}, u32[]{:S(2)}, u32[]{:S(2)}) async-start(f32[32,32,256]{2,1,0:T(8,128)} %bitcast.26), calls=%async_computation.2 | async-start | bytes 2097152 | tf_op jit(solution)/shard_map/all_to_all | solution.py:143

commit v3 on v2

--- a/solution.py
+++ b/solution.py
@@ -7,10 +7,15 @@
 
 BLOCK = 128
 ROUNDS = 2
+HALVES = 2
 
 
 EPS = 1e-05
 PRECISE = lax.Precision.HIGHEST
+
+
+def pl_cdiv(a, b):
+    return -(-a // b)
 
 
 def swapped(array, axis, apart):
@@ -117,36 +122,58 @@
     source = jnp.sum(jnp.where(chosen, order[None, :] + 1, 0), axis=1) - 1
     filled = source >= 0
     places = jnp.where(filled, within[jnp.maximum(source, 0)], row_count)
-    place_in = lax.all_to_all(
-        places.reshape(devices, capacity), ("row", "col"), 0, 0, tiled=True
-    ).reshape(-1)
     outbox = x_scan[jnp.maximum(source, 0)]
-    inbox = lax.all_to_all(
-        outbox.reshape(devices, capacity, feat_count), ("row", "col"), 0, 0, tiled=True
-    ).reshape(-1, feat_count)
-    landing = place_in[None, :] == order[:, None]
-    arrival = jnp.sum(jnp.where(landing, slots[None, :], 0), axis=1)
-    hidden = inbox[arrival]
-    aggregate = hidden + interior(hidden, tile_values[0], tile_coords[0], counts[0, 0], False)
-    aggregate = boundary_forward(aggregate, hidden, boundary_rows, coupling, counts)
+    width = feat_count // HALVES
+    lanes = 128 * pl_cdiv(capacity, 128)
+    tags = jnp.zeros((devices, lanes), jnp.float32).at[:, :capacity].set(
+        places.reshape(devices, capacity).astype(jnp.float32)
+    )
+    hidden_parts, agg_parts = [], []
+    arrival = None
+    for half in range(HALVES):
+        piece = outbox[:, half * width : (half + 1) * width].reshape(devices, capacity * width)
+        if half == 0:
+            piece = jnp.concatenate([piece, tags], axis=1)
+        got = lax.all_to_all(piece, ("row", "col"), 0, 0, tiled=True)
+        if agg_parts:
+            got, agg_parts[-1] = lax.optimization_barrier((got, agg_parts[-1]))
+        if half == 0:
+            place_in = got[:, capacity * width : capacity * width + capacity]
+            place_in = place_in.astype(jnp.int32).reshape(-1)
+            landing = place_in[None, :] == order[:, None]
+            arrival = jnp.sum(jnp.where(landing, slots[None, :], 0), axis=1)
+        inbox = got[:, : capacity * width].reshape(devices * capacity, width)
+        part = inbox[arrival]
+        total = part + interior(part, tile_values[0], tile_coords[0], counts[0, 0], False)
+        total = boundary_forward(total, part, boundary_rows, coupling, counts)
+        hidden_parts.append(part)
+        agg_parts.append(total)
+    hidden = jnp.concatenate(hidden_parts, axis=1)
+    aggregate = jnp.concatenate(agg_parts, axis=1)
     activation, pullback = jax.vjp(layer_piece, aggregate, weight, norm_gain)
     output = hidden + activation
     grad_agg, grad_weight, grad_gain = pullback(cotangent)
     weight_sum, gain_sum = summed_everywhere(grad_weight, grad_gain, devices)
-    grad_nodes = (
-        cotangent
-        + grad_agg
-        + interior(grad_agg, tile_values[0], tile_coords[0], counts[0, 0], True)
-    )
-    grad_nodes = boundary_backward(grad_nodes, grad_agg, boundary_rows, coupling, counts)
-    reply = grad_nodes[jnp.minimum(place_in, row_count - 1)]
-    returned = lax.all_to_all(
-        reply.reshape(devices, capacity, feat_count),
-        ("row", "col"),
-        split_axis=0,
-        concat_axis=0,
-        tiled=True,
-    )
+    back_index = jnp.minimum(place_in, row_count - 1)
+    returned_parts = []
+    for half in range(HALVES):
+        cols = slice(half * width, (half + 1) * width)
+        grad_part = grad_agg[:, cols]
+        nodes = (
+            cotangent[:, cols]
+            + grad_part
+            + interior(grad_part, tile_values[0], tile_coords[0], counts[0, 0], True)
+        )
+        nodes = boundary_backward(nodes, grad_part, boundary_rows, coupling, counts)
+        if returned_parts:
+            returned_parts[-1], nodes = lax.optimization_barrier((returned_parts[-1], nodes))
+        reply = nodes[back_index]
+        returned_parts.append(
+            lax.all_to_all(
+                reply.reshape(devices, capacity, width), ("row", "col"), 0, 0, tiled=True
+            )
+        )
+    returned = jnp.concatenate(returned_parts, axis=2)
     x_grad = returned.reshape(-1, feat_count)[bucket]
     node_scale = 1.0 / math.sqrt(row_count * devices)
     return (output, x_grad, weight_sum * node_scale, gain_sum * node_scale)

time: 146 us -> 163 us (1.12)
  other arithmetic: 16.6 us -> 28.4 us
  waiting for transfers between devices: 62.6 us -> 52.9 us
  local copies, waits for them, and re-layouts: 29.6 us -> 38.8 us
  starting transfers between devices: 26.6 us -> 30.3 us
    ppermute x4 -> x8, waiting for transfers between devices: 9.81 us -> 3.35 us  [swapped(): lax.ppermute(array, axis, [(i, i ^ 1 << apart) for i in range(lax.axis_si...]
    all_to_all x1, waiting for transfers between devices: 4.49 us -> 0.01 us  [summed_everywhere(): gathered = lax.all_to_all(pieces, ('row', 'col'), 0, 0, tiled=True)]
    all_to_all x1, waiting for transfers between devices: 0.01 us -> 4.11 us  [summed_everywhere(): lax.all_to_all(jnp.broadcast_to(chunk, pieces.shape), ('row', 'col'), 0,...]
    gather x2 -> x4, local copies, waits for them, and re-layouts: 6.24 us -> 10.1 us  [the longest x2 8.07 us: on_device(): reply = nodes[back_index]]
    all_to_all x3 -> x4, waiting for transfers between devices: 48.3 us -> 45.4 us  [the longest x2 27.8 us: on_device(): lax.all_to_all(reply.reshape(devices, capacity, width), ('row', 'col'), 0...]
    scatter-add x2 -> x4, other arithmetic: 2.98 us -> 5.65 us  [boundary_forward(): total = total.at[picked].add(contrib)]
    scatter-add x2 -> x4, other arithmetic: 2.98 us -> 5.47 us  [boundary_backward(): total = total.at[picked].add(received * own_mask)]
    all_to_all x3 -> x4, starting transfers between devices: 16.7 us -> 18.7 us  [the longest x2 10.4 us: on_device(): got = lax.all_to_all(piece, ('row', 'col'), 0, 0, tiled=True)]
  transfers between devices with their start and end apart: 9 -> 14, of which waited for: 6 -> 7; matrix products, arithmetic and copies ran while one was open for 19% -> 28% of each run, Pallas kernels for 0% -> 0%
where the time goes in v3:
time: 163 us
  waiting for transfers between devices  52.9 us (32%)
  local copies, waits for them, and re-layouts  38.8 us (24%)
  starting transfers between devices  30.3 us (19%)
  other arithmetic  28.4 us (17%)
  matrix products  10.5 us (6%)
  between operations  1.76 us (1%)
    all_to_all x2, waiting for transfers between devices, on_device(): lax.all_to_all(reply.reshape(devices, capacity, width), ('row', 'col'), 0...  27.8 us
    all_to_all x2, waiting for transfers between devices, on_device(): got = lax.all_to_all(piece, ('row', 'col'), 0, 0, tiled=True)  17.6 us
    all_to_all x2, starting transfers between devices, on_device(): got = lax.all_to_all(piece, ('row', 'col'), 0, 0, tiled=True)  10.4 us
    all_to_all x2, starting transfers between devices, on_device(): lax.all_to_all(reply.reshape(devices, capacity, width), ('row', 'col'), 0...  8.37 us
    gather x2, local copies, waits for them, and re-layouts, on_device(): reply = nodes[back_index]  8.07 us
    gather x1, local copies, waits for them, and re-layouts, on_device(): places = jnp.where(filled, within[jnp.maximum(source, 0)], row_count)  6.87 us
    scatter-add x4, other arithmetic, boundary_forward(): total = total.at[picked].add(contrib)  5.65 us
    scatter-add x4, other arithmetic, boundary_backward(): total = total.at[picked].add(received * own_mask)  5.47 us
  transfers between devices with their start and end apart: 14, of which 7 were waited for; matrix products, arithmetic and copies ran while one was open for 28% of the time, Pallas kernels for 0%

profile of v3, /device:TPU:0, one launch (start us, length us, event | category | flops | bytes accessed | tf_op | source)
XLA Modules:
  0.0 162.5 jit_solution(774297704994460174)
XLA Ops:
  0.6 0.7 add_select_fusion
  2.6 3.5 %gather_fusion = f32[1024,256]{1,0:T(8,128)S(1)} fusion(f32[512,256]{1,0:T(8,128)S(1)} %copy-done, s32[1024]{0:T(1024)S(1)} %maximum_clamp_fusion), kind=kCustom, calls=%fused_computation | custom fusion | bytes 2101248 | tf_op jit(solution)/shard_map/gather | solution.py:125
  6.0 0.9 fusion.59
  6.9 7.3 %all-to-all-start.1 = ((f32[32,1,4096]{2,1,0:T(1,128)}), f32[32,1,4096]{2,1,0:T(1,128)S(1)}, u32[]{:S(2)}, u32[]{:S(2)}) async-start(f32[32,1,4096]{2,1,0:T(1,128)} %bitcast.2), calls=%async_computation.1 | async-start | bytes 1048576 | tf_op jit(solution)/shard_map/all_to_all | solution.py:137
  14.2 6.9 %gather_fusion.1 = s32[1024]{0:T(1024)S(1)} fusion(s32[512]{0:T(512)S(1)} %get-tuple-element.34, s32[1024]{0:T(1024)S(1)} %maximum_clamp_fusion), kind=kCustom, calls=%fused_computation.1 | custom fusion | bytes 12288 | tf_op jit(solution)/shard_map/gather | solution.py:124
  22.6 1.2 all_to_all.32
  23.8 6.0 %all-to-all-done.1 = f32[32,1,4096]{2,1,0:T(1,128)S(1)} async-done(((f32[32,1,4096]{2,1,0:T(1,128)}), f32[32,1,4096]{2,1,0:T(1,128)S(1)}, u32[]{:S(2)}, u32[]{:S(2)}) %all-to-all-start.1) | async-done | bytes 524320 | tf_op jit(solution)/shard_map/all_to_all | solution.py:137
  29.8 3.1 %all-to-all-start = ((f32[32,1,4224]{2,1,0:T(1,128)}), f32[32,1,4224]{2,1,0:T(1,128)S(1)}, u32[]{:S(2)}, u32[]{:S(2)}) async-start(f32[32,1,4224]{2,1,0:T(1,128)} %all_to_all.32), calls=%async_computation | async-start | bytes 1081344 | tf_op jit(solution)/shard_map/all_to_all | solution.py:137
  34.1 0.7 compare_convert_fusion.1
  37.0 11.7 %all-to-all-done = f32[32,1,4224]{2,1,0:T(1,128)S(1)} async-done(((f32[32,1,4224]{2,1,0:T(1,128)}), f32[32,1,4224]{2,1,0:T(1,128)S(1)}, u32[]{:S(2)}, u32[]{:S(2)}) %all-to-all-start) | async-done | bytes 540704 | tf_op jit(solution)/shard_map/all_to_all | solution.py:137
  50.0 1.0 gather_fusion.2
  53.2 0.7 gather_fusion.3
  54.0 0.7 fusion.16
  54.7 1.0 scatter_fusion
  55.8 1.4 collective-permute-start.1
  57.6 2.8 %collective-permute-done.1 = f32[128,128]{0,1:T(8,128)S(1)} collective-permute-done((f32[128,128]{0,1:T(8,128)S(1)}, f32[128,128]{0,1:T(8,128)S(1)}, u32[]{:S(2)}, u32[]{:S(2)}) %collective-permute-start.1) | collective-permute-done | bytes 65568 | tf_op jit(solution)/shard_map/ppermute | solution.py:22
  60.8 1.4 scatter_fusion.1
  62.2 1.4 scatter_fusion.2
  63.7 1.0 gather_fusion.6
  64.7 0.8 gather_fusion.8
  65.5 0.8 gather_fusion.9
  66.5 1.2 collective-permute-start.3
  67.6 0.7 gather_fusion.7
  68.4 0.7 fusion.15
  69.1 1.0 scatter_fusion.3
  71.5 1.4 scatter_fusion.4
  72.9 1.5 scatter_fusion.5
  74.7 1.5 maximum_add_fusion
  76.2 1.2 fusion.7
  77.4 0.8 multiply_reduce_fusion
  78.5 0.8 gather_fusion.15
  79.2 0.8 gather_fusion.16
  80.0 0.8 gather_fusion.11
  80.8 0.8 gather_fusion.12
  81.6 1.1 all_to_all.43
  82.6 3.3 %all-to-all-start.4 = ((f32[32,1,2056]{2,1,0:T(1,128)}), f32[32,1,2056]{2,1,0:T(1,128)}, u32[]{:S(2)}, u32[]{:S(2)}) async-start(f32[32,1,2056]{2,1,0:T(1,128)} %all_to_all.43), calls=%async_computation.4 | async-start | bytes 557056 | tf_op jit(solution)/shard_map/all_to_all | solution.py:86
  86.7 0.8 convolution_bitcast_fusion
  87.6 0.8 convolution_bitcast_fusion.2
  88.5 1.7 %collective-permute-start.5 = (f32[128,128]{0,1:T(8,128)}, f32[128,128]{0,1:T(8,128)}, u32[]{:S(2)}, u32[]{:S(2)}) collective-permute-start(f32[128,128]{0,1:T(8,128)} %convolution_bitcast_fusion.2), channel_id=1, source_target_pairs={{0,2},{1,3},{2,0},{3,1},{4,6},{5,7},{6,4},{7,5},{8,10},{9,11},{10,... | collective-permute-start | bytes 196616 | tf_op jit(solution)/shard_map/ppermute | solution.py:22
  91.0 0.7 gather_fusion.10
  91.7 1.1 fusion.14
  92.8 0.7 gather_fusion.14
  93.5 1.1 fusion.13
  94.7 1.0 scatter_fusion.6
  95.8 1.0 scatter_fusion.9
  96.9 0.9 broadcast_multiply_fusion
  97.9 0.9 broadcast_multiply_fusion.4
  98.9 1.4 scatter_fusion.7
  100.3 1.4 scatter_fusion.8
  101.7 4.0 %gather_fusion.13 = f32[1024,128]{1,0:T(8,128)} fusion(f32[512,128]{1,0:T(8,128)S(1)} %scatter_fusion.8, s32[1024]{0:T(1024)S(1)} %broadcast_clamp_fusion), kind=kCustom, calls=%fused_computation.13 | custom fusion | bytes 1052672 | tf_op jit(solution)/shard_map/gather | solution.py:170
  105.7 5.8 %all-to-all-start.2 = ((f32[32,32,128]{2,1,0:T(8,128)}), f32[32,32,128]{2,1,0:T(8,128)S(1)}, u32[]{:S(2)}, u32[]{:S(2)}) async-start(f32[32,32,128]{2,1,0:T(8,128)} %bitcast.29), calls=%async_computation.2 | async-start | bytes 1048576 | tf_op jit(solution)/shard_map/all_to_all | solution.py:172
  111.5 1.1 reduce_sum.80
  112.6 14.4 %all-to-all-done.2 = f32[32,32,128]{2,1,0:T(8,128)S(1)} async-done(((f32[32,32,128]{2,1,0:T(8,128)}), f32[32,32,128]{2,1,0:T(8,128)S(1)}, u32[]{:S(2)}, u32[]{:S(2)}) %all-to-all-start.2) | async-done | bytes 524320 | tf_op jit(solution)/shard_map/all_to_all | solution.py:172
  127.0 0.8 broadcast_in_dim.43
  127.9 3.1 %all-to-all-start.5 = ((f32[32,1,2056]{2,1,0:T(1,128)}), f32[32,1,2056]{2,1,0:T(1,128)S(1)}, u32[]{:S(2)}, u32[]{:S(2)}) async-start(f32[32,1,2056]{2,1,0:T(1,128)} %broadcast_in_dim.43), calls=%async_computation.5 | async-start | bytes 557056 | tf_op jit(solution)/shard_map/all_to_all | solution.py:88
  131.1 1.4 scatter_fusion.10
  132.5 1.4 scatter_fusion.11
  133.9 4.0 %gather_fusion.17 = f32[1024,128]{1,0:T(8,128)} fusion(f32[512,128]{1,0:T(8,128)S(1)} %scatter_fusion.11, s32[1024]{0:T(1024)S(1)} %broadcast_clamp_fusion), kind=kCustom, calls=%fused_computation.17 | custom fusion | bytes 1052672 | tf_op jit(solution)/shard_map/gather | solution.py:170
  137.9 4.1 %all-to-all-done.5 = f32[32,1,2056]{2,1,0:T(1,128)S(1)} async-done(((f32[32,1,2056]{2,1,0:T(1,128)}), f32[32,1,2056]{2,1,0:T(1,128)S(1)}, u32[]{:S(2)}, u32[]{:S(2)}) %all-to-all-start.5) | async-done | bytes 263200 | tf_op jit(solution)/shard_map/all_to_all | solution.py:88
  142.0 2.6 %all-to-all-start.3 = ((f32[32,32,128]{2,1,0:T(8,128)}), f32[32,32,128]{2,1,0:T(8,128)S(1)}, u32[]{:S(2)}, u32[]{:S(2)}) async-start(f32[32,32,128]{2,1,0:T(8,128)} %bitcast.34), calls=%async_computation.3 | async-start | bytes 1048576 | tf_op jit(solution)/shard_map/all_to_all | solution.py:172
  144.7 0.7 reduce.8
  146.1 0.7 slice_multiply_fusion
  146.9 13.3 %all-to-all-done.3 = f32[32,32,128]{2,1,0:T(8,128)S(1)} async-done(((f32[32,32,128]{2,1,0:T(8,128)}), f32[32,32,128]{2,1,0:T(8,128)S(1)}, u32[]{:S(2)}, u32[]{:S(2)}) %all-to-all-start.3) | async-done | bytes 524320 | tf_op jit(solution)/shard_map/all_to_all | solution.py:172
  160.3 2.2 %gather_fusion.18 = f32[512,256]{1,0:T(8,128)} fusion(f32[1024,256]{1,0:T(8,128)S(1)} %bitcast.93, s32[1024]{0:T(1024)S(1)} %pad_clamp_fusion), kind=kCustom, calls=%fused_computation.18 | custom fusion | bytes 1050624 | tf_op jit(solution)/shard_map/gather | solution.py:177
  (146 shorter events, 15.4 us)
Async XLA Ops:
  0.6 1.9 %copy-start = (f32[512,256]{1,0:T(8,128)S(1)}, f32[512,256]{1,0:T(8,128)}, u32[]{:S(2)}) copy-start(f32[512,256]{1,0:T(8,128)} %param.12) | copy-start | bytes 1572868
  6.9 22.9 %all-to-all-start.1 = ((f32[32,1,4096]{2,1,0:T(1,128)}), f32[32,1,4096]{2,1,0:T(1,128)S(1)}, u32[]{:S(2)}, u32[]{:S(2)}) async-start(f32[32,1,4096]{2,1,0:T(1,128)} %bitcast.2), calls=%async_computation.1 | async-start | bytes 1048576 | tf_op jit(solution)/shard_map/all_to_all | solution.py:137
  22.6 10.2 %copy-start.23 = (s32[1,3]{1,0:T(1,128)S(1)}, s32[1,3]{1,0:T(1,128)}, u32[]{:S(2)}) copy-start(s32[1,3]{1,0:T(1,128)} %param.18) | copy-start | bytes 40
  22.6 12.8 %copy-start.24 = (s32[1,8,2]{1,2,0:T(2,128)S(1)}, s32[1,8,2]{1,2,0:T(2,128)}, u32[]{:S(2)}) copy-start(s32[1,8,2]{1,2,0:T(2,128)} %param.17) | copy-start | bytes 196
  22.6 12.8 %copy-start.25 = (s32[1,2,128]{2,1,0:T(2,128)S(1)}, s32[1,2,128]{2,1,0:T(2,128)}, u32[]{:S(2)}) copy-start(s32[1,2,128]{2,1,0:T(2,128)} %param.19) | copy-start | bytes 3076
  29.8 18.9 %all-to-all-start = ((f32[32,1,4224]{2,1,0:T(1,128)}), f32[32,1,4224]{2,1,0:T(1,128)S(1)}, u32[]{:S(2)}, u32[]{:S(2)}) async-start(f32[32,1,4224]{2,1,0:T(1,128)} %all_to_all.32), calls=%async_computation | async-start | bytes 1081344 | tf_op jit(solution)/shard_map/all_to_all | solution.py:137
  35.4 18.5 %copy-start.13 = (f32[8]{0:T(128)}, f32[8]{0:T(128)S(1)}, u32[]{:S(2)}) copy-start(f32[8]{0:T(128)S(1)} %compare_convert_fusion.2) | copy-start | bytes 100
  35.5 13.3 %copy-start.16 = (s32[8]{0:T(128)}, s32[8]{0:T(128)S(1)}, u32[]{:S(2)}) copy-start(s32[8]{0:T(128)S(1)} %get-tuple-element.38) | copy-start | bytes 100
  35.5 13.3 %copy-start.19 = (s32[8]{0:T(128)}, s32[8]{0:T(128)S(1)}, u32[]{:S(2)}) copy-start(s32[8]{0:T(128)S(1)} %get-tuple-element.39) | copy-start | bytes 100
  35.5 13.3 %copy-start.5 = (s32[128]{0:T(128)}, s32[128]{0:T(128)S(1)}, u32[]{:S(2)}) copy-start(s32[128]{0:T(128)S(1)} %get-tuple-element.37) | copy-start | bytes 1540
  36.1 15.0 %copy-start.11 = (s32[1024]{0:T(1024)}, s32[1024]{0:T(1024)S(1)}, u32[]{:S(2)}) copy-start(s32[1024]{0:T(1024)S(1)} %get-tuple-element.52) | copy-start | bytes 12292
  36.7 15.1 %copy-start.12 = (s32[1024]{0:T(1024)}, s32[1024]{0:T(1024)S(1)}, u32[]{:S(2)}) copy-start(s32[1024]{0:T(1024)S(1)} %get-tuple-element.53) | copy-start | bytes 12292
  50.0 1.1 copy-start.9
  51.7 2.2 %copy-start.1 = (f32[1,8,128,128]{3,2,1,0:T(8,128)S(1)}, f32[1,8,128,128]{3,2,1,0:T(8,128)}, u32[]{:S(2)}) copy-start(f32[1,8,128,128]{3,2,1,0:T(8,128)} %param.16) | copy-start | bytes 1572868
  53.2 4.1 %collective-permute-start = (f32[128,128]{0,1:T(8,128)}, f32[128,128]{0,1:T(8,128)S(1)}, u32[]{:S(2)}, u32[]{:S(2)}) collective-permute-start(f32[128,128]{0,1:T(8,128)} %broadcast_multiply_fusion.7), channel_id=1, source_target_pairs={{0,1},{1,0},{2,3},{3,2},{4,5},{5,4},{6,7},{7,6},{8,9},{9,8},{10,11... | collective-permute-start | bytes 196616 | tf_op jit(solution)/shard_map/ppermute | solution.py:22
  53.9 0.7 copy-start.20
  54.7 1.1 copy-start.8
  54.7 2.6 %copy-start.2 = (f32[1,2,128,128]{3,2,1,0:T(8,128)S(1)}, f32[1,2,128,128]{3,2,1,0:T(8,128)}, u32[]{:S(2)}) copy-start(f32[1,2,128,128]{3,2,1,0:T(8,128)} %param.20) | copy-start | bytes 393220
  55.8 5.0 %copy-start.6 = (s32[128]{0:T(128)S(1)}, s32[128]{0:T(128)}, u32[]{:S(2)}) copy-start(s32[128]{0:T(128)} %copy-done.5) | copy-start | bytes 1540
  55.8 4.6 %collective-permute-start.1 = (f32[128,128]{0,1:T(8,128)S(1)}, f32[128,128]{0,1:T(8,128)S(1)}, u32[]{:S(2)}, u32[]{:S(2)}) collective-permute-start(f32[128,128]{0,1:T(8,128)S(1)} %broadcast_multiply_fusion.3), channel_id=1, source_target_pairs={{0,2},{1,3},{2,0},{3,1},{4,6},{5,7},{6,4},{7,5},{8,10},{9,11},{10,... | collective-permute-start | bytes 196616 | tf_op jit(solution)/shard_map/ppermute | solution.py:22
  62.2 1.5 copy-start.10
  65.5 2.9 %copy-start.14 = (f32[8]{0:T(128)S(1)}, f32[8]{0:T(128)}, u32[]{:S(2)}) copy-start(f32[8]{0:T(128)} %copy-done.13) | copy-start | bytes 100
  66.5 4.3 %collective-permute-start.3 = (f32[128,128]{0,1:T(8,128)S(1)}, f32[128,128]{0,1:T(8,128)S(1)}, u32[]{:S(2)}, u32[]{:S(2)}) collective-permute-start(f32[128,128]{0,1:T(8,128)S(1)} %broadcast_multiply_fusion.2), channel_id=1, source_target_pairs={{0,2},{1,3},{2,0},{3,1},{4,6},{5,7},{6,4},{7,5},{8,10},{9,11},{10,... | collective-permute-start | bytes 196616 | tf_op jit(solution)/shard_map/ppermute | solution.py:22
  67.6 3.5 %collective-permute-start.2 = (f32[128,128]{0,1:T(8,128)S(1)}, f32[128,128]{0,1:T(8,128)S(1)}, u32[]{:S(2)}, u32[]{:S(2)}) collective-permute-start(f32[128,128]{0,1:T(8,128)S(1)} %broadcast_multiply_fusion.6), channel_id=1, source_target_pairs={{0,1},{1,0},{2,3},{3,2},{4,5},{5,4},{6,7},{7,6},{8,9},{9,8},{10,11... | collective-permute-start | bytes 196616 | tf_op jit(solution)/shard_map/ppermute | solution.py:22
  68.4 0.7 copy-start.21
  72.9 1.8 %copy-start.26 = (f32[256]{0:T(256)S(1)}, f32[256]{0:T(256)}, u32[]{:S(2)}) copy-start(f32[256]{0:T(256)} %param.15) | copy-start | bytes 3076
  72.9 1.8 %copy-start.27 = (f32[256,256]{1,0:T(8,128)S(1)}, f32[256,256]{1,0:T(8,128)}, u32[]{:S(2)}) copy-start(f32[256,256]{1,0:T(8,128)} %param.14) | copy-start | bytes 786436
  74.7 1.5 copy-start.3
  82.6 23.1 %all-to-all-start.4 = ((f32[32,1,2056]{2,1,0:T(1,128)}), f32[32,1,2056]{2,1,0:T(1,128)}, u32[]{:S(2)}, u32[]{:S(2)}) async-start(f32[32,1,2056]{2,1,0:T(1,128)} %all_to_all.43), calls=%async_computation.4 | async-start | bytes 557056 | tf_op jit(solution)/shard_map/all_to_all | solution.py:86
  86.3 5.4 %copy-start.15 = (f32[8]{0:T(128)S(1)}, f32[8]{0:T(128)}, u32[]{:S(2)}) copy-start(f32[8]{0:T(128)} %copy-done.13) | copy-start | bytes 100
  88.5 8.4 %collective-permute-start.5 = (f32[128,128]{0,1:T(8,128)}, f32[128,128]{0,1:T(8,128)}, u32[]{:S(2)}, u32[]{:S(2)}) collective-permute-start(f32[128,128]{0,1:T(8,128)} %convolution_bitcast_fusion.2), channel_id=1, source_target_pairs={{0,2},{1,3},{2,0},{3,1},{4,6},{5,7},{6,4},{7,5},{8,10},{9,11},{10,... | collective-permute-start | bytes 196616 | tf_op jit(solution)/shard_map/ppermute | solution.py:22
  90.1 6.8 %collective-permute-start.7 = (f32[128,128]{0,1:T(8,128)}, f32[128,128]{0,1:T(8,128)}, u32[]{:S(2)}, u32[]{:S(2)}) collective-permute-start(f32[128,128]{0,1:T(8,128)} %convolution_bitcast_fusion), channel_id=1, source_target_pairs={{0,2},{1,3},{2,0},{3,1},{4,6},{5,7},{6,4},{7,5},{8,10},{9,11},{10,... | collective-permute-start | bytes 196616 | tf_op jit(solution)/shard_map/ppermute | solution.py:22
  90.5 7.4 %collective-permute-start.4 = (f32[128,128]{0,1:T(8,128)S(1)}, f32[128,128]{0,1:T(8,128)}, u32[]{:S(2)}, u32[]{:S(2)}) collective-permute-start(f32[128,128]{0,1:T(8,128)S(1)} %convolution_bitcast_fusion.3), channel_id=1, source_target_pairs={{0,1},{1,0},{2,3},{3,2},{4,5},{5,4},{6,7},{7,6},{8,9},{9,8},{10,11... | collective-permute-start | bytes 196616 | tf_op jit(solution)/shard_map/ppermute | solution.py:22
  90.5 7.4 %collective-permute-start.6 = (f32[128,128]{0,1:T(8,128)S(1)}, f32[128,128]{0,1:T(8,128)}, u32[]{:S(2)}, u32[]{:S(2)}) collective-permute-start(f32[128,128]{0,1:T(8,128)S(1)} %convolution_bitcast_fusion.1), channel_id=1, source_target_pairs={{0,1},{1,0},{2,3},{3,2},{4,5},{5,4},{6,7},{7,6},{8,9},{9,8},{10,11... | collective-permute-start | bytes 196616 | tf_op jit(solution)/shard_map/ppermute | solution.py:22
  93.5 1.1 copy-start.17
  94.6 1.1 copy-start.18
  95.7 1.1 copy-start.4
  96.8 2.1 %copy-start.7 = (s32[128]{0:T(128)S(1)}, s32[128]{0:T(128)}, u32[]{:S(2)}) copy-start(s32[128]{0:T(128)} %copy-done.5) | copy-start | bytes 1540
  105.7 21.3 %all-to-all-start.2 = ((f32[32,32,128]{2,1,0:T(8,128)}), f32[32,32,128]{2,1,0:T(8,128)S(1)}, u32[]{:S(2)}, u32[]{:S(2)}) async-start(f32[32,32,128]{2,1,0:T(8,128)} %bitcast.29), calls=%async_computation.2 | async-start | bytes 1048576 | tf_op jit(solution)/shard_map/all_to_all | solution.py:172
  127.9 14.2 %all-to-all-start.5 = ((f32[32,1,2056]{2,1,0:T(1,128)}), f32[32,1,2056]{2,1,0:T(1,128)S(1)}, u32[]{:S(2)}, u32[]{:S(2)}) async-start(f32[32,1,2056]{2,1,0:T(1,128)} %broadcast_in_dim.43), calls=%async_computation.5 | async-start | bytes 557056 | tf_op jit(solution)/shard_map/all_to_all | solution.py:88
  137.9 6.7 %copy-start.22 = (s32[512]{0:T(512)S(1)}, s32[512]{0:T(512)}, u32[]{:S(2)}) copy-start(s32[512]{0:T(512)} %get-tuple-element.26) | copy-start | bytes 6148
  142.0 18.2 %all-to-all-start.3 = ((f32[32,32,128]{2,1,0:T(8,128)}), f32[32,32,128]{2,1,0:T(8,128)S(1)}, u32[]{:S(2)}, u32[]{:S(2)}) async-start(f32[32,32,128]{2,1,0:T(8,128)} %bitcast.34), calls=%async_computation.3 | async-start | bytes 1048576 | tf_op jit(solution)/shard_map/all_to_all | solution.py:172

commit v4 on v2

--- a/solution.py
+++ b/solution.py
@@ -117,13 +117,17 @@
     source = jnp.sum(jnp.where(chosen, order[None, :] + 1, 0), axis=1) - 1
     filled = source >= 0
     places = jnp.where(filled, within[jnp.maximum(source, 0)], row_count)
-    place_in = lax.all_to_all(
-        places.reshape(devices, capacity), ("row", "col"), 0, 0, tiled=True
-    ).reshape(-1)
-    outbox = x_scan[jnp.maximum(source, 0)]
-    inbox = lax.all_to_all(
-        outbox.reshape(devices, capacity, feat_count), ("row", "col"), 0, 0, tiled=True
-    ).reshape(-1, feat_count)
+    outbox = x_scan[jnp.maximum(source, 0)].reshape(devices, capacity * feat_count)
+    lanes = 128 * (-(-capacity // 128))
+    tags = jnp.zeros((devices, lanes), jnp.float32).at[:, :capacity].set(
+        places.reshape(devices, capacity).astype(jnp.float32)
+    )
+    got = lax.all_to_all(
+        jnp.concatenate([outbox, tags], axis=1), ("row", "col"), 0, 0, tiled=True
+    )
+    inbox = got[:, : capacity * feat_count].reshape(devices * capacity, feat_count)
+    place_in = got[:, capacity * feat_count : capacity * feat_count + capacity]
+    place_in = place_in.astype(jnp.int32).reshape(-1)
     landing = place_in[None, :] == order[:, None]
     arrival = jnp.sum(jnp.where(landing, slots[None, :], 0), axis=1)
     hidden = inbox[arrival]

time: 146 us -> 136 us (0.932)
  waiting for transfers between devices: 62.6 us -> 50.8 us
  starting transfers between devices: 26.6 us -> 21.4 us
  other arithmetic: 16.6 us -> 21.2 us
    ppermute x4, waiting for transfers between devices: 9.81 us -> 0.01 us  [swapped(): lax.ppermute(array, axis, [(i, i ^ 1 << apart) for i in range(lax.axis_si...]
    all_to_all x2 -> x1, starting transfers between devices: 11.3 us -> 7.3 us  [on_device(): lax.all_to_all(jnp.concatenate([outbox, tags], axis=1), ('row', 'col'), 0...]
    mul x2, other arithmetic: 0.02 us -> 1.83 us  [boundary_backward(): total = total.at[picked].add(received * own_mask)]
    all_to_all x2 -> x1, waiting for transfers between devices: 24.2 us -> 22.8 us  [on_device(): lax.all_to_all(jnp.concatenate([outbox, tags], axis=1), ('row', 'col'), 0...]
  transfers between devices with their start and end apart: 9 -> 8, of which waited for: 6 -> 4; matrix products, arithmetic and copies ran while one was open for 19% -> 21% of each run, Pallas kernels for 0% -> 0%
where the time goes in v4:
time: 136 us; the launch traced here: 135 us
  waiting for transfers between devices  50.8 us (37%)
  local copies, waits for them, and re-layouts  30.3 us (22%)
  starting transfers between devices  21.4 us (16%)
  other arithmetic  21.2 us (16%)
  matrix products  9.79 us (7%)
  between operations  1.43 us (1%)
    all_to_all x1, waiting for transfers between devices, on_device(): lax.all_to_all(reply.reshape(devices, capacity, feat_count), ('row', 'col...  24 us
    all_to_all x1, waiting for transfers between devices, on_device(): lax.all_to_all(jnp.concatenate([outbox, tags], axis=1), ('row', 'col'), 0...  22.8 us
    all_to_all x1, starting transfers between devices, on_device(): lax.all_to_all(jnp.concatenate([outbox, tags], axis=1), ('row', 'col'), 0...  7.3 us
    gather x1, local copies, waits for them, and re-layouts, on_device(): places = jnp.where(filled, within[jnp.maximum(source, 0)], row_count)  6.87 us
    all_to_all x1, starting transfers between devices, on_device(): lax.all_to_all(reply.reshape(devices, capacity, feat_count), ('row', 'col...  5.15 us
    gather x1, local copies, waits for them, and re-layouts, on_device(): reply = grad_nodes[jnp.minimum(place_in, row_count - 1)]  4.65 us
    dot_general x2, matrix products, interior(): jnp.einsum(form, tile_values * live_mask[:, None, None], source, precisio...  4.29 us
    ppermute x4, starting transfers between devices, swapped(): lax.ppermute(array, axis, [(i, i ^ 1 << apart) for i in range(lax.axis_si...  3.53 us
  transfers between devices with their start and end apart: 8, of which 4 were waited for; matrix products, arithmetic and copies ran while one was open for 21% of the time, Pallas kernels for 0%

profile of v4, /device:TPU:0, one launch (start us, length us, event | category | flops | bytes accessed | tf_op | source)
XLA Modules:
  0.0 134.9 jit_solution(16148753949609889403)
XLA Ops:
  0.6 0.6 compare_reduce_fusion
  1.3 0.7 add_select_fusion.1
  2.0 0.3 fusion.2
  2.3 0.6 compare_select_fusion.2
  2.8 0.3 select_reduce_fusion.1
  3.1 6.9 %gather_fusion.1 = s32[1024]{0:T(1024)S(1)} fusion(s32[512]{0:T(512)S(1)} %get-tuple-element.21, s32[1024]{0:T(1024)S(1)} %maximum_clamp_fusion), kind=kCustom, calls=%fused_computation.1 | custom fusion | bytes 12288 | tf_op jit(solution)/shard_map/gather | solution.py:119
  10.0 0.7 convert_select_fusion
  10.7 3.5 %gather_fusion = f32[1024,256]{1,0:T(8,128)S(1)} fusion(f32[512,256]{1,0:T(8,128)S(1)} %copy-done, s32[1024]{0:T(1024)S(1)} %maximum_clamp_fusion), kind=kCustom, calls=%fused_computation | custom fusion | bytes 2101248 | tf_op jit(solution)/shard_map/gather | solution.py:120
  14.2 0.2 reshape.236
  14.5 1.7 %all_to_all.21 = f32[32,1,8320]{2,1,0:T(1,128)} reshape(f32[32,8320]{1,0:T(8,128)S(1)} %select_maximum_fusion) | data formatting | bytes 2129920 | tf_op jit(solution)/shard_map/all_to_all | solution.py:125
  16.2 7.3 %all-to-all-start = ((f32[32,1,8320]{2,1,0:T(1,128)}), f32[32,1,8320]{2,1,0:T(1,128)S(1)}, u32[]{:S(2)}, u32[]{:S(2)}) async-start(f32[32,1,8320]{2,1,0:T(1,128)} %all_to_all.21), calls=%async_computation | async-start | bytes 2129920 | tf_op jit(solution)/shard_map/all_to_all | solution.py:125
  23.5 0.6 fusion.41
  24.1 0.6 compare_convert_fusion
  24.8 0.7 compare_convert_fusion.1
  25.4 1.2 compare_convert_fusion.2
  26.7 0.6 pad_clamp_fusion.1
  27.3 22.8 %all-to-all-done = f32[32,1,8320]{2,1,0:T(1,128)S(1)} async-done(((f32[32,1,8320]{2,1,0:T(1,128)}), f32[32,1,8320]{2,1,0:T(1,128)S(1)}, u32[]{:S(2)}, u32[]{:S(2)}) %all-to-all-start) | async-done | bytes 1064992 | tf_op jit(solution)/shard_map/all_to_all | solution.py:125
  50.5 0.3 select_reduce_fusion
  51.0 1.6 %gather_fusion.2 = f32[512,256]{1,0:T(8,128)S(1)} fusion(f32[1024,256]{1,0:T(8,128)S(1)} %reshape.237, s32[1024]{0:T(1024)S(1)} %pad_clamp_fusion.5), kind=kCustom, calls=%fused_computation.2 | custom fusion | bytes 1050624 | tf_op jit(solution)/shard_map/gather | solution.py:133
  52.6 0.8 gather_fusion.5
  53.4 0.8 gather_fusion.4
  54.3 0.7 broadcast_multiply_fusion.3
  55.0 1.5 %collective-permute-start.1 = (f32[128,256]{0,1:T(8,128)S(1)}, f32[128,256]{0,1:T(8,128)S(1)}, u32[]{:S(2)}, u32[]{:S(2)}) collective-permute-start(f32[128,256]{0,1:T(8,128)S(1)} %broadcast_multiply_fusion.1), channel_id=1, source_target_pairs={{0,2},{1,3},{2,0},{3,1},{4,6},{5,7},{6,4},{7,5},{8,10},{9,11},{10,... | collective-permute-start | bytes 393224 | tf_op jit(solution)/shard_map/ppermute | solution.py:17
  56.5 0.7 gather_fusion.3
  57.2 2.1 %fusion.6 = f32[8,128,256]{2,1,0:T(8,128)S(1)} fusion(f32[8,128,256]{2,1,0:T(8,128)S(1)} %gather_fusion.3, f32[1,8,128,128]{3,2,1,0:T(8,128)} %param.16, f32[8]{0:T(128)} %compare_convert_fusion.2), kind=kOutput, calls=%fused_computation.46 | convolution fusion | flops 402784256 | bytes 2621472 | tf_op jit(solution)/shard_map/tij,tjf->tif/dot_general | solution.py:37
  59.4 1.4 %scatter_fusion = f32[4,128,256]{2,1,0:T(8,128)S(1)} fusion(f32[4,128,256]{2,1,0:T(8,128)S(1)} %broadcast.237.clone, s32[8]{0:T(128)} %copy-done.20, f32[8,128,256]{2,1,0:T(8,128)S(1)} %fusion.6), kind=kCustom, calls=%fused_computation.11 | custom fusion | flops 262144 | bytes 3145760 | tf_op jit(solution)/shard_map/scatter-add | solution.py:38
  61.0 0.6 broadcast_clamp_fusion
  61.6 0.2 copy-done.1
  61.8 0.3 fusion.1
  62.2 0.3 fusion
  62.6 1.5 %scatter_fusion.1 = f32[512,256]{1,0:T(8,128)S(1)} fusion(f32[512,256]{1,0:T(8,128)S(1)} %bitcast_add_fusion.1, s32[128]{0:T(128)S(1)} %copy-done.13, f32[128,256]{1,0:T(8,128)S(1)} %copy.43), kind=kCustom, calls=%fused_computation.12 | custom fusion | flops 32768 | bytes 393728 | tf_op jit(solution)/shard_map/scatter-add | solution.py:57
  64.1 1.7 %scatter_fusion.2 = f32[512,256]{1,0:T(8,128)S(1)} fusion(f32[512,256]{1,0:T(8,128)S(1)} %scatter_fusion.1, s32[128]{0:T(128)S(1)} %get-tuple-element.22, f32[128,256]{1,0:T(8,128)S(1)} %copy.45), kind=kCustom, calls=%fused_computation.13 | custom fusion | flops 32768 | bytes 393728 | tf_op jit(solution)/shard_map/scatter-add | solution.py:57
  66.0 1.5 %multiply_add_fusion = (f32[512,256]{1,0:T(8,128)}, f32[512,256]{1,0:T(8,128)S(1)}) fusion(f32[512,256]{1,0:T(8,128)S(1)} %gather_fusion.2, f32[256,256]{1,0:T(8,128)S(1)} %copy-done.24, f32[512,256]{1,0:T(8,128)S(1)} %scatter_fusion.2, f32[256]{0:T(256)S(1)} %copy-done.23, f32[512]{0:T(512)S(1)} %fusion.33), kind=kOutput, calls=%fused_computation.42 | convolution fusion | flops 403570688 | bytes 2362368 | tf_op jit(solution)/shard_map/jvp()/dot_general | solution.py:24
  67.5 1.2 fusion.7
  68.6 0.8 multiply_reduce_fusion
  69.5 0.2 add_add_fusion
  69.7 0.9 gather_fusion.8
  70.6 0.9 gather_fusion.7
  71.5 1.1 all_to_all.28
  72.6 2.8 %all-to-all-start.2 = ((f32[32,1,2056]{2,1,0:T(1,128)}), f32[32,1,2056]{2,1,0:T(1,128)S(1)}, u32[]{:S(2)}, u32[]{:S(2)}) async-start(f32[32,1,2056]{2,1,0:T(1,128)} %all_to_all.28), calls=%async_computation.2 | async-start | bytes 557056 | tf_op jit(solution)/shard_map/all_to_all | solution.py:81
  75.6 0.9 convolution_bitcast_fusion.1
  76.6 0.3 collective-permute-start.2
  76.8 0.3 convolution_bitcast_fusion
  77.1 1.7 %collective-permute-start.3 = (f32[128,256]{0,1:T(8,128)S(1)}, f32[128,256]{0,1:T(8,128)}, u32[]{:S(2)}, u32[]{:S(2)}) collective-permute-start(f32[128,256]{0,1:T(8,128)S(1)} %convolution_bitcast_fusion), channel_id=1, source_target_pairs={{0,2},{1,3},{2,0},{3,1},{4,6},{5,7},{6,4},{7,5},{8,10},{9,11},{10,... | collective-permute-start | bytes 393224 | tf_op jit(solution)/shard_map/ppermute | solution.py:17
  78.8 0.7 gather_fusion.6
  79.6 2.2 %fusion.5 = f32[8,128,256]{2,1,0:T(8,128)S(1)} fusion(f32[8,128,256]{2,1,0:T(8,128)S(1)} %gather_fusion.6, f32[1,8,128,128]{3,2,1,0:T(8,128)} %param.16, f32[8]{0:T(128)} %compare_convert_fusion.2), kind=kOutput, calls=%fused_computation.45 | convolution fusion | flops 402784256 | bytes 2621472 | tf_op jit(solution)/shard_map/tji,tjf->tif/dot_general | solution.py:37
  81.8 1.4 %scatter_fusion.3 = f32[4,128,256]{2,1,0:T(8,128)S(1)} fusion(f32[4,128,256]{2,1,0:T(8,128)S(1)} %broadcast.237, s32[8]{0:T(128)} %copy-done.19, f32[8,128,256]{2,1,0:T(8,128)S(1)} %fusion.5), kind=kCustom, calls=%fused_computation.14 | custom fusion | flops 262144 | bytes 3145760 | tf_op jit(solution)/shard_map/scatter-add | solution.py:38
  83.3 3.3 %all-to-all-done.2 = f32[32,1,2056]{2,1,0:T(1,128)S(1)} async-done(((f32[32,1,2056]{2,1,0:T(1,128)}), f32[32,1,2056]{2,1,0:T(1,128)S(1)}, u32[]{:S(2)}, u32[]{:S(2)}) %all-to-all-start.2) | async-done | bytes 263200 | tf_op jit(solution)/shard_map/all_to_all | solution.py:81
  86.7 0.9 broadcast_in_dim.43
  87.6 2.6 %all-to-all-start.3 = ((f32[32,1,2056]{2,1,0:T(1,128)}), f32[32,1,2056]{2,1,0:T(1,128)S(1)}, u32[]{:S(2)}, u32[]{:S(2)}) async-start(f32[32,1,2056]{2,1,0:T(1,128)} %broadcast_in_dim.43), calls=%async_computation.3 | async-start | bytes 557056 | tf_op jit(solution)/shard_map/all_to_all | solution.py:83
  90.3 0.5 copy-done.9
  90.8 0.9 broadcast_multiply_fusion.2
  91.8 0.9 broadcast_multiply_fusion
  92.9 1.5 %scatter_fusion.4 = f32[512,256]{1,0:T(8,128)S(1)} fusion(f32[512,256]{1,0:T(8,128)S(1)} %bitcast_add_fusion, s32[128]{0:T(128)S(1)} %copy-done.14, f32[128,256]{1,0:T(8,128)S(1)} %copy.48), kind=kCustom, calls=%fused_computation.15 | custom fusion | flops 32768 | bytes 393728 | tf_op jit(solution)/shard_map/scatter-add | solution.py:73
  94.4 1.5 %scatter_fusion.5 = f32[512,256]{1,0:T(8,128)S(1)} fusion(f32[512,256]{1,0:T(8,128)S(1)} %scatter_fusion.4, s32[128]{0:T(128)S(1)} %copy-done.11, f32[128,256]{1,0:T(8,128)S(1)} %copy.50), kind=kCustom, calls=%fused_computation.16 | custom fusion | flops 32768 | bytes 393728 | tf_op jit(solution)/shard_map/scatter-add | solution.py:73
  95.9 4.7 %gather_fusion.9 = f32[1024,256]{1,0:T(8,128)} fusion(f32[512,256]{1,0:T(8,128)S(1)} %scatter_fusion.5, s32[1024]{0:T(1024)S(1)} %copy-done.4), kind=kCustom, calls=%fused_computation.9 | custom fusion | bytes 2101248 | tf_op jit(solution)/shard_map/gather | solution.py:146
  100.6 0.7 all-to-all-done.3
  101.3 5.1 %all-to-all-start.1 = ((f32[32,32,256]{2,1,0:T(8,128)}), f32[32,32,256]{2,1,0:T(8,128)S(1)}, u32[]{:S(2)}, u32[]{:S(2)}) async-start(f32[32,32,256]{2,1,0:T(8,128)} %bitcast.24), calls=%async_computation.1 | async-start | bytes 2097152 | tf_op jit(solution)/shard_map/all_to_all | solution.py:147
  106.4 0.7 reduce.8
  107.1 0.2 reshape.245
  107.3 0.6 slice_multiply_fusion.1
  107.9 0.7 slice_multiply_fusion
  108.6 24.0 %all-to-all-done.1 = f32[32,32,256]{2,1,0:T(8,128)S(1)} async-done(((f32[32,32,256]{2,1,0:T(8,128)}), f32[32,32,256]{2,1,0:T(8,128)S(1)}, u32[]{:S(2)}, u32[]{:S(2)}) %all-to-all-start.1) | async-done | bytes 1048608 | tf_op jit(solution)/shard_map/all_to_all | solution.py:147
  132.7 2.2 %gather_fusion.10 = f32[512,256]{1,0:T(8,128)} fusion(f32[1024,256]{1,0:T(8,128)S(1)} %bitcast.62, s32[1024]{0:T(1024)S(1)} %pad_clamp_fusion), kind=kCustom, calls=%fused_computation.10 | custom fusion | bytes 1050624 | tf_op jit(solution)/shard_map/gather | solution.py:154
  (88 shorter events, 2.1 us)
Async XLA Ops:
  0.6 10.1 %copy-start = (f32[512,256]{1,0:T(8,128)S(1)}, f32[512,256]{1,0:T(8,128)}, u32[]{:S(2)}) copy-start(f32[512,256]{1,0:T(8,128)} %param.12) | copy-start | bytes 1572868
  16.2 7.3 %copy-start.18 = (s32[1,3]{1,0:T(1,128)S(1)}, s32[1,3]{1,0:T(1,128)}, u32[]{:S(2)}) copy-start(s32[1,3]{1,0:T(1,128)} %param.18) | copy-start | bytes 40
  16.2 10.4 %copy-start.21 = (s32[1,2,128]{2,1,0:T(2,128)S(1)}, s32[1,2,128]{2,1,0:T(2,128)}, u32[]{:S(2)}) copy-start(s32[1,2,128]{2,1,0:T(2,128)} %param.19) | copy-start | bytes 3076
  16.2 10.5 %copy-start.22 = (s32[1,8,2]{1,2,0:T(2,128)S(1)}, s32[1,8,2]{1,2,0:T(2,128)}, u32[]{:S(2)}) copy-start(s32[1,8,2]{1,2,0:T(2,128)} %param.17) | copy-start | bytes 196
  16.2 33.9 %all-to-all-start = ((f32[32,1,8320]{2,1,0:T(1,128)}), f32[32,1,8320]{2,1,0:T(1,128)S(1)}, u32[]{:S(2)}, u32[]{:S(2)}) async-start(f32[32,1,8320]{2,1,0:T(1,128)} %all_to_all.21), calls=%async_computation | async-start | bytes 2129920 | tf_op jit(solution)/shard_map/all_to_all | solution.py:125
  24.8 37.4 %copy-start.5 = (f32[128]{0:T(128)}, f32[128]{0:T(128)S(1)}, u32[]{:S(2)}) copy-start(f32[128]{0:T(128)S(1)} %compare_convert_fusion) | copy-start | bytes 1540
  25.4 50.2 %copy-start.8 = (f32[128]{0:T(128)}, f32[128]{0:T(128)S(1)}, u32[]{:S(2)}) copy-start(f32[128]{0:T(128)S(1)} %compare_convert_fusion.1) | copy-start | bytes 1540
  26.6 23.5 %copy-start.12 = (s32[128]{0:T(128)}, s32[128]{0:T(128)S(1)}, u32[]{:S(2)}) copy-start(s32[128]{0:T(128)S(1)} %get-tuple-element.23) | copy-start | bytes 1540
  26.6 37.4 %copy-start.10 = (s32[128]{0:T(128)}, s32[128]{0:T(128)S(1)}, u32[]{:S(2)}) copy-start(s32[128]{0:T(128)S(1)} %get-tuple-element.22) | copy-start | bytes 1540
  26.7 25.9 %copy-start.17 = (s32[1024]{0:T(1024)}, s32[1024]{0:T(1024)S(1)}, u32[]{:S(2)}) copy-start(s32[1024]{0:T(1024)S(1)} %get-tuple-element.35) | copy-start | bytes 12292
  26.7 26.7 %copy-start.16 = (s32[1024]{0:T(1024)}, s32[1024]{0:T(1024)S(1)}, u32[]{:S(2)}) copy-start(s32[1024]{0:T(1024)S(1)} %get-tuple-element.36) | copy-start | bytes 12292
  26.7 24.2 %copy-start.19 = (s32[8]{0:T(128)}, s32[8]{0:T(128)S(1)}, u32[]{:S(2)}) copy-start(s32[8]{0:T(128)S(1)} %get-tuple-element.24) | copy-start | bytes 100
  26.7 24.2 %copy-start.20 = (s32[8]{0:T(128)}, s32[8]{0:T(128)S(1)}, u32[]{:S(2)}) copy-start(s32[8]{0:T(128)S(1)} %get-tuple-element.25) | copy-start | bytes 100
  54.9 6.6 %collective-permute-start = (f32[128,256]{0,1:T(8,128)}, f32[128,256]{0,1:T(8,128)S(1)}, u32[]{:S(2)}, u32[]{:S(2)}) collective-permute-start(f32[128,256]{0,1:T(8,128)} %broadcast_multiply_fusion.3), channel_id=1, source_target_pairs={{0,1},{1,0},{2,3},{3,2},{4,5},{5,4},{6,7},{7,6},{8,9},{9,8},{10,11... | collective-permute-start | bytes 393224 | tf_op jit(solution)/shard_map/ppermute | solution.py:17
  55.0 7.2 %collective-permute-start.1 = (f32[128,256]{0,1:T(8,128)S(1)}, f32[128,256]{0,1:T(8,128)S(1)}, u32[]{:S(2)}, u32[]{:S(2)}) collective-permute-start(f32[128,256]{0,1:T(8,128)S(1)} %broadcast_multiply_fusion.1), channel_id=1, source_target_pairs={{0,2},{1,3},{2,0},{3,1},{4,6},{5,7},{6,4},{7,5},{8,10},{9,11},{10,... | collective-permute-start | bytes 393224 | tf_op jit(solution)/shard_map/ppermute | solution.py:17
  60.9 0.9 copy-start.1
  60.9 1.7 %copy-start.13 = (s32[128]{0:T(128)S(1)}, s32[128]{0:T(128)}, u32[]{:S(2)}) copy-start(s32[128]{0:T(128)} %copy-done.12) | copy-start | bytes 1540
  64.1 1.9 %copy-start.23 = (f32[256]{0:T(256)S(1)}, f32[256]{0:T(256)}, u32[]{:S(2)}) copy-start(f32[256]{0:T(256)} %param.15) | copy-start | bytes 3076
  64.1 1.9 %copy-start.24 = (f32[256,256]{1,0:T(8,128)S(1)}, f32[256,256]{1,0:T(8,128)}, u32[]{:S(2)}) copy-start(f32[256,256]{1,0:T(8,128)} %param.14) | copy-start | bytes 786436
  66.0 1.5 %copy-start.2 = (f32[512,256]{1,0:T(8,128)S(1)}, f32[512,256]{1,0:T(8,128)}, u32[]{:S(2)}) copy-start(f32[512,256]{1,0:T(8,128)} %param.21) | copy-start | bytes 1572868
  71.5 5.3 %copy-start.6 = (f32[128]{0:T(128)S(1)}, f32[128]{0:T(128)}, u32[]{:S(2)}) copy-start(f32[128]{0:T(128)} %copy-done.5) | copy-start | bytes 1540
  72.6 13.9 %all-to-all-start.2 = ((f32[32,1,2056]{2,1,0:T(1,128)}), f32[32,1,2056]{2,1,0:T(1,128)S(1)}, u32[]{:S(2)}, u32[]{:S(2)}) async-start(f32[32,1,2056]{2,1,0:T(1,128)} %all_to_all.28), calls=%async_computation.2 | async-start | bytes 557056 | tf_op jit(solution)/shard_map/all_to_all | solution.py:81
  76.6 13.7 %collective-permute-start.2 = (f32[128,256]{0,1:T(8,128)}, f32[128,256]{0,1:T(8,128)}, u32[]{:S(2)}, u32[]{:S(2)}) collective-permute-start(f32[128,256]{0,1:T(8,128)} %convolution_bitcast_fusion.1), channel_id=1, source_target_pairs={{0,1},{1,0},{2,3},{3,2},{4,5},{5,4},{6,7},{7,6},{8,9},{9,8},{10,11... | collective-permute-start | bytes 393224 | tf_op jit(solution)/shard_map/ppermute | solution.py:17
  77.1 14.7 %collective-permute-start.3 = (f32[128,256]{0,1:T(8,128)S(1)}, f32[128,256]{0,1:T(8,128)}, u32[]{:S(2)}, u32[]{:S(2)}) collective-permute-start(f32[128,256]{0,1:T(8,128)S(1)} %convolution_bitcast_fusion), channel_id=1, source_target_pairs={{0,2},{1,3},{2,0},{3,1},{4,6},{5,7},{6,4},{7,5},{8,10},{9,11},{10,... | collective-permute-start | bytes 393224 | tf_op jit(solution)/shard_map/ppermute | solution.py:17
  83.2 6.9 %copy-start.3 = (f32[512,256]{1,0:T(8,128)S(1)}, f32[512,256]{1,0:T(8,128)}, u32[]{:S(2)}) copy-start(f32[512,256]{1,0:T(8,128)} %param.21) | copy-start | bytes 1572868
  87.6 13.7 %all-to-all-start.3 = ((f32[32,1,2056]{2,1,0:T(1,128)}), f32[32,1,2056]{2,1,0:T(1,128)S(1)}, u32[]{:S(2)}, u32[]{:S(2)}) async-start(f32[32,1,2056]{2,1,0:T(1,128)} %broadcast_in_dim.43), calls=%async_computation.3 | async-start | bytes 557056 | tf_op jit(solution)/shard_map/all_to_all | solution.py:83
  90.2 0.6 copy-start.9
  90.2 1.7 %copy-start.7 = (f32[128]{0:T(128)S(1)}, f32[128]{0:T(128)}, u32[]{:S(2)}) copy-start(f32[128]{0:T(128)} %copy-done.5) | copy-start | bytes 1540
  90.2 2.7 %copy-start.14 = (s32[128]{0:T(128)S(1)}, s32[128]{0:T(128)}, u32[]{:S(2)}) copy-start(s32[128]{0:T(128)} %copy-done.12) | copy-start | bytes 1540
  92.9 1.5 %copy-start.11 = (s32[128]{0:T(128)S(1)}, s32[128]{0:T(128)}, u32[]{:S(2)}) copy-start(s32[128]{0:T(128)} %copy-done.10) | copy-start | bytes 1540
  94.4 1.5 %copy-start.4 = (s32[1024]{0:T(1024)S(1)}, s32[1024]{0:T(1024)}, u32[]{:S(2)}) copy-start(s32[1024]{0:T(1024)} %broadcast_clamp_fusion) | copy-start | bytes 12292
  100.6 5.8 %copy-start.15 = (s32[512]{0:T(512)S(1)}, s32[512]{0:T(512)}, u32[]{:S(2)}) copy-start(s32[512]{0:T(512)} %get-tuple-element.18) | copy-start | bytes 6148
  101.3 31.4 %all-to-all-start.1 = ((f32[32,32,256]{2,1,0:T(8,128)}), f32[32,32,256]{2,1,0:T(8,128)S(1)}, u32[]{:S(2)}, u32[]{:S(2)}) async-start(f32[32,32,256]{2,1,0:T(8,128)} %bitcast.24), calls=%async_computation.1 | async-start | bytes 2097152 | tf_op jit(solution)/shard_map/all_to_all | solution.py:147

commit v5 on v4

--- a/solution.py
+++ b/solution.py
@@ -25,53 +25,70 @@
     )
 
 
-def interior(hidden, tile_values, tile_coords, live_count, transpose):
-    feat_count = hidden.shape[1]
-    blocks = hidden.reshape(-1, BLOCK, feat_count)
-    if transpose:
-        source_col, target_col, form = (0, 1, "tji,tjf->tif")
-    else:
-        source_col, target_col, form = (1, 0, "tij,tjf->tif")
-    live_mask = (jnp.arange(tile_values.shape[0]) < live_count).astype(jnp.float32)
-    source = blocks[tile_coords[:, source_col]]
-    product = jnp.einsum(form, tile_values * live_mask[:, None, None], source, precision=PRECISE)
-    result = jnp.zeros_like(blocks).at[tile_coords[:, target_col]].add(product)
-    return result.reshape(hidden.shape)
+def dense_tiles(tile_values, tile_coords, live_count, rows):
+    slots, block, _ = tile_values.shape
+    grid = rows // block
+    cells = jnp.arange(grid, dtype=jnp.int32)
+    live = jnp.arange(slots) < live_count
+    at_row = (tile_coords[:, 0, None] == cells[None, :]) & live[:, None]
+    at_col = tile_coords[:, 1, None] == cells[None, :]
+    where_to = (at_row[:, :, None] & at_col[:, None, :]).reshape(slots, grid * grid)
+    placed = lax.dot_general(
+        where_to.astype(jnp.float32),
+        tile_values.reshape(slots, block * block),
+        (((0,), (0,)), ((), ())),
+        precision=PRECISE,
+        preferred_element_type=jnp.float32,
+    )
+    placed = placed.reshape(grid, grid, block, block).transpose(0, 2, 1, 3)
+    return placed.reshape(rows, rows)
 
 
-def boundary_forward(total, hidden, boundary_rows, coupling, counts):
+def pickers(boundary_rows, counts, rows):
+    picked = boundary_rows[0].reshape(-1)
+    live = (jnp.arange(BLOCK)[None, :] < counts[0, 1 : 1 + ROUNDS][:, None]).reshape(-1)
+    hit = picked[:, None] == jnp.arange(rows, dtype=jnp.int32)[None, :]
+    return jnp.where(hit & live[:, None], 1.0, 0.0).astype(jnp.float32)
+
+
+def spread(chooser, values):
+    return lax.dot_general(
+        chooser, values, (((0,), (0,)), ((), ())), precision=PRECISE,
+        preferred_element_type=jnp.float32,
+    )
+
+
+def boundary_forward(total, hidden, chooser, coupling):
+    picks = jnp.dot(chooser, hidden, precision=PRECISE, preferred_element_type=jnp.float32)
+    contribs = []
     for round_index in range(ROUNDS):
-        picked = boundary_rows[0, round_index]
-        own_mask = (jnp.arange(BLOCK) < counts[0, 1 + round_index]).astype(jnp.float32)[:, None]
-        outgoing = hidden[picked] * own_mask
+        outgoing = picks[round_index * BLOCK : (round_index + 1) * BLOCK]
         received = swapped(outgoing, "col", round_index)
-        contrib = (
+        contribs.append(
             jnp.dot(
                 coupling[0, round_index],
                 received,
                 precision=PRECISE,
                 preferred_element_type=jnp.float32,
             )
-            * own_mask
         )
-        total = total.at[picked].add(contrib)
-    return total
+    return total + spread(chooser, jnp.concatenate(contribs, axis=0))
 
 
-def boundary_backward(total, grad_agg, boundary_rows, coupling, counts):
+def boundary_backward(total, grad_agg, chooser, coupling):
+    picks = jnp.dot(chooser, grad_agg, precision=PRECISE, preferred_element_type=jnp.float32)
+    arrived = []
     for round_index in range(ROUNDS):
-        picked = boundary_rows[0, round_index]
-        own_mask = (jnp.arange(BLOCK) < counts[0, 1 + round_index]).astype(jnp.float32)[:, None]
-        outgoing = grad_agg[picked] * own_mask
-        carried = jnp.dot(
-            coupling[0, round_index].T,
+        outgoing = picks[round_index * BLOCK : (round_index + 1) * BLOCK]
+        carried = lax.dot_general(
+            coupling[0, round_index],
             outgoing,
+            (((0,), (0,)), ((), ())),
             precision=PRECISE,
             preferred_element_type=jnp.float32,
         )
-        received = swapped(carried, "col", round_index)
-        total = total.at[picked].add(received * own_mask)
-    return total
+        arrived.append(swapped(carried, "col", round_index))
+    return total + spread(chooser, jnp.concatenate(arrived, axis=0))
 
 
 def summed_everywhere(grad_weight, grad_gain, devices):
@@ -116,7 +133,9 @@
     chosen = bucket[None, :] == slots[:, None]
     source = jnp.sum(jnp.where(chosen, order[None, :] + 1, 0), axis=1) - 1
     filled = source >= 0
-    places = jnp.where(filled, within[jnp.maximum(source, 0)], row_count)
+    places = jnp.where(
+        filled, jnp.sum(jnp.where(chosen, within[None, :], 0), axis=1), row_count
+    )
     outbox = x_scan[jnp.maximum(source, 0)].reshape(devices, capacity * feat_count)
     lanes = 128 * (-(-capacity // 128))
     tags = jnp.zeros((devices, lanes), jnp.float32).at[:, :capacity].set(
@@ -131,18 +150,18 @@
     landing = place_in[None, :] == order[:, None]
     arrival = jnp.sum(jnp.where(landing, slots[None, :], 0), axis=1)
     hidden = inbox[arrival]
-    aggregate = hidden + interior(hidden, tile_values[0], tile_coords[0], counts[0, 0], False)
-    aggregate = boundary_forward(aggregate, hidden, boundary_rows, coupling, counts)
+    tiles = dense_tiles(tile_values[0], tile_coords[0], counts[0, 0], row_count)
+    chooser = pickers(boundary_rows, counts, row_count)
+    aggregate = hidden + jnp.dot(
+        tiles, hidden, precision=PRECISE, preferred_element_type=jnp.float32
+    )
+    aggregate = boundary_forward(aggregate, hidden, chooser, coupling)
     activation, pullback = jax.vjp(layer_piece, aggregate, weight, norm_gain)
     output = hidden + activation
     grad_agg, grad_weight, grad_gain = pullback(cotangent)
     weight_sum, gain_sum = summed_everywhere(grad_weight, grad_gain, devices)
-    grad_nodes = (
-        cotangent
-        + grad_agg
-        + interior(grad_agg, tile_values[0], tile_coords[0], counts[0, 0], True)
-    )
-    grad_nodes = boundary_backward(grad_nodes, grad_agg, boundary_rows, coupling, counts)
+    grad_nodes = cotangent + grad_agg + spread(tiles, grad_agg)
+    grad_nodes = boundary_backward(grad_nodes, grad_agg, chooser, coupling)
     reply = grad_nodes[jnp.minimum(place_in, row_count - 1)]
     returned = lax.all_to_all(
         reply.reshape(devices, capacity, feat_count),

time: 136 us -> 125 us (0.919)
  other arithmetic: 21.2 us -> 5.33 us
  waiting for transfers between devices: 50.8 us -> 61.7 us
  local copies, waits for them, and re-layouts: 30.3 us -> 21.6 us
  matrix products: 9.79 us -> 14.8 us
    gather x11 -> x0, local copies, waits for them, and re-layouts: 12 us -> none  [the longest x1 6.87 us: on_device(): places = jnp.where(filled, within[jnp.maximum(source, 0)], row_count)]
    scatter-add x6 -> x0, other arithmetic: 9.03 us -> none  [the longest x2 3.16 us: boundary_forward(): total = total.at[picked].add(contrib)]
    ppermute x4, waiting for transfers between devices: 0.01 us -> 4.1 us  [swapped(): lax.ppermute(array, axis, [(i, i ^ 1 << apart) for i in range(lax.axis_si...]
    dot_general x4 -> x9, matrix products: 5.47 us -> 9.54 us  [the longest x3 4.05 us: spread(): lax.dot_general(chooser, values, (((0,), (0,)), ((), ())), precision=PREC...]
    all_to_all x1, waiting for transfers between devices: 3.28 us -> 6.32 us  [summed_everywhere(): gathered = lax.all_to_all(pieces, ('row', 'col'), 0, 0, tiled=True)]
    mul x4 -> x0, other arithmetic: 2.52 us -> none  [the longest x2 1.83 us: boundary_backward(): total = total.at[picked].add(received * own_mask)]
    convert_element_type x3 -> x0, other arithmetic: 2.48 us -> none  [the longest x2 1.3 us: boundary_forward(): (jnp.arange(BLOCK) < counts[0, 1 + round_index]).astype(jnp.float32)]
    all_to_all x1, waiting for transfers between devices: 0.69 us -> 2.94 us  [summed_everywhere(): lax.all_to_all(jnp.broadcast_to(chunk, pieces.shape), ('row', 'col'), 0,...]
  transfers between devices with their start and end apart: 8 -> 8, of which waited for: 4 -> 5; matrix products, arithmetic and copies ran while one was open for 21% -> 13% of each run, Pallas kernels for 0% -> 0%
where the time goes in v5:
time: 125 us
  waiting for transfers between devices  61.7 us (49%)
  local copies, waits for them, and re-layouts  21.6 us (17%)
  starting transfers between devices  20.2 us (16%)
  matrix products  14.8 us (12%)
  other arithmetic  5.33 us (4%)
    all_to_all x1, waiting for transfers between devices, on_device(): lax.all_to_all(jnp.concatenate([outbox, tags], axis=1), ('row', 'col'), 0...  24.3 us
    all_to_all x1, waiting for transfers between devices, on_device(): lax.all_to_all(reply.reshape(devices, capacity, feat_count), ('row', 'col...  24.1 us
    all_to_all x1, starting transfers between devices, on_device(): lax.all_to_all(jnp.concatenate([outbox, tags], axis=1), ('row', 'col'), 0...  7.41 us
    all_to_all x1, waiting for transfers between devices, summed_everywhere(): gathered = lax.all_to_all(pieces, ('row', 'col'), 0, 0, tiled=True)  6.32 us
    gather x1, local copies, waits for them, and re-layouts, on_device(): reply = grad_nodes[jnp.minimum(place_in, row_count - 1)]  4.65 us
    dot_general x3, matrix products, layer_piece(): jnp.dot(normed, weight, precision=PRECISE, preferred_element_type=jnp.flo...  4.4 us
    ppermute x4, waiting for transfers between devices, swapped(): lax.ppermute(array, axis, [(i, i ^ 1 << apart) for i in range(lax.axis_si...  4.1 us
    dot_general x3, matrix products, spread(): lax.dot_general(chooser, values, (((0,), (0,)), ((), ())), precision=PREC...  4.05 us
  transfers between devices with their start and end apart: 8, of which 5 were waited for; matrix products, arithmetic and copies ran while one was open for 13% of the time, Pallas kernels for 0%

profile of v5, /device:TPU:0, one launch (start us, length us, event | category | flops | bytes accessed | tf_op | source)
XLA Modules:
  0.0 124.7 jit_solution(16057628009869413198)
XLA Ops:
  0.6 0.0 copy-start
  0.6 0.6 compare_reduce_fusion
  1.3 0.7 add_select_fusion
  2.0 0.3 fusion.1
  2.3 0.6 select_reduce_fusion.2
  2.9 0.7 convert_select_fusion
  3.6 0.1 reshape.248
  3.7 3.5 %gather_fusion = f32[1024,256]{1,0:T(8,128)S(1)} fusion(f32[512,256]{1,0:T(8,128)S(1)} %copy-done, s32[1024]{0:T(1024)S(1)} %maximum_clamp_fusion), kind=kCustom, calls=%fused_computation | custom fusion | bytes 2101248 | tf_op jit(solution)/shard_map/gather | solution.py:139
  7.1 0.2 reshape.239
  7.3 0.1 select_maximum_fusion
  7.4 1.8 %all_to_all.21 = f32[32,1,8320]{2,1,0:T(1,128)} reshape(f32[32,8320]{1,0:T(8,128)S(1)} %select_maximum_fusion) | data formatting | bytes 2129920 | tf_op jit(solution)/shard_map/all_to_all | solution.py:144
  9.2 7.4 %all-to-all-start = ((f32[32,1,8320]{2,1,0:T(1,128)}), f32[32,1,8320]{2,1,0:T(1,128)}, u32[]{:S(2)}, u32[]{:S(2)}) async-start(f32[32,1,8320]{2,1,0:T(1,128)} %all_to_all.21), calls=%async_computation | async-start | bytes 2129920 | tf_op jit(solution)/shard_map/all_to_all | solution.py:144
  16.6 0.0 copy-start.5
  16.6 1.0 copy.38
  17.7 0.1 slice_bitcast_fusion
  17.7 0.1 compare_bitcast_fusion
  17.9 1.0 fusion.15
  18.8 24.3 %all-to-all-done = f32[32,1,8320]{2,1,0:T(1,128)} async-done(((f32[32,1,8320]{2,1,0:T(1,128)}), f32[32,1,8320]{2,1,0:T(1,128)}, u32[]{:S(2)}, u32[]{:S(2)}) %all-to-all-start) | async-done | bytes 1064992 | tf_op jit(solution)/shard_map/all_to_all | solution.py:144
  43.2 1.3 %copy.66 = f32[32,1,8320]{2,0,1:T(8,128)S(1)} copy(f32[32,1,8320]{2,1,0:T(1,128)} %all-to-all-done) | data formatting | bytes 2129920
  44.5 1.0 slice.85
  45.6 0.1 min.18
  45.6 0.1 eq.100
  45.7 0.3 select_reduce_fusion
  46.0 1.4 %reshape.240 = f32[1024,256]{1,0:T(8,128)S(1)} reshape(f32[32,8192]{1,0:T(8,128)} %slice.85) | data formatting | bytes 2097152 | tf_op jit(solution)/shard_map/reshape | solution.py:147
  47.4 0.0 copy-start.6
  47.4 1.6 %gather_fusion.1 = f32[512,256]{1,0:T(8,128)S(1)} fusion(f32[1024,256]{1,0:T(8,128)S(1)} %reshape.240, s32[1024]{0:T(1024)S(1)} %pad_clamp_fusion.1), kind=kCustom, calls=%fused_computation.1 | custom fusion | bytes 1050624 | tf_op jit(solution)/shard_map/gather | solution.py:152
  49.0 0.0 copy-start.2
  49.0 0.2 copy.36
  49.2 0.7 fusion.9
  50.0 0.1 collective-permute-start
  50.1 1.5 %collective-permute-start.1 = (f32[128,256]{1,0:T(8,128)S(1)}, f32[128,256]{1,0:T(8,128)S(1)}, u32[]{:S(2)}, u32[]{:S(2)}) collective-permute-start(f32[128,256]{1,0:T(8,128)S(1)} %get-tuple-element.23), channel_id=1, source_target_pairs={{0,2},{1,3},{2,0},{3,1},{4,6},{5,7},{6,4},{7,5},{8,10},{9,11},{10,... | collective-permute-start | bytes 393224 | tf_op jit(solution)/shard_map/ppermute | solution.py:17
  51.6 0.3 convolution_bitcast_fusion.3
  51.9 4.1 %collective-permute-done.1 = f32[128,256]{1,0:T(8,128)S(1)} collective-permute-done((f32[128,256]{1,0:T(8,128)S(1)}, f32[128,256]{1,0:T(8,128)S(1)}, u32[]{:S(2)}, u32[]{:S(2)}) %collective-permute-start.1) | collective-permute-done | bytes 131104 | tf_op jit(solution)/shard_map/ppermute | solution.py:17
  56.0 0.3 convolution_bitcast_fusion.2
  56.3 0.8 fusion.7
  57.1 0.0 copy-start.9
  57.1 1.1 multiply_reduce_fusion.2
  58.3 1.9 %multiply_add_fusion = (f32[512,256]{1,0:T(8,128)}, f32[512,256]{1,0:T(8,128)S(1)}) fusion(f32[512,256]{1,0:T(8,128)S(1)} %gather_fusion.1, f32[256,256]{1,0:T(8,128)S(1)} %copy-done.12, f32[512,256]{0,1:T(8,128)S(1)} %get-tuple-element.29, f32[256]{0:T(256)S(1)} %copy-done.9, f32[512]{0:T(512)S(1)} %fusion.71), kind=kOutput, calls=%fused_computation.43 | convolution fusion | flops 403570688 | bytes 2362368 | tf_op jit(solution)/shard_map/jvp()/dot_general | solution.py:24
  60.2 0.8 fusion.22
  61.0 1.7 %multiply_reduce_fusion = (f32[256]{0:T(256)S(1)}, f32[512]{0:T(512)S(1)}, f32[512,256]{0,1:T(8,128)}) fusion(f32[512,256]{0,1:T(8,128)S(1)} %get-tuple-element.29, f32[512]{0:T(512)S(1)} %fusion.71, f32[256]{0:T(256)S(1)} %copy-done.9, f32[256,256]{1,0:T(8,128)S(1)} %copy-done.12, f32[512,256]{1,0:T(8,128)S(1)} %get-tuple-element.31, ...), kind=kOutput, calls=%fused_computation.41 | convolution fusion | flops 404618496 | bytes 2365440 | tf_op jit(solution)/shard_map/transpose(jvp())/dot_general | solution.py:24
  62.8 1.1 all_to_all.28
  63.9 3.8 %all-to-all-start.2 = ((f32[32,1,2056]{2,1,0:T(1,128)}), f32[32,1,2056]{2,1,0:T(1,128)S(1)}, u32[]{:S(2)}, u32[]{:S(2)}) async-start(f32[32,1,2056]{2,1,0:T(1,128)} %all_to_all.28), calls=%async_computation.2 | async-start | bytes 557056 | tf_op jit(solution)/shard_map/all_to_all | solution.py:98
  67.7 1.9 %fusion.5 = f32[256,256]{1,0:T(8,128)S(1)} fusion(s32[256]{0:T(256)S(1)} %bitcast.90, pred[256]{0:T(512)(128)(4,1)S(1)} %compare_bitcast_fusion, f32[512,256]{0,1:T(8,128)S(1)} %get-tuple-element.29, f32[512,256]{0,1:T(8,128)} %get-tuple-element.32, f32[512]{0:T(512)S(1)} %multiply_multiply_fusion, f32[256]{0:T(256)S(1)} %copy-done.9, f32[512]{0:T(512)S(1)} %fusion.71), kind=kOutput, calls=%fused_computation.26 | convolution fusion | flops 403701760 | bytes 1317120 | tf_op jit(solution)/shard_map/dot_general | solution.py:79
  69.6 0.0 copy-start.1
  69.6 0.4 convolution_bitcast_fusion.1
  70.0 0.1 collective-permute-start.2
  70.2 0.4 convolution_bitcast_fusion
  70.6 1.7 %collective-permute-start.3 = (f32[128,256]{0,1:T(8,128)S(1)}, f32[128,256]{0,1:T(8,128)S(1)}, u32[]{:S(2)}, u32[]{:S(2)}) collective-permute-start(f32[128,256]{0,1:T(8,128)S(1)} %convolution_bitcast_fusion), channel_id=1, source_target_pairs={{0,2},{1,3},{2,0},{3,1},{4,6},{5,7},{6,4},{7,5},{8,10},{9,11},{10,... | collective-permute-start | bytes 393224 | tf_op jit(solution)/shard_map/ppermute | solution.py:17
  72.3 6.3 %all-to-all-done.2 = f32[32,1,2056]{2,1,0:T(1,128)S(1)} async-done(((f32[32,1,2056]{2,1,0:T(1,128)}), f32[32,1,2056]{2,1,0:T(1,128)S(1)}, u32[]{:S(2)}, u32[]{:S(2)}) %all-to-all-start.2) | async-done | bytes 263200 | tf_op jit(solution)/shard_map/all_to_all | solution.py:98
  78.6 0.2 reduce_sum.90
  78.8 0.9 broadcast_in_dim.90
  79.6 2.6 %all-to-all-start.3 = ((f32[32,1,2056]{2,1,0:T(1,128)}), f32[32,1,2056]{2,1,0:T(1,128)S(1)}, u32[]{:S(2)}, u32[]{:S(2)}) async-start(f32[32,1,2056]{2,1,0:T(1,128)} %broadcast_in_dim.90), calls=%async_computation.3 | async-start | bytes 557056 | tf_op jit(solution)/shard_map/all_to_all | solution.py:100
  82.3 2.4 %convolution_add_fusion = f32[512,256]{0,1:T(8,128)S(1)} fusion(f32[64,8,4,128]{3,2,1,0:T(4,128)S(1)} %bitcast.81, f32[512,256]{0,1:T(8,128)S(1)} %copy-done.1, f32[512,256]{0,1:T(8,128)S(1)} %get-tuple-element.29, f32[512]{0:T(512)S(1)} %multiply_multiply_fusion, f32[512]{0:T(512)S(1)} %fusion.71, f32[512,256]{0,1:T(8,128)} %get-tuple-element.32, ...), kind=kOutput, calls=%fused_computation.9 | convolution fusion | flops 806879232 | bytes 3150848 | tf_op jit(solution)/shard_map/dot_general | solution.py:55
  84.7 0.8 convolution_add_fusion.2
  85.5 0.2 copy.41
  85.7 4.7 %gather_fusion.2 = f32[1024,256]{1,0:T(8,128)} fusion(f32[512,256]{1,0:T(8,128)S(1)} %copy.41, s32[1024]{0:T(1024)S(1)} %broadcast_clamp_fusion), kind=kCustom, calls=%fused_computation.2 | custom fusion | bytes 2101248 | tf_op jit(solution)/shard_map/gather | solution.py:165
  90.4 2.9 %all-to-all-done.3 = f32[32,1,2056]{2,1,0:T(1,128)S(1)} async-done(((f32[32,1,2056]{2,1,0:T(1,128)}), f32[32,1,2056]{2,1,0:T(1,128)S(1)}, u32[]{:S(2)}, u32[]{:S(2)}) %all-to-all-start.3) | async-done | bytes 263200 | tf_op jit(solution)/shard_map/all_to_all | solution.py:100
  93.3 2.9 %all-to-all-start.1 = ((f32[32,32,256]{2,1,0:T(8,128)}), f32[32,32,256]{2,1,0:T(8,128)S(1)}, u32[]{:S(2)}, u32[]{:S(2)}) async-start(f32[32,32,256]{2,1,0:T(8,128)} %bitcast.25), calls=%async_computation.1 | async-start | bytes 2097152 | tf_op jit(solution)/shard_map/all_to_all | solution.py:166
  96.2 0.7 reduce.8
  96.9 0.2 reshape.245
  97.1 0.6 slice_multiply_fusion.1
  97.7 0.7 slice_multiply_fusion
  98.4 24.1 %all-to-all-done.1 = f32[32,32,256]{2,1,0:T(8,128)S(1)} async-done(((f32[32,32,256]{2,1,0:T(8,128)}), f32[32,32,256]{2,1,0:T(8,128)S(1)}, u32[]{:S(2)}, u32[]{:S(2)}) %all-to-all-start.1) | async-done | bytes 1048608 | tf_op jit(solution)/shard_map/all_to_all | solution.py:166
  122.5 2.2 %gather_fusion.3 = f32[512,256]{1,0:T(8,128)} fusion(f32[1024,256]{1,0:T(8,128)S(1)} %bitcast.79, s32[1024]{0:T(1024)S(1)} %pad_clamp_fusion), kind=kCustom, calls=%fused_computation.3 | custom fusion | bytes 1050624 | tf_op jit(solution)/shard_map/gather | solution.py:173
  (41 shorter events, 0.2 us)
Async XLA Ops:
  0.6 3.0 %copy-start = (f32[512,256]{1,0:T(8,128)S(1)}, f32[512,256]{1,0:T(8,128)}, u32[]{:S(2)}) copy-start(f32[512,256]{1,0:T(8,128)} %param.12) | copy-start | bytes 1572868
  9.2 7.4 %copy-start.3 = (f32[512,256]{1,0:T(8,128)S(1)}, f32[512,256]{1,0:T(8,128)}, u32[]{:S(2)}) copy-start(f32[512,256]{1,0:T(8,128)} %param.21) | copy-start | bytes 1572868
  9.2 8.4 %copy-start.13 = (s32[1,3]{1,0:T(1,128)S(1)}, s32[1,3]{1,0:T(1,128)}, u32[]{:S(2)}) copy-start(s32[1,3]{1,0:T(1,128)} %param.18) | copy-start | bytes 40
  9.2 8.6 %copy-start.11 = (s32[1,8,2]{1,2,0:T(2,128)S(1)}, s32[1,8,2]{1,2,0:T(2,128)}, u32[]{:S(2)}) copy-start(s32[1,8,2]{1,2,0:T(2,128)} %param.17) | copy-start | bytes 196
  9.2 34.0 %all-to-all-start = ((f32[32,1,8320]{2,1,0:T(1,128)}), f32[32,1,8320]{2,1,0:T(1,128)}, u32[]{:S(2)}, u32[]{:S(2)}) async-start(f32[32,1,8320]{2,1,0:T(1,128)} %all_to_all.21), calls=%async_computation | async-start | bytes 2129920 | tf_op jit(solution)/shard_map/all_to_all | solution.py:144
  16.6 1.2 copy-start.5
  17.8 49.9 %copy-start.7 = (pred[256]{0:T(512)(128)(4,1)}, pred[256]{0:T(512)(128)(4,1)S(1)}, u32[]{:S(2)}) copy-start(pred[256]{0:T(512)(128)(4,1)S(1)} %compare_bitcast_fusion) | copy-start | bytes 772
  47.4 1.8 %copy-start.6 = (s32[1,2,128]{2,1,0:T(2,128)S(1)}, s32[1,2,128]{2,1,0:T(2,128)}, u32[]{:S(2)}) copy-start(s32[1,2,128]{2,1,0:T(2,128)} %param.19) | copy-start | bytes 3076
  49.0 2.6 %copy-start.2 = (f32[1,2,128,128]{3,2,1,0:T(8,128)S(1)}, f32[1,2,128,128]{3,2,1,0:T(8,128)}, u32[]{:S(2)}) copy-start(f32[1,2,128,128]{3,2,1,0:T(8,128)} %param.20) | copy-start | bytes 393220
  50.0 1.6 %collective-permute-start = (f32[128,256]{1,0:T(8,128)S(1)}, f32[128,256]{1,0:T(8,128)S(1)}, u32[]{:S(2)}, u32[]{:S(2)}) collective-permute-start(f32[128,256]{1,0:T(8,128)S(1)} %get-tuple-element.22), channel_id=1, source_target_pairs={{0,1},{1,0},{2,3},{3,2},{4,5},{5,4},{6,7},{7,6},{8,9},{9,8},{10,11... | collective-permute-start | bytes 393224 | tf_op jit(solution)/shard_map/ppermute | solution.py:17
  50.1 5.9 %collective-permute-start.1 = (f32[128,256]{1,0:T(8,128)S(1)}, f32[128,256]{1,0:T(8,128)S(1)}, u32[]{:S(2)}, u32[]{:S(2)}) collective-permute-start(f32[128,256]{1,0:T(8,128)S(1)} %get-tuple-element.23), channel_id=1, source_target_pairs={{0,2},{1,3},{2,0},{3,1},{4,6},{5,7},{6,4},{7,5},{8,10},{9,11},{10,... | collective-permute-start | bytes 393224 | tf_op jit(solution)/shard_map/ppermute | solution.py:17
  57.1 1.2 copy-start.9
  57.1 1.2 copy-start.12
  58.3 1.9 %copy-start.4 = (f32[512,256]{1,0:T(8,128)S(1)}, f32[512,256]{1,0:T(8,128)}, u32[]{:S(2)}) copy-start(f32[512,256]{1,0:T(8,128)} %param.21) | copy-start | bytes 1572868
  63.9 14.7 %all-to-all-start.2 = ((f32[32,1,2056]{2,1,0:T(1,128)}), f32[32,1,2056]{2,1,0:T(1,128)S(1)}, u32[]{:S(2)}, u32[]{:S(2)}) async-start(f32[32,1,2056]{2,1,0:T(1,128)} %all_to_all.28), calls=%async_computation.2 | async-start | bytes 557056 | tf_op jit(solution)/shard_map/all_to_all | solution.py:98
  69.6 12.6 %copy-start.1 = (f32[512,256]{0,1:T(8,128)S(1)}, f32[512,256]{0,1:T(8,128)}, u32[]{:S(2)}) copy-start(f32[512,256]{0,1:T(8,128)} %copy.38) | copy-start | bytes 1572868
  69.6 12.6 %copy-start.10 = (f32[256]{0:T(256)S(1)}, f32[256]{0:T(256)}, u32[]{:S(2)}) copy-start(f32[256]{0:T(256)} %param.15) | copy-start | bytes 3076
  70.0 14.7 %collective-permute-start.2 = (f32[128,256]{0,1:T(8,128)S(1)}, f32[128,256]{0,1:T(8,128)S(1)}, u32[]{:S(2)}, u32[]{:S(2)}) collective-permute-start(f32[128,256]{0,1:T(8,128)S(1)} %convolution_bitcast_fusion.1), channel_id=1, source_target_pairs={{0,1},{1,0},{2,3},{3,2},{4,5},{5,4},{6,7},{7,6},{8,9},{9,8},{10,11... | collective-permute-start | bytes 393224 | tf_op jit(solution)/shard_map/ppermute | solution.py:17
  70.6 14.1 %collective-permute-start.3 = (f32[128,256]{0,1:T(8,128)S(1)}, f32[128,256]{0,1:T(8,128)S(1)}, u32[]{:S(2)}, u32[]{:S(2)}) collective-permute-start(f32[128,256]{0,1:T(8,128)S(1)} %convolution_bitcast_fusion), channel_id=1, source_target_pairs={{0,2},{1,3},{2,0},{3,1},{4,6},{5,7},{6,4},{7,5},{8,10},{9,11},{10,... | collective-permute-start | bytes 393224 | tf_op jit(solution)/shard_map/ppermute | solution.py:17
  79.6 13.7 %all-to-all-start.3 = ((f32[32,1,2056]{2,1,0:T(1,128)}), f32[32,1,2056]{2,1,0:T(1,128)S(1)}, u32[]{:S(2)}, u32[]{:S(2)}) async-start(f32[32,1,2056]{2,1,0:T(1,128)} %broadcast_in_dim.90), calls=%async_computation.3 | async-start | bytes 557056 | tf_op jit(solution)/shard_map/all_to_all | solution.py:100
  82.3 2.4 %copy-start.8 = (pred[256]{0:T(512)(128)(4,1)S(1)}, pred[256]{0:T(512)(128)(4,1)}, u32[]{:S(2)}) copy-start(pred[256]{0:T(512)(128)(4,1)} %copy-done.7) | copy-start | bytes 772
  93.3 29.1 %all-to-all-start.1 = ((f32[32,32,256]{2,1,0:T(8,128)}), f32[32,32,256]{2,1,0:T(8,128)S(1)}, u32[]{:S(2)}, u32[]{:S(2)}) async-start(f32[32,32,256]{2,1,0:T(8,128)} %bitcast.25), calls=%async_computation.1 | async-start | bytes 2097152 | tf_op jit(solution)/shard_map/all_to_all | solution.py:166

commit v6 on v5

--- a/solution.py
+++ b/solution.py
@@ -91,16 +91,33 @@
     return total + spread(chooser, jnp.concatenate(arrived, axis=0))
 
 
+def butterfly_steps():
+    steps = []
+    for axis in ("col", "row"):
+        size = lax.axis_size(axis)
+        steps += [(axis, bit) for bit in range(size.bit_length() - 1)]
+    return steps
+
+
 def summed_everywhere(grad_weight, grad_gain, devices):
     packed = jnp.concatenate([grad_weight, grad_gain[None]], 0)
     rows, width = packed.shape
-    pieces = packed.reshape(devices, -1)
-    gathered = lax.all_to_all(pieces, ("row", "col"), 0, 0, tiled=True)
-    chunk = jnp.sum(gathered, axis=0, keepdims=True)
-    spread = lax.all_to_all(
-        jnp.broadcast_to(chunk, pieces.shape), ("row", "col"), 0, 0, tiled=True
-    )
-    total = spread.reshape(rows, width)
+    piece = packed.reshape(-1)
+    steps = butterfly_steps()
+    for axis, bit in steps:
+        half = piece.shape[0] // 2
+        side = (lax.axis_index(axis) >> bit) & 1
+        keep = lax.dynamic_slice_in_dim(piece, side * half, half)
+        send = lax.dynamic_slice_in_dim(piece, (1 - side) * half, half)
+        piece = keep + swapped(send, axis, bit)
+    for axis, bit in reversed(steps):
+        half = piece.shape[0]
+        side = (lax.axis_index(axis) >> bit) & 1
+        other = swapped(piece, axis, bit)
+        joined = jnp.zeros((2 * half,), piece.dtype)
+        joined = lax.dynamic_update_slice_in_dim(joined, piece, side * half, 0)
+        piece = lax.dynamic_update_slice_in_dim(joined, other, (1 - side) * half, 0)
+    total = piece.reshape(rows, width)
     return total[:-1], total[-1]
 
 

time: 125 us -> 147 us (1.18)
  local copies, waits for them, and re-layouts: 21.6 us -> 28.4 us
  waiting for transfers between devices: 61.7 us -> 67.7 us
  starting transfers between devices: 20.2 us -> 23.8 us
  other arithmetic: 5.33 us -> 8.67 us
  matrix products: 14.8 us -> 16.7 us
    ppermute x4 -> x14, waiting for transfers between devices: 4.1 us -> 19.5 us  [swapped(): lax.ppermute(array, axis, [(i, i ^ 1 << apart) for i in range(lax.axis_si...]
    ppermute x4 -> x14, starting transfers between devices: 3.49 us -> 12.8 us  [swapped(): lax.ppermute(array, axis, [(i, i ^ 1 << apart) for i in range(lax.axis_si...]
    all_to_all x2 -> x0, waiting for transfers between devices: 9.26 us -> none  [the longest x1 6.32 us: summed_everywhere(): gathered = lax.all_to_all(pieces, ('row', 'col'), 0, 0, tiled=True)]
    all_to_all x2 -> x0, starting transfers between devices: 6.4 us -> none  [the longest x1 3.81 us: summed_everywhere(): gathered = lax.all_to_all(pieces, ('row', 'col'), 0, 0, tiled=True)]
    dynamic_update_slice x0 -> x9, local copies, waits for them, and re-layouts: none -> 5.58 us  [the longest x4 3.01 us: summed_everywhere(): joined = lax.dynamic_update_slice_in_dim(joined, piece, side * half, 0)]
    add x0 -> x4, other arithmetic: none -> 2.8 us  [summed_everywhere(): piece = keep + swapped(send, axis, bit)]
    dynamic_slice x0 -> x5, local copies, waits for them, and re-layouts: none -> 2.02 us  [summed_everywhere(): send = lax.dynamic_slice_in_dim(piece, (1 - side) * half, half)]
    dot_general x3, matrix products: 4.05 us -> 5.74 us  [spread(): lax.dot_general(chooser, values, (((0,), (0,)), ((), ())), precision=PREC...]
  transfers between devices with their start and end apart: 8 -> 16, of which waited for: 5 -> 11; matrix products, arithmetic and copies ran while one was open for 13% -> 16% of each run, Pallas kernels for 0% -> 0%
where the time goes in v6:
time: 147 us
  waiting for transfers between devices  67.7 us (46%)
  local copies, waits for them, and re-layouts  28.4 us (19%)
  starting transfers between devices  23.8 us (16%)
  matrix products  16.7 us (11%)
  other arithmetic  8.67 us (6%)
    all_to_all x1, waiting for transfers between devices, on_device(): lax.all_to_all(jnp.concatenate([outbox, tags], axis=1), ('row', 'col'), 0...  25.7 us
    all_to_all x1, waiting for transfers between devices, on_device(): lax.all_to_all(reply.reshape(devices, capacity, feat_count), ('row', 'col...  22.5 us
    ppermute x14, waiting for transfers between devices, swapped(): lax.ppermute(array, axis, [(i, i ^ 1 << apart) for i in range(lax.axis_si...  19.5 us
    ppermute x14, starting transfers between devices, swapped(): lax.ppermute(array, axis, [(i, i ^ 1 << apart) for i in range(lax.axis_si...  12.8 us
    all_to_all x1, starting transfers between devices, on_device(): lax.all_to_all(jnp.concatenate([outbox, tags], axis=1), ('row', 'col'), 0...  7.48 us
    dot_general x3, matrix products, spread(): lax.dot_general(chooser, values, (((0,), (0,)), ((), ())), precision=PREC...  5.74 us
    gather x1, local copies, waits for them, and re-layouts, on_device(): reply = grad_nodes[jnp.minimum(place_in, row_count - 1)]  4.69 us
    dot_general x3, matrix products, layer_piece(): jnp.dot(normed, weight, precision=PRECISE, preferred_element_type=jnp.flo...  4.4 us
  transfers between devices with their start and end apart: 16, of which 11 were waited for; matrix products, arithmetic and copies ran while one was open for 16% of the time, Pallas kernels for 0%

profile of v6, /device:TPU:0, one launch (start us, length us, event | category | flops | bytes accessed | tf_op | source)
XLA Modules:
  0.0 146.5 jit_solution(17489266967575154724)
XLA Ops:
  0.6 0.6 compare_reduce_fusion
  1.3 0.7 add_select_fusion
  2.3 0.6 compare_select_fusion.2
  2.8 0.6 select_reduce_fusion.2
  3.5 0.7 convert_select_fusion
  4.2 3.5 %gather_fusion = f32[1024,256]{1,0:T(8,128)S(1)} fusion(f32[512,256]{1,0:T(8,128)S(1)} %copy-done, s32[1024]{0:T(1024)S(1)} %maximum_clamp_fusion), kind=kCustom, calls=%fused_computation | custom fusion | bytes 2101248 | tf_op jit(solution)/shard_map/gather | solution.py:156
  8.0 1.7 %all_to_all.11 = f32[32,1,8320]{2,1,0:T(1,128)} reshape(f32[32,8320]{1,0:T(8,128)S(1)} %select_maximum_fusion) | data formatting | bytes 2129920 | tf_op jit(solution)/shard_map/all_to_all | solution.py:161
  9.7 7.5 %all-to-all-start = ((f32[32,1,8320]{2,1,0:T(1,128)}), f32[32,1,8320]{2,1,0:T(1,128)S(1)}, u32[]{:S(2)}, u32[]{:S(2)}) async-start(f32[32,1,8320]{2,1,0:T(1,128)} %all_to_all.11), calls=%async_computation | async-start | bytes 2129920 | tf_op jit(solution)/shard_map/all_to_all | solution.py:161
  17.4 0.5 iota_compare_fusion.8
  17.9 25.7 %all-to-all-done = f32[32,1,8320]{2,1,0:T(1,128)S(1)} async-done(((f32[32,1,8320]{2,1,0:T(1,128)}), f32[32,1,8320]{2,1,0:T(1,128)S(1)}, u32[]{:S(2)}, u32[]{:S(2)}) %all-to-all-start) | async-done | bytes 1064992 | tf_op jit(solution)/shard_map/all_to_all | solution.py:161
  43.7 1.1 slice.95
  45.2 1.4 reshape.241
  46.6 1.6 %gather_fusion.1 = f32[512,256]{1,0:T(8,128)S(1)} fusion(f32[1024,256]{1,0:T(8,128)S(1)} %reshape.241, s32[1024]{0:T(1024)S(1)} %pad_clamp_fusion.1), kind=kCustom, calls=%fused_computation.1 | custom fusion | bytes 1050624 | tf_op jit(solution)/shard_map/gather | solution.py:169
  48.2 0.7 fusion.9
  48.9 0.7 fusion.86
  49.6 1.0 fusion.15
  50.6 1.0 copy.35
  51.6 1.5 collective-permute-start.1
  53.4 4.1 %collective-permute-done.1 = f32[128,256]{1,0:T(8,128)S(1)} collective-permute-done((f32[128,256]{1,0:T(8,128)S(1)}, f32[128,256]{1,0:T(8,128)S(1)}, u32[]{:S(2)}, u32[]{:S(2)}) %collective-permute-start.1) | collective-permute-done | bytes 131104 | tf_op jit(solution)/shard_map/ppermute | solution.py:17
  57.8 1.5 %fusion.7 = f32[512,256]{0,1:T(8,128)S(1)} fusion(f32[128,256]{1,0:T(8,128)S(1)} %convolution_bitcast_fusion.2, f32[128,256]{1,0:T(8,128)S(1)} %convolution_bitcast_fusion.3, s32[256]{0:T(256)} %bitcast.87, pred[256]{0:T(512)(128)(4,1)} %copy-done.17), kind=kOutput, calls=%fused_computation.28 | convolution fusion | flops 403111936 | bytes 787712 | tf_op jit(solution)/shard_map/dot_general | solution.py:55
  59.4 1.1 multiply_reduce_fusion.2
  60.6 1.9 %multiply_add_fusion = (f32[512,256]{1,0:T(8,128)}, f32[512,256]{1,0:T(8,128)S(1)}) fusion(f32[512,256]{1,0:T(8,128)S(1)} %gather_fusion.1, f32[256,256]{1,0:T(8,128)S(1)} %copy-done.22, f32[512,256]{0,1:T(8,128)S(1)} %get-tuple-element.31, f32[256]{0:T(256)S(1)} %copy-done.20, f32[512]{0:T(512)S(1)} %fusion.71), kind=kOutput, calls=%fused_computation.43 | convolution fusion | flops 403570688 | bytes 2362368 | tf_op jit(solution)/shard_map/jvp()/dot_general | solution.py:24
  62.5 0.8 fusion.22
  63.3 1.7 %multiply_reduce_fusion = (f32[256]{0:T(256)S(1)}, f32[512]{0:T(512)S(1)}, f32[512,256]{0,1:T(8,128)}) fusion(f32[512,256]{0,1:T(8,128)S(1)} %get-tuple-element.31, f32[512]{0:T(512)S(1)} %fusion.71, f32[256]{0:T(256)S(1)} %copy-done.20, f32[256,256]{1,0:T(8,128)S(1)} %copy-done.22, f32[512,256]{1,0:T(8,128)S(1)} %get-tuple-element.33, ...), kind=kOutput, calls=%fused_computation.41 | convolution fusion | flops 404618496 | bytes 2365440 | tf_op jit(solution)/shard_map/transpose(jvp())/dot_general | solution.py:24
  65.1 0.8 dynamic_slice.31
  65.8 1.3 copy.37
  67.1 0.4 collective-permute-done.4
  67.5 1.7 %dynamic-slice_add_fusion = f32[32896]{0:T(1024)} fusion(f32[32896]{0:T(1024)} %collective-permute-done.4, f32[65792]{0:T(1024)S(1)} %reshape.246, s32[]{:T(128)S(6)} %select_n.112), kind=kLoop, calls=%fused_computation.82 | loop fusion | flops 32896 | bytes 394756 | tf_op jit(solution)/shard_map/add | solution.py:112
  69.2 1.0 dynamic_slice.33
  70.2 1.5 %collective-permute-start.5 = (f32[16448]{0:T(1024)S(1)}, f32[16448]{0:T(1024)S(1)}, u32[]{:S(2)}, u32[]{:S(2)}) collective-permute-start(f32[16448]{0:T(1024)S(1)} %dynamic_slice.33), channel_id=1, source_target_pairs={{0,2},{1,3},{2,0},{3,1},{4,6},{5,7},{6,4},{7,5},{8,10},{9,11},{10,... | collective-permute-start | bytes 197384 | tf_op jit(solution)/shard_map/ppermute | solution.py:17
  71.8 2.8 %collective-permute-done.5 = f32[16448]{0:T(1024)S(1)} collective-permute-done((f32[16448]{0:T(1024)S(1)}, f32[16448]{0:T(1024)S(1)}, u32[]{:S(2)}, u32[]{:S(2)}) %collective-permute-start.5) | collective-permute-done | bytes 65824 | tf_op jit(solution)/shard_map/ppermute | solution.py:17
  74.6 1.0 dynamic-slice_add_fusion.1
  75.6 1.5 %collective-permute-start.6 = (f32[8224]{0:T(1024)S(1)}, f32[8224]{0:T(1024)S(1)}, u32[]{:S(2)}, u32[]{:S(2)}) collective-permute-start(f32[8224]{0:T(1024)S(1)} %dynamic_slice.35), channel_id=1, source_target_pairs={{0,4},{4,0},{8,12},{12,8},{16,20},{20,16},{24,28},{28,24},{1,5},{5... | collective-permute-start | bytes 98696 | tf_op jit(solution)/shard_map/ppermute | solution.py:17
  77.1 2.5 %collective-permute-done.6 = f32[8224]{0:T(1024)S(1)} collective-permute-done((f32[8224]{0:T(1024)S(1)}, f32[8224]{0:T(1024)S(1)}, u32[]{:S(2)}, u32[]{:S(2)}) %collective-permute-start.6) | collective-permute-done | bytes 32928 | tf_op jit(solution)/shard_map/ppermute | solution.py:17
  79.8 0.7 collective-permute-start.7
  80.5 0.6 broadcast_clamp_fusion
  81.1 2.4 %collective-permute-done.7 = f32[4112]{0:T(1024)S(1)} collective-permute-done((f32[4112]{0:T(1024)S(1)}, f32[4112]{0:T(1024)S(1)}, u32[]{:S(2)}, u32[]{:S(2)}) %collective-permute-start.7) | collective-permute-done | bytes 16480 | tf_op jit(solution)/shard_map/ppermute | solution.py:17
  83.7 1.0 collective-permute-start.8
  84.8 3.6 %collective-permute-done.8 = f32[2056]{0:T(1024)S(1)} collective-permute-done((f32[2056]{0:T(1024)S(1)}, f32[2056]{0:T(1024)S(1)}, u32[]{:S(2)}, u32[]{:S(2)}) %collective-permute-start.8) | collective-permute-done | bytes 8256 | tf_op jit(solution)/shard_map/ppermute | solution.py:17
  88.3 0.4 fusion.85
  88.7 1.1 collective-permute-start.9
  89.8 2.1 %fusion.5 = f32[256,256]{1,0:T(8,128)S(1)} fusion(s32[256]{0:T(256)S(1)} %bitcast.89, pred[256]{0:T(512)(128)(4,1)S(1)} %copy-done.18, f32[512,256]{0,1:T(8,128)} %copy-done.2, f32[512,256]{0,1:T(8,128)} %get-tuple-element.34, f32[512]{0:T(512)S(1)} %multiply_multiply_fusion, f32[256]{0:T(256)S(1)} %copy-done.20, f32[512]{0:T(512)S(1)} %fusion.71), kind=kOutput, calls=%fused_computation.26 | convolution fusion | flops 403701760 | bytes 1317120 | tf_op jit(solution)/shard_map/dot_general | solution.py:79
  91.9 1.5 collective-permute-done.9
  93.6 0.8 collective-permute-start.10
  94.4 0.4 convolution_bitcast_fusion
  94.8 0.4 dynamic_update_slice.32
  95.3 2.1 %collective-permute-done.10 = f32[4112]{0:T(1024)S(1)} collective-permute-done((f32[4112]{0:T(1024)S(1)}, f32[4112]{0:T(1024)S(1)}, u32[]{:S(2)}, u32[]{:S(2)}) %collective-permute-start.10) | collective-permute-done | bytes 16480 | tf_op jit(solution)/shard_map/ppermute | solution.py:17
  97.7 1.6 %collective-permute-start.11 = (f32[8224]{0:T(1024)S(1)}, f32[8224]{0:T(1024)S(1)}, u32[]{:S(2)}, u32[]{:S(2)}) collective-permute-start(f32[8224]{0:T(1024)S(1)} %dynamic_update_slice.33), channel_id=1, source_target_pairs={{0,4},{4,0},{8,12},{12,8},{16,20},{20,16},{24,28},{28,24},{1,5},{5... | collective-permute-start | bytes 98696 | tf_op jit(solution)/shard_map/ppermute | solution.py:17
  99.7 1.5 %collective-permute-start.3 = (f32[128,256]{0,1:T(8,128)S(1)}, f32[128,256]{0,1:T(8,128)}, u32[]{:S(2)}, u32[]{:S(2)}) collective-permute-start(f32[128,256]{0,1:T(8,128)S(1)} %convolution_bitcast_fusion), channel_id=1, source_target_pairs={{0,2},{1,3},{2,0},{3,1},{4,6},{5,7},{6,4},{7,5},{8,10},{9,11},{10,... | collective-permute-start | bytes 393224 | tf_op jit(solution)/shard_map/ppermute | solution.py:17
  101.2 0.6 dynamic_update_slice.34
  101.8 0.5 dynamic_update_slice.35
  102.3 1.4 collective-permute-start.12
  103.7 2.4 %convolution_add_fusion = f32[512,256]{0,1:T(8,128)S(1)} fusion(f32[64,8,4,128]{3,2,1,0:T(4,128)S(1)} %bitcast.80, f32[512,256]{0,1:T(8,128)S(1)} %copy.37, f32[512,256]{0,1:T(8,128)S(1)} %copy-done.3, f32[512]{0:T(512)} %copy-done.10, f32[512]{0:T(512)} %copy-done.11, f32[512,256]{0,1:T(8,128)} %get-tuple-element.34, f32[256]{0:T(256)} %param.15), kind=kOutput, calls=%fused_computation.9 | convolution fusion | flops 806879232 | bytes 3150848 | tf_op jit(solution)/shard_map/dot_general | solution.py:55
  106.2 0.8 dynamic_update_slice.36
  107.1 0.6 dynamic_update_slice.37
  107.9 1.8 %convolution_add_fusion.2 = f32[512,256]{0,1:T(8,128)S(1)} fusion(f32[512,256]{0,1:T(8,128)S(1)} %convolution_add_fusion, f32[128,256]{0,1:T(8,128)} %collective-permute-done.3, f32[128,256]{0,1:T(8,128)} %collective-permute-done.2, s32[256]{0:T(256)S(1)} %bitcast.90, pred[256]{0:T(512)(128)(4,1)S(1)} %copy-done.19), kind=kOutput, calls=%fused_computation.12 | convolution fusion | flops 403243008 | bytes 1312000 | tf_op jit(solution)/shard_map/dot_general | solution.py:55
  109.9 4.7 %gather_fusion.2 = f32[1024,256]{1,0:T(8,128)} fusion(f32[512,256]{1,0:T(8,128)S(1)} %copy.40, s32[1024]{0:T(1024)S(1)} %copy-done.8), kind=kCustom, calls=%fused_computation.2 | custom fusion | bytes 2101248 | tf_op jit(solution)/shard_map/gather | solution.py:182
  114.6 3.5 %all-to-all-start.1 = ((f32[32,32,256]{2,1,0:T(8,128)}), f32[32,32,256]{2,1,0:T(8,128)S(1)}, u32[]{:S(2)}, u32[]{:S(2)}) async-start(f32[32,32,256]{2,1,0:T(8,128)} %bitcast.25), calls=%async_computation.1 | async-start | bytes 2097152 | tf_op jit(solution)/shard_map/all_to_all | solution.py:183
  118.1 1.2 dynamic_update_slice.38
  119.4 1.1 dynamic_update_slice.39
  120.5 0.8 mul.169
  121.2 0.6 slice_multiply_fusion.1
  121.8 22.5 %all-to-all-done.1 = f32[32,32,256]{2,1,0:T(8,128)S(1)} async-done(((f32[32,32,256]{2,1,0:T(8,128)}), f32[32,32,256]{2,1,0:T(8,128)S(1)}, u32[]{:S(2)}, u32[]{:S(2)}) %all-to-all-start.1) | async-done | bytes 1048608 | tf_op jit(solution)/shard_map/all_to_all | solution.py:183
  144.3 2.2 %gather_fusion.3 = f32[512,256]{1,0:T(8,128)} fusion(f32[1024,256]{1,0:T(8,128)S(1)} %bitcast.78, s32[1024]{0:T(1024)S(1)} %pad_clamp_fusion), kind=kCustom, calls=%fused_computation.3 | custom fusion | bytes 1050624 | tf_op jit(solution)/shard_map/gather | solution.py:190
  (98 shorter events, 3.9 us)
Async XLA Ops:
  0.6 3.6 %copy-start = (f32[512,256]{1,0:T(8,128)S(1)}, f32[512,256]{1,0:T(8,128)}, u32[]{:S(2)}) copy-start(f32[512,256]{1,0:T(8,128)} %param.12) | copy-start | bytes 1572868
  9.7 7.5 %copy-start.23 = (s32[1,3]{1,0:T(1,128)S(1)}, s32[1,3]{1,0:T(1,128)}, u32[]{:S(2)}) copy-start(s32[1,3]{1,0:T(1,128)} %param.18) | copy-start | bytes 40
  9.7 7.7 %copy-start.21 = (s32[1,8,2]{1,2,0:T(2,128)S(1)}, s32[1,8,2]{1,2,0:T(2,128)}, u32[]{:S(2)}) copy-start(s32[1,8,2]{1,2,0:T(2,128)} %param.17) | copy-start | bytes 196
  9.7 33.9 %all-to-all-start = ((f32[32,1,8320]{2,1,0:T(1,128)}), f32[32,1,8320]{2,1,0:T(1,128)S(1)}, u32[]{:S(2)}, u32[]{:S(2)}) async-start(f32[32,1,8320]{2,1,0:T(1,128)} %all_to_all.11), calls=%async_computation | async-start | bytes 2129920 | tf_op jit(solution)/shard_map/all_to_all | solution.py:161
  17.4 30.8 %copy-start.17 = (pred[256]{0:T(512)(128)(4,1)}, pred[256]{0:T(512)(128)(4,1)S(1)}, u32[]{:S(2)}) copy-start(pred[256]{0:T(512)(128)(4,1)S(1)} %compare_bitcast_fusion) | copy-start | bytes 772
  46.6 1.6 %copy-start.12 = (s32[1,2,128]{2,1,0:T(2,128)S(1)}, s32[1,2,128]{2,1,0:T(2,128)}, u32[]{:S(2)}) copy-start(s32[1,2,128]{2,1,0:T(2,128)} %param.19) | copy-start | bytes 3076
  48.2 1.5 copy-start.7
  48.2 1.4 copy-start.15
  48.2 1.4 copy-start.16
  49.6 3.5 %collective-permute-start = (f32[128,256]{1,0:T(8,128)}, f32[128,256]{1,0:T(8,128)S(1)}, u32[]{:S(2)}, u32[]{:S(2)}) collective-permute-start(f32[128,256]{1,0:T(8,128)} %get-tuple-element.24), channel_id=1, source_target_pairs={{0,1},{1,0},{2,3},{3,2},{4,5},{5,4},{6,7},{7,6},{8,9},{9,8},{10,11... | collective-permute-start | bytes 393224 | tf_op jit(solution)/shard_map/ppermute | solution.py:17
  49.6 3.5 %copy-start.4 = (f32[1,2,128,128]{3,2,1,0:T(8,128)S(1)}, f32[1,2,128,128]{3,2,1,0:T(8,128)}, u32[]{:S(2)}) copy-start(f32[1,2,128,128]{3,2,1,0:T(8,128)} %param.20) | copy-start | bytes 393220
  51.6 7.7 %copy-start.1 = (f32[512,256]{0,1:T(8,128)S(1)}, f32[512,256]{0,1:T(8,128)}, u32[]{:S(2)}) copy-start(f32[512,256]{0,1:T(8,128)} %copy.35) | copy-start | bytes 1572868
  51.6 5.9 %collective-permute-start.1 = (f32[128,256]{1,0:T(8,128)S(1)}, f32[128,256]{1,0:T(8,128)S(1)}, u32[]{:S(2)}, u32[]{:S(2)}) collective-permute-start(f32[128,256]{1,0:T(8,128)S(1)} %get-tuple-element.25), channel_id=1, source_target_pairs={{0,2},{1,3},{2,0},{3,1},{4,6},{5,7},{6,4},{7,5},{8,10},{9,11},{10,... | collective-permute-start | bytes 393224 | tf_op jit(solution)/shard_map/ppermute | solution.py:17
  59.3 1.2 copy-start.20
  59.4 1.2 copy-start.22
  60.5 4.5 %copy-start.2 = (f32[512,256]{0,1:T(8,128)}, f32[512,256]{0,1:T(8,128)S(1)}, u32[]{:S(2)}) copy-start(f32[512,256]{0,1:T(8,128)S(1)} %get-tuple-element.31) | copy-start | bytes 1572868
  60.5 29.3 %copy-start.11 = (f32[512]{0:T(512)}, f32[512]{0:T(512)S(1)}, u32[]{:S(2)}) copy-start(f32[512]{0:T(512)S(1)} %fusion.71) | copy-start | bytes 6148
  60.6 1.9 %copy-start.6 = (f32[512,256]{1,0:T(8,128)S(1)}, f32[512,256]{1,0:T(8,128)}, u32[]{:S(2)}) copy-start(f32[512,256]{1,0:T(8,128)} %param.21) | copy-start | bytes 1572868
  65.8 1.7 %collective-permute-start.4 = (f32[32896]{0:T(1024)}, f32[32896]{0:T(1024)}, u32[]{:S(2)}, u32[]{:S(2)}) collective-permute-start(f32[32896]{0:T(1024)} %dynamic_slice.31), channel_id=1, source_target_pairs={{0,1},{1,0},{2,3},{3,2},{4,5},{5,4},{6,7},{7,6},{8,9},{9,8},{10,11... | collective-permute-start | bytes 394760 | tf_op jit(solution)/shard_map/ppermute | solution.py:17
  65.8 24.0 %copy-start.13 = (s32[1,2,128]{2,1,0:T(2,128)S(1)}, s32[1,2,128]{2,1,0:T(2,128)}, u32[]{:S(2)}) copy-start(s32[1,2,128]{2,1,0:T(2,128)} %param.19) | copy-start | bytes 3076
  65.8 24.0 %copy-start.18 = (pred[256]{0:T(512)(128)(4,1)S(1)}, pred[256]{0:T(512)(128)(4,1)}, u32[]{:S(2)}) copy-start(pred[256]{0:T(512)(128)(4,1)} %copy-done.17) | copy-start | bytes 772
  69.2 25.2 %copy-start.5 = (f32[1,2,128,128]{3,2,1,0:T(8,128)S(1)}, f32[1,2,128,128]{3,2,1,0:T(8,128)}, u32[]{:S(2)}) copy-start(f32[1,2,128,128]{3,2,1,0:T(8,128)} %param.20) | copy-start | bytes 393220
  70.2 4.4 %collective-permute-start.5 = (f32[16448]{0:T(1024)S(1)}, f32[16448]{0:T(1024)S(1)}, u32[]{:S(2)}, u32[]{:S(2)}) collective-permute-start(f32[16448]{0:T(1024)S(1)} %dynamic_slice.33), channel_id=1, source_target_pairs={{0,2},{1,3},{2,0},{3,1},{4,6},{5,7},{6,4},{7,5},{8,10},{9,11},{10,... | collective-permute-start | bytes 197384 | tf_op jit(solution)/shard_map/ppermute | solution.py:17
  75.6 4.0 %collective-permute-start.6 = (f32[8224]{0:T(1024)S(1)}, f32[8224]{0:T(1024)S(1)}, u32[]{:S(2)}, u32[]{:S(2)}) collective-permute-start(f32[8224]{0:T(1024)S(1)} %dynamic_slice.35), channel_id=1, source_target_pairs={{0,4},{4,0},{8,12},{12,8},{16,20},{20,16},{24,28},{28,24},{1,5},{5... | collective-permute-start | bytes 98696 | tf_op jit(solution)/shard_map/ppermute | solution.py:17
  79.8 3.8 %collective-permute-start.7 = (f32[4112]{0:T(1024)S(1)}, f32[4112]{0:T(1024)S(1)}, u32[]{:S(2)}, u32[]{:S(2)}) collective-permute-start(f32[4112]{0:T(1024)S(1)} %dynamic_slice.37), channel_id=1, source_target_pairs={{0,8},{4,12},{8,0},{12,4},{16,24},{20,28},{24,16},{28,20},{1,9},{5... | collective-permute-start | bytes 49352 | tf_op jit(solution)/shard_map/ppermute | solution.py:17
  83.7 4.6 %collective-permute-start.8 = (f32[2056]{0:T(1024)S(1)}, f32[2056]{0:T(1024)S(1)}, u32[]{:S(2)}, u32[]{:S(2)}) collective-permute-start(f32[2056]{0:T(1024)S(1)} %dynamic_slice.39), channel_id=1, source_target_pairs={{0,16},{4,20},{8,24},{12,28},{16,0},{20,4},{24,8},{28,12},{1,17},{... | collective-permute-start | bytes 24680 | tf_op jit(solution)/shard_map/ppermute | solution.py:17
  84.8 14.9 %copy-start.10 = (f32[512]{0:T(512)}, f32[512]{0:T(512)S(1)}, u32[]{:S(2)}) copy-start(f32[512]{0:T(512)S(1)} %multiply_multiply_fusion) | copy-start | bytes 6148
  88.7 4.7 %collective-permute-start.9 = (f32[2056]{0:T(1024)S(1)}, f32[2056]{0:T(1024)S(1)}, u32[]{:S(2)}, u32[]{:S(2)}) collective-permute-start(f32[2056]{0:T(1024)S(1)} %get-tuple-element.21), channel_id=1, source_target_pairs={{0,16},{4,20},{8,24},{12,28},{16,0},{20,4},{24,8},{28,12},{1,17},{... | collective-permute-start | bytes 24680 | tf_op jit(solution)/shard_map/ppermute | solution.py:17
  89.8 13.9 %copy-start.3 = (f32[512,256]{0,1:T(8,128)S(1)}, f32[512,256]{0,1:T(8,128)}, u32[]{:S(2)}) copy-start(f32[512,256]{0,1:T(8,128)} %copy-done.2) | copy-start | bytes 1572868
  93.6 3.8 %collective-permute-start.10 = (f32[4112]{0:T(1024)S(1)}, f32[4112]{0:T(1024)S(1)}, u32[]{:S(2)}, u32[]{:S(2)}) collective-permute-start(f32[4112]{0:T(1024)S(1)} %dynamic_update_slice.31), channel_id=1, source_target_pairs={{0,8},{4,12},{8,0},{12,4},{16,24},{20,28},{24,16},{28,20},{1,9},{5... | collective-permute-start | bytes 49352 | tf_op jit(solution)/shard_map/ppermute | solution.py:17
  97.7 4.1 %collective-permute-start.11 = (f32[8224]{0:T(1024)S(1)}, f32[8224]{0:T(1024)S(1)}, u32[]{:S(2)}, u32[]{:S(2)}) collective-permute-start(f32[8224]{0:T(1024)S(1)} %dynamic_update_slice.33), channel_id=1, source_target_pairs={{0,4},{4,0},{8,12},{12,8},{16,20},{20,16},{24,28},{28,24},{1,5},{5... | collective-permute-start | bytes 98696 | tf_op jit(solution)/shard_map/ppermute | solution.py:17
  99.7 8.2 %collective-permute-start.2 = (f32[128,256]{0,1:T(8,128)S(1)}, f32[128,256]{0,1:T(8,128)}, u32[]{:S(2)}, u32[]{:S(2)}) collective-permute-start(f32[128,256]{0,1:T(8,128)S(1)} %convolution_bitcast_fusion.1), channel_id=1, source_target_pairs={{0,1},{1,0},{2,3},{3,2},{4,5},{5,4},{6,7},{7,6},{8,9},{9,8},{10,11... | collective-permute-start | bytes 393224 | tf_op jit(solution)/shard_map/ppermute | solution.py:17
  99.7 8.1 %collective-permute-start.3 = (f32[128,256]{0,1:T(8,128)S(1)}, f32[128,256]{0,1:T(8,128)}, u32[]{:S(2)}, u32[]{:S(2)}) collective-permute-start(f32[128,256]{0,1:T(8,128)S(1)} %convolution_bitcast_fusion), channel_id=1, source_target_pairs={{0,2},{1,3},{2,0},{3,1},{4,6},{5,7},{6,4},{7,5},{8,10},{9,11},{10,... | collective-permute-start | bytes 393224 | tf_op jit(solution)/shard_map/ppermute | solution.py:17
  102.3 5.6 %copy-start.14 = (s32[1,2,128]{2,1,0:T(2,128)S(1)}, s32[1,2,128]{2,1,0:T(2,128)}, u32[]{:S(2)}) copy-start(s32[1,2,128]{2,1,0:T(2,128)} %param.19) | copy-start | bytes 3076
  102.3 5.6 %copy-start.19 = (pred[256]{0:T(512)(128)(4,1)S(1)}, pred[256]{0:T(512)(128)(4,1)}, u32[]{:S(2)}) copy-start(pred[256]{0:T(512)(128)(4,1)} %copy-done.17) | copy-start | bytes 772
  102.3 4.9 %collective-permute-start.12 = (f32[16448]{0:T(1024)S(1)}, f32[16448]{0:T(1024)S(1)}, u32[]{:S(2)}, u32[]{:S(2)}) collective-permute-start(f32[16448]{0:T(1024)S(1)} %dynamic_update_slice.35), channel_id=1, source_target_pairs={{0,2},{1,3},{2,0},{3,1},{4,6},{5,7},{6,4},{7,5},{8,10},{9,11},{10,... | collective-permute-start | bytes 197384 | tf_op jit(solution)/shard_map/ppermute | solution.py:17
  107.7 2.1 %copy-start.8 = (s32[1024]{0:T(1024)S(1)}, s32[1024]{0:T(1024)}, u32[]{:S(2)}) copy-start(s32[1024]{0:T(1024)} %broadcast_clamp_fusion) | copy-start | bytes 12292
  107.8 11.6 %collective-permute-start.13 = (f32[32896]{0:T(1024)S(1)}, f32[32896]{0:T(1024)S(1)}, u32[]{:S(2)}, u32[]{:S(2)}) collective-permute-start(f32[32896]{0:T(1024)S(1)} %dynamic_update_slice.37), channel_id=1, source_target_pairs={{0,1},{1,0},{2,3},{3,2},{4,5},{5,4},{6,7},{7,6},{8,9},{9,8},{10,11... | collective-permute-start | bytes 394760 | tf_op jit(solution)/shard_map/ppermute | solution.py:17
  114.6 3.5 %copy-start.9 = (s32[512]{0:T(512)S(1)}, s32[512]{0:T(512)}, u32[]{:S(2)}) copy-start(s32[512]{0:T(512)} %get-tuple-element.22) | copy-start | bytes 6148
  114.6 29.7 %all-to-all-start.1 = ((f32[32,32,256]{2,1,0:T(8,128)}), f32[32,32,256]{2,1,0:T(8,128)S(1)}, u32[]{:S(2)}, u32[]{:S(2)}) async-start(f32[32,32,256]{2,1,0:T(8,128)} %bitcast.25), calls=%async_computation.1 | async-start | bytes 2097152 | tf_op jit(solution)/shard_map/all_to_all | solution.py:183

commit v7 on v5

--- a/solution.py
+++ b/solution.py
@@ -102,6 +102,19 @@
     )
     total = spread.reshape(rows, width)
     return total[:-1], total[-1]
+
+
+def exact_pick(chooser, values, transposed=False):
+    hi = lax.reduce_precision(values, 8, 7)
+    rest = values - hi
+    mid = lax.reduce_precision(rest, 8, 7)
+    parts = jnp.concatenate([hi, mid, rest - mid], axis=1).astype(jnp.bfloat16)
+    dims = (((0,), (0,)), ((), ())) if transposed else (((1,), (0,)), ((), ()))
+    out = lax.dot_general(
+        chooser.astype(jnp.bfloat16), parts, dims, preferred_element_type=jnp.float32
+    )
+    width = values.shape[1]
+    return (out[:, :width] + out[:, width : 2 * width]) + out[:, 2 * width :]
 
 
 def on_device(
@@ -136,7 +149,7 @@
     places = jnp.where(
         filled, jnp.sum(jnp.where(chosen, within[None, :], 0), axis=1), row_count
     )
-    outbox = x_scan[jnp.maximum(source, 0)].reshape(devices, capacity * feat_count)
+    outbox = exact_pick(chosen, x_scan).reshape(devices, capacity * feat_count)
     lanes = 128 * (-(-capacity // 128))
     tags = jnp.zeros((devices, lanes), jnp.float32).at[:, :capacity].set(
         places.reshape(devices, capacity).astype(jnp.float32)
@@ -148,8 +161,7 @@
     place_in = got[:, capacity * feat_count : capacity * feat_count + capacity]
     place_in = place_in.astype(jnp.int32).reshape(-1)
     landing = place_in[None, :] == order[:, None]
-    arrival = jnp.sum(jnp.where(landing, slots[None, :], 0), axis=1)
-    hidden = inbox[arrival]
+    hidden = exact_pick(landing, inbox)
     tiles = dense_tiles(tile_values[0], tile_coords[0], counts[0, 0], row_count)
     chooser = pickers(boundary_rows, counts, row_count)
     aggregate = hidden + jnp.dot(
@@ -162,7 +174,7 @@
     weight_sum, gain_sum = summed_everywhere(grad_weight, grad_gain, devices)
     grad_nodes = cotangent + grad_agg + spread(tiles, grad_agg)
     grad_nodes = boundary_backward(grad_nodes, grad_agg, chooser, coupling)
-    reply = grad_nodes[jnp.minimum(place_in, row_count - 1)]
+    reply = exact_pick(landing, grad_nodes, transposed=True)
     returned = lax.all_to_all(
         reply.reshape(devices, capacity, feat_count),
         ("row", "col"),
@@ -170,7 +182,7 @@
         concat_axis=0,
         tiled=True,
     )
-    x_grad = returned.reshape(-1, feat_count)[bucket]
+    x_grad = exact_pick(chosen, returned.reshape(-1, feat_count), transposed=True)
     node_scale = 1.0 / math.sqrt(row_count * devices)
     return (output, x_grad, weight_sum * node_scale, gain_sum * node_scale)
 

time: 125 us -> 121 us (0.968)
  local copies, waits for them, and re-layouts: 21.6 us -> 5.19 us
  waiting for transfers between devices: 61.7 us -> 67.6 us
  other arithmetic: 5.33 us -> 9.01 us
  matrix products: 14.8 us -> 16.9 us
    gather x5 -> x0, local copies, waits for them, and re-layouts: 12.1 us -> none  [the longest x1 4.65 us: on_device(): reply = grad_nodes[jnp.minimum(place_in, row_count - 1)]]
    all_to_all x1, waiting for transfers between devices: 2.94 us -> 8.87 us  [summed_everywhere(): lax.all_to_all(jnp.broadcast_to(chunk, pieces.shape), ('row', 'col'), 0,...]
    all_to_all x1, waiting for transfers between devices: 6.32 us -> 1.77 us  [summed_everywhere(): gathered = lax.all_to_all(pieces, ('row', 'col'), 0, 0, tiled=True)]
    dot_general x0 -> x4, matrix products: none -> 4.37 us  [exact_pick(): lax.dot_general(chooser.astype(jnp.bfloat16), parts, dims, preferred_elem...]
    ppermute x4, waiting for transfers between devices: 4.1 us -> 6.77 us  [swapped(): lax.ppermute(array, axis, [(i, i ^ 1 << apart) for i in range(lax.axis_si...]
    add x0 -> x5, other arithmetic: none -> 2.38 us  [the longest x4 2.37 us: exact_pick(): return out[:, :width] + out[:, width:2 * width] + out[:, 2 * width:]]
    all_to_all x1, waiting for transfers between devices: 24.3 us -> 26.2 us  [on_device(): lax.all_to_all(jnp.concatenate([outbox, tags], axis=1), ('row', 'col'), 0...]
    unnamed x30 -> x17, local copies, waits for them, and re-layouts: 2.38 us -> 0.65 us
  transfers between devices with their start and end apart: 8 -> 8, of which waited for: 5 -> 6; matrix products, arithmetic and copies ran while one was open for 13% -> 7% of each run, Pallas kernels for 0% -> 0%
where the time goes in v7:
time: 121 us
  waiting for transfers between devices  67.6 us (56%)
  starting transfers between devices  21 us (17%)
  matrix products  16.9 us (14%)
  other arithmetic  9.01 us (7%)
  local copies, waits for them, and re-layouts  5.19 us (4%)
    all_to_all x1, waiting for transfers between devices, on_device(): lax.all_to_all(jnp.concatenate([outbox, tags], axis=1), ('row', 'col'), 0...  26.2 us
    all_to_all x1, waiting for transfers between devices, on_device(): lax.all_to_all(reply.reshape(devices, capacity, feat_count), ('row', 'col...  24 us
    all_to_all x1, waiting for transfers between devices, summed_everywhere(): lax.all_to_all(jnp.broadcast_to(chunk, pieces.shape), ('row', 'col'), 0,...  8.87 us
    all_to_all x1, starting transfers between devices, on_device(): lax.all_to_all(jnp.concatenate([outbox, tags], axis=1), ('row', 'col'), 0...  7.48 us
    ppermute x4, waiting for transfers between devices, swapped(): lax.ppermute(array, axis, [(i, i ^ 1 << apart) for i in range(lax.axis_si...  6.77 us
    dot_general x4, matrix products, exact_pick(): lax.dot_general(chooser.astype(jnp.bfloat16), parts, dims, preferred_elem...  4.37 us
    all_to_all x1, starting transfers between devices, summed_everywhere(): gathered = lax.all_to_all(pieces, ('row', 'col'), 0, 0, tiled=True)  4.34 us
    dot_general x3, matrix products, spread(): lax.dot_general(chooser, values, (((0,), (0,)), ((), ())), precision=PREC...  3.87 us
  transfers between devices with their start and end apart: 8, of which 6 were waited for; matrix products, arithmetic and copies ran while one was open for 7% of the time, Pallas kernels for 0%

profile of v7, /device:TPU:0, one launch (start us, length us, event | category | flops | bytes accessed | tf_op | source)
XLA Modules:
  0.0 120.7 jit_solution(17556458634154215462)
XLA Ops:
  0.6 0.0 copy-start
  0.6 0.6 compare_reduce_fusion
  1.3 0.7 add_select_fusion
  2.0 0.3 fusion.15
  2.3 0.6 select_reduce_fusion.1
  2.9 0.7 convert_select_fusion
  3.6 0.1 reshape.199
  3.6 1.2 reduce-precision_convert_fusion.7
  4.8 1.0 fusion.3
  5.8 0.2 slice_add_fusion.2
  6.1 0.2 reshape.190
  6.3 0.1 select_maximum_fusion
  6.3 1.7 %all_to_all.21 = f32[32,1,8320]{2,1,0:T(1,128)} reshape(f32[32,8320]{1,0:T(8,128)S(1)} %select_maximum_fusion) | data formatting | bytes 2129920 | tf_op jit(solution)/shard_map/all_to_all | solution.py:157
  8.0 7.5 %all-to-all-start = ((f32[32,1,8320]{2,1,0:T(1,128)}), f32[32,1,8320]{2,1,0:T(1,128)S(1)}, u32[]{:S(2)}, u32[]{:S(2)}) async-start(f32[32,1,8320]{2,1,0:T(1,128)} %all_to_all.21), calls=%async_computation | async-start | bytes 2129920 | tf_op jit(solution)/shard_map/all_to_all | solution.py:157
  15.6 0.1 slice_bitcast_fusion
  15.7 0.1 compare_bitcast_fusion
  15.8 26.2 %all-to-all-done = f32[32,1,8320]{2,1,0:T(1,128)S(1)} async-done(((f32[32,1,8320]{2,1,0:T(1,128)}), f32[32,1,8320]{2,1,0:T(1,128)S(1)}, u32[]{:S(2)}, u32[]{:S(2)}) %all-to-all-start) | async-done | bytes 1064992 | tf_op jit(solution)/shard_map/all_to_all | solution.py:157
  41.9 0.1 copy.58
  42.0 0.1 slice.129
  42.1 0.2 reshape.191
  42.3 0.2 reduce-precision_convert_fusion.3
  42.5 0.1 eq.100
  42.6 1.0 fusion.1
  43.7 0.0 copy-start.2
  43.7 0.1 slice_add_fusion.6
  43.8 0.5 copy-done.5
  44.3 0.7 fusion.29
  45.1 1.5 %collective-permute-start.1 = (f32[128,256]{1,0:T(8,128)S(1)}, f32[128,256]{1,0:T(8,128)S(1)}, u32[]{:S(2)}, u32[]{:S(2)}) collective-permute-start(f32[128,256]{1,0:T(8,128)S(1)} %get-tuple-element.33), channel_id=1, source_target_pairs={{0,2},{1,3},{2,0},{3,1},{4,6},{5,7},{6,4},{7,5},{8,10},{9,11},{10,... | collective-permute-start | bytes 393224 | tf_op jit(solution)/shard_map/ppermute | solution.py:17
  46.6 1.0 fusion.47
  47.6 0.1 collective-permute-start
  47.7 2.4 %collective-permute-done.1 = f32[128,256]{1,0:T(8,128)S(1)} collective-permute-done((f32[128,256]{1,0:T(8,128)S(1)}, f32[128,256]{1,0:T(8,128)S(1)}, u32[]{:S(2)}, u32[]{:S(2)}) %collective-permute-start.1) | collective-permute-done | bytes 131104 | tf_op jit(solution)/shard_map/ppermute | solution.py:17
  50.1 0.3 convolution_bitcast_fusion.2
  50.4 0.3 convolution_bitcast_fusion.3
  50.7 0.9 fusion.27
  51.6 1.1 multiply_reduce_fusion.2
  52.7 1.5 %multiply_add_fusion = (f32[512,256]{1,0:T(8,128)}, f32[512,256]{1,0:T(8,128)S(1)}) fusion(f32[512,256]{1,0:T(8,128)S(1)} %slice_add_fusion.6, f32[256,256]{1,0:T(8,128)S(1)} %copy-done, f32[512,256]{1,0:T(8,128)S(1)} %get-tuple-element.39, f32[256]{0:T(256)S(1)} %copy-done.4, f32[512]{0:T(512)S(1)} %fusion.103), kind=kOutput, calls=%fused_computation.94 | convolution fusion | flops 403570688 | bytes 2362368 | tf_op jit(solution)/shard_map/jvp()/dot_general | solution.py:24
  54.2 1.2 fusion.54
  55.3 0.8 multiply_reduce_fusion
  56.2 0.9 fusion.25
  57.0 0.4 convolution_bitcast_fusion.1
  57.4 0.4 convolution_bitcast_fusion
  57.9 1.1 all_to_all.28
  59.0 4.3 %all-to-all-start.2 = ((f32[32,1,2056]{2,1,0:T(1,128)}), f32[32,1,2056]{2,1,0:T(1,128)S(1)}, u32[]{:S(2)}, u32[]{:S(2)}) async-start(f32[32,1,2056]{2,1,0:T(1,128)} %all_to_all.28), calls=%async_computation.2 | async-start | bytes 557056 | tf_op jit(solution)/shard_map/all_to_all | solution.py:98
  63.3 0.1 collective-permute-start.2
  63.4 1.7 %collective-permute-start.3 = (f32[128,256]{0,1:T(8,128)S(1)}, f32[128,256]{0,1:T(8,128)S(1)}, u32[]{:S(2)}, u32[]{:S(2)}) collective-permute-start(f32[128,256]{0,1:T(8,128)S(1)} %convolution_bitcast_fusion), channel_id=1, source_target_pairs={{0,2},{1,3},{2,0},{3,1},{4,6},{5,7},{6,4},{7,5},{8,10},{9,11},{10,... | collective-permute-start | bytes 393224 | tf_op jit(solution)/shard_map/ppermute | solution.py:17
  65.1 2.0 %convolution_add_fusion.1 = f32[512,256]{1,0:T(8,128)S(1)} fusion(f32[64,8,4,128]{3,2,1,0:T(4,128)S(1)} %bitcast.83, f32[512,256]{1,0:T(8,128)S(1)} %copy-done.3, f32[512,256]{1,0:T(8,128)S(1)} %get-tuple-element.39, f32[512]{0:T(512)S(1)} %multiply_multiply_fusion, f32[512]{0:T(512)S(1)} %fusion.103, f32[512,256]{1,0:T(8,128)S(1)} %get-tuple-element.42, ...), kind=kOutput, calls=%fused_computation.28 | convolution fusion | flops 806879232 | bytes 3150848 | tf_op jit(solution)/shard_map/dot_general | solution.py:55
  67.1 4.3 %collective-permute-done.3 = f32[128,256]{0,1:T(8,128)S(1)} collective-permute-done((f32[128,256]{0,1:T(8,128)S(1)}, f32[128,256]{0,1:T(8,128)S(1)}, u32[]{:S(2)}, u32[]{:S(2)}) %collective-permute-start.3) | collective-permute-done | bytes 131104 | tf_op jit(solution)/shard_map/ppermute | solution.py:17
  71.5 1.0 reduce-precision_convert_fusion.5
  72.4 1.8 %all-to-all-done.2 = f32[32,1,2056]{2,1,0:T(1,128)S(1)} async-done(((f32[32,1,2056]{2,1,0:T(1,128)}), f32[32,1,2056]{2,1,0:T(1,128)S(1)}, u32[]{:S(2)}, u32[]{:S(2)}) %all-to-all-start.2) | async-done | bytes 263200 | tf_op jit(solution)/shard_map/all_to_all | solution.py:98
  74.2 0.2 reduce_sum.77
  74.4 0.9 broadcast_in_dim.71
  75.2 3.1 %all-to-all-start.3 = ((f32[32,1,2056]{2,1,0:T(1,128)}), f32[32,1,2056]{2,1,0:T(1,128)S(1)}, u32[]{:S(2)}, u32[]{:S(2)}) async-start(f32[32,1,2056]{2,1,0:T(1,128)} %broadcast_in_dim.71), calls=%async_computation.3 | async-start | bytes 557056 | tf_op jit(solution)/shard_map/all_to_all | solution.py:100
  78.3 1.0 fusion
  79.4 1.2 slice_add_fusion
  80.6 8.9 %all-to-all-done.3 = f32[32,1,2056]{2,1,0:T(1,128)S(1)} async-done(((f32[32,1,2056]{2,1,0:T(1,128)}), f32[32,1,2056]{2,1,0:T(1,128)S(1)}, u32[]{:S(2)}, u32[]{:S(2)}) %all-to-all-start.3) | async-done | bytes 263200 | tf_op jit(solution)/shard_map/all_to_all | solution.py:100
  89.4 2.6 %all-to-all-start.1 = ((f32[32,32,256]{2,1,0:T(8,128)}), f32[32,32,256]{2,1,0:T(8,128)S(1)}, u32[]{:S(2)}, u32[]{:S(2)}) async-start(f32[32,32,256]{2,1,0:T(8,128)} %bitcast.22), calls=%async_computation.1 | async-start | bytes 2097152 | tf_op jit(solution)/shard_map/all_to_all | solution.py:178
  92.1 0.7 reduce.8
  92.8 0.2 reshape.196
  93.0 0.6 slice_multiply_fusion.1
  93.5 0.7 slice_multiply_fusion
  94.3 24.0 %all-to-all-done.1 = f32[32,32,256]{2,1,0:T(8,128)S(1)} async-done(((f32[32,32,256]{2,1,0:T(8,128)}), f32[32,32,256]{2,1,0:T(8,128)S(1)}, u32[]{:S(2)}, u32[]{:S(2)}) %all-to-all-start.1) | async-done | bytes 1048608 | tf_op jit(solution)/shard_map/all_to_all | solution.py:178
  118.3 0.2 reduce-precision_convert_fusion.1
  118.6 1.2 %fusion.2 = f32[512,768]{1,0:T(8,128)S(1)} fusion(bf16[1024,256]{1,0:T(8,128)(2,1)S(1)} %get-tuple-element.21, bf16[1024,256]{1,0:T(8,128)(2,1)S(1)} %get-tuple-element.22, bf16[1024,256]{1,0:T(8,128)(2,1)S(1)} %get-tuple-element.20, s32[512]{0:T(512)S(1)} %convert_add_fusion), kind=kOutput, calls=%fused_computation.6 | convolution fusion | flops 810549248 | bytes 3147776 | tf_op jit(solution)/shard_map/dot_general | solution.py:113
  119.8 0.9 slice_add_fusion.4
  (24 shorter events, 0.2 us)
Async XLA Ops:
  0.6 52.0 %copy-start = (f32[256,256]{1,0:T(8,128)S(1)}, f32[256,256]{1,0:T(8,128)}, u32[]{:S(2)}) copy-start(f32[256,256]{1,0:T(8,128)} %param.14) | copy-start | bytes 786436
  8.0 7.5 %copy-start.7 = (s32[1,3]{1,0:T(1,128)S(1)}, s32[1,3]{1,0:T(1,128)}, u32[]{:S(2)}) copy-start(s32[1,3]{1,0:T(1,128)} %param.18) | copy-start | bytes 40
  8.0 7.7 %copy-start.6 = (s32[1,8,2]{1,2,0:T(2,128)S(1)}, s32[1,8,2]{1,2,0:T(2,128)}, u32[]{:S(2)}) copy-start(s32[1,8,2]{1,2,0:T(2,128)} %param.17) | copy-start | bytes 196
  8.0 33.9 %all-to-all-start = ((f32[32,1,8320]{2,1,0:T(1,128)}), f32[32,1,8320]{2,1,0:T(1,128)S(1)}, u32[]{:S(2)}, u32[]{:S(2)}) async-start(f32[32,1,8320]{2,1,0:T(1,128)} %all_to_all.21), calls=%async_computation | async-start | bytes 2129920 | tf_op jit(solution)/shard_map/all_to_all | solution.py:157
  43.6 0.7 copy-start.5
  43.7 2.9 %copy-start.2 = (f32[1,8,128,128]{3,2,1,0:T(8,128)S(1)}, f32[1,8,128,128]{3,2,1,0:T(8,128)}, u32[]{:S(2)}) copy-start(f32[1,8,128,128]{3,2,1,0:T(8,128)} %param.16) | copy-start | bytes 1572868
  43.8 6.3 %copy-start.1 = (f32[1,2,128,128]{3,2,1,0:T(8,128)S(1)}, f32[1,2,128,128]{3,2,1,0:T(8,128)}, u32[]{:S(2)}) copy-start(f32[1,2,128,128]{3,2,1,0:T(8,128)} %param.20) | copy-start | bytes 393220
  45.1 5.0 %collective-permute-start.1 = (f32[128,256]{1,0:T(8,128)S(1)}, f32[128,256]{1,0:T(8,128)S(1)}, u32[]{:S(2)}, u32[]{:S(2)}) collective-permute-start(f32[128,256]{1,0:T(8,128)S(1)} %get-tuple-element.33), channel_id=1, source_target_pairs={{0,2},{1,3},{2,0},{3,1},{4,6},{5,7},{6,4},{7,5},{8,10},{9,11},{10,... | collective-permute-start | bytes 393224 | tf_op jit(solution)/shard_map/ppermute | solution.py:17
  47.6 2.8 %collective-permute-start = (f32[128,256]{1,0:T(8,128)S(1)}, f32[128,256]{1,0:T(8,128)S(1)}, u32[]{:S(2)}, u32[]{:S(2)}) collective-permute-start(f32[128,256]{1,0:T(8,128)S(1)} %get-tuple-element.32), channel_id=1, source_target_pairs={{0,1},{1,0},{2,3},{3,2},{4,5},{5,4},{6,7},{7,6},{8,9},{9,8},{10,11... | collective-permute-start | bytes 393224 | tf_op jit(solution)/shard_map/ppermute | solution.py:17
  50.7 2.0 %copy-start.4 = (f32[256]{0:T(256)S(1)}, f32[256]{0:T(256)}, u32[]{:S(2)}) copy-start(f32[256]{0:T(256)} %param.15) | copy-start | bytes 3076
  52.7 1.5 %copy-start.3 = (f32[512,256]{1,0:T(8,128)S(1)}, f32[512,256]{1,0:T(8,128)}, u32[]{:S(2)}) copy-start(f32[512,256]{1,0:T(8,128)} %param.21) | copy-start | bytes 1572868
  59.0 15.2 %all-to-all-start.2 = ((f32[32,1,2056]{2,1,0:T(1,128)}), f32[32,1,2056]{2,1,0:T(1,128)S(1)}, u32[]{:S(2)}, u32[]{:S(2)}) async-start(f32[32,1,2056]{2,1,0:T(1,128)} %all_to_all.28), calls=%async_computation.2 | async-start | bytes 557056 | tf_op jit(solution)/shard_map/all_to_all | solution.py:98
  63.3 3.8 %collective-permute-start.2 = (f32[128,256]{0,1:T(8,128)S(1)}, f32[128,256]{0,1:T(8,128)S(1)}, u32[]{:S(2)}, u32[]{:S(2)}) collective-permute-start(f32[128,256]{0,1:T(8,128)S(1)} %convolution_bitcast_fusion.1), channel_id=1, source_target_pairs={{0,1},{1,0},{2,3},{3,2},{4,5},{5,4},{6,7},{7,6},{8,9},{9,8},{10,11... | collective-permute-start | bytes 393224 | tf_op jit(solution)/shard_map/ppermute | solution.py:17
  63.4 8.0 %collective-permute-start.3 = (f32[128,256]{0,1:T(8,128)S(1)}, f32[128,256]{0,1:T(8,128)S(1)}, u32[]{:S(2)}, u32[]{:S(2)}) collective-permute-start(f32[128,256]{0,1:T(8,128)S(1)} %convolution_bitcast_fusion), channel_id=1, source_target_pairs={{0,2},{1,3},{2,0},{3,1},{4,6},{5,7},{6,4},{7,5},{8,10},{9,11},{10,... | collective-permute-start | bytes 393224 | tf_op jit(solution)/shard_map/ppermute | solution.py:17
  75.2 14.2 %all-to-all-start.3 = ((f32[32,1,2056]{2,1,0:T(1,128)}), f32[32,1,2056]{2,1,0:T(1,128)S(1)}, u32[]{:S(2)}, u32[]{:S(2)}) async-start(f32[32,1,2056]{2,1,0:T(1,128)} %broadcast_in_dim.71), calls=%async_computation.3 | async-start | bytes 557056 | tf_op jit(solution)/shard_map/all_to_all | solution.py:100
  89.4 28.9 %all-to-all-start.1 = ((f32[32,32,256]{2,1,0:T(8,128)}), f32[32,32,256]{2,1,0:T(8,128)S(1)}, u32[]{:S(2)}, u32[]{:S(2)}) async-start(f32[32,32,256]{2,1,0:T(8,128)} %bitcast.22), calls=%async_computation.1 | async-start | bytes 2097152 | tf_op jit(solution)/shard_map/all_to_all | solution.py:178

commit v8 on v7

--- a/solution.py
+++ b/solution.py
@@ -91,17 +91,11 @@
     return total + spread(chooser, jnp.concatenate(arrived, axis=0))
 
 
-def summed_everywhere(grad_weight, grad_gain, devices):
+def summed_share(grad_weight, grad_gain, devices):
     packed = jnp.concatenate([grad_weight, grad_gain[None]], 0)
-    rows, width = packed.shape
     pieces = packed.reshape(devices, -1)
     gathered = lax.all_to_all(pieces, ("row", "col"), 0, 0, tiled=True)
-    chunk = jnp.sum(gathered, axis=0, keepdims=True)
-    spread = lax.all_to_all(
-        jnp.broadcast_to(chunk, pieces.shape), ("row", "col"), 0, 0, tiled=True
-    )
-    total = spread.reshape(rows, width)
-    return total[:-1], total[-1]
+    return jnp.sum(gathered, axis=0, keepdims=True)
 
 
 def exact_pick(chooser, values, transposed=False):
@@ -171,18 +165,20 @@
     activation, pullback = jax.vjp(layer_piece, aggregate, weight, norm_gain)
     output = hidden + activation
     grad_agg, grad_weight, grad_gain = pullback(cotangent)
-    weight_sum, gain_sum = summed_everywhere(grad_weight, grad_gain, devices)
+    share = summed_share(grad_weight, grad_gain, devices)
     grad_nodes = cotangent + grad_agg + spread(tiles, grad_agg)
     grad_nodes = boundary_backward(grad_nodes, grad_agg, chooser, coupling)
     reply = exact_pick(landing, grad_nodes, transposed=True)
-    returned = lax.all_to_all(
-        reply.reshape(devices, capacity, feat_count),
-        ("row", "col"),
-        split_axis=0,
-        concat_axis=0,
-        tiled=True,
-    )
-    x_grad = exact_pick(chosen, returned.reshape(-1, feat_count), transposed=True)
+    flat = capacity * feat_count
+    payload = jnp.concatenate(
+        [reply.reshape(devices, flat), jnp.broadcast_to(share, (devices, share.shape[1]))],
+        axis=1,
+    )
+    back = lax.all_to_all(payload, ("row", "col"), 0, 0, tiled=True)
+    returned = back[:, :flat].reshape(devices * capacity, feat_count)
+    total = back[:, flat:].reshape(feat_count + 1, feat_count)
+    weight_sum, gain_sum = total[:-1], total[-1]
+    x_grad = exact_pick(chosen, returned, transposed=True)
     node_scale = 1.0 / math.sqrt(row_count * devices)
     return (output, x_grad, weight_sum * node_scale, gain_sum * node_scale)
 

time: 121 us -> 119 us (0.983)
  blocking collectives: 0 us -> 35.6 us
  waiting for transfers between devices: 67.6 us -> 37.3 us
  starting transfers between devices: 21 us -> 14 us
  other arithmetic: 9.01 us -> 7.48 us
    all_to_all x0 -> x1, blocking collectives: none -> 35.6 us  [on_device(): back = lax.all_to_all(payload, ('row', 'col'), 0, 0, tiled=True)]
    all_to_all x3 -> x1, waiting for transfers between devices: 34.7 us -> 8.65 us  [summed_share(): gathered = lax.all_to_all(pieces, ('row', 'col'), 0, 0, tiled=True)]
    all_to_all x3 -> x1, starting transfers between devices: 10.1 us -> 3.05 us  [summed_share(): gathered = lax.all_to_all(pieces, ('row', 'col'), 0, 0, tiled=True)]
    ppermute x4, waiting for transfers between devices: 6.77 us -> 2.44 us  [swapped(): lax.ppermute(array, axis, [(i, i ^ 1 << apart) for i in range(lax.axis_si...]
  transfers between devices with their start and end apart: 8 -> 6, of which waited for: 6 -> 3; matrix products, arithmetic and copies ran while one was open for 7% -> 4% of each run, Pallas kernels for 0% -> 0%
where the time goes in v8:
time: 119 us; the launch traced here: 118 us
  waiting for transfers between devices  37.3 us (31%)
  blocking collectives  35.6 us (30%)
  matrix products  17.1 us (14%)
  starting transfers between devices  14 us (12%)
  other arithmetic  7.48 us (6%)
  local copies, waits for them, and re-layouts  5.79 us (5%)
    all_to_all x1, blocking collectives, on_device(): back = lax.all_to_all(payload, ('row', 'col'), 0, 0, tiled=True)  35.6 us
    all_to_all x1, waiting for transfers between devices, on_device(): lax.all_to_all(jnp.concatenate([outbox, tags], axis=1), ('row', 'col'), 0...  26.2 us
    all_to_all x1, waiting for transfers between devices, summed_share(): gathered = lax.all_to_all(pieces, ('row', 'col'), 0, 0, tiled=True)  8.65 us
    all_to_all x1, starting transfers between devices, on_device(): lax.all_to_all(jnp.concatenate([outbox, tags], axis=1), ('row', 'col'), 0...  7.48 us
    dot_general x4, matrix products, exact_pick(): lax.dot_general(chooser.astype(jnp.bfloat16), parts, dims, preferred_elem...  4.36 us
    dot_general x3, matrix products, spread(): lax.dot_general(chooser, values, (((0,), (0,)), ((), ())), precision=PREC...  3.88 us
    dot_general x3, matrix products, layer_piece(): jnp.dot(normed, weight, precision=PRECISE, preferred_element_type=jnp.flo...  3.71 us
    ppermute x4, starting transfers between devices, swapped(): lax.ppermute(array, axis, [(i, i ^ 1 << apart) for i in range(lax.axis_si...  3.43 us
  transfers between devices with their start and end apart: 6, of which 3 were waited for; matrix products, arithmetic and copies ran while one was open for 4% of the time, Pallas kernels for 0%

profile of v8, /device:TPU:0, one launch (start us, length us, event | category | flops | bytes accessed | tf_op | source)
XLA Modules:
  0.0 118.4 jit_solution(9097856340309505364)
XLA Ops:
  0.6 0.0 copy-start
  0.6 0.6 compare_reduce_fusion
  1.3 0.7 add_select_fusion
  2.0 0.3 fusion.15
  2.3 0.6 select_reduce_fusion.1
  2.9 0.7 convert_select_fusion
  3.6 0.1 reshape.195
  3.6 1.2 reduce-precision_convert_fusion.7
  4.8 1.0 fusion.3
  5.8 0.2 slice_add_fusion.2
  6.1 0.2 reshape.186
  6.3 0.1 select_maximum_fusion
  6.3 1.7 %all_to_all.22 = f32[32,1,8320]{2,1,0:T(1,128)} reshape(f32[32,8320]{1,0:T(8,128)S(1)} %select_maximum_fusion) | data formatting | bytes 2129920 | tf_op jit(solution)/shard_map/all_to_all | solution.py:151
  8.1 7.5 %all-to-all-start = ((f32[32,1,8320]{2,1,0:T(1,128)}), f32[32,1,8320]{2,1,0:T(1,128)S(1)}, u32[]{:S(2)}, u32[]{:S(2)}) async-start(f32[32,1,8320]{2,1,0:T(1,128)} %all_to_all.22), calls=%async_computation | async-start | bytes 2129920 | tf_op jit(solution)/shard_map/all_to_all | solution.py:151
  15.6 0.1 slice_bitcast_fusion
  15.7 0.1 compare_bitcast_fusion
  15.8 26.2 %all-to-all-done = f32[32,1,8320]{2,1,0:T(1,128)S(1)} async-done(((f32[32,1,8320]{2,1,0:T(1,128)}), f32[32,1,8320]{2,1,0:T(1,128)S(1)}, u32[]{:S(2)}, u32[]{:S(2)}) %all-to-all-start) | async-done | bytes 1064992 | tf_op jit(solution)/shard_map/all_to_all | solution.py:151
  41.9 0.1 copy.61
  42.0 0.1 slice.137
  42.1 0.2 reshape.187
  42.3 0.2 reduce-precision_convert_fusion.3
  42.5 0.1 eq.100
  42.6 1.0 fusion.1
  43.7 0.0 copy-start.5
  43.7 0.1 slice_add_fusion.6
  43.8 0.5 copy-done.5
  44.3 0.7 fusion.29
  45.1 1.5 %collective-permute-start.1 = (f32[128,256]{1,0:T(8,128)S(1)}, f32[128,256]{1,0:T(8,128)S(1)}, u32[]{:S(2)}, u32[]{:S(2)}) collective-permute-start(f32[128,256]{1,0:T(8,128)S(1)} %get-tuple-element.33), channel_id=1, source_target_pairs={{0,2},{1,3},{2,0},{3,1},{4,6},{5,7},{6,4},{7,5},{8,10},{9,11},{10,... | collective-permute-start | bytes 393224 | tf_op jit(solution)/shard_map/ppermute | solution.py:17
  46.6 1.0 fusion.47
  47.6 0.1 collective-permute-start
  47.7 2.4 %collective-permute-done.1 = f32[128,256]{1,0:T(8,128)S(1)} collective-permute-done((f32[128,256]{1,0:T(8,128)S(1)}, f32[128,256]{1,0:T(8,128)S(1)}, u32[]{:S(2)}, u32[]{:S(2)}) %collective-permute-start.1) | collective-permute-done | bytes 131104 | tf_op jit(solution)/shard_map/ppermute | solution.py:17
  50.1 0.3 convolution_bitcast_fusion.2
  50.4 0.3 convolution_bitcast_fusion.3
  50.7 0.9 fusion.27
  51.6 1.1 multiply_reduce_fusion.2
  52.7 1.5 %multiply_add_fusion = (f32[512,256]{1,0:T(8,128)}, f32[512,256]{1,0:T(8,128)S(1)}) fusion(f32[512,256]{1,0:T(8,128)S(1)} %slice_add_fusion.6, f32[256,256]{1,0:T(8,128)S(1)} %copy-done, f32[512,256]{1,0:T(8,128)S(1)} %get-tuple-element.39, f32[256]{0:T(256)S(1)} %copy-done.4, f32[512]{0:T(512)S(1)} %fusion.103), kind=kOutput, calls=%fused_computation.96 | convolution fusion | flops 403570688 | bytes 2362368 | tf_op jit(solution)/shard_map/jvp()/dot_general | solution.py:24
  54.2 0.9 multiply_reduce_fusion
  55.0 0.9 fusion.25
  55.9 0.4 convolution_bitcast_fusion.1
  56.3 0.4 convolution_bitcast_fusion
  56.7 2.0 %convolution_add_fusion.1 = f32[512,256]{1,0:T(8,128)S(1)} fusion(f32[64,8,4,128]{3,2,1,0:T(4,128)S(1)} %bitcast.78, f32[512,256]{1,0:T(8,128)S(1)} %copy-done.3, f32[512,256]{1,0:T(8,128)S(1)} %get-tuple-element.39, f32[512]{0:T(512)S(1)} %multiply_multiply_fusion, f32[512]{0:T(512)S(1)} %fusion.103, f32[512,256]{1,0:T(8,128)S(1)} %get-tuple-element.42, ...), kind=kOutput, calls=%fused_computation.30 | convolution fusion | flops 806879232 | bytes 3150848 | tf_op jit(solution)/shard_map/dot_general | solution.py:55
  58.7 0.1 collective-permute-start.2
  58.8 1.8 %collective-permute-start.3 = (f32[128,256]{0,1:T(8,128)S(1)}, f32[128,256]{0,1:T(8,128)S(1)}, u32[]{:S(2)}, u32[]{:S(2)}) collective-permute-start(f32[128,256]{0,1:T(8,128)S(1)} %convolution_bitcast_fusion), channel_id=1, source_target_pairs={{0,2},{1,3},{2,0},{3,1},{4,6},{5,7},{6,4},{7,5},{8,10},{9,11},{10,... | collective-permute-start | bytes 393224 | tf_op jit(solution)/shard_map/ppermute | solution.py:17
  60.6 1.4 %fusion.54 = f32[256,256]{1,0:T(8,128)S(1)} fusion(f32[512,256]{1,0:T(8,128)S(1)} %get-tuple-element.39, f32[256]{0:T(256)S(1)} %copy-done.4, f32[512]{0:T(512)S(1)} %fusion.103, f32[512,256]{1,0:T(8,128)S(1)} %get-tuple-element.41, f32[512,256]{1,0:T(8,128)S(1)} %copy-done.3), kind=kOutput, calls=%fused_computation.101 | convolution fusion | flops 404094976 | bytes 1838080 | tf_op jit(solution)/shard_map/transpose(jvp())/dot_general | solution.py:24
  62.0 1.1 all_to_all.30
  63.1 3.1 %all-to-all-start.1 = ((f32[32,1,2056]{2,1,0:T(1,128)}), f32[32,1,2056]{2,1,0:T(1,128)S(1)}, u32[]{:S(2)}, u32[]{:S(2)}) async-start(f32[32,1,2056]{2,1,0:T(1,128)} %all_to_all.30), calls=%async_computation.1 | async-start | bytes 557056 | tf_op jit(solution)/shard_map/all_to_all | solution.py:97
  66.2 1.0 reduce-precision_convert_fusion.5
  67.1 1.0 fusion
  68.2 0.2 slice_add_fusion
  68.4 0.2 reshape.189
  68.6 8.6 %all-to-all-done.1 = f32[32,1,2056]{2,1,0:T(1,128)S(1)} async-done(((f32[32,1,2056]{2,1,0:T(1,128)}), f32[32,1,2056]{2,1,0:T(1,128)S(1)}, u32[]{:S(2)}, u32[]{:S(2)}) %all-to-all-start.1) | async-done | bytes 263200 | tf_op jit(solution)/shard_map/all_to_all | solution.py:97
  77.2 0.2 reduce_sum.77
  77.4 0.1 pad_maximum_fusion
  77.5 0.9 all_to_all.27
  78.5 35.6 %all_to_all.34 = f32[32,1,10248]{2,1,0:T(1,128)S(1)} all-to-all(f32[32,1,10248]{2,1,0:T(1,128)S(1)} %all_to_all.27), channel_id=1, replica_groups=mesh['row'=8,'col'=4] {'row','col'}, dimensions={0} | all-to-all | bytes 2623488 | tf_op jit(solution)/shard_map/all_to_all | solution.py:177
  114.1 0.1 copy.60
  114.2 0.1 slice.148
  114.3 0.2 reshape.192
  114.5 0.7 slice_multiply_fusion
  115.2 0.6 slice_multiply_fusion.1
  115.8 0.2 reshape.191
  116.0 0.2 reduce-precision_convert_fusion.1
  116.2 1.2 %fusion.2 = f32[512,768]{1,0:T(8,128)S(1)} fusion(bf16[1024,256]{1,0:T(8,128)(2,1)S(1)} %get-tuple-element.21, bf16[1024,256]{1,0:T(8,128)(2,1)S(1)} %get-tuple-element.22, bf16[1024,256]{1,0:T(8,128)(2,1)S(1)} %get-tuple-element.20, s32[512]{0:T(512)S(1)} %convert_add_fusion), kind=kOutput, calls=%fused_computation.6 | convolution fusion | flops 810549248 | bytes 3147776 | tf_op jit(solution)/shard_map/dot_general | solution.py:107
  117.5 0.9 slice_add_fusion.4
  (27 shorter events, 0.2 us)
Async XLA Ops:
  0.6 52.1 %copy-start = (f32[256,256]{1,0:T(8,128)S(1)}, f32[256,256]{1,0:T(8,128)}, u32[]{:S(2)}) copy-start(f32[256,256]{1,0:T(8,128)} %param.14) | copy-start | bytes 786436
  8.0 7.5 %copy-start.7 = (s32[1,3]{1,0:T(1,128)S(1)}, s32[1,3]{1,0:T(1,128)}, u32[]{:S(2)}) copy-start(s32[1,3]{1,0:T(1,128)} %param.18) | copy-start | bytes 40
  8.0 7.7 %copy-start.6 = (s32[1,8,2]{1,2,0:T(2,128)S(1)}, s32[1,8,2]{1,2,0:T(2,128)}, u32[]{:S(2)}) copy-start(s32[1,8,2]{1,2,0:T(2,128)} %param.17) | copy-start | bytes 196
  8.1 33.9 %all-to-all-start = ((f32[32,1,8320]{2,1,0:T(1,128)}), f32[32,1,8320]{2,1,0:T(1,128)S(1)}, u32[]{:S(2)}, u32[]{:S(2)}) async-start(f32[32,1,8320]{2,1,0:T(1,128)} %all_to_all.22), calls=%async_computation | async-start | bytes 2129920 | tf_op jit(solution)/shard_map/all_to_all | solution.py:151
  43.7 0.7 copy-start.5
  43.7 2.9 %copy-start.2 = (f32[1,8,128,128]{3,2,1,0:T(8,128)S(1)}, f32[1,8,128,128]{3,2,1,0:T(8,128)}, u32[]{:S(2)}) copy-start(f32[1,8,128,128]{3,2,1,0:T(8,128)} %param.16) | copy-start | bytes 1572868
  43.8 6.3 %copy-start.1 = (f32[1,2,128,128]{3,2,1,0:T(8,128)S(1)}, f32[1,2,128,128]{3,2,1,0:T(8,128)}, u32[]{:S(2)}) copy-start(f32[1,2,128,128]{3,2,1,0:T(8,128)} %param.20) | copy-start | bytes 393220
  45.1 5.0 %collective-permute-start.1 = (f32[128,256]{1,0:T(8,128)S(1)}, f32[128,256]{1,0:T(8,128)S(1)}, u32[]{:S(2)}, u32[]{:S(2)}) collective-permute-start(f32[128,256]{1,0:T(8,128)S(1)} %get-tuple-element.33), channel_id=1, source_target_pairs={{0,2},{1,3},{2,0},{3,1},{4,6},{5,7},{6,4},{7,5},{8,10},{9,11},{10,... | collective-permute-start | bytes 393224 | tf_op jit(solution)/shard_map/ppermute | solution.py:17
  47.6 2.8 %collective-permute-start = (f32[128,256]{1,0:T(8,128)S(1)}, f32[128,256]{1,0:T(8,128)S(1)}, u32[]{:S(2)}, u32[]{:S(2)}) collective-permute-start(f32[128,256]{1,0:T(8,128)S(1)} %get-tuple-element.32), channel_id=1, source_target_pairs={{0,1},{1,0},{2,3},{3,2},{4,5},{5,4},{6,7},{7,6},{8,9},{9,8},{10,11... | collective-permute-start | bytes 393224 | tf_op jit(solution)/shard_map/ppermute | solution.py:17
  50.7 2.0 %copy-start.4 = (f32[256]{0:T(256)S(1)}, f32[256]{0:T(256)}, u32[]{:S(2)}) copy-start(f32[256]{0:T(256)} %param.15) | copy-start | bytes 3076
  52.7 1.5 %copy-start.3 = (f32[512,256]{1,0:T(8,128)S(1)}, f32[512,256]{1,0:T(8,128)}, u32[]{:S(2)}) copy-start(f32[512,256]{1,0:T(8,128)} %param.21) | copy-start | bytes 1572868
  58.7 7.4 %collective-permute-start.2 = (f32[128,256]{0,1:T(8,128)S(1)}, f32[128,256]{0,1:T(8,128)S(1)}, u32[]{:S(2)}, u32[]{:S(2)}) collective-permute-start(f32[128,256]{0,1:T(8,128)S(1)} %convolution_bitcast_fusion.1), channel_id=1, source_target_pairs={{0,1},{1,0},{2,3},{3,2},{4,5},{5,4},{6,7},{7,6},{8,9},{9,8},{10,11... | collective-permute-start | bytes 393224 | tf_op jit(solution)/shard_map/ppermute | solution.py:17
  58.8 7.4 %collective-permute-start.3 = (f32[128,256]{0,1:T(8,128)S(1)}, f32[128,256]{0,1:T(8,128)S(1)}, u32[]{:S(2)}, u32[]{:S(2)}) collective-permute-start(f32[128,256]{0,1:T(8,128)S(1)} %convolution_bitcast_fusion), channel_id=1, source_target_pairs={{0,2},{1,3},{2,0},{3,1},{4,6},{5,7},{6,4},{7,5},{8,10},{9,11},{10,... | collective-permute-start | bytes 393224 | tf_op jit(solution)/shard_map/ppermute | solution.py:17
  63.1 14.2 %all-to-all-start.1 = ((f32[32,1,2056]{2,1,0:T(1,128)}), f32[32,1,2056]{2,1,0:T(1,128)S(1)}, u32[]{:S(2)}, u32[]{:S(2)}) async-start(f32[32,1,2056]{2,1,0:T(1,128)} %all_to_all.30), calls=%async_computation.1 | async-start | bytes 557056 | tf_op jit(solution)/shard_map/all_to_all | solution.py:97

commit v9 on v8

--- a/solution.py
+++ b/solution.py
@@ -165,7 +165,8 @@
     activation, pullback = jax.vjp(layer_piece, aggregate, weight, norm_gain)
     output = hidden + activation
     grad_agg, grad_weight, grad_gain = pullback(cotangent)
-    share = summed_share(grad_weight, grad_gain, devices)
+    node_scale = 1.0 / math.sqrt(row_count * devices)
+    share = summed_share(grad_weight, grad_gain, devices) * node_scale
     grad_nodes = cotangent + grad_agg + spread(tiles, grad_agg)
     grad_nodes = boundary_backward(grad_nodes, grad_agg, chooser, coupling)
     reply = exact_pick(landing, grad_nodes, transposed=True)
@@ -179,8 +180,7 @@
     total = back[:, flat:].reshape(feat_count + 1, feat_count)
     weight_sum, gain_sum = total[:-1], total[-1]
     x_grad = exact_pick(chosen, returned, transposed=True)
-    node_scale = 1.0 / math.sqrt(row_count * devices)
-    return (output, x_grad, weight_sum * node_scale, gain_sum * node_scale)
+    return (output, x_grad, weight_sum, gain_sum)
 
 
 def solution(mesh):

time: 119 us -> 119 us (level)
  local copies, waits for them, and re-layouts: 5.79 us -> 7.07 us
  other arithmetic: 7.48 us -> 6.21 us
    slice x0 -> x2, local copies, waits for them, and re-layouts: none -> 1.28 us  [on_device(): weight_sum, gain_sum = (total[:-1], total[-1])]
    mul x2 -> x1, other arithmetic: 1.29 us -> 0.01 us  [on_device(): share = summed_share(grad_weight, grad_gain, devices) * node_scale]
where the time goes in v9:
time: 119 us; the launch traced here: 118 us
  waiting for transfers between devices  37.3 us (31%)
  blocking collectives  35.6 us (30%)
  matrix products  17.1 us (14%)
  starting transfers between devices  14 us (12%)
  local copies, waits for them, and re-layouts  7.07 us (6%)
  other arithmetic  6.21 us (5%)
    all_to_all x1, blocking collectives, on_device(): back = lax.all_to_all(payload, ('row', 'col'), 0, 0, tiled=True)  35.6 us
    all_to_all x1, waiting for transfers between devices, on_device(): lax.all_to_all(jnp.concatenate([outbox, tags], axis=1), ('row', 'col'), 0...  26.2 us
    all_to_all x1, waiting for transfers between devices, summed_share(): gathered = lax.all_to_all(pieces, ('row', 'col'), 0, 0, tiled=True)  8.65 us
    all_to_all x1, starting transfers between devices, on_device(): lax.all_to_all(jnp.concatenate([outbox, tags], axis=1), ('row', 'col'), 0...  7.48 us
    dot_general x4, matrix products, exact_pick(): lax.dot_general(chooser.astype(jnp.bfloat16), parts, dims, preferred_elem...  4.36 us
    dot_general x3, matrix products, spread(): lax.dot_general(chooser, values, (((0,), (0,)), ((), ())), precision=PREC...  3.88 us
    dot_general x3, matrix products, layer_piece(): jnp.dot(normed, weight, precision=PRECISE, preferred_element_type=jnp.flo...  3.71 us
    ppermute x4, starting transfers between devices, swapped(): lax.ppermute(array, axis, [(i, i ^ 1 << apart) for i in range(lax.axis_si...  3.43 us
  transfers between devices with their start and end apart: 6, of which 3 were waited for; matrix products, arithmetic and copies ran while one was open for 4% of the time, Pallas kernels for 0%

profile of v9, /device:TPU:0, one launch (start us, length us, event | category | flops | bytes accessed | tf_op | source)
XLA Modules:
  0.0 118.4 jit_solution(2768365096986583483)
XLA Ops:
  0.6 0.0 copy-start
  0.6 0.6 compare_reduce_fusion
  1.3 0.7 add_select_fusion
  2.0 0.3 fusion.15
  2.3 0.6 select_reduce_fusion.1
  2.9 0.7 convert_select_fusion
  3.6 0.1 reshape.196
  3.6 1.2 reduce-precision_convert_fusion.7
  4.8 1.0 fusion.3
  5.8 0.2 slice_add_fusion.2
  6.1 0.2 reshape.187
  6.3 0.1 select_maximum_fusion
  6.3 1.7 %all_to_all.22 = f32[32,1,8320]{2,1,0:T(1,128)} reshape(f32[32,8320]{1,0:T(8,128)S(1)} %select_maximum_fusion) | data formatting | bytes 2129920 | tf_op jit(solution)/shard_map/all_to_all | solution.py:151
  8.1 7.5 %all-to-all-start = ((f32[32,1,8320]{2,1,0:T(1,128)}), f32[32,1,8320]{2,1,0:T(1,128)S(1)}, u32[]{:S(2)}, u32[]{:S(2)}) async-start(f32[32,1,8320]{2,1,0:T(1,128)} %all_to_all.22), calls=%async_computation | async-start | bytes 2129920 | tf_op jit(solution)/shard_map/all_to_all | solution.py:151
  15.6 0.1 slice_bitcast_fusion
  15.7 0.1 compare_bitcast_fusion
  15.8 26.2 %all-to-all-done = f32[32,1,8320]{2,1,0:T(1,128)S(1)} async-done(((f32[32,1,8320]{2,1,0:T(1,128)}), f32[32,1,8320]{2,1,0:T(1,128)S(1)}, u32[]{:S(2)}, u32[]{:S(2)}) %all-to-all-start) | async-done | bytes 1064992 | tf_op jit(solution)/shard_map/all_to_all | solution.py:151
  41.9 0.1 copy.61
  42.0 0.1 slice.137
  42.1 0.2 reshape.188
  42.3 0.2 reduce-precision_convert_fusion.3
  42.5 0.1 eq.100
  42.6 1.0 fusion.1
  43.7 0.0 copy-start.5
  43.7 0.1 slice_add_fusion.6
  43.8 0.5 copy-done.5
  44.3 0.7 fusion.29
  45.1 1.5 %collective-permute-start.1 = (f32[128,256]{1,0:T(8,128)S(1)}, f32[128,256]{1,0:T(8,128)S(1)}, u32[]{:S(2)}, u32[]{:S(2)}) collective-permute-start(f32[128,256]{1,0:T(8,128)S(1)} %get-tuple-element.33), channel_id=1, source_target_pairs={{0,2},{1,3},{2,0},{3,1},{4,6},{5,7},{6,4},{7,5},{8,10},{9,11},{10,... | collective-permute-start | bytes 393224 | tf_op jit(solution)/shard_map/ppermute | solution.py:17
  46.6 1.0 fusion.47
  47.6 0.1 collective-permute-start
  47.7 2.4 %collective-permute-done.1 = f32[128,256]{1,0:T(8,128)S(1)} collective-permute-done((f32[128,256]{1,0:T(8,128)S(1)}, f32[128,256]{1,0:T(8,128)S(1)}, u32[]{:S(2)}, u32[]{:S(2)}) %collective-permute-start.1) | collective-permute-done | bytes 131104 | tf_op jit(solution)/shard_map/ppermute | solution.py:17
  50.1 0.3 convolution_bitcast_fusion.2
  50.4 0.3 convolution_bitcast_fusion.3
  50.7 0.9 fusion.27
  51.6 1.1 multiply_reduce_fusion.2
  52.7 1.5 %multiply_add_fusion = (f32[512,256]{1,0:T(8,128)}, f32[512,256]{1,0:T(8,128)S(1)}) fusion(f32[512,256]{1,0:T(8,128)S(1)} %slice_add_fusion.6, f32[256,256]{1,0:T(8,128)S(1)} %copy-done, f32[512,256]{1,0:T(8,128)S(1)} %get-tuple-element.39, f32[256]{0:T(256)S(1)} %copy-done.4, f32[512]{0:T(512)S(1)} %fusion.103), kind=kOutput, calls=%fused_computation.96 | convolution fusion | flops 403570688 | bytes 2362368 | tf_op jit(solution)/shard_map/jvp()/dot_general | solution.py:24
  54.2 0.9 multiply_reduce_fusion
  55.0 0.9 fusion.25
  55.9 0.4 convolution_bitcast_fusion.1
  56.3 0.4 convolution_bitcast_fusion
  56.7 2.0 %convolution_add_fusion.1 = f32[512,256]{1,0:T(8,128)S(1)} fusion(f32[64,8,4,128]{3,2,1,0:T(4,128)S(1)} %bitcast.78, f32[512,256]{1,0:T(8,128)S(1)} %copy-done.3, f32[512,256]{1,0:T(8,128)S(1)} %get-tuple-element.39, f32[512]{0:T(512)S(1)} %multiply_multiply_fusion, f32[512]{0:T(512)S(1)} %fusion.103, f32[512,256]{1,0:T(8,128)S(1)} %get-tuple-element.42, ...), kind=kOutput, calls=%fused_computation.30 | convolution fusion | flops 806879232 | bytes 3150848 | tf_op jit(solution)/shard_map/dot_general | solution.py:55
  58.7 0.1 collective-permute-start.2
  58.8 1.8 %collective-permute-start.3 = (f32[128,256]{0,1:T(8,128)S(1)}, f32[128,256]{0,1:T(8,128)S(1)}, u32[]{:S(2)}, u32[]{:S(2)}) collective-permute-start(f32[128,256]{0,1:T(8,128)S(1)} %convolution_bitcast_fusion), channel_id=1, source_target_pairs={{0,2},{1,3},{2,0},{3,1},{4,6},{5,7},{6,4},{7,5},{8,10},{9,11},{10,... | collective-permute-start | bytes 393224 | tf_op jit(solution)/shard_map/ppermute | solution.py:17
  60.6 1.4 %fusion.54 = f32[256,256]{1,0:T(8,128)S(1)} fusion(f32[512,256]{1,0:T(8,128)S(1)} %get-tuple-element.39, f32[256]{0:T(256)S(1)} %copy-done.4, f32[512]{0:T(512)S(1)} %fusion.103, f32[512,256]{1,0:T(8,128)S(1)} %get-tuple-element.41, f32[512,256]{1,0:T(8,128)S(1)} %copy-done.3), kind=kOutput, calls=%fused_computation.101 | convolution fusion | flops 404094976 | bytes 1838080 | tf_op jit(solution)/shard_map/transpose(jvp())/dot_general | solution.py:24
  62.0 1.1 all_to_all.30
  63.1 3.1 %all-to-all-start.1 = ((f32[32,1,2056]{2,1,0:T(1,128)}), f32[32,1,2056]{2,1,0:T(1,128)S(1)}, u32[]{:S(2)}, u32[]{:S(2)}) async-start(f32[32,1,2056]{2,1,0:T(1,128)} %all_to_all.30), calls=%async_computation.1 | async-start | bytes 557056 | tf_op jit(solution)/shard_map/all_to_all | solution.py:97
  66.2 1.0 reduce-precision_convert_fusion.5
  67.1 1.0 fusion
  68.2 0.2 slice_add_fusion
  68.4 0.2 reshape.190
  68.6 8.6 %all-to-all-done.1 = f32[32,1,2056]{2,1,0:T(1,128)S(1)} async-done(((f32[32,1,2056]{2,1,0:T(1,128)}), f32[32,1,2056]{2,1,0:T(1,128)S(1)}, u32[]{:S(2)}, u32[]{:S(2)}) %all-to-all-start.1) | async-done | bytes 263200 | tf_op jit(solution)/shard_map/all_to_all | solution.py:97
  77.2 0.2 reduce_sum.77
  77.4 0.1 pad_maximum_fusion
  77.6 0.9 all_to_all.27
  78.5 35.6 %all_to_all.34 = f32[32,1,10248]{2,1,0:T(1,128)S(1)} all-to-all(f32[32,1,10248]{2,1,0:T(1,128)S(1)} %all_to_all.27), channel_id=1, replica_groups=mesh['row'=8,'col'=4] {'row','col'}, dimensions={0} | all-to-all | bytes 2623488 | tf_op jit(solution)/shard_map/all_to_all | solution.py:178
  114.1 0.1 copy.60
  114.2 0.1 slice.148
  114.3 0.2 reshape.193
  114.5 0.7 slice.153
  115.2 0.6 slice.154
  115.8 0.2 reshape.192
  116.0 0.2 reduce-precision_convert_fusion.1
  116.2 1.2 %fusion.2 = f32[512,768]{1,0:T(8,128)S(1)} fusion(bf16[1024,256]{1,0:T(8,128)(2,1)S(1)} %get-tuple-element.21, bf16[1024,256]{1,0:T(8,128)(2,1)S(1)} %get-tuple-element.22, bf16[1024,256]{1,0:T(8,128)(2,1)S(1)} %get-tuple-element.20, s32[512]{0:T(512)S(1)} %convert_add_fusion), kind=kOutput, calls=%fused_computation.6 | convolution fusion | flops 810549248 | bytes 3147776 | tf_op jit(solution)/shard_map/dot_general | solution.py:107
  117.5 0.9 slice_add_fusion.4
  (28 shorter events, 0.2 us)
Async XLA Ops:
  0.6 52.1 %copy-start = (f32[256,256]{1,0:T(8,128)S(1)}, f32[256,256]{1,0:T(8,128)}, u32[]{:S(2)}) copy-start(f32[256,256]{1,0:T(8,128)} %param.14) | copy-start | bytes 786436
  8.0 7.5 %copy-start.7 = (s32[1,3]{1,0:T(1,128)S(1)}, s32[1,3]{1,0:T(1,128)}, u32[]{:S(2)}) copy-start(s32[1,3]{1,0:T(1,128)} %param.18) | copy-start | bytes 40
  8.0 7.7 %copy-start.6 = (s32[1,8,2]{1,2,0:T(2,128)S(1)}, s32[1,8,2]{1,2,0:T(2,128)}, u32[]{:S(2)}) copy-start(s32[1,8,2]{1,2,0:T(2,128)} %param.17) | copy-start | bytes 196
  8.1 33.9 %all-to-all-start = ((f32[32,1,8320]{2,1,0:T(1,128)}), f32[32,1,8320]{2,1,0:T(1,128)S(1)}, u32[]{:S(2)}, u32[]{:S(2)}) async-start(f32[32,1,8320]{2,1,0:T(1,128)} %all_to_all.22), calls=%async_computation | async-start | bytes 2129920 | tf_op jit(solution)/shard_map/all_to_all | solution.py:151
  43.7 0.7 copy-start.5
  43.7 2.9 %copy-start.2 = (f32[1,8,128,128]{3,2,1,0:T(8,128)S(1)}, f32[1,8,128,128]{3,2,1,0:T(8,128)}, u32[]{:S(2)}) copy-start(f32[1,8,128,128]{3,2,1,0:T(8,128)} %param.16) | copy-start | bytes 1572868
  43.8 6.3 %copy-start.1 = (f32[1,2,128,128]{3,2,1,0:T(8,128)S(1)}, f32[1,2,128,128]{3,2,1,0:T(8,128)}, u32[]{:S(2)}) copy-start(f32[1,2,128,128]{3,2,1,0:T(8,128)} %param.20) | copy-start | bytes 393220
  45.1 5.0 %collective-permute-start.1 = (f32[128,256]{1,0:T(8,128)S(1)}, f32[128,256]{1,0:T(8,128)S(1)}, u32[]{:S(2)}, u32[]{:S(2)}) collective-permute-start(f32[128,256]{1,0:T(8,128)S(1)} %get-tuple-element.33), channel_id=1, source_target_pairs={{0,2},{1,3},{2,0},{3,1},{4,6},{5,7},{6,4},{7,5},{8,10},{9,11},{10,... | collective-permute-start | bytes 393224 | tf_op jit(solution)/shard_map/ppermute | solution.py:17
  47.6 2.8 %collective-permute-start = (f32[128,256]{1,0:T(8,128)S(1)}, f32[128,256]{1,0:T(8,128)S(1)}, u32[]{:S(2)}, u32[]{:S(2)}) collective-permute-start(f32[128,256]{1,0:T(8,128)S(1)} %get-tuple-element.32), channel_id=1, source_target_pairs={{0,1},{1,0},{2,3},{3,2},{4,5},{5,4},{6,7},{7,6},{8,9},{9,8},{10,11... | collective-permute-start | bytes 393224 | tf_op jit(solution)/shard_map/ppermute | solution.py:17
  50.7 2.0 %copy-start.4 = (f32[256]{0:T(256)S(1)}, f32[256]{0:T(256)}, u32[]{:S(2)}) copy-start(f32[256]{0:T(256)} %param.15) | copy-start | bytes 3076
  52.7 1.5 %copy-start.3 = (f32[512,256]{1,0:T(8,128)S(1)}, f32[512,256]{1,0:T(8,128)}, u32[]{:S(2)}) copy-start(f32[512,256]{1,0:T(8,128)} %param.21) | copy-start | bytes 1572868
  58.7 7.4 %collective-permute-start.2 = (f32[128,256]{0,1:T(8,128)S(1)}, f32[128,256]{0,1:T(8,128)S(1)}, u32[]{:S(2)}, u32[]{:S(2)}) collective-permute-start(f32[128,256]{0,1:T(8,128)S(1)} %convolution_bitcast_fusion.1), channel_id=1, source_target_pairs={{0,1},{1,0},{2,3},{3,2},{4,5},{5,4},{6,7},{7,6},{8,9},{9,8},{10,11... | collective-permute-start | bytes 393224 | tf_op jit(solution)/shard_map/ppermute | solution.py:17
  58.8 7.4 %collective-permute-start.3 = (f32[128,256]{0,1:T(8,128)S(1)}, f32[128,256]{0,1:T(8,128)S(1)}, u32[]{:S(2)}, u32[]{:S(2)}) collective-permute-start(f32[128,256]{0,1:T(8,128)S(1)} %convolution_bitcast_fusion), channel_id=1, source_target_pairs={{0,2},{1,3},{2,0},{3,1},{4,6},{5,7},{6,4},{7,5},{8,10},{9,11},{10,... | collective-permute-start | bytes 393224 | tf_op jit(solution)/shard_map/ppermute | solution.py:17
  63.1 14.2 %all-to-all-start.1 = ((f32[32,1,2056]{2,1,0:T(1,128)}), f32[32,1,2056]{2,1,0:T(1,128)S(1)}, u32[]{:S(2)}, u32[]{:S(2)}) async-start(f32[32,1,2056]{2,1,0:T(1,128)} %all_to_all.30), calls=%async_computation.1 | async-start | bytes 557056 | tf_op jit(solution)/shard_map/all_to_all | solution.py:97

commit v10 on v9

--- a/solution.py
+++ b/solution.py
@@ -75,27 +75,23 @@
     return total + spread(chooser, jnp.concatenate(contribs, axis=0))
 
 
-def boundary_backward(total, grad_agg, chooser, coupling):
+def boundary_backward(total, grad_agg, chooser, coupling, anchor):
     picks = jnp.dot(chooser, grad_agg, precision=PRECISE, preferred_element_type=jnp.float32)
-    arrived = []
+    carried = []
     for round_index in range(ROUNDS):
         outgoing = picks[round_index * BLOCK : (round_index + 1) * BLOCK]
-        carried = lax.dot_general(
-            coupling[0, round_index],
-            outgoing,
-            (((0,), (0,)), ((), ())),
-            precision=PRECISE,
-            preferred_element_type=jnp.float32,
+        carried.append(
+            lax.dot_general(
+                coupling[0, round_index],
+                outgoing,
+                (((0,), (0,)), ((), ())),
+                precision=PRECISE,
+                preferred_element_type=jnp.float32,
+            )
         )
-        arrived.append(swapped(carried, "col", round_index))
-    return total + spread(chooser, jnp.concatenate(arrived, axis=0))
-
-
-def summed_share(grad_weight, grad_gain, devices):
-    packed = jnp.concatenate([grad_weight, grad_gain[None]], 0)
-    pieces = packed.reshape(devices, -1)
-    gathered = lax.all_to_all(pieces, ("row", "col"), 0, 0, tiled=True)
-    return jnp.sum(gathered, axis=0, keepdims=True)
+    anchor, carried = lax.optimization_barrier((anchor, carried))
+    arrived = [swapped(block, "col", r) for r, block in enumerate(carried)]
+    return total + spread(chooser, jnp.concatenate(arrived, axis=0)), anchor
 
 
 def exact_pick(chooser, values, transposed=False):
@@ -166,9 +162,11 @@
     output = hidden + activation
     grad_agg, grad_weight, grad_gain = pullback(cotangent)
     node_scale = 1.0 / math.sqrt(row_count * devices)
-    share = summed_share(grad_weight, grad_gain, devices) * node_scale
+    pieces = jnp.concatenate([grad_weight, grad_gain[None]], 0).reshape(devices, -1)
+    gathered = lax.all_to_all(pieces, ("row", "col"), 0, 0, tiled=True)
     grad_nodes = cotangent + grad_agg + spread(tiles, grad_agg)
-    grad_nodes = boundary_backward(grad_nodes, grad_agg, chooser, coupling)
+    grad_nodes, gathered = boundary_backward(grad_nodes, grad_agg, chooser, coupling, gathered)
+    share = jnp.sum(gathered, axis=0, keepdims=True) * node_scale
     reply = exact_pick(landing, grad_nodes, transposed=True)
     flat = capacity * feat_count
     payload = jnp.concatenate(

time: 119 us -> 123 us (1.034)
  matrix products: 17.1 us -> 20.6 us
    ppermute x4, waiting for transfers between devices: 2.44 us -> 7.07 us  [swapped(): lax.ppermute(array, axis, [(i, i ^ 1 << apart) for i in range(lax.axis_si...]
    all_to_all x1, waiting for transfers between devices: 8.65 us -> 4.87 us  [on_device(): gathered = lax.all_to_all(pieces, ('row', 'col'), 0, 0, tiled=True)]
    dot_general x3, matrix products: 3.88 us -> 5.78 us  [spread(): lax.dot_general(chooser, values, (((0,), (0,)), ((), ())), precision=PREC...]
    ppermute x4, starting transfers between devices: 3.43 us -> 2.05 us  [swapped(): lax.ppermute(array, axis, [(i, i ^ 1 << apart) for i in range(lax.axis_si...]
    all_to_all x1, starting transfers between devices: 3.05 us -> 4.34 us  [on_device(): gathered = lax.all_to_all(pieces, ('row', 'col'), 0, 0, tiled=True)]
  transfers between devices with their start and end apart: 6 -> 6, of which waited for: 3 -> 4; matrix products, arithmetic and copies ran while one was open for 4% -> 6% of each run, Pallas kernels for 0% -> 0%
where the time goes in v10:
time: 123 us
  waiting for transfers between devices  38.1 us (31%)
  blocking collectives  35.7 us (29%)
  matrix products  20.6 us (17%)
  starting transfers between devices  13.9 us (11%)
  local copies, waits for them, and re-layouts  7.52 us (6%)
  other arithmetic  6.09 us (5%)
    all_to_all x1, blocking collectives, on_device(): back = lax.all_to_all(payload, ('row', 'col'), 0, 0, tiled=True)  35.7 us
    all_to_all x1, waiting for transfers between devices, on_device(): lax.all_to_all(jnp.concatenate([outbox, tags], axis=1), ('row', 'col'), 0...  26.2 us
    all_to_all x1, starting transfers between devices, on_device(): lax.all_to_all(jnp.concatenate([outbox, tags], axis=1), ('row', 'col'), 0...  7.47 us
    ppermute x4, waiting for transfers between devices, swapped(): lax.ppermute(array, axis, [(i, i ^ 1 << apart) for i in range(lax.axis_si...  7.07 us
    dot_general x3, matrix products, spread(): lax.dot_general(chooser, values, (((0,), (0,)), ((), ())), precision=PREC...  5.78 us
    all_to_all x1, waiting for transfers between devices, on_device(): gathered = lax.all_to_all(pieces, ('row', 'col'), 0, 0, tiled=True)  4.87 us
    dot_general x4, matrix products, exact_pick(): lax.dot_general(chooser.astype(jnp.bfloat16), parts, dims, preferred_elem...  4.37 us
    all_to_all x1, starting transfers between devices, on_device(): gathered = lax.all_to_all(pieces, ('row', 'col'), 0, 0, tiled=True)  4.34 us
  transfers between devices with their start and end apart: 6, of which 4 were waited for; matrix products, arithmetic and copies ran while one was open for 6% of the time, Pallas kernels for 0%

profile of v10, /device:TPU:0, one launch (start us, length us, event | category | flops | bytes accessed | tf_op | source)
XLA Modules:
  0.0 123.0 jit_solution(9424375223800202325)
XLA Ops:
  0.6 0.0 copy-start
  0.6 0.6 compare_reduce_fusion
  1.3 0.7 add_select_fusion
  2.0 0.3 fusion.15
  2.3 0.6 select_reduce_fusion.1
  2.9 0.7 convert_select_fusion
  3.6 0.1 reshape.196
  3.7 1.2 reduce-precision_convert_fusion.7
  4.8 1.0 fusion.3
  5.9 0.2 slice_add_fusion.2
  6.1 0.2 reshape.187
  6.3 0.1 select_maximum_fusion
  6.4 1.7 %all_to_all.24 = f32[32,1,8320]{2,1,0:T(1,128)} reshape(f32[32,8320]{1,0:T(8,128)S(1)} %select_maximum_fusion) | data formatting | bytes 2129920 | tf_op jit(solution)/shard_map/all_to_all | solution.py:147
  8.1 7.5 %all-to-all-start = ((f32[32,1,8320]{2,1,0:T(1,128)}), f32[32,1,8320]{2,1,0:T(1,128)S(1)}, u32[]{:S(2)}, u32[]{:S(2)}) async-start(f32[32,1,8320]{2,1,0:T(1,128)} %all_to_all.24), calls=%async_computation | async-start | bytes 2129920 | tf_op jit(solution)/shard_map/all_to_all | solution.py:147
  15.6 0.1 slice_bitcast_fusion
  15.7 0.1 compare_bitcast_fusion
  15.8 26.2 %all-to-all-done = f32[32,1,8320]{2,1,0:T(1,128)S(1)} async-done(((f32[32,1,8320]{2,1,0:T(1,128)}), f32[32,1,8320]{2,1,0:T(1,128)S(1)}, u32[]{:S(2)}, u32[]{:S(2)}) %all-to-all-start) | async-done | bytes 1064992 | tf_op jit(solution)/shard_map/all_to_all | solution.py:147
  42.0 0.1 copy.63
  42.0 0.1 slice.137
  42.1 0.2 reshape.188
  42.3 0.3 reduce-precision_convert_fusion.3
  42.6 0.1 eq.100
  42.6 1.0 fusion.1
  43.7 0.1 slice_add_fusion.6
  43.8 0.5 copy-done.11
  44.4 0.7 fusion.29
  45.1 1.5 %collective-permute-start.1 = (f32[128,256]{1,0:T(8,128)S(1)}, f32[128,256]{1,0:T(8,128)S(1)}, u32[]{:S(2)}, u32[]{:S(2)}) collective-permute-start(f32[128,256]{1,0:T(8,128)S(1)} %get-tuple-element.39), channel_id=1, source_target_pairs={{0,2},{1,3},{2,0},{3,1},{4,6},{5,7},{6,4},{7,5},{8,10},{9,11},{10,... | collective-permute-start | bytes 393224 | tf_op jit(solution)/shard_map/ppermute | solution.py:17
  46.7 1.0 fusion.47
  47.6 0.1 collective-permute-start
  47.7 2.4 %collective-permute-done.1 = f32[128,256]{1,0:T(8,128)S(1)} collective-permute-done((f32[128,256]{1,0:T(8,128)S(1)}, f32[128,256]{1,0:T(8,128)S(1)}, u32[]{:S(2)}, u32[]{:S(2)}) %collective-permute-start.1) | collective-permute-done | bytes 131104 | tf_op jit(solution)/shard_map/ppermute | solution.py:17
  50.2 0.3 convolution_bitcast_fusion.2
  50.4 0.3 convolution_bitcast_fusion.3
  50.7 0.9 fusion.27
  51.6 1.1 multiply_reduce_fusion.2
  52.8 1.5 %multiply_add_fusion = (f32[512,256]{1,0:T(8,128)}, f32[512,256]{1,0:T(8,128)S(1)}) fusion(f32[512,256]{1,0:T(8,128)S(1)} %slice_add_fusion.6, f32[256,256]{1,0:T(8,128)S(1)} %copy-done, f32[512,256]{1,0:T(8,128)S(1)} %get-tuple-element.45, f32[256]{0:T(256)S(1)} %copy-done.10, f32[512]{0:T(512)S(1)} %fusion.103), kind=kOutput, calls=%fused_computation.96 | convolution fusion | flops 403570688 | bytes 2362368 | tf_op jit(solution)/shard_map/jvp()/dot_general | solution.py:24
  54.2 1.5 %multiply_reduce_fusion = (f32[256]{0:T(256)S(1)}, f32[512]{0:T(512)S(1)}, f32[512,256]{1,0:T(8,128)}) fusion(f32[512,256]{1,0:T(8,128)S(1)} %get-tuple-element.45, f32[512]{0:T(512)S(1)} %fusion.103, f32[256]{0:T(256)S(1)} %copy-done.10, f32[256,256]{1,0:T(8,128)S(1)} %copy-done, f32[512,256]{1,0:T(8,128)S(1)} %get-tuple-element.47, ...), kind=kOutput, calls=%fused_computation.94 | convolution fusion | flops 404618496 | bytes 2365440 | tf_op jit(solution)/shard_map/transpose(jvp())/dot_general | solution.py:24
  55.8 1.2 fusion.54
  57.0 1.1 all_to_all.33
  58.1 4.3 %all-to-all-start.1 = ((f32[32,1,2056]{2,1,0:T(1,128)}), f32[32,1,2056]{2,1,0:T(1,128)S(1)}, u32[]{:S(2)}, u32[]{:S(2)}) async-start(f32[32,1,2056]{2,1,0:T(1,128)} %all_to_all.33), calls=%async_computation.1 | async-start | bytes 557056 | tf_op jit(solution)/shard_map/all_to_all | solution.py:166
  62.5 1.9 %fusion.25 = f32[256,256]{1,0:T(8,128)S(1)} fusion(s32[256]{0:T(256)S(1)} %bitcast.90, pred[256]{0:T(512)(128)(4,1)S(1)} %compare_bitcast_fusion, f32[512,256]{1,0:T(8,128)S(1)} %get-tuple-element.45, f32[512,256]{1,0:T(8,128)} %get-tuple-element.48, f32[512]{0:T(512)S(1)} %multiply_multiply_fusion, f32[256]{0:T(256)S(1)} %copy-done.10, f32[512]{0:T(512)S(1)} %fusion.103), kind=kOutput, calls=%fused_computation.55 | convolution fusion | flops 403701760 | bytes 1317120 | tf_op jit(solution)/shard_map/dot_general | solution.py:79
  64.4 0.4 convolution_bitcast_fusion.1
  64.8 0.4 convolution_bitcast_fusion
  65.2 3.3 %convolution_add_fusion.1 = f32[512,256]{1,0:T(8,128)S(1)} fusion(f32[64,8,4,128]{3,2,1,0:T(4,128)S(1)} %bitcast.81, f32[512,256]{1,0:T(8,128)S(1)} %copy-done.3, f32[512,256]{1,0:T(8,128)S(1)} %get-tuple-element.45, f32[512]{0:T(512)} %copy-done.6, f32[512]{0:T(512)} %copy-done.7, f32[512,256]{1,0:T(8,128)} %get-tuple-element.48, f32[256]{0:T(256)} %param.15), kind=kOutput, calls=%fused_computation.30 | convolution fusion | flops 806879232 | bytes 3150848 | tf_op jit(solution)/shard_map/dot_general | solution.py:55
  68.4 4.9 %all-to-all-done.1 = f32[32,1,2056]{2,1,0:T(1,128)S(1)} async-done(((f32[32,1,2056]{2,1,0:T(1,128)}), f32[32,1,2056]{2,1,0:T(1,128)S(1)}, u32[]{:S(2)}, u32[]{:S(2)}) %all-to-all-start.1) | async-done | bytes 263200 | tf_op jit(solution)/shard_map/all_to_all | solution.py:166
  73.3 0.2 collective-permute-start.3
  73.5 0.3 collective-permute-start.2
  73.9 4.6 %collective-permute-done.3 = f32[128,256]{0,1:T(8,128)S(1)} collective-permute-done((f32[128,256]{0,1:T(8,128)S(1)}, f32[128,256]{0,1:T(8,128)S(1)}, u32[]{:S(2)}, u32[]{:S(2)}) %collective-permute-start.3) | collective-permute-done | bytes 131104 | tf_op jit(solution)/shard_map/ppermute | solution.py:17
  78.5 1.6 %reduce-precision_convert_fusion.5 = (bf16[512,256]{1,0:T(8,128)(2,1)S(1)}, bf16[512,256]{1,0:T(8,128)(2,1)S(1)}, bf16[512,256]{1,0:T(8,128)(2,1)S(1)}) fusion(f32[512,256]{1,0:T(8,128)S(1)} %convolution_add_fusion.1, f32[128,256]{0,1:T(8,128)S(1)} %collective-permute-done.3, f32[128,256]{0,1:T(8,128)S(1)} %collective-permute-done.2, s32[256]{0:T(256)} %bitcast.87, ...), kind=kOutput, calls=%fused_computation.78 | convolution fusion | flops 404160512 | bytes 1574144 | tf_op jit(solution)/shard_map/dot_general | solution.py:55
  80.1 1.0 fusion
  81.2 0.2 slice_add_fusion
  81.4 0.2 reshape.191
  81.6 0.1 pad_maximum_fusion
  81.7 0.9 all_to_all.30
  82.6 35.7 %all_to_all.37 = f32[32,1,10248]{2,1,0:T(1,128)S(1)} all-to-all(f32[32,1,10248]{2,1,0:T(1,128)S(1)} %all_to_all.30), channel_id=1, replica_groups=mesh['row'=8,'col'=4] {'row','col'}, dimensions={0} | all-to-all | bytes 2623488 | tf_op jit(solution)/shard_map/all_to_all | solution.py:176
  118.3 0.1 copy.62
  118.4 0.1 slice.148
  118.5 0.2 reshape.193
  118.7 0.7 slice.153
  119.5 0.6 slice.154
  120.0 0.2 reshape.192
  120.2 0.2 reduce-precision_convert_fusion.1
  120.4 0.4 copy-done.5
  120.9 1.2 %fusion.2 = f32[512,768]{1,0:T(8,128)S(1)} fusion(bf16[1024,256]{1,0:T(8,128)(2,1)S(1)} %get-tuple-element.27, bf16[1024,256]{1,0:T(8,128)(2,1)S(1)} %get-tuple-element.28, bf16[1024,256]{1,0:T(8,128)(2,1)S(1)} %get-tuple-element.26, s32[512]{0:T(512)S(1)} %copy-done.5), kind=kOutput, calls=%fused_computation.6 | convolution fusion | flops 810549248 | bytes 3147776 | tf_op jit(solution)/shard_map/dot_general | solution.py:103
  122.1 0.9 slice_add_fusion.4
  (43 shorter events, 0.3 us)
Async XLA Ops:
  0.6 52.1 %copy-start = (f32[256,256]{1,0:T(8,128)S(1)}, f32[256,256]{1,0:T(8,128)}, u32[]{:S(2)}) copy-start(f32[256,256]{1,0:T(8,128)} %param.14) | copy-start | bytes 786436
  2.3 3.6 %copy-start.4 = (s32[512]{0:T(512)}, s32[512]{0:T(512)S(1)}, u32[]{:S(2)}) copy-start(s32[512]{0:T(512)S(1)} %convert_add_fusion) | copy-start | bytes 6148
  8.1 7.5 %copy-start.14 = (s32[1,3]{1,0:T(1,128)S(1)}, s32[1,3]{1,0:T(1,128)}, u32[]{:S(2)}) copy-start(s32[1,3]{1,0:T(1,128)} %param.18) | copy-start | bytes 40
  8.1 7.7 %copy-start.12 = (s32[1,8,2]{1,2,0:T(2,128)S(1)}, s32[1,8,2]{1,2,0:T(2,128)}, u32[]{:S(2)}) copy-start(s32[1,8,2]{1,2,0:T(2,128)} %param.17) | copy-start | bytes 196
  8.1 33.9 %all-to-all-start = ((f32[32,1,8320]{2,1,0:T(1,128)}), f32[32,1,8320]{2,1,0:T(1,128)S(1)}, u32[]{:S(2)}, u32[]{:S(2)}) async-start(f32[32,1,8320]{2,1,0:T(1,128)} %all_to_all.24), calls=%async_computation | async-start | bytes 2129920 | tf_op jit(solution)/shard_map/all_to_all | solution.py:147
  15.8 46.7 %copy-start.13 = (pred[256]{0:T(512)(128)(4,1)}, pred[256]{0:T(512)(128)(4,1)S(1)}, u32[]{:S(2)}) copy-start(pred[256]{0:T(512)(128)(4,1)S(1)} %compare_bitcast_fusion) | copy-start | bytes 772
  42.6 1.1 copy-start.8
  43.7 0.7 copy-start.11
  43.7 2.9 %copy-start.2 = (f32[1,8,128,128]{3,2,1,0:T(8,128)S(1)}, f32[1,8,128,128]{3,2,1,0:T(8,128)}, u32[]{:S(2)}) copy-start(f32[1,8,128,128]{3,2,1,0:T(8,128)} %param.16) | copy-start | bytes 1572868
  43.8 6.3 %copy-start.1 = (f32[1,2,128,128]{3,2,1,0:T(8,128)S(1)}, f32[1,2,128,128]{3,2,1,0:T(8,128)}, u32[]{:S(2)}) copy-start(f32[1,2,128,128]{3,2,1,0:T(8,128)} %param.20) | copy-start | bytes 393220
  45.1 5.0 %collective-permute-start.1 = (f32[128,256]{1,0:T(8,128)S(1)}, f32[128,256]{1,0:T(8,128)S(1)}, u32[]{:S(2)}, u32[]{:S(2)}) collective-permute-start(f32[128,256]{1,0:T(8,128)S(1)} %get-tuple-element.39), channel_id=1, source_target_pairs={{0,2},{1,3},{2,0},{3,1},{4,6},{5,7},{6,4},{7,5},{8,10},{9,11},{10,... | collective-permute-start | bytes 393224 | tf_op jit(solution)/shard_map/ppermute | solution.py:17
  47.6 2.8 %collective-permute-start = (f32[128,256]{1,0:T(8,128)S(1)}, f32[128,256]{1,0:T(8,128)S(1)}, u32[]{:S(2)}, u32[]{:S(2)}) collective-permute-start(f32[128,256]{1,0:T(8,128)S(1)} %get-tuple-element.38), channel_id=1, source_target_pairs={{0,1},{1,0},{2,3},{3,2},{4,5},{5,4},{6,7},{7,6},{8,9},{9,8},{10,11... | collective-permute-start | bytes 393224 | tf_op jit(solution)/shard_map/ppermute | solution.py:17
  50.7 2.0 %copy-start.10 = (f32[256]{0:T(256)S(1)}, f32[256]{0:T(256)}, u32[]{:S(2)}) copy-start(f32[256]{0:T(256)} %param.15) | copy-start | bytes 3076
  52.7 1.5 %copy-start.3 = (f32[512,256]{1,0:T(8,128)S(1)}, f32[512,256]{1,0:T(8,128)}, u32[]{:S(2)}) copy-start(f32[512,256]{1,0:T(8,128)} %param.21) | copy-start | bytes 1572868
  52.7 9.7 %copy-start.7 = (f32[512]{0:T(512)}, f32[512]{0:T(512)S(1)}, u32[]{:S(2)}) copy-start(f32[512]{0:T(512)S(1)} %fusion.103) | copy-start | bytes 6148
  57.0 7.8 %copy-start.6 = (f32[512]{0:T(512)}, f32[512]{0:T(512)S(1)}, u32[]{:S(2)}) copy-start(f32[512]{0:T(512)S(1)} %multiply_multiply_fusion) | copy-start | bytes 6148
  58.1 15.2 %all-to-all-start.1 = ((f32[32,1,2056]{2,1,0:T(1,128)}), f32[32,1,2056]{2,1,0:T(1,128)S(1)}, u32[]{:S(2)}, u32[]{:S(2)}) async-start(f32[32,1,2056]{2,1,0:T(1,128)} %all_to_all.33), calls=%async_computation.1 | async-start | bytes 557056 | tf_op jit(solution)/shard_map/all_to_all | solution.py:166
  68.4 11.7 %copy-start.9 = (s32[1024]{0:T(1024)S(1)}, s32[1024]{0:T(1024)}, u32[]{:S(2)}) copy-start(s32[1024]{0:T(1024)} %copy-done.8) | copy-start | bytes 12292
  73.3 5.1 %collective-permute-start.3 = (f32[128,256]{0,1:T(8,128)S(1)}, f32[128,256]{0,1:T(8,128)S(1)}, u32[]{:S(2)}, u32[]{:S(2)}) collective-permute-start(f32[128,256]{0,1:T(8,128)S(1)} %convolution_bitcast_fusion), channel_id=1, source_target_pairs={{0,2},{1,3},{2,0},{3,1},{4,6},{5,7},{6,4},{7,5},{8,10},{9,11},{10,... | collective-permute-start | bytes 393224 | tf_op jit(solution)/shard_map/ppermute | solution.py:17
  73.5 5.0 %collective-permute-start.2 = (f32[128,256]{0,1:T(8,128)S(1)}, f32[128,256]{0,1:T(8,128)S(1)}, u32[]{:S(2)}, u32[]{:S(2)}) collective-permute-start(f32[128,256]{0,1:T(8,128)S(1)} %convolution_bitcast_fusion.1), channel_id=1, source_target_pairs={{0,1},{1,0},{2,3},{3,2},{4,5},{5,4},{6,7},{7,6},{8,9},{9,8},{10,11... | collective-permute-start | bytes 393224 | tf_op jit(solution)/shard_map/ppermute | solution.py:17
  120.2 0.7 copy-start.5

commit v11 on v9

--- a/solution.py
+++ b/solution.py
@@ -138,11 +138,8 @@
     bucket = target * capacity + ranked
     slots = jnp.arange(devices * capacity, dtype=jnp.int32)
     chosen = bucket[None, :] == slots[:, None]
-    source = jnp.sum(jnp.where(chosen, order[None, :] + 1, 0), axis=1) - 1
-    filled = source >= 0
-    places = jnp.where(
-        filled, jnp.sum(jnp.where(chosen, within[None, :], 0), axis=1), row_count
-    )
+    tag = jnp.sum(jnp.where(chosen, within[None, :] + 1, 0), axis=1)
+    places = jnp.where(tag > 0, tag - 1, row_count)
     outbox = exact_pick(chosen, x_scan).reshape(devices, capacity * feat_count)
     lanes = 128 * (-(-capacity // 128))
     tags = jnp.zeros((devices, lanes), jnp.float32).at[:, :capacity].set(

time: 119 us -> 118 us (level)
  no operation moved by 1% of the time
where the time goes in v11:
time: 118 us
  waiting for transfers between devices  37.3 us (32%)
  blocking collectives  35.6 us (30%)
  matrix products  17.1 us (14%)
  starting transfers between devices  14 us (12%)
  local copies, waits for them, and re-layouts  7.06 us (6%)
  other arithmetic  5.86 us (5%)
    all_to_all x1, blocking collectives, on_device(): back = lax.all_to_all(payload, ('row', 'col'), 0, 0, tiled=True)  35.6 us
    all_to_all x1, waiting for transfers between devices, on_device(): lax.all_to_all(jnp.concatenate([outbox, tags], axis=1), ('row', 'col'), 0...  26.2 us
    all_to_all x1, waiting for transfers between devices, summed_share(): gathered = lax.all_to_all(pieces, ('row', 'col'), 0, 0, tiled=True)  8.65 us
    all_to_all x1, starting transfers between devices, on_device(): lax.all_to_all(jnp.concatenate([outbox, tags], axis=1), ('row', 'col'), 0...  7.48 us
    dot_general x4, matrix products, exact_pick(): lax.dot_general(chooser.astype(jnp.bfloat16), parts, dims, preferred_elem...  4.36 us
    dot_general x3, matrix products, spread(): lax.dot_general(chooser, values, (((0,), (0,)), ((), ())), precision=PREC...  3.88 us
    dot_general x3, matrix products, layer_piece(): jnp.dot(normed, weight, precision=PRECISE, preferred_element_type=jnp.flo...  3.71 us
    ppermute x4, starting transfers between devices, swapped(): lax.ppermute(array, axis, [(i, i ^ 1 << apart) for i in range(lax.axis_si...  3.43 us
  transfers between devices with their start and end apart: 6, of which 3 were waited for; matrix products, arithmetic and copies ran while one was open for 4% of the time, Pallas kernels for 0%

profile of v11, /device:TPU:0, one launch (start us, length us, event | category | flops | bytes accessed | tf_op | source)
XLA Modules:
  0.0 118.0 jit_solution(4508577513437232668)
XLA Ops:
  0.6 0.0 copy-start
  0.6 0.6 compare_reduce_fusion
  1.3 0.7 add_select_fusion.1
  2.0 0.3 fusion.15
  2.3 1.2 reduce-precision_convert_fusion.7
  3.4 1.0 fusion.3
  4.5 0.2 slice_add_fusion.2
  4.7 0.2 reshape.187
  4.9 0.3 select_reduce_fusion
  5.2 0.7 convert_select_fusion
  5.8 0.1 reshape.188
  5.9 0.1 select_maximum_fusion
  6.0 1.7 %all_to_all.22 = f32[32,1,8320]{2,1,0:T(1,128)} reshape(f32[32,8320]{1,0:T(8,128)S(1)} %select_maximum_fusion) | data formatting | bytes 2129920 | tf_op jit(solution)/shard_map/all_to_all | solution.py:148
  7.7 7.5 %all-to-all-start = ((f32[32,1,8320]{2,1,0:T(1,128)}), f32[32,1,8320]{2,1,0:T(1,128)S(1)}, u32[]{:S(2)}, u32[]{:S(2)}) async-start(f32[32,1,8320]{2,1,0:T(1,128)} %all_to_all.22), calls=%async_computation | async-start | bytes 2129920 | tf_op jit(solution)/shard_map/all_to_all | solution.py:148
  15.2 0.1 slice_bitcast_fusion
  15.3 0.1 compare_bitcast_fusion
  15.4 26.2 %all-to-all-done = f32[32,1,8320]{2,1,0:T(1,128)S(1)} async-done(((f32[32,1,8320]{2,1,0:T(1,128)}), f32[32,1,8320]{2,1,0:T(1,128)S(1)}, u32[]{:S(2)}, u32[]{:S(2)}) %all-to-all-start) | async-done | bytes 1064992 | tf_op jit(solution)/shard_map/all_to_all | solution.py:148
  41.6 0.1 copy.61
  41.7 0.1 slice.137
  41.7 0.2 reshape.189
  41.9 0.2 reduce-precision_convert_fusion.3
  42.2 0.1 eq.100
  42.2 1.0 fusion.1
  43.3 0.0 copy-start.5
  43.3 0.1 slice_add_fusion.6
  43.4 0.5 copy-done.5
  44.0 0.7 fusion.29
  44.7 1.5 %collective-permute-start.1 = (f32[128,256]{1,0:T(8,128)S(1)}, f32[128,256]{1,0:T(8,128)S(1)}, u32[]{:S(2)}, u32[]{:S(2)}) collective-permute-start(f32[128,256]{1,0:T(8,128)S(1)} %get-tuple-element.31), channel_id=1, source_target_pairs={{0,2},{1,3},{2,0},{3,1},{4,6},{5,7},{6,4},{7,5},{8,10},{9,11},{10,... | collective-permute-start | bytes 393224 | tf_op jit(solution)/shard_map/ppermute | solution.py:17
  46.2 1.0 fusion.47
  47.2 0.1 collective-permute-start
  47.3 2.4 %collective-permute-done.1 = f32[128,256]{1,0:T(8,128)S(1)} collective-permute-done((f32[128,256]{1,0:T(8,128)S(1)}, f32[128,256]{1,0:T(8,128)S(1)}, u32[]{:S(2)}, u32[]{:S(2)}) %collective-permute-start.1) | collective-permute-done | bytes 131104 | tf_op jit(solution)/shard_map/ppermute | solution.py:17
  49.8 0.3 convolution_bitcast_fusion.2
  50.0 0.3 convolution_bitcast_fusion.3
  50.3 0.9 fusion.27
  51.2 1.1 multiply_reduce_fusion.2
  52.3 1.5 %multiply_add_fusion = (f32[512,256]{1,0:T(8,128)}, f32[512,256]{1,0:T(8,128)S(1)}) fusion(f32[512,256]{1,0:T(8,128)S(1)} %slice_add_fusion.6, f32[256,256]{1,0:T(8,128)S(1)} %copy-done, f32[512,256]{1,0:T(8,128)S(1)} %get-tuple-element.37, f32[256]{0:T(256)S(1)} %copy-done.4, f32[512]{0:T(512)S(1)} %fusion.104), kind=kOutput, calls=%fused_computation.95 | convolution fusion | flops 403570688 | bytes 2362368 | tf_op jit(solution)/shard_map/jvp()/dot_general | solution.py:24
  53.8 0.9 multiply_reduce_fusion
  54.7 0.9 fusion.25
  55.5 0.4 convolution_bitcast_fusion.1
  55.9 0.4 convolution_bitcast_fusion
  56.3 2.0 %convolution_add_fusion.1 = f32[512,256]{1,0:T(8,128)S(1)} fusion(f32[64,8,4,128]{3,2,1,0:T(4,128)S(1)} %bitcast.78, f32[512,256]{1,0:T(8,128)S(1)} %copy-done.3, f32[512,256]{1,0:T(8,128)S(1)} %get-tuple-element.37, f32[512]{0:T(512)S(1)} %multiply_multiply_fusion, f32[512]{0:T(512)S(1)} %fusion.104, f32[512,256]{1,0:T(8,128)S(1)} %get-tuple-element.40, ...), kind=kOutput, calls=%fused_computation.29 | convolution fusion | flops 806879232 | bytes 3150848 | tf_op jit(solution)/shard_map/dot_general | solution.py:55
  58.4 0.1 collective-permute-start.2
  58.4 1.8 %collective-permute-start.3 = (f32[128,256]{0,1:T(8,128)S(1)}, f32[128,256]{0,1:T(8,128)S(1)}, u32[]{:S(2)}, u32[]{:S(2)}) collective-permute-start(f32[128,256]{0,1:T(8,128)S(1)} %convolution_bitcast_fusion), channel_id=1, source_target_pairs={{0,2},{1,3},{2,0},{3,1},{4,6},{5,7},{6,4},{7,5},{8,10},{9,11},{10,... | collective-permute-start | bytes 393224 | tf_op jit(solution)/shard_map/ppermute | solution.py:17
  60.2 1.4 %fusion.54 = f32[256,256]{1,0:T(8,128)S(1)} fusion(f32[512,256]{1,0:T(8,128)S(1)} %get-tuple-element.37, f32[256]{0:T(256)S(1)} %copy-done.4, f32[512]{0:T(512)S(1)} %fusion.104, f32[512,256]{1,0:T(8,128)S(1)} %get-tuple-element.39, f32[512,256]{1,0:T(8,128)S(1)} %copy-done.3), kind=kOutput, calls=%fused_computation.100 | convolution fusion | flops 404094976 | bytes 1838080 | tf_op jit(solution)/shard_map/transpose(jvp())/dot_general | solution.py:24
  61.6 1.1 all_to_all.30
  62.7 3.1 %all-to-all-start.1 = ((f32[32,1,2056]{2,1,0:T(1,128)}), f32[32,1,2056]{2,1,0:T(1,128)S(1)}, u32[]{:S(2)}, u32[]{:S(2)}) async-start(f32[32,1,2056]{2,1,0:T(1,128)} %all_to_all.30), calls=%async_computation.1 | async-start | bytes 557056 | tf_op jit(solution)/shard_map/all_to_all | solution.py:97
  65.8 1.0 reduce-precision_convert_fusion.5
  66.8 1.0 fusion
  67.8 0.2 slice_add_fusion
  68.0 0.2 reshape.191
  68.2 8.6 %all-to-all-done.1 = f32[32,1,2056]{2,1,0:T(1,128)S(1)} async-done(((f32[32,1,2056]{2,1,0:T(1,128)}), f32[32,1,2056]{2,1,0:T(1,128)S(1)}, u32[]{:S(2)}, u32[]{:S(2)}) %all-to-all-start.1) | async-done | bytes 263200 | tf_op jit(solution)/shard_map/all_to_all | solution.py:97
  76.9 0.2 reduce_sum.67
  77.1 0.1 pad_maximum_fusion
  77.2 0.9 all_to_all.27
  78.1 35.6 %all_to_all.34 = f32[32,1,10248]{2,1,0:T(1,128)S(1)} all-to-all(f32[32,1,10248]{2,1,0:T(1,128)S(1)} %all_to_all.27), channel_id=1, replica_groups=mesh['row'=8,'col'=4] {'row','col'}, dimensions={0} | all-to-all | bytes 2623488 | tf_op jit(solution)/shard_map/all_to_all | solution.py:175
  113.7 0.1 copy.60
  113.8 0.1 slice.148
  113.9 0.2 reshape.194
  114.2 0.7 slice.153
  114.9 0.6 slice.154
  115.4 0.2 reshape.193
  115.6 0.2 reduce-precision_convert_fusion.1
  115.9 1.2 %fusion.2 = f32[512,768]{1,0:T(8,128)S(1)} fusion(bf16[1024,256]{1,0:T(8,128)(2,1)S(1)} %get-tuple-element.19, bf16[1024,256]{1,0:T(8,128)(2,1)S(1)} %get-tuple-element.20, bf16[1024,256]{1,0:T(8,128)(2,1)S(1)} %get-tuple-element.18, s32[512]{0:T(512)S(1)} %convert_add_fusion), kind=kOutput, calls=%fused_computation.5 | convolution fusion | flops 810549248 | bytes 3147776 | tf_op jit(solution)/shard_map/dot_general | solution.py:107
  117.1 0.9 slice_add_fusion.4
  (28 shorter events, 0.2 us)
Async XLA Ops:
  0.6 51.7 %copy-start = (f32[256,256]{1,0:T(8,128)S(1)}, f32[256,256]{1,0:T(8,128)}, u32[]{:S(2)}) copy-start(f32[256,256]{1,0:T(8,128)} %param.14) | copy-start | bytes 786436
  7.7 7.5 %copy-start.7 = (s32[1,3]{1,0:T(1,128)S(1)}, s32[1,3]{1,0:T(1,128)}, u32[]{:S(2)}) copy-start(s32[1,3]{1,0:T(1,128)} %param.18) | copy-start | bytes 40
  7.7 7.7 %copy-start.6 = (s32[1,8,2]{1,2,0:T(2,128)S(1)}, s32[1,8,2]{1,2,0:T(2,128)}, u32[]{:S(2)}) copy-start(s32[1,8,2]{1,2,0:T(2,128)} %param.17) | copy-start | bytes 196
  7.7 33.9 %all-to-all-start = ((f32[32,1,8320]{2,1,0:T(1,128)}), f32[32,1,8320]{2,1,0:T(1,128)S(1)}, u32[]{:S(2)}, u32[]{:S(2)}) async-start(f32[32,1,8320]{2,1,0:T(1,128)} %all_to_all.22), calls=%async_computation | async-start | bytes 2129920 | tf_op jit(solution)/shard_map/all_to_all | solution.py:148
  43.3 0.7 copy-start.5
  43.3 2.9 %copy-start.2 = (f32[1,8,128,128]{3,2,1,0:T(8,128)S(1)}, f32[1,8,128,128]{3,2,1,0:T(8,128)}, u32[]{:S(2)}) copy-start(f32[1,8,128,128]{3,2,1,0:T(8,128)} %param.16) | copy-start | bytes 1572868
  43.4 6.3 %copy-start.1 = (f32[1,2,128,128]{3,2,1,0:T(8,128)S(1)}, f32[1,2,128,128]{3,2,1,0:T(8,128)}, u32[]{:S(2)}) copy-start(f32[1,2,128,128]{3,2,1,0:T(8,128)} %param.20) | copy-start | bytes 393220
  44.7 5.0 %collective-permute-start.1 = (f32[128,256]{1,0:T(8,128)S(1)}, f32[128,256]{1,0:T(8,128)S(1)}, u32[]{:S(2)}, u32[]{:S(2)}) collective-permute-start(f32[128,256]{1,0:T(8,128)S(1)} %get-tuple-element.31), channel_id=1, source_target_pairs={{0,2},{1,3},{2,0},{3,1},{4,6},{5,7},{6,4},{7,5},{8,10},{9,11},{10,... | collective-permute-start | bytes 393224 | tf_op jit(solution)/shard_map/ppermute | solution.py:17
  47.2 2.8 %collective-permute-start = (f32[128,256]{1,0:T(8,128)S(1)}, f32[128,256]{1,0:T(8,128)S(1)}, u32[]{:S(2)}, u32[]{:S(2)}) collective-permute-start(f32[128,256]{1,0:T(8,128)S(1)} %get-tuple-element.30), channel_id=1, source_target_pairs={{0,1},{1,0},{2,3},{3,2},{4,5},{5,4},{6,7},{7,6},{8,9},{9,8},{10,11... | collective-permute-start | bytes 393224 | tf_op jit(solution)/shard_map/ppermute | solution.py:17
  50.3 2.0 %copy-start.4 = (f32[256]{0:T(256)S(1)}, f32[256]{0:T(256)}, u32[]{:S(2)}) copy-start(f32[256]{0:T(256)} %param.15) | copy-start | bytes 3076
  52.3 1.5 %copy-start.3 = (f32[512,256]{1,0:T(8,128)S(1)}, f32[512,256]{1,0:T(8,128)}, u32[]{:S(2)}) copy-start(f32[512,256]{1,0:T(8,128)} %param.21) | copy-start | bytes 1572868
  58.4 7.4 %collective-permute-start.2 = (f32[128,256]{0,1:T(8,128)S(1)}, f32[128,256]{0,1:T(8,128)S(1)}, u32[]{:S(2)}, u32[]{:S(2)}) collective-permute-start(f32[128,256]{0,1:T(8,128)S(1)} %convolution_bitcast_fusion.1), channel_id=1, source_target_pairs={{0,1},{1,0},{2,3},{3,2},{4,5},{5,4},{6,7},{7,6},{8,9},{9,8},{10,11... | collective-permute-start | bytes 393224 | tf_op jit(solution)/shard_map/ppermute | solution.py:17
  58.4 7.4 %collective-permute-start.3 = (f32[128,256]{0,1:T(8,128)S(1)}, f32[128,256]{0,1:T(8,128)S(1)}, u32[]{:S(2)}, u32[]{:S(2)}) collective-permute-start(f32[128,256]{0,1:T(8,128)S(1)} %convolution_bitcast_fusion), channel_id=1, source_target_pairs={{0,2},{1,3},{2,0},{3,1},{4,6},{5,7},{6,4},{7,5},{8,10},{9,11},{10,... | collective-permute-start | bytes 393224 | tf_op jit(solution)/shard_map/ppermute | solution.py:17
  62.7 14.2 %all-to-all-start.1 = ((f32[32,1,2056]{2,1,0:T(1,128)}), f32[32,1,2056]{2,1,0:T(1,128)S(1)}, u32[]{:S(2)}, u32[]{:S(2)}) async-start(f32[32,1,2056]{2,1,0:T(1,128)} %all_to_all.30), calls=%async_computation.1 | async-start | bytes 557056 | tf_op jit(solution)/shard_map/all_to_all | solution.py:97

commit v12 on v11

--- a/solution.py
+++ b/solution.py
@@ -11,6 +11,7 @@
 
 EPS = 1e-05
 PRECISE = lax.Precision.HIGHEST
+DENSE = lax.Precision.HIGH
 
 
 def swapped(array, axis, apart):
@@ -21,7 +22,7 @@
     inv_scale = lax.rsqrt(jnp.mean(aggregate * aggregate, axis=-1, keepdims=True) + EPS)
     normed = aggregate * inv_scale * norm_gain
     return jax.nn.silu(
-        jnp.dot(normed, weight, precision=PRECISE, preferred_element_type=jnp.float32)
+        jnp.dot(normed, weight, precision=DENSE, preferred_element_type=jnp.float32)
     )
 
 
@@ -51,9 +52,9 @@
     return jnp.where(hit & live[:, None], 1.0, 0.0).astype(jnp.float32)
 
 
-def spread(chooser, values):
+def spread(chooser, values, precision=PRECISE):
     return lax.dot_general(
-        chooser, values, (((0,), (0,)), ((), ())), precision=PRECISE,
+        chooser, values, (((0,), (0,)), ((), ())), precision=precision,
         preferred_element_type=jnp.float32,
     )
 
@@ -68,7 +69,7 @@
             jnp.dot(
                 coupling[0, round_index],
                 received,
-                precision=PRECISE,
+                precision=DENSE,
                 preferred_element_type=jnp.float32,
             )
         )
@@ -84,7 +85,7 @@
             coupling[0, round_index],
             outgoing,
             (((0,), (0,)), ((), ())),
-            precision=PRECISE,
+            precision=DENSE,
             preferred_element_type=jnp.float32,
         )
         arrived.append(swapped(carried, "col", round_index))
@@ -156,7 +157,7 @@
     tiles = dense_tiles(tile_values[0], tile_coords[0], counts[0, 0], row_count)
     chooser = pickers(boundary_rows, counts, row_count)
     aggregate = hidden + jnp.dot(
-        tiles, hidden, precision=PRECISE, preferred_element_type=jnp.float32
+        tiles, hidden, precision=DENSE, preferred_element_type=jnp.float32
     )
     aggregate = boundary_forward(aggregate, hidden, chooser, coupling)
     activation, pullback = jax.vjp(layer_piece, aggregate, weight, norm_gain)
@@ -164,7 +165,7 @@
     grad_agg, grad_weight, grad_gain = pullback(cotangent)
     node_scale = 1.0 / math.sqrt(row_count * devices)
     share = summed_share(grad_weight, grad_gain, devices) * node_scale
-    grad_nodes = cotangent + grad_agg + spread(tiles, grad_agg)
+    grad_nodes = cotangent + grad_agg + spread(tiles, grad_agg, DENSE)
     grad_nodes = boundary_backward(grad_nodes, grad_agg, chooser, coupling)
     reply = exact_pick(landing, grad_nodes, transposed=True)
     flat = capacity * feat_count

time: 118 us -> 116 us (0.983)
  matrix products: 17.1 us -> 14.6 us
    dot_general x9, matrix products: 9.19 us -> 6.83 us  [the longest x3 3.07 us: spread(): lax.dot_general(chooser, values, (((0,), (0,)), ((), ())), precision=prec...]
where the time goes in v12:
time: 116 us; the launch traced here: 115 us
  waiting for transfers between devices  37.1 us (32%)
  blocking collectives  35.6 us (31%)
  matrix products  14.6 us (13%)
  starting transfers between devices  14.2 us (12%)
  local copies, waits for them, and re-layouts  7.06 us (6%)
  other arithmetic  5.86 us (5%)
    all_to_all x1, blocking collectives, on_device(): back = lax.all_to_all(payload, ('row', 'col'), 0, 0, tiled=True)  35.6 us
    all_to_all x1, waiting for transfers between devices, on_device(): lax.all_to_all(jnp.concatenate([outbox, tags], axis=1), ('row', 'col'), 0...  26.2 us
    all_to_all x1, waiting for transfers between devices, summed_share(): gathered = lax.all_to_all(pieces, ('row', 'col'), 0, 0, tiled=True)  8.43 us
    all_to_all x1, starting transfers between devices, on_device(): lax.all_to_all(jnp.concatenate([outbox, tags], axis=1), ('row', 'col'), 0...  7.48 us
    dot_general x4, matrix products, exact_pick(): lax.dot_general(chooser.astype(jnp.bfloat16), parts, dims, preferred_elem...  4.37 us
    ppermute x4, starting transfers between devices, swapped(): lax.ppermute(array, axis, [(i, i ^ 1 << apart) for i in range(lax.axis_si...  3.43 us
    all_to_all x1, starting transfers between devices, summed_share(): gathered = lax.all_to_all(pieces, ('row', 'col'), 0, 0, tiled=True)  3.27 us
    dot_general x3, matrix products, spread(): lax.dot_general(chooser, values, (((0,), (0,)), ((), ())), precision=prec...  3.07 us
  transfers between devices with their start and end apart: 6, of which 3 were waited for; matrix products, arithmetic and copies ran while one was open for 4% of the time, Pallas kernels for 0%

profile of v12, /device:TPU:0, one launch (start us, length us, event | category | flops | bytes accessed | tf_op | source)
XLA Modules:
  0.0 115.4 jit_solution(4332849289283784637)
XLA Ops:
  0.6 0.0 copy-start
  0.6 0.6 compare_reduce_fusion
  1.3 0.7 add_select_fusion.1
  2.0 0.3 fusion.15
  2.3 1.2 %reduce-precision_convert_fusion.7 = (bf16[512,256]{1,0:T(8,128)(2,1)S(1)}, bf16[512,256]{1,0:T(8,128)(2,1)S(1)}, bf16[512,256]{1,0:T(8,128)(2,1)S(1)}) fusion(f32[512,256]{1,0:T(8,128)} %param.12), kind=kLoop, calls=%fused_computation.81 | loop fusion | flops 917504 | bytes 1310720 | tf_op jit(solution)/shard_map/convert.9
  3.4 1.0 fusion.3
  4.5 0.2 slice_add_fusion.2
  4.7 0.2 reshape.187
  4.9 0.3 select_reduce_fusion
  5.2 0.7 convert_select_fusion
  5.8 0.1 reshape.188
  5.9 0.1 select_maximum_fusion
  6.0 1.7 %all_to_all.22 = f32[32,1,8320]{2,1,0:T(1,128)} reshape(f32[32,8320]{1,0:T(8,128)S(1)} %select_maximum_fusion) | data formatting | bytes 2129920 | tf_op jit(solution)/shard_map/all_to_all | solution.py:149
  7.7 7.5 %all-to-all-start = ((f32[32,1,8320]{2,1,0:T(1,128)}), f32[32,1,8320]{2,1,0:T(1,128)S(1)}, u32[]{:S(2)}, u32[]{:S(2)}) async-start(f32[32,1,8320]{2,1,0:T(1,128)} %all_to_all.22), calls=%async_computation | async-start | bytes 2129920 | tf_op jit(solution)/shard_map/all_to_all | solution.py:149
  15.2 0.1 slice_bitcast_fusion
  15.3 0.1 compare_bitcast_fusion
  15.4 26.2 %all-to-all-done = f32[32,1,8320]{2,1,0:T(1,128)S(1)} async-done(((f32[32,1,8320]{2,1,0:T(1,128)}), f32[32,1,8320]{2,1,0:T(1,128)S(1)}, u32[]{:S(2)}, u32[]{:S(2)}) %all-to-all-start) | async-done | bytes 1064992 | tf_op jit(solution)/shard_map/all_to_all | solution.py:149
  41.6 0.1 copy.61
  41.7 0.1 slice.137
  41.7 0.2 reshape.189
  41.9 0.2 reduce-precision_convert_fusion.3
  42.2 0.1 eq.100
  42.2 1.0 fusion.1
  43.3 0.0 copy-start.2
  43.3 0.1 slice_add_fusion.6
  43.4 0.5 copy-done.5
  44.0 0.7 fusion.29
  44.7 1.5 %collective-permute-start.1 = (f32[128,256]{1,0:T(8,128)S(1)}, f32[128,256]{1,0:T(8,128)S(1)}, u32[]{:S(2)}, u32[]{:S(2)}) collective-permute-start(f32[128,256]{1,0:T(8,128)S(1)} %get-tuple-element.31), channel_id=1, source_target_pairs={{0,2},{1,3},{2,0},{3,1},{4,6},{5,7},{6,4},{7,5},{8,10},{9,11},{10,... | collective-permute-start | bytes 393224 | tf_op jit(solution)/shard_map/ppermute | solution.py:18
  46.3 1.0 fusion.47
  47.2 0.1 collective-permute-start
  47.3 2.4 %collective-permute-done.1 = f32[128,256]{1,0:T(8,128)S(1)} collective-permute-done((f32[128,256]{1,0:T(8,128)S(1)}, f32[128,256]{1,0:T(8,128)S(1)}, u32[]{:S(2)}, u32[]{:S(2)}) %collective-permute-start.1) | collective-permute-done | bytes 131104 | tf_op jit(solution)/shard_map/ppermute | solution.py:18
  49.8 0.2 convolution_bitcast_fusion.2
  50.0 0.2 convolution_bitcast_fusion.3
  50.2 0.9 fusion.27
  51.1 0.7 multiply_reduce_fusion.2
  51.8 1.3 %multiply_add_fusion = (f32[512,256]{1,0:T(8,128)}, f32[512,256]{1,0:T(8,128)S(1)}) fusion(f32[512,256]{1,0:T(8,128)S(1)} %slice_add_fusion.6, f32[256,256]{1,0:T(8,128)S(1)} %copy-done, f32[512,256]{1,0:T(8,128)S(1)} %get-tuple-element.37, f32[256]{0:T(256)S(1)} %copy-done.4, f32[512]{0:T(512)S(1)} %fusion.104), kind=kOutput, calls=%fused_computation.95 | convolution fusion | flops 202244096 | bytes 2362368 | tf_op jit(solution)/shard_map/jvp()/dot_general | solution.py:25
  53.1 0.6 multiply_reduce_fusion
  53.8 0.9 fusion.25
  54.6 0.3 convolution_bitcast_fusion.1
  54.9 0.3 convolution_bitcast_fusion
  55.2 1.2 %convolution_add_fusion.1 = f32[512,256]{1,0:T(8,128)S(1)} fusion(f32[64,8,4,128]{3,2,1,0:T(4,128)S(1)} %bitcast.78, f32[512,256]{1,0:T(8,128)S(1)} %copy-done.3, f32[512,256]{1,0:T(8,128)S(1)} %get-tuple-element.37, f32[512]{0:T(512)S(1)} %multiply_multiply_fusion, f32[512]{0:T(512)S(1)} %fusion.104, f32[512,256]{1,0:T(8,128)S(1)} %get-tuple-element.40, ...), kind=kOutput, calls=%fused_computation.29 | convolution fusion | flops 404226048 | bytes 3150848 | tf_op jit(solution)/shard_map/dot_general | solution.py:56
  56.4 0.1 collective-permute-start.2
  56.5 1.8 %collective-permute-start.3 = (f32[128,256]{0,1:T(8,128)S(1)}, f32[128,256]{0,1:T(8,128)S(1)}, u32[]{:S(2)}, u32[]{:S(2)}) collective-permute-start(f32[128,256]{0,1:T(8,128)S(1)} %convolution_bitcast_fusion), channel_id=1, source_target_pairs={{0,2},{1,3},{2,0},{3,1},{4,6},{5,7},{6,4},{7,5},{8,10},{9,11},{10,... | collective-permute-start | bytes 393224 | tf_op jit(solution)/shard_map/ppermute | solution.py:18
  58.3 0.8 fusion.54
  59.1 1.1 all_to_all.30
  60.2 3.3 %all-to-all-start.1 = ((f32[32,1,2056]{2,1,0:T(1,128)}), f32[32,1,2056]{2,1,0:T(1,128)S(1)}, u32[]{:S(2)}, u32[]{:S(2)}) async-start(f32[32,1,2056]{2,1,0:T(1,128)} %all_to_all.30), calls=%async_computation.1 | async-start | bytes 557056 | tf_op jit(solution)/shard_map/all_to_all | solution.py:98
  63.5 1.0 reduce-precision_convert_fusion.5
  64.4 1.1 fusion
  65.5 0.2 slice_add_fusion
  65.7 0.2 reshape.191
  65.9 8.4 %all-to-all-done.1 = f32[32,1,2056]{2,1,0:T(1,128)S(1)} async-done(((f32[32,1,2056]{2,1,0:T(1,128)}), f32[32,1,2056]{2,1,0:T(1,128)S(1)}, u32[]{:S(2)}, u32[]{:S(2)}) %all-to-all-start.1) | async-done | bytes 263200 | tf_op jit(solution)/shard_map/all_to_all | solution.py:98
  74.3 0.2 reduce_sum.67
  74.5 0.1 pad_maximum_fusion
  74.6 0.9 all_to_all.27
  75.5 35.6 %all_to_all.34 = f32[32,1,10248]{2,1,0:T(1,128)S(1)} all-to-all(f32[32,1,10248]{2,1,0:T(1,128)S(1)} %all_to_all.27), channel_id=1, replica_groups=mesh['row'=8,'col'=4] {'row','col'}, dimensions={0} | all-to-all | bytes 2623488 | tf_op jit(solution)/shard_map/all_to_all | solution.py:176
  111.2 0.1 copy.60
  111.3 0.1 slice.148
  111.4 0.2 reshape.194
  111.6 0.7 slice.153
  112.3 0.6 slice.154
  112.9 0.2 reshape.193
  113.0 0.2 reduce-precision_convert_fusion.1
  113.3 1.2 %fusion.2 = f32[512,768]{1,0:T(8,128)S(1)} fusion(bf16[1024,256]{1,0:T(8,128)(2,1)S(1)} %get-tuple-element.19, bf16[1024,256]{1,0:T(8,128)(2,1)S(1)} %get-tuple-element.20, bf16[1024,256]{1,0:T(8,128)(2,1)S(1)} %get-tuple-element.18, s32[512]{0:T(512)S(1)} %convert_add_fusion), kind=kOutput, calls=%fused_computation.5 | convolution fusion | flops 810549248 | bytes 3147776 | tf_op jit(solution)/shard_map/dot_general | solution.py:108
  114.6 0.9 slice_add_fusion.4
  (28 shorter events, 0.2 us)
Async XLA Ops:
  0.6 51.2 %copy-start = (f32[256,256]{1,0:T(8,128)S(1)}, f32[256,256]{1,0:T(8,128)}, u32[]{:S(2)}) copy-start(f32[256,256]{1,0:T(8,128)} %param.14) | copy-start | bytes 786436
  7.7 7.5 %copy-start.7 = (s32[1,3]{1,0:T(1,128)S(1)}, s32[1,3]{1,0:T(1,128)}, u32[]{:S(2)}) copy-start(s32[1,3]{1,0:T(1,128)} %param.18) | copy-start | bytes 40
  7.7 7.7 %copy-start.6 = (s32[1,8,2]{1,2,0:T(2,128)S(1)}, s32[1,8,2]{1,2,0:T(2,128)}, u32[]{:S(2)}) copy-start(s32[1,8,2]{1,2,0:T(2,128)} %param.17) | copy-start | bytes 196
  7.7 33.9 %all-to-all-start = ((f32[32,1,8320]{2,1,0:T(1,128)}), f32[32,1,8320]{2,1,0:T(1,128)S(1)}, u32[]{:S(2)}, u32[]{:S(2)}) async-start(f32[32,1,8320]{2,1,0:T(1,128)} %all_to_all.22), calls=%async_computation | async-start | bytes 2129920 | tf_op jit(solution)/shard_map/all_to_all | solution.py:149
  43.3 0.7 copy-start.5
  43.3 2.9 %copy-start.2 = (f32[1,8,128,128]{3,2,1,0:T(8,128)S(1)}, f32[1,8,128,128]{3,2,1,0:T(8,128)}, u32[]{:S(2)}) copy-start(f32[1,8,128,128]{3,2,1,0:T(8,128)} %param.16) | copy-start | bytes 1572868
  43.4 6.3 %copy-start.1 = (f32[1,2,128,128]{3,2,1,0:T(8,128)S(1)}, f32[1,2,128,128]{3,2,1,0:T(8,128)}, u32[]{:S(2)}) copy-start(f32[1,2,128,128]{3,2,1,0:T(8,128)} %param.20) | copy-start | bytes 393220
  44.7 5.0 %collective-permute-start.1 = (f32[128,256]{1,0:T(8,128)S(1)}, f32[128,256]{1,0:T(8,128)S(1)}, u32[]{:S(2)}, u32[]{:S(2)}) collective-permute-start(f32[128,256]{1,0:T(8,128)S(1)} %get-tuple-element.31), channel_id=1, source_target_pairs={{0,2},{1,3},{2,0},{3,1},{4,6},{5,7},{6,4},{7,5},{8,10},{9,11},{10,... | collective-permute-start | bytes 393224 | tf_op jit(solution)/shard_map/ppermute | solution.py:18
  47.2 2.7 %collective-permute-start = (f32[128,256]{1,0:T(8,128)S(1)}, f32[128,256]{1,0:T(8,128)S(1)}, u32[]{:S(2)}, u32[]{:S(2)}) collective-permute-start(f32[128,256]{1,0:T(8,128)S(1)} %get-tuple-element.30), channel_id=1, source_target_pairs={{0,1},{1,0},{2,3},{3,2},{4,5},{5,4},{6,7},{7,6},{8,9},{9,8},{10,11... | collective-permute-start | bytes 393224 | tf_op jit(solution)/shard_map/ppermute | solution.py:18
  50.2 1.6 %copy-start.4 = (f32[256]{0:T(256)S(1)}, f32[256]{0:T(256)}, u32[]{:S(2)}) copy-start(f32[256]{0:T(256)} %param.15) | copy-start | bytes 3076
  51.8 1.3 %copy-start.3 = (f32[512,256]{1,0:T(8,128)S(1)}, f32[512,256]{1,0:T(8,128)}, u32[]{:S(2)}) copy-start(f32[512,256]{1,0:T(8,128)} %param.21) | copy-start | bytes 1572868
  56.4 7.0 %collective-permute-start.2 = (f32[128,256]{0,1:T(8,128)S(1)}, f32[128,256]{0,1:T(8,128)S(1)}, u32[]{:S(2)}, u32[]{:S(2)}) collective-permute-start(f32[128,256]{0,1:T(8,128)S(1)} %convolution_bitcast_fusion.1), channel_id=1, source_target_pairs={{0,1},{1,0},{2,3},{3,2},{4,5},{5,4},{6,7},{7,6},{8,9},{9,8},{10,11... | collective-permute-start | bytes 393224 | tf_op jit(solution)/shard_map/ppermute | solution.py:18
  56.5 7.0 %collective-permute-start.3 = (f32[128,256]{0,1:T(8,128)S(1)}, f32[128,256]{0,1:T(8,128)S(1)}, u32[]{:S(2)}, u32[]{:S(2)}) collective-permute-start(f32[128,256]{0,1:T(8,128)S(1)} %convolution_bitcast_fusion), channel_id=1, source_target_pairs={{0,2},{1,3},{2,0},{3,1},{4,6},{5,7},{6,4},{7,5},{8,10},{9,11},{10,... | collective-permute-start | bytes 393224 | tf_op jit(solution)/shard_map/ppermute | solution.py:18
  60.2 14.2 %all-to-all-start.1 = ((f32[32,1,2056]{2,1,0:T(1,128)}), f32[32,1,2056]{2,1,0:T(1,128)S(1)}, u32[]{:S(2)}, u32[]{:S(2)}) async-start(f32[32,1,2056]{2,1,0:T(1,128)} %all_to_all.30), calls=%async_computation.1 | async-start | bytes 557056 | tf_op jit(solution)/shard_map/all_to_all | solution.py:98

commit v13 on v12

--- a/solution.py
+++ b/solution.py
@@ -92,13 +92,6 @@
     return total + spread(chooser, jnp.concatenate(arrived, axis=0))
 
 
-def summed_share(grad_weight, grad_gain, devices):
-    packed = jnp.concatenate([grad_weight, grad_gain[None]], 0)
-    pieces = packed.reshape(devices, -1)
-    gathered = lax.all_to_all(pieces, ("row", "col"), 0, 0, tiled=True)
-    return jnp.sum(gathered, axis=0, keepdims=True)
-
-
 def exact_pick(chooser, values, transposed=False):
     hi = lax.reduce_precision(values, 8, 7)
     rest = values - hi
@@ -164,8 +157,11 @@
     output = hidden + activation
     grad_agg, grad_weight, grad_gain = pullback(cotangent)
     node_scale = 1.0 / math.sqrt(row_count * devices)
-    share = summed_share(grad_weight, grad_gain, devices) * node_scale
-    grad_nodes = cotangent + grad_agg + spread(tiles, grad_agg, DENSE)
+    pieces = jnp.concatenate([grad_weight, grad_gain[None]], 0).reshape(devices, -1)
+    gathered = lax.all_to_all(pieces, ("row", "col"), 0, 0, tiled=True)
+    gathered, tile_input = lax.optimization_barrier((gathered, grad_agg))
+    share = jnp.sum(gathered, axis=0, keepdims=True) * node_scale
+    grad_nodes = cotangent + grad_agg + spread(tiles, tile_input, DENSE)
     grad_nodes = boundary_backward(grad_nodes, grad_agg, chooser, coupling)
     reply = exact_pick(landing, grad_nodes, transposed=True)
     flat = capacity * feat_count

time: 116 us -> 118 us (1.017)
  waiting for transfers between devices: 37.1 us -> 35.4 us
  matrix products: 14.6 us -> 15.9 us
    all_to_all x1, waiting for transfers between devices: 8.43 us -> 6.57 us  [on_device(): gathered = lax.all_to_all(pieces, ('row', 'col'), 0, 0, tiled=True)]
    add_any x0 -> x1, other arithmetic: none -> 1.25 us  [layer_piece(): aggregate * aggregate]
where the time goes in v13:
time: 118 us
  blocking collectives  35.6 us (30%)
  waiting for transfers between devices  35.4 us (30%)
  matrix products  15.9 us (13%)
  starting transfers between devices  14.9 us (13%)
  local copies, waits for them, and re-layouts  7.55 us (6%)
  other arithmetic  6.95 us (6%)
  between operations  1.2 us (1%)
    all_to_all x1, blocking collectives, on_device(): back = lax.all_to_all(payload, ('row', 'col'), 0, 0, tiled=True)  35.6 us
    all_to_all x1, waiting for transfers between devices, on_device(): lax.all_to_all(jnp.concatenate([outbox, tags], axis=1), ('row', 'col'), 0...  26.4 us
    all_to_all x1, starting transfers between devices, on_device(): lax.all_to_all(jnp.concatenate([outbox, tags], axis=1), ('row', 'col'), 0...  7.3 us
    all_to_all x1, waiting for transfers between devices, on_device(): gathered = lax.all_to_all(pieces, ('row', 'col'), 0, 0, tiled=True)  6.57 us
    dot_general x4, matrix products, exact_pick(): lax.dot_general(chooser.astype(jnp.bfloat16), parts, dims, preferred_elem...  4.38 us
    all_to_all x1, starting transfers between devices, on_device(): gathered = lax.all_to_all(pieces, ('row', 'col'), 0, 0, tiled=True)  4.3 us
    dot_general x3, matrix products, spread(): lax.dot_general(chooser, values, (((0,), (0,)), ((), ())), precision=prec...  3.82 us
    dot_general x3, matrix products, layer_piece(): jnp.dot(normed, weight, precision=DENSE, preferred_element_type=jnp.float32)  3.35 us
  transfers between devices with their start and end apart: 6, of which 3 were waited for; matrix products, arithmetic and copies ran while one was open for 4% of the time, Pallas kernels for 0%

profile of v13, /device:TPU:0, one launch (start us, length us, event | category | flops | bytes accessed | tf_op | source)
XLA Modules:
  0.0 117.5 jit_solution(9510776023883348327)
XLA Ops:
  0.6 0.0 copy-start
  0.6 0.6 compare_reduce_fusion
  1.3 0.7 add_select_fusion.1
  2.0 0.3 fusion.15
  2.3 0.3 select_reduce_fusion
  2.6 0.7 convert_select_fusion
  3.2 0.1 reshape.188
  3.3 1.2 reduce-precision_convert_fusion.7
  4.5 1.0 fusion.3
  5.5 0.2 slice_add_fusion.2
  5.7 0.2 reshape.187
  5.9 0.1 select_maximum_fusion
  6.0 1.7 %all_to_all.24 = f32[32,1,8320]{2,1,0:T(1,128)} reshape(f32[32,8320]{1,0:T(8,128)S(1)} %select_maximum_fusion) | data formatting | bytes 2129920 | tf_op jit(solution)/shard_map/all_to_all | solution.py:142
  7.7 7.3 %all-to-all-start = ((f32[32,1,8320]{2,1,0:T(1,128)}), f32[32,1,8320]{2,1,0:T(1,128)S(1)}, u32[]{:S(2)}, u32[]{:S(2)}) async-start(f32[32,1,8320]{2,1,0:T(1,128)} %all_to_all.24), calls=%async_computation | async-start | bytes 2129920 | tf_op jit(solution)/shard_map/all_to_all | solution.py:142
  15.1 0.1 slice_bitcast_fusion
  15.2 0.1 compare_bitcast_fusion
  15.3 26.4 %all-to-all-done = f32[32,1,8320]{2,1,0:T(1,128)S(1)} async-done(((f32[32,1,8320]{2,1,0:T(1,128)}), f32[32,1,8320]{2,1,0:T(1,128)S(1)}, u32[]{:S(2)}, u32[]{:S(2)}) %all-to-all-start) | async-done | bytes 1064992 | tf_op jit(solution)/shard_map/all_to_all | solution.py:142
  41.6 0.1 copy.63
  41.7 0.1 slice.137
  41.8 0.2 reshape.189
  42.0 0.2 reduce-precision_convert_fusion.3
  42.2 0.1 eq.100
  42.3 1.0 fusion.1
  43.4 0.1 slice_add_fusion.6
  43.5 0.5 copy-done.6
  44.0 0.7 fusion.29
  44.8 1.5 %collective-permute-start.1 = (f32[128,256]{1,0:T(8,128)S(1)}, f32[128,256]{1,0:T(8,128)S(1)}, u32[]{:S(2)}, u32[]{:S(2)}) collective-permute-start(f32[128,256]{1,0:T(8,128)S(1)} %get-tuple-element.35), channel_id=1, source_target_pairs={{0,2},{1,3},{2,0},{3,1},{4,6},{5,7},{6,4},{7,5},{8,10},{9,11},{10,... | collective-permute-start | bytes 393224 | tf_op jit(solution)/shard_map/ppermute | solution.py:18
  46.3 1.0 fusion.47
  47.3 0.1 collective-permute-start
  47.4 2.4 %collective-permute-done.1 = f32[128,256]{1,0:T(8,128)S(1)} collective-permute-done((f32[128,256]{1,0:T(8,128)S(1)}, f32[128,256]{1,0:T(8,128)S(1)}, u32[]{:S(2)}, u32[]{:S(2)}) %collective-permute-start.1) | collective-permute-done | bytes 131104 | tf_op jit(solution)/shard_map/ppermute | solution.py:18
  49.8 0.2 convolution_bitcast_fusion.2
  50.0 0.2 convolution_bitcast_fusion.3
  50.2 0.9 fusion.27
  51.2 0.7 multiply_reduce_fusion.2
  51.9 1.3 %multiply_add_fusion = (f32[512,256]{1,0:T(8,128)}, f32[512,256]{1,0:T(8,128)S(1)}) fusion(f32[512,256]{1,0:T(8,128)S(1)} %slice_add_fusion.6, f32[256,256]{1,0:T(8,128)S(1)} %copy-done, f32[512,256]{1,0:T(8,128)S(1)} %get-tuple-element.41, f32[256]{0:T(256)S(1)} %copy-done.13, f32[512]{0:T(512)S(1)} %fusion.104), kind=kOutput, calls=%fused_computation.95 | convolution fusion | flops 202244096 | bytes 2362368 | tf_op jit(solution)/shard_map/jvp()/dot_general | solution.py:25
  53.1 1.3 %multiply_reduce_fusion.1 = (f32[512]{0:T(512)S(1)}, f32[256]{0:T(256)S(1)}, f32[512,256]{1,0:T(8,128)}) fusion(f32[512,256]{1,0:T(8,128)S(1)} %get-tuple-element.41, f32[256]{0:T(256)S(1)} %copy-done.13, f32[512]{0:T(512)S(1)} %fusion.104, f32[256,256]{1,0:T(8,128)S(1)} %copy-done, f32[512,256]{1,0:T(8,128)S(1)} %get-tuple-element.43, ...), kind=kOutput, calls=%fused_computation.94 | convolution fusion | flops 203291904 | bytes 2365440 | tf_op jit(solution)/shard_map/transpose(jvp())/dot_general | solution.py:25
  54.5 0.7 fusion.54
  55.3 1.1 all_to_all.33
  56.4 4.3 %all-to-all-start.1 = ((f32[32,1,2056]{2,1,0:T(1,128)}), f32[32,1,2056]{2,1,0:T(1,128)S(1)}, u32[]{:S(2)}, u32[]{:S(2)}) async-start(f32[32,1,2056]{2,1,0:T(1,128)} %all_to_all.33), calls=%async_computation.1 | async-start | bytes 557056 | tf_op jit(solution)/shard_map/all_to_all | solution.py:161
  60.7 1.2 %add_add_fusion = f32[512,256]{1,0:T(8,128)S(1)} fusion(f32[512,256]{1,0:T(8,128)S(1)} %get-tuple-element.41, f32[512,256]{1,0:T(8,128)} %get-tuple-element.44, f32[512]{0:T(512)S(1)} %multiply_multiply_fusion, f32[256]{0:T(256)S(1)} %copy-done.13, f32[512]{0:T(512)S(1)} %fusion.104), kind=kLoop, calls=%fused_computation.72 | loop fusion | flops 655360 | bytes 1577984 | tf_op jit(solution)/shard_map/transpose(jvp())/add_any | solution.py:22
  62.0 0.7 fusion.25
  62.7 0.3 convolution_bitcast_fusion
  63.0 1.7 %collective-permute-start.3 = (f32[128,256]{0,1:T(8,128)S(1)}, f32[128,256]{0,1:T(8,128)}, u32[]{:S(2)}, u32[]{:S(2)}) collective-permute-start(f32[128,256]{0,1:T(8,128)S(1)} %convolution_bitcast_fusion), channel_id=1, source_target_pairs={{0,2},{1,3},{2,0},{3,1},{4,6},{5,7},{6,4},{7,5},{8,10},{9,11},{10,... | collective-permute-start | bytes 393224 | tf_op jit(solution)/shard_map/ppermute | solution.py:18
  64.6 0.3 convolution_bitcast_fusion.1
  64.9 0.1 collective-permute-start.2
  65.0 6.6 %all-to-all-done.1 = f32[32,1,2056]{2,1,0:T(1,128)S(1)} async-done(((f32[32,1,2056]{2,1,0:T(1,128)}), f32[32,1,2056]{2,1,0:T(1,128)S(1)}, u32[]{:S(2)}, u32[]{:S(2)}) %all-to-all-start.1) | async-done | bytes 263200 | tf_op jit(solution)/shard_map/all_to_all | solution.py:161
  71.6 1.0 convolution_add_fusion.1
  72.7 1.9 %reduce-precision_convert_fusion.5 = (bf16[512,256]{1,0:T(8,128)(2,1)S(1)}, bf16[512,256]{1,0:T(8,128)(2,1)S(1)}, bf16[512,256]{1,0:T(8,128)(2,1)S(1)}) fusion(f32[512,256]{1,0:T(8,128)S(1)} %convolution_add_fusion.1, f32[128,256]{0,1:T(8,128)} %collective-permute-done.3, f32[128,256]{0,1:T(8,128)} %collective-permute-done.2, s32[256]{0:T(256)S(1)} %bitcast.92, ...), kind=kOutput, calls=%fused_computation.77 | convolution fusion | flops 404160512 | bytes 1574144 | tf_op jit(solution)/shard_map/dot_general | solution.py:56
  74.6 1.1 fusion
  75.7 0.2 slice_add_fusion
  75.9 0.2 reshape.192
  76.1 0.1 pad_maximum_fusion
  76.3 0.9 all_to_all.30
  77.2 35.6 %all_to_all.37 = f32[32,1,10248]{2,1,0:T(1,128)S(1)} all-to-all(f32[32,1,10248]{2,1,0:T(1,128)S(1)} %all_to_all.30), channel_id=1, replica_groups=mesh['row'=8,'col'=4] {'row','col'}, dimensions={0} | all-to-all | bytes 2623488 | tf_op jit(solution)/shard_map/all_to_all | solution.py:172
  112.8 0.1 copy.62
  112.9 0.1 slice.148
  113.0 0.2 reshape.194
  113.2 0.7 slice.153
  113.9 0.6 slice.154
  114.5 0.2 reshape.193
  114.7 0.2 reduce-precision_convert_fusion.1
  114.9 0.4 copy-done.5
  115.4 1.2 %fusion.2 = f32[512,768]{1,0:T(8,128)S(1)} fusion(bf16[1024,256]{1,0:T(8,128)(2,1)S(1)} %get-tuple-element.23, bf16[1024,256]{1,0:T(8,128)(2,1)S(1)} %get-tuple-element.24, bf16[1024,256]{1,0:T(8,128)(2,1)S(1)} %get-tuple-element.22, s32[512]{0:T(512)S(1)} %copy-done.5), kind=kOutput, calls=%fused_computation.5 | convolution fusion | flops 810549248 | bytes 3147776 | tf_op jit(solution)/shard_map/dot_general | solution.py:101
  116.6 0.9 slice_add_fusion.4
  (44 shorter events, 0.3 us)
Async XLA Ops:
  0.6 51.2 %copy-start = (f32[256,256]{1,0:T(8,128)S(1)}, f32[256,256]{1,0:T(8,128)}, u32[]{:S(2)}) copy-start(f32[256,256]{1,0:T(8,128)} %param.14) | copy-start | bytes 786436
  2.3 3.2 %copy-start.4 = (s32[512]{0:T(512)}, s32[512]{0:T(512)S(1)}, u32[]{:S(2)}) copy-start(s32[512]{0:T(512)S(1)} %convert_add_fusion) | copy-start | bytes 6148
  7.7 7.3 %copy-start.14 = (s32[1,3]{1,0:T(1,128)S(1)}, s32[1,3]{1,0:T(1,128)}, u32[]{:S(2)}) copy-start(s32[1,3]{1,0:T(1,128)} %param.18) | copy-start | bytes 40
  7.7 7.5 %copy-start.12 = (s32[1,8,2]{1,2,0:T(2,128)S(1)}, s32[1,8,2]{1,2,0:T(2,128)}, u32[]{:S(2)}) copy-start(s32[1,8,2]{1,2,0:T(2,128)} %param.17) | copy-start | bytes 196
  7.7 33.9 %all-to-all-start = ((f32[32,1,8320]{2,1,0:T(1,128)}), f32[32,1,8320]{2,1,0:T(1,128)S(1)}, u32[]{:S(2)}, u32[]{:S(2)}) async-start(f32[32,1,8320]{2,1,0:T(1,128)} %all_to_all.24), calls=%async_computation | async-start | bytes 2129920 | tf_op jit(solution)/shard_map/all_to_all | solution.py:142
  15.2 46.7 %copy-start.10 = (pred[256]{0:T(512)(128)(4,1)}, pred[256]{0:T(512)(128)(4,1)S(1)}, u32[]{:S(2)}) copy-start(pred[256]{0:T(512)(128)(4,1)S(1)} %compare_bitcast_fusion) | copy-start | bytes 772
  42.3 1.1 copy-start.8
  43.3 0.7 copy-start.6
  43.4 2.9 %copy-start.3 = (f32[1,8,128,128]{3,2,1,0:T(8,128)S(1)}, f32[1,8,128,128]{3,2,1,0:T(8,128)}, u32[]{:S(2)}) copy-start(f32[1,8,128,128]{3,2,1,0:T(8,128)} %param.16) | copy-start | bytes 1572868
  43.5 6.3 %copy-start.2 = (f32[1,2,128,128]{3,2,1,0:T(8,128)S(1)}, f32[1,2,128,128]{3,2,1,0:T(8,128)}, u32[]{:S(2)}) copy-start(f32[1,2,128,128]{3,2,1,0:T(8,128)} %param.20) | copy-start | bytes 393220
  44.8 5.0 %collective-permute-start.1 = (f32[128,256]{1,0:T(8,128)S(1)}, f32[128,256]{1,0:T(8,128)S(1)}, u32[]{:S(2)}, u32[]{:S(2)}) collective-permute-start(f32[128,256]{1,0:T(8,128)S(1)} %get-tuple-element.35), channel_id=1, source_target_pairs={{0,2},{1,3},{2,0},{3,1},{4,6},{5,7},{6,4},{7,5},{8,10},{9,11},{10,... | collective-permute-start | bytes 393224 | tf_op jit(solution)/shard_map/ppermute | solution.py:18
  47.3 2.7 %collective-permute-start = (f32[128,256]{1,0:T(8,128)S(1)}, f32[128,256]{1,0:T(8,128)S(1)}, u32[]{:S(2)}, u32[]{:S(2)}) collective-permute-start(f32[128,256]{1,0:T(8,128)S(1)} %get-tuple-element.34), channel_id=1, source_target_pairs={{0,1},{1,0},{2,3},{3,2},{4,5},{5,4},{6,7},{7,6},{8,9},{9,8},{10,11... | collective-permute-start | bytes 393224 | tf_op jit(solution)/shard_map/ppermute | solution.py:18
  50.2 1.6 %copy-start.13 = (f32[256]{0:T(256)S(1)}, f32[256]{0:T(256)}, u32[]{:S(2)}) copy-start(f32[256]{0:T(256)} %param.15) | copy-start | bytes 3076
  51.8 1.3 %copy-start.1 = (f32[512,256]{1,0:T(8,128)S(1)}, f32[512,256]{1,0:T(8,128)}, u32[]{:S(2)}) copy-start(f32[512,256]{1,0:T(8,128)} %param.21) | copy-start | bytes 1572868
  56.4 15.2 %all-to-all-start.1 = ((f32[32,1,2056]{2,1,0:T(1,128)}), f32[32,1,2056]{2,1,0:T(1,128)S(1)}, u32[]{:S(2)}, u32[]{:S(2)}) async-start(f32[32,1,2056]{2,1,0:T(1,128)} %all_to_all.33), calls=%async_computation.1 | async-start | bytes 557056 | tf_op jit(solution)/shard_map/all_to_all | solution.py:161
  63.0 9.7 %collective-permute-start.3 = (f32[128,256]{0,1:T(8,128)S(1)}, f32[128,256]{0,1:T(8,128)}, u32[]{:S(2)}, u32[]{:S(2)}) collective-permute-start(f32[128,256]{0,1:T(8,128)S(1)} %convolution_bitcast_fusion), channel_id=1, source_target_pairs={{0,2},{1,3},{2,0},{3,1},{4,6},{5,7},{6,4},{7,5},{8,10},{9,11},{10,... | collective-permute-start | bytes 393224 | tf_op jit(solution)/shard_map/ppermute | solution.py:18
  64.9 7.7 %copy-start.7 = (s32[1,2,128]{2,1,0:T(2,128)S(1)}, s32[1,2,128]{2,1,0:T(2,128)}, u32[]{:S(2)}) copy-start(s32[1,2,128]{2,1,0:T(2,128)} %param.19) | copy-start | bytes 3076
  64.9 7.7 %copy-start.11 = (pred[256]{0:T(512)(128)(4,1)S(1)}, pred[256]{0:T(512)(128)(4,1)}, u32[]{:S(2)}) copy-start(pred[256]{0:T(512)(128)(4,1)} %copy-done.10) | copy-start | bytes 772
  64.9 7.7 %collective-permute-start.2 = (f32[128,256]{0,1:T(8,128)S(1)}, f32[128,256]{0,1:T(8,128)}, u32[]{:S(2)}, u32[]{:S(2)}) collective-permute-start(f32[128,256]{0,1:T(8,128)S(1)} %convolution_bitcast_fusion.1), channel_id=1, source_target_pairs={{0,1},{1,0},{2,3},{3,2},{4,5},{5,4},{6,7},{7,6},{8,9},{9,8},{10,11... | collective-permute-start | bytes 393224 | tf_op jit(solution)/shard_map/ppermute | solution.py:18
  71.6 3.0 %copy-start.9 = (s32[1024]{0:T(1024)S(1)}, s32[1024]{0:T(1024)}, u32[]{:S(2)}) copy-start(s32[1024]{0:T(1024)} %copy-done.8) | copy-start | bytes 12292
  114.7 0.7 copy-start.5

commit v14 on v13

--- a/solution.py
+++ b/solution.py
@@ -18,12 +18,24 @@
     return lax.ppermute(array, axis, [(i, i ^ 1 << apart) for i in range(lax.axis_size(axis))])
 
 
-def layer_piece(aggregate, weight, norm_gain):
-    inv_scale = lax.rsqrt(jnp.mean(aggregate * aggregate, axis=-1, keepdims=True) + EPS)
-    normed = aggregate * inv_scale * norm_gain
-    return jax.nn.silu(
-        jnp.dot(normed, weight, precision=DENSE, preferred_element_type=jnp.float32)
-    )
+def layer_both(aggregate, weight, norm_gain, cotangent):
+    scale = lax.rsqrt(jnp.mean(aggregate * aggregate, axis=-1, keepdims=True) + EPS)
+    unit = aggregate * scale
+    pre = jnp.dot(unit * norm_gain, weight, precision=DENSE, preferred_element_type=jnp.float32)
+    gate = jax.nn.sigmoid(pre)
+    activation = pre * gate
+    grad_pre = cotangent * (gate * (1.0 + pre * (1.0 - gate)))
+    g_normed = lax.dot_general(
+        grad_pre, weight, (((1,), (1,)), ((), ())), precision=DENSE,
+        preferred_element_type=jnp.float32,
+    )
+    v = g_normed * norm_gain
+    grad_agg = scale * (v - unit * jnp.mean(v * unit, axis=-1, keepdims=True))
+    moment = lax.dot_general(
+        unit, grad_pre, (((0,), (0,)), ((), ())), precision=DENSE,
+        preferred_element_type=jnp.float32,
+    )
+    return activation, grad_agg, moment
 
 
 def dense_tiles(tile_values, tile_coords, live_count, rows):
@@ -153,15 +165,14 @@
         tiles, hidden, precision=DENSE, preferred_element_type=jnp.float32
     )
     aggregate = boundary_forward(aggregate, hidden, chooser, coupling)
-    activation, pullback = jax.vjp(layer_piece, aggregate, weight, norm_gain)
+    activation, grad_agg, moment = layer_both(aggregate, weight, norm_gain, cotangent)
     output = hidden + activation
-    grad_agg, grad_weight, grad_gain = pullback(cotangent)
     node_scale = 1.0 / math.sqrt(row_count * devices)
-    pieces = jnp.concatenate([grad_weight, grad_gain[None]], 0).reshape(devices, -1)
-    gathered = lax.all_to_all(pieces, ("row", "col"), 0, 0, tiled=True)
-    gathered, tile_input = lax.optimization_barrier((gathered, grad_agg))
-    share = jnp.sum(gathered, axis=0, keepdims=True) * node_scale
-    grad_nodes = cotangent + grad_agg + spread(tiles, tile_input, DENSE)
+    gathered = lax.all_to_all(
+        moment.reshape(devices, -1, feat_count), ("row", "col"), 0, 0, tiled=True
+    )
+    share = jnp.sum(gathered, axis=0).reshape(1, -1)
+    grad_nodes = cotangent + grad_agg + spread(tiles, grad_agg, DENSE)
     grad_nodes = boundary_backward(grad_nodes, grad_agg, chooser, coupling)
     reply = exact_pick(landing, grad_nodes, transposed=True)
     flat = capacity * feat_count
@@ -171,8 +182,9 @@
     )
     back = lax.all_to_all(payload, ("row", "col"), 0, 0, tiled=True)
     returned = back[:, :flat].reshape(devices * capacity, feat_count)
-    total = back[:, flat:].reshape(feat_count + 1, feat_count)
-    weight_sum, gain_sum = total[:-1], total[-1]
+    moment_sum = back[:, flat:].reshape(feat_count, feat_count)
+    weight_sum = moment_sum * norm_gain[:, None] * node_scale
+    gain_sum = jnp.sum(moment_sum * weight, axis=1) * node_scale
     x_grad = exact_pick(chosen, returned, transposed=True)
     return (output, x_grad, weight_sum, gain_sum)
 

time: 118 us -> 115 us (0.975)
  local copies, waits for them, and re-layouts: 7.55 us -> 4.81 us
  waiting for transfers between devices: 35.4 us -> 36.6 us
    all_to_all x1, waiting for transfers between devices: 6.57 us -> 7.94 us  [on_device(): lax.all_to_all(moment.reshape(devices, -1, feat_count), ('row', 'col'), 0...]
    slice x3 -> x1, local copies, waits for them, and re-layouts: 1.3 us -> 0.02 us  [on_device(): moment_sum = back[:, flat:].reshape(feat_count, feat_count)]
    add_any x1 -> x0, other arithmetic: 1.25 us -> none  [layer_piece(): aggregate * aggregate]
  transfers between devices with their start and end apart: 6 -> 6, of which waited for: 3 -> 3; matrix products, arithmetic and copies ran while one was open for 4% -> 5% of each run, Pallas kernels for 0% -> 0%
where the time goes in v14:
time: 115 us; the launch traced here: 114 us
  waiting for transfers between devices  36.6 us (32%)
  blocking collectives  35.5 us (31%)
  matrix products  15.2 us (13%)
  starting transfers between devices  14.2 us (12%)
  other arithmetic  7.12 us (6%)
  local copies, waits for them, and re-layouts  4.81 us (4%)
    all_to_all x1, blocking collectives, on_device(): back = lax.all_to_all(payload, ('row', 'col'), 0, 0, tiled=True)  35.5 us
    all_to_all x1, waiting for transfers between devices, on_device(): lax.all_to_all(jnp.concatenate([outbox, tags], axis=1), ('row', 'col'), 0...  26.2 us
    all_to_all x1, waiting for transfers between devices, on_device(): lax.all_to_all(moment.reshape(devices, -1, feat_count), ('row', 'col'), 0...  7.94 us
    all_to_all x1, starting transfers between devices, on_device(): lax.all_to_all(jnp.concatenate([outbox, tags], axis=1), ('row', 'col'), 0...  7.48 us
    dot_general x4, matrix products, exact_pick(): lax.dot_general(chooser.astype(jnp.bfloat16), parts, dims, preferred_elem...  4.36 us
    ppermute x4, starting transfers between devices, swapped(): lax.ppermute(array, axis, [(i, i ^ 1 << apart) for i in range(lax.axis_si...  3.43 us
    all_to_all x1, starting transfers between devices, on_device(): lax.all_to_all(moment.reshape(devices, -1, feat_count), ('row', 'col'), 0...  3.26 us
    dot_general x3, matrix products, spread(): lax.dot_general(chooser, values, (((0,), (0,)), ((), ())), precision=prec...  3.07 us
  transfers between devices with their start and end apart: 6, of which 3 were waited for; matrix products, arithmetic and copies ran while one was open for 5% of the time, Pallas kernels for 0%

profile of v14, /device:TPU:0, one launch (start us, length us, event | category | flops | bytes accessed | tf_op | source)
XLA Modules:
  0.0 114.4 jit_solution(9708837009877059496)
XLA Ops:
  0.6 0.6 compare_reduce_fusion
  1.3 0.7 add_select_fusion.1
  2.0 0.3 fusion.15
  2.3 1.2 %reduce-precision_convert_fusion.7 = (bf16[512,256]{1,0:T(8,128)(2,1)S(1)}, bf16[512,256]{1,0:T(8,128)(2,1)S(1)}, bf16[512,256]{1,0:T(8,128)(2,1)S(1)}) fusion(f32[512,256]{1,0:T(8,128)} %param.12), kind=kLoop, calls=%fused_computation.81 | loop fusion | flops 917504 | bytes 1310720 | tf_op jit(solution)/shard_map/convert.9
  3.4 1.0 fusion.3
  4.5 0.2 slice_add_fusion.2
  4.7 0.2 reshape.176
  4.9 0.3 select_reduce_fusion
  5.2 0.7 convert_select_fusion
  5.8 0.1 reshape.177
  5.9 0.1 select_maximum_fusion
  6.0 1.7 %all_to_all.19 = f32[32,1,8320]{2,1,0:T(1,128)} reshape(f32[32,8320]{1,0:T(8,128)S(1)} %select_maximum_fusion) | data formatting | bytes 2129920 | tf_op jit(solution)/shard_map/all_to_all | solution.py:154
  7.7 7.5 %all-to-all-start = ((f32[32,1,8320]{2,1,0:T(1,128)}), f32[32,1,8320]{2,1,0:T(1,128)S(1)}, u32[]{:S(2)}, u32[]{:S(2)}) async-start(f32[32,1,8320]{2,1,0:T(1,128)} %all_to_all.19), calls=%async_computation | async-start | bytes 2129920 | tf_op jit(solution)/shard_map/all_to_all | solution.py:154
  15.2 0.1 slice_bitcast_fusion
  15.3 0.1 compare_bitcast_fusion
  15.4 26.2 %all-to-all-done = f32[32,1,8320]{2,1,0:T(1,128)S(1)} async-done(((f32[32,1,8320]{2,1,0:T(1,128)}), f32[32,1,8320]{2,1,0:T(1,128)S(1)}, u32[]{:S(2)}, u32[]{:S(2)}) %all-to-all-start) | async-done | bytes 1064992 | tf_op jit(solution)/shard_map/all_to_all | solution.py:154
  41.6 0.1 copy.57
  41.6 0.1 slice.129
  41.7 0.2 reshape.178
  41.9 0.2 reduce-precision_convert_fusion.3
  42.2 0.1 eq.100
  42.2 1.0 fusion.1
  43.3 0.0 copy-start.4
  43.3 0.0 copy-start.1
  43.3 0.1 slice_add_fusion.6
  43.4 0.0 copy-start
  43.4 0.5 copy-done.4
  44.0 0.7 fusion.29
  44.7 1.5 %collective-permute-start.1 = (f32[128,256]{1,0:T(8,128)S(1)}, f32[128,256]{1,0:T(8,128)S(1)}, u32[]{:S(2)}, u32[]{:S(2)}) collective-permute-start(f32[128,256]{1,0:T(8,128)S(1)} %get-tuple-element.31), channel_id=1, source_target_pairs={{0,2},{1,3},{2,0},{3,1},{4,6},{5,7},{6,4},{7,5},{8,10},{9,11},{10,... | collective-permute-start | bytes 393224 | tf_op jit(solution)/shard_map/ppermute | solution.py:18
  46.2 1.0 fusion.45
  47.2 0.1 collective-permute-start
  47.3 2.4 %collective-permute-done.1 = f32[128,256]{1,0:T(8,128)S(1)} collective-permute-done((f32[128,256]{1,0:T(8,128)S(1)}, f32[128,256]{1,0:T(8,128)S(1)}, u32[]{:S(2)}, u32[]{:S(2)}) %collective-permute-start.1) | collective-permute-done | bytes 131104 | tf_op jit(solution)/shard_map/ppermute | solution.py:18
  49.7 0.2 convolution_bitcast_fusion.3
  50.0 0.2 convolution_bitcast_fusion.4
  50.2 0.0 copy-start.3
  50.2 0.0 copy-start.5
  50.2 0.9 fusion.27
  51.1 0.7 multiply_reduce_fusion.1
  51.8 1.3 %multiply_add_fusion = (f32[512,256]{1,0:T(8,128)}, f32[512,256]{1,0:T(8,128)S(1)}) fusion(f32[512,256]{1,0:T(8,128)S(1)} %slice_add_fusion.6, f32[256,256]{1,0:T(8,128)S(1)} %copy-done.3, f32[512,256]{1,0:T(8,128)S(1)} %get-tuple-element.37, f32[256]{0:T(256)S(1)} %copy-done.5, f32[512]{0:T(512)S(1)} %add_rsqrt_fusion), kind=kOutput, calls=%fused_computation.94 | convolution fusion | flops 202244096 | bytes 2362368 | tf_op jit(solution)/shard_map/dot_general | solution.py:24
  53.1 0.6 multiply_reduce_fusion
  53.7 0.8 fusion.25
  54.5 0.3 convolution_bitcast_fusion.2
  54.8 0.3 convolution_bitcast_fusion.1
  55.1 1.2 %convolution_add_fusion.1 = f32[512,256]{1,0:T(8,128)S(1)} fusion(f32[64,8,4,128]{3,2,1,0:T(4,128)S(1)} %bitcast.80, f32[512,256]{1,0:T(8,128)S(1)} %copy-done.2, f32[512,256]{1,0:T(8,128)S(1)} %get-tuple-element.41, f32[512]{0:T(512)S(1)} %broadcast_multiply_fusion, f32[512,256]{1,0:T(8,128)S(1)} %get-tuple-element.37, f32[512]{0:T(512)S(1)} %add_rsqrt_fusion), kind=kOutput, calls=%fused_computation.29 | convolution fusion | flops 403963904 | bytes 3149824 | tf_op jit(solution)/shard_map/dot_general | solution.py:68
  56.4 0.1 collective-permute-start.2
  56.4 1.8 %collective-permute-start.3 = (f32[128,256]{0,1:T(8,128)S(1)}, f32[128,256]{0,1:T(8,128)S(1)}, u32[]{:S(2)}, u32[]{:S(2)}) collective-permute-start(f32[128,256]{0,1:T(8,128)S(1)} %convolution_bitcast_fusion.1), channel_id=1, source_target_pairs={{0,2},{1,3},{2,0},{3,1},{4,6},{5,7},{6,4},{7,5},{8,10},{9,11},{10,... | collective-permute-start | bytes 393224 | tf_op jit(solution)/shard_map/ppermute | solution.py:18
  58.2 1.4 %convolution_bitcast_fusion = f32[32,8,256]{2,1,0:T(8,128)} fusion(f32[512,256]{1,0:T(8,128)S(1)} %get-tuple-element.37, f32[512]{0:T(512)S(1)} %add_rsqrt_fusion, f32[512,256]{1,0:T(8,128)S(1)} %copy-done.2, f32[512,256]{1,0:T(8,128)S(1)} %get-tuple-element.39), kind=kOutput, calls=%fused_computation.32 | convolution fusion | flops 202506240 | bytes 1837056 | tf_op jit(solution)/shard_map/dot_general | solution.py:34
  59.6 3.3 %all-to-all-start.1 = ((f32[32,8,256]{2,1,0:T(8,128)}), f32[32,8,256]{2,1,0:T(8,128)S(1)}, u32[]{:S(2)}, u32[]{:S(2)}) async-start(f32[32,8,256]{2,1,0:T(8,128)} %convolution_bitcast_fusion), calls=%async_computation.1 | async-start | bytes 524288 | tf_op jit(solution)/shard_map/all_to_all | solution.py:171
  62.9 0.9 reduce-precision_convert_fusion.5
  63.9 1.1 fusion
  64.9 0.2 slice_add_fusion
  65.2 0.2 reshape.180
  65.4 7.9 %all-to-all-done.1 = f32[32,8,256]{2,1,0:T(8,128)S(1)} async-done(((f32[32,8,256]{2,1,0:T(8,128)}), f32[32,8,256]{2,1,0:T(8,128)S(1)}, u32[]{:S(2)}, u32[]{:S(2)}) %all-to-all-start.1) | async-done | bytes 262176 | tf_op jit(solution)/shard_map/all_to_all | solution.py:171
  73.4 0.1 pad_maximum_fusion
  73.5 0.9 all_to_all.23
  74.4 35.5 %all_to_all.29 = f32[32,1,10240]{2,1,0:T(1,128)S(1)} all-to-all(f32[32,1,10240]{2,1,0:T(1,128)S(1)} %all_to_all.23), channel_id=1, replica_groups=mesh['row'=8,'col'=4] {'row','col'}, dimensions={0} | all-to-all | bytes 2621440 | tf_op jit(solution)/shard_map/all_to_all | solution.py:183
  109.8 0.4 copy.56
  110.2 0.1 slice.140
  110.3 0.2 reshape.182
  110.5 0.2 reduce-precision_convert_fusion.1
  110.8 1.2 %fusion.2 = f32[512,768]{1,0:T(8,128)S(1)} fusion(bf16[1024,256]{1,0:T(8,128)(2,1)S(1)} %get-tuple-element.17, bf16[1024,256]{1,0:T(8,128)(2,1)S(1)} %get-tuple-element.18, bf16[1024,256]{1,0:T(8,128)(2,1)S(1)} %get-tuple-element.16, s32[512]{0:T(512)S(1)} %convert_add_fusion), kind=kOutput, calls=%fused_computation.5 | convolution fusion | flops 810549248 | bytes 3147776 | tf_op jit(solution)/shard_map/dot_general | solution.py:113
  112.0 0.9 slice_add_fusion.4
  112.9 0.9 multiply_reduce_fusion.2
  113.8 0.6 broadcast_multiply_fusion.1
  (26 shorter events, 0.2 us)
Async XLA Ops:
  7.7 7.5 %copy-start.7 = (s32[1,3]{1,0:T(1,128)S(1)}, s32[1,3]{1,0:T(1,128)}, u32[]{:S(2)}) copy-start(s32[1,3]{1,0:T(1,128)} %param.18) | copy-start | bytes 40
  7.7 7.7 %copy-start.6 = (s32[1,8,2]{1,2,0:T(2,128)S(1)}, s32[1,8,2]{1,2,0:T(2,128)}, u32[]{:S(2)}) copy-start(s32[1,8,2]{1,2,0:T(2,128)} %param.17) | copy-start | bytes 196
  7.7 33.9 %all-to-all-start = ((f32[32,1,8320]{2,1,0:T(1,128)}), f32[32,1,8320]{2,1,0:T(1,128)S(1)}, u32[]{:S(2)}, u32[]{:S(2)}) async-start(f32[32,1,8320]{2,1,0:T(1,128)} %all_to_all.19), calls=%async_computation | async-start | bytes 2129920 | tf_op jit(solution)/shard_map/all_to_all | solution.py:154
  43.3 0.7 copy-start.4
  43.3 2.9 %copy-start.1 = (f32[1,8,128,128]{3,2,1,0:T(8,128)S(1)}, f32[1,8,128,128]{3,2,1,0:T(8,128)}, u32[]{:S(2)}) copy-start(f32[1,8,128,128]{3,2,1,0:T(8,128)} %param.16) | copy-start | bytes 1572868
  43.4 6.3 %copy-start = (f32[1,2,128,128]{3,2,1,0:T(8,128)S(1)}, f32[1,2,128,128]{3,2,1,0:T(8,128)}, u32[]{:S(2)}) copy-start(f32[1,2,128,128]{3,2,1,0:T(8,128)} %param.20) | copy-start | bytes 393220
  44.7 5.0 %collective-permute-start.1 = (f32[128,256]{1,0:T(8,128)S(1)}, f32[128,256]{1,0:T(8,128)S(1)}, u32[]{:S(2)}, u32[]{:S(2)}) collective-permute-start(f32[128,256]{1,0:T(8,128)S(1)} %get-tuple-element.31), channel_id=1, source_target_pairs={{0,2},{1,3},{2,0},{3,1},{4,6},{5,7},{6,4},{7,5},{8,10},{9,11},{10,... | collective-permute-start | bytes 393224 | tf_op jit(solution)/shard_map/ppermute | solution.py:18
  47.2 2.7 %collective-permute-start = (f32[128,256]{1,0:T(8,128)S(1)}, f32[128,256]{1,0:T(8,128)S(1)}, u32[]{:S(2)}, u32[]{:S(2)}) collective-permute-start(f32[128,256]{1,0:T(8,128)S(1)} %get-tuple-element.30), channel_id=1, source_target_pairs={{0,1},{1,0},{2,3},{3,2},{4,5},{5,4},{6,7},{7,6},{8,9},{9,8},{10,11... | collective-permute-start | bytes 393224 | tf_op jit(solution)/shard_map/ppermute | solution.py:18
  50.2 1.6 %copy-start.3 = (f32[256,256]{1,0:T(8,128)S(1)}, f32[256,256]{1,0:T(8,128)}, u32[]{:S(2)}) copy-start(f32[256,256]{1,0:T(8,128)} %param.14) | copy-start | bytes 786436
  50.2 1.6 %copy-start.5 = (f32[256]{0:T(256)S(1)}, f32[256]{0:T(256)}, u32[]{:S(2)}) copy-start(f32[256]{0:T(256)} %param.15) | copy-start | bytes 3076
  51.8 1.3 %copy-start.2 = (f32[512,256]{1,0:T(8,128)S(1)}, f32[512,256]{1,0:T(8,128)}, u32[]{:S(2)}) copy-start(f32[512,256]{1,0:T(8,128)} %param.21) | copy-start | bytes 1572868
  56.4 6.5 %collective-permute-start.2 = (f32[128,256]{0,1:T(8,128)S(1)}, f32[128,256]{0,1:T(8,128)S(1)}, u32[]{:S(2)}, u32[]{:S(2)}) collective-permute-start(f32[128,256]{0,1:T(8,128)S(1)} %convolution_bitcast_fusion.2), channel_id=1, source_target_pairs={{0,1},{1,0},{2,3},{3,2},{4,5},{5,4},{6,7},{7,6},{8,9},{9,8},{10,11... | collective-permute-start | bytes 393224 | tf_op jit(solution)/shard_map/ppermute | solution.py:18
  56.4 6.5 %collective-permute-start.3 = (f32[128,256]{0,1:T(8,128)S(1)}, f32[128,256]{0,1:T(8,128)S(1)}, u32[]{:S(2)}, u32[]{:S(2)}) collective-permute-start(f32[128,256]{0,1:T(8,128)S(1)} %convolution_bitcast_fusion.1), channel_id=1, source_target_pairs={{0,2},{1,3},{2,0},{3,1},{4,6},{5,7},{6,4},{7,5},{8,10},{9,11},{10,... | collective-permute-start | bytes 393224 | tf_op jit(solution)/shard_map/ppermute | solution.py:18
  59.6 13.6 %all-to-all-start.1 = ((f32[32,8,256]{2,1,0:T(8,128)}), f32[32,8,256]{2,1,0:T(8,128)S(1)}, u32[]{:S(2)}, u32[]{:S(2)}) async-start(f32[32,8,256]{2,1,0:T(8,128)} %convolution_bitcast_fusion), calls=%async_computation.1 | async-start | bytes 524288 | tf_op jit(solution)/shard_map/all_to_all | solution.py:171

commit v15 on v14

--- a/solution.py
+++ b/solution.py
@@ -108,13 +108,11 @@
     hi = lax.reduce_precision(values, 8, 7)
     rest = values - hi
     mid = lax.reduce_precision(rest, 8, 7)
-    parts = jnp.concatenate([hi, mid, rest - mid], axis=1).astype(jnp.bfloat16)
-    dims = (((0,), (0,)), ((), ())) if transposed else (((1,), (0,)), ((), ()))
-    out = lax.dot_general(
-        chooser.astype(jnp.bfloat16), parts, dims, preferred_element_type=jnp.float32
-    )
-    width = values.shape[1]
-    return (out[:, :width] + out[:, width : 2 * width]) + out[:, 2 * width :]
+    parts = jnp.concatenate([hi, mid, rest - mid], axis=0).astype(jnp.bfloat16)
+    axis = 0 if transposed else 1
+    wide = jnp.concatenate([chooser] * 3, axis=axis).astype(jnp.bfloat16)
+    dims = (((axis,), (0,)), ((), ()))
+    return lax.dot_general(wide, parts, dims, preferred_element_type=jnp.float32)
 
 
 def on_device(

time: 115 us -> 114 us (level)
  blocking collectives: 35.5 us -> 0 us
  waiting for transfers between devices: 36.6 us -> 67.5 us
  starting transfers between devices: 14.2 us -> 16.8 us
  local copies, waits for them, and re-layouts: 4.81 us -> 6.84 us
    all_to_all x1 -> x0, blocking collectives: 35.5 us -> none  [on_device(): back = lax.all_to_all(payload, ('row', 'col'), 0, 0, tiled=True)]
    all_to_all x0 -> x1, waiting for transfers between devices: none -> 30.9 us  [on_device(): back = lax.all_to_all(payload, ('row', 'col'), 0, 0, tiled=True)]
    all_to_all x0 -> x1, starting transfers between devices: none -> 2.67 us  [on_device(): back = lax.all_to_all(payload, ('row', 'col'), 0, 0, tiled=True)]
    dot_general x4, matrix products: 4.36 us -> 5.76 us  [exact_pick(): lax.dot_general(wide, parts, dims, preferred_element_type=jnp.float32)]
    add x4 -> x0, other arithmetic: 1.4 us -> none  [exact_pick(): return out[:, :width] + out[:, width:2 * width] + out[:, 2 * width:]]
  transfers between devices with their start and end apart: 6 -> 7, of which waited for: 3 -> 4; matrix products, arithmetic and copies ran while one was open for 5% -> 5% of each run, Pallas kernels for 0% -> 0%
where the time goes in v15:
time: 114 us
  waiting for transfers between devices  67.5 us (59%)
  starting transfers between devices  16.8 us (15%)
  matrix products  15 us (13%)
  local copies, waits for them, and re-layouts  6.84 us (6%)
  other arithmetic  6.6 us (6%)
    all_to_all x1, waiting for transfers between devices, on_device(): back = lax.all_to_all(payload, ('row', 'col'), 0, 0, tiled=True)  30.9 us
    all_to_all x1, waiting for transfers between devices, on_device(): lax.all_to_all(jnp.concatenate([outbox, tags], axis=1), ('row', 'col'), 0...  26.2 us
    all_to_all x1, waiting for transfers between devices, on_device(): lax.all_to_all(moment.reshape(devices, -1, feat_count), ('row', 'col'), 0...  8.22 us
    all_to_all x1, starting transfers between devices, on_device(): lax.all_to_all(jnp.concatenate([outbox, tags], axis=1), ('row', 'col'), 0...  7.47 us
    dot_general x4, matrix products, exact_pick(): lax.dot_general(wide, parts, dims, preferred_element_type=jnp.float32)  5.76 us
    ppermute x4, starting transfers between devices, swapped(): lax.ppermute(array, axis, [(i, i ^ 1 << apart) for i in range(lax.axis_si...  3.43 us
    all_to_all x1, starting transfers between devices, on_device(): lax.all_to_all(moment.reshape(devices, -1, feat_count), ('row', 'col'), 0...  3.26 us
    another operation x5, other arithmetic  3.14 us
  transfers between devices with their start and end apart: 7, of which 4 were waited for; matrix products, arithmetic and copies ran while one was open for 5% of the time, Pallas kernels for 0%

profile of v15, /device:TPU:0, one launch (start us, length us, event | category | flops | bytes accessed | tf_op | source)
XLA Modules:
  0.0 113.9 jit_solution(4036117643863801964)
XLA Ops:
  0.6 0.6 compare_reduce_fusion
  1.3 0.7 add_select_fusion.1
  2.0 0.3 fusion.30
  2.3 0.4 iota_compare_fusion.1
  2.6 0.0 copy-start.2
  2.7 1.4 %reduce-precision_convert_fusion.7 = (bf16[512,256]{1,0:T(8,128)(2,1)S(1)}, bf16[512,256]{1,0:T(8,128)(2,1)S(1)}, bf16[512,256]{1,0:T(8,128)(2,1)S(1)}) fusion(f32[512,256]{1,0:T(8,128)} %param.12), kind=kLoop, calls=%fused_computation.89 | loop fusion | flops 917504 | bytes 1310720 | tf_op jit(solution)/shard_map/convert.9
  4.0 1.0 fusion
  5.0 0.2 reshape.176
  5.2 0.3 select_reduce_fusion
  5.5 0.7 convert_select_fusion
  6.2 0.1 reshape.177
  6.2 0.1 select_maximum_fusion
  6.3 1.7 %all_to_all.19 = f32[32,1,8320]{2,1,0:T(1,128)} reshape(f32[32,8320]{1,0:T(8,128)S(1)} %select_maximum_fusion) | data formatting | bytes 2129920 | tf_op jit(solution)/shard_map/all_to_all | solution.py:152
  8.0 7.5 %all-to-all-start = ((f32[32,1,8320]{2,1,0:T(1,128)}), f32[32,1,8320]{2,1,0:T(1,128)S(1)}, u32[]{:S(2)}, u32[]{:S(2)}) async-start(f32[32,1,8320]{2,1,0:T(1,128)} %all_to_all.19), calls=%async_computation | async-start | bytes 2129920 | tf_op jit(solution)/shard_map/all_to_all | solution.py:152
  15.6 0.1 slice_bitcast_fusion
  15.6 0.1 compare_bitcast_fusion
  15.7 26.2 %all-to-all-done = f32[32,1,8320]{2,1,0:T(1,128)S(1)} async-done(((f32[32,1,8320]{2,1,0:T(1,128)}), f32[32,1,8320]{2,1,0:T(1,128)S(1)}, u32[]{:S(2)}, u32[]{:S(2)}) %all-to-all-start) | async-done | bytes 1064992 | tf_op jit(solution)/shard_map/all_to_all | solution.py:152
  41.9 0.1 copy.68
  42.0 0.1 slice.78
  42.1 0.2 reshape.178
  42.3 0.2 reduce-precision_convert_fusion.3
  42.5 0.1 eq.100
  42.6 0.3 iota_compare_fusion
  42.9 0.0 copy-start.4
  42.9 1.2 %fusion.6 = f32[512,256]{0,1:T(8,128)S(1)} fusion(pred[512,1024]{1,0:T(32,128)(4,1)S(1)} %iota_compare_fusion, bf16[1024,256]{1,0:T(8,128)(2,1)S(1)} %get-tuple-element.32, bf16[1024,256]{1,0:T(8,128)(2,1)S(1)} %get-tuple-element.33, bf16[1024,256]{1,0:T(8,128)(2,1)S(1)} %get-tuple-element.31), kind=kOutput, calls=%fused_computation.6 | convolution fusion | flops 813170688 | bytes 2621440 | tf_op jit(solution)/shard_map/dot_general | solution.py:115
  44.1 0.0 copy-start.1
  44.1 0.7 fusion.40
  44.9 1.5 %collective-permute-start.1 = (f32[128,256]{1,0:T(8,128)S(1)}, f32[128,256]{1,0:T(8,128)S(1)}, u32[]{:S(2)}, u32[]{:S(2)}) collective-permute-start(f32[128,256]{1,0:T(8,128)S(1)} %get-tuple-element.43), channel_id=1, source_target_pairs={{0,2},{1,3},{2,0},{3,1},{4,6},{5,7},{6,4},{7,5},{8,10},{9,11},{10,... | collective-permute-start | bytes 393224 | tf_op jit(solution)/shard_map/ppermute | solution.py:18
  46.4 1.0 fusion.56
  47.4 0.2 copy.37
  47.6 0.1 collective-permute-start
  47.7 2.2 %collective-permute-done.1 = f32[128,256]{1,0:T(8,128)S(1)} collective-permute-done((f32[128,256]{1,0:T(8,128)S(1)}, f32[128,256]{1,0:T(8,128)S(1)}, u32[]{:S(2)}, u32[]{:S(2)}) %collective-permute-start.1) | collective-permute-done | bytes 131104 | tf_op jit(solution)/shard_map/ppermute | solution.py:18
  49.9 0.2 convolution_bitcast_fusion.3
  50.1 0.2 convolution_bitcast_fusion.4
  50.3 0.8 fusion.38
  51.2 0.0 copy-start.9
  51.2 0.7 multiply_reduce_fusion.1
  51.9 0.3 copy-done.7
  52.1 0.6 multiply_add_fusion
  52.7 0.6 multiply_reduce_fusion
  53.4 0.7 fusion.36
  54.1 0.3 convolution_bitcast_fusion.2
  54.4 0.3 convolution_bitcast_fusion.1
  54.7 0.6 convolution_add_fusion.1
  55.4 0.1 collective-permute-start.2
  55.4 1.8 %collective-permute-start.3 = (f32[128,256]{0,1:T(8,128)S(1)}, f32[128,256]{0,1:T(8,128)S(1)}, u32[]{:S(2)}, u32[]{:S(2)}) collective-permute-start(f32[128,256]{0,1:T(8,128)S(1)} %convolution_bitcast_fusion.1), channel_id=1, source_target_pairs={{0,2},{1,3},{2,0},{3,1},{4,6},{5,7},{6,4},{7,5},{8,10},{9,11},{10,... | collective-permute-start | bytes 393224 | tf_op jit(solution)/shard_map/ppermute | solution.py:18
  57.2 1.3 %convolution_bitcast_fusion = f32[32,8,256]{2,1,0:T(8,128)} fusion(f32[512,256]{0,1:T(8,128)S(1)} %get-tuple-element.49, f32[512]{0:T(512)S(1)} %add_rsqrt_fusion, f32[512,256]{0,1:T(8,128)S(1)} %copy.37, f32[512,256]{0,1:T(8,128)S(1)} %get-tuple-element.51), kind=kOutput, calls=%fused_computation.48 | convolution fusion | flops 202506240 | bytes 1837056 | tf_op jit(solution)/shard_map/dot_general | solution.py:34
  58.5 3.3 %all-to-all-start.1 = ((f32[32,8,256]{2,1,0:T(8,128)}), f32[32,8,256]{2,1,0:T(8,128)S(1)}, u32[]{:S(2)}, u32[]{:S(2)}) async-start(f32[32,8,256]{2,1,0:T(8,128)} %convolution_bitcast_fusion), calls=%async_computation.1 | async-start | bytes 524288 | tf_op jit(solution)/shard_map/all_to_all | solution.py:169
  61.8 0.9 reduce-precision_convert_fusion.5
  62.7 1.0 fusion.18
  63.7 0.2 reshape.180
  63.9 8.2 %all-to-all-done.1 = f32[32,8,256]{2,1,0:T(8,128)S(1)} async-done(((f32[32,8,256]{2,1,0:T(8,128)}), f32[32,8,256]{2,1,0:T(8,128)S(1)}, u32[]{:S(2)}, u32[]{:S(2)}) %all-to-all-start.1) | async-done | bytes 262176 | tf_op jit(solution)/shard_map/all_to_all | solution.py:169
  72.2 0.1 pad_maximum_fusion
  72.3 2.0 %all_to_all.23 = f32[32,1,10240]{2,1,0:T(1,128)} reshape(f32[32,10240]{1,0:T(8,128)S(1)} %pad_maximum_fusion) | data formatting | bytes 2621440 | tf_op jit(solution)/shard_map/all_to_all | solution.py:181
  74.3 2.7 %all-to-all-start.2 = ((f32[32,1,10240]{2,1,0:T(1,128)}), f32[32,1,10240]{2,1,0:T(1,128)S(1)}, u32[]{:S(2)}, u32[]{:S(2)}) async-start(f32[32,1,10240]{2,1,0:T(1,128)} %all_to_all.23), calls=%async_computation.2 | async-start | bytes 2621440 | tf_op jit(solution)/shard_map/all_to_all | solution.py:181
  76.9 1.0 copy.40
  77.9 30.9 %all-to-all-done.2 = f32[32,1,10240]{2,1,0:T(1,128)S(1)} async-done(((f32[32,1,10240]{2,1,0:T(1,128)}), f32[32,1,10240]{2,1,0:T(1,128)S(1)}, u32[]{:S(2)}, u32[]{:S(2)}) %all-to-all-start.2) | async-done | bytes 1310752 | tf_op jit(solution)/shard_map/all_to_all | solution.py:181
  108.8 0.4 copy.67
  109.2 0.1 slice.83
  109.3 0.2 reshape.182
  109.5 0.2 reduce-precision_convert_fusion.1
  109.8 0.9 multiply_reduce_fusion.2
  110.7 0.6 broadcast_multiply_fusion.1
  111.3 2.6 %fusion.12 = f32[512,256]{1,0:T(8,128)} fusion(pred[1024,512]{1,0:T(32,128)(4,1)S(1)} %copy-done.3, bf16[1024,256]{1,0:T(8,128)(2,1)S(1)} %get-tuple-element.29, bf16[1024,256]{1,0:T(8,128)(2,1)S(1)} %get-tuple-element.30, bf16[1024,256]{1,0:T(8,128)(2,1)S(1)} %get-tuple-element.28), kind=kOutput, calls=%fused_computation.12 | convolution fusion | flops 813170688 | bytes 2621440 | tf_op jit(solution)/shard_map/dot_general | solution.py:115
  (35 shorter events, 0.3 us)
Async XLA Ops:
  2.6 1.4 %copy-start.2 = (pred[1024,512]{1,0:T(32,128)(4,1)}, pred[1024,512]{1,0:T(32,128)(4,1)S(1)}, u32[]{:S(2)}) copy-start(pred[1024,512]{1,0:T(32,128)(4,1)S(1)} %iota_compare_fusion.1) | copy-start | bytes 1572868
  8.0 7.5 %copy-start.11 = (s32[1,3]{1,0:T(1,128)S(1)}, s32[1,3]{1,0:T(1,128)}, u32[]{:S(2)}) copy-start(s32[1,3]{1,0:T(1,128)} %param.18) | copy-start | bytes 40
  8.0 7.7 %copy-start.10 = (s32[1,8,2]{1,2,0:T(2,128)S(1)}, s32[1,8,2]{1,2,0:T(2,128)}, u32[]{:S(2)}) copy-start(s32[1,8,2]{1,2,0:T(2,128)} %param.17) | copy-start | bytes 196
  8.0 33.9 %all-to-all-start = ((f32[32,1,8320]{2,1,0:T(1,128)}), f32[32,1,8320]{2,1,0:T(1,128)S(1)}, u32[]{:S(2)}, u32[]{:S(2)}) async-start(f32[32,1,8320]{2,1,0:T(1,128)} %all_to_all.19), calls=%async_computation | async-start | bytes 2129920 | tf_op jit(solution)/shard_map/all_to_all | solution.py:152
  42.9 1.2 %copy-start.4 = (pred[512,1024]{1,0:T(32,128)(4,1)}, pred[512,1024]{1,0:T(32,128)(4,1)S(1)}, u32[]{:S(2)}) copy-start(pred[512,1024]{1,0:T(32,128)(4,1)S(1)} %iota_compare_fusion) | copy-start | bytes 1572868
  42.9 1.2 %copy-start.8 = (s32[1,2,128]{2,1,0:T(2,128)S(1)}, s32[1,2,128]{2,1,0:T(2,128)}, u32[]{:S(2)}) copy-start(s32[1,2,128]{2,1,0:T(2,128)} %param.19) | copy-start | bytes 3076
  44.1 2.3 %copy-start.6 = (f32[1,8,128,128]{3,2,1,0:T(8,128)S(1)}, f32[1,8,128,128]{3,2,1,0:T(8,128)}, u32[]{:S(2)}) copy-start(f32[1,8,128,128]{3,2,1,0:T(8,128)} %param.16) | copy-start | bytes 1572868
  44.1 3.3 %copy-start.1 = (f32[512,256]{1,0:T(8,128)S(1)}, f32[512,256]{1,0:T(8,128)}, u32[]{:S(2)}) copy-start(f32[512,256]{1,0:T(8,128)} %param.21) | copy-start | bytes 1572868
  44.9 5.0 %collective-permute-start.1 = (f32[128,256]{1,0:T(8,128)S(1)}, f32[128,256]{1,0:T(8,128)S(1)}, u32[]{:S(2)}, u32[]{:S(2)}) collective-permute-start(f32[128,256]{1,0:T(8,128)S(1)} %get-tuple-element.43), channel_id=1, source_target_pairs={{0,2},{1,3},{2,0},{3,1},{4,6},{5,7},{6,4},{7,5},{8,10},{9,11},{10,... | collective-permute-start | bytes 393224 | tf_op jit(solution)/shard_map/ppermute | solution.py:18
  46.4 3.5 %copy-start = (f32[1,2,128,128]{3,2,1,0:T(8,128)S(1)}, f32[1,2,128,128]{3,2,1,0:T(8,128)}, u32[]{:S(2)}) copy-start(f32[1,2,128,128]{3,2,1,0:T(8,128)} %param.20) | copy-start | bytes 393220
  47.6 2.5 %collective-permute-start = (f32[128,256]{1,0:T(8,128)S(1)}, f32[128,256]{1,0:T(8,128)S(1)}, u32[]{:S(2)}, u32[]{:S(2)}) collective-permute-start(f32[128,256]{1,0:T(8,128)S(1)} %get-tuple-element.42), channel_id=1, source_target_pairs={{0,1},{1,0},{2,3},{3,2},{4,5},{5,4},{6,7},{7,6},{8,9},{9,8},{10,11... | collective-permute-start | bytes 393224 | tf_op jit(solution)/shard_map/ppermute | solution.py:18
  51.2 1.0 copy-start.7
  51.2 0.9 copy-start.9
  55.4 6.4 %collective-permute-start.2 = (f32[128,256]{0,1:T(8,128)S(1)}, f32[128,256]{0,1:T(8,128)S(1)}, u32[]{:S(2)}, u32[]{:S(2)}) collective-permute-start(f32[128,256]{0,1:T(8,128)S(1)} %convolution_bitcast_fusion.2), channel_id=1, source_target_pairs={{0,1},{1,0},{2,3},{3,2},{4,5},{5,4},{6,7},{7,6},{8,9},{9,8},{10,11... | collective-permute-start | bytes 393224 | tf_op jit(solution)/shard_map/ppermute | solution.py:18
  55.4 6.3 %collective-permute-start.3 = (f32[128,256]{0,1:T(8,128)S(1)}, f32[128,256]{0,1:T(8,128)S(1)}, u32[]{:S(2)}, u32[]{:S(2)}) collective-permute-start(f32[128,256]{0,1:T(8,128)S(1)} %convolution_bitcast_fusion.1), channel_id=1, source_target_pairs={{0,2},{1,3},{2,0},{3,1},{4,6},{5,7},{6,4},{7,5},{8,10},{9,11},{10,... | collective-permute-start | bytes 393224 | tf_op jit(solution)/shard_map/ppermute | solution.py:18
  58.5 4.2 %copy-start.5 = (pred[512,1024]{1,0:T(32,128)(4,1)S(1)}, pred[512,1024]{1,0:T(32,128)(4,1)}, u32[]{:S(2)}) copy-start(pred[512,1024]{1,0:T(32,128)(4,1)} %copy-done.4) | copy-start | bytes 1572868
  58.5 13.6 %all-to-all-start.1 = ((f32[32,8,256]{2,1,0:T(8,128)}), f32[32,8,256]{2,1,0:T(8,128)S(1)}, u32[]{:S(2)}, u32[]{:S(2)}) async-start(f32[32,8,256]{2,1,0:T(8,128)} %convolution_bitcast_fusion), calls=%async_computation.1 | async-start | bytes 524288 | tf_op jit(solution)/shard_map/all_to_all | solution.py:169
  74.3 34.6 %all-to-all-start.2 = ((f32[32,1,10240]{2,1,0:T(1,128)}), f32[32,1,10240]{2,1,0:T(1,128)S(1)}, u32[]{:S(2)}, u32[]{:S(2)}) async-start(f32[32,1,10240]{2,1,0:T(1,128)} %all_to_all.23), calls=%async_computation.2 | async-start | bytes 2621440 | tf_op jit(solution)/shard_map/all_to_all | solution.py:181
  109.8 1.5 %copy-start.3 = (pred[1024,512]{1,0:T(32,128)(4,1)S(1)}, pred[1024,512]{1,0:T(32,128)(4,1)}, u32[]{:S(2)}) copy-start(pred[1024,512]{1,0:T(32,128)(4,1)} %copy-done.2) | copy-start | bytes 1572868

commit v16 on v15

--- a/solution.py
+++ b/solution.py
@@ -72,7 +72,7 @@
 
 
 def boundary_forward(total, hidden, chooser, coupling):
-    picks = jnp.dot(chooser, hidden, precision=PRECISE, preferred_element_type=jnp.float32)
+    picks = exact_pick(chooser, hidden)
     contribs = []
     for round_index in range(ROUNDS):
         outgoing = picks[round_index * BLOCK : (round_index + 1) * BLOCK]
@@ -85,11 +85,11 @@
                 preferred_element_type=jnp.float32,
             )
         )
-    return total + spread(chooser, jnp.concatenate(contribs, axis=0))
+    return total + exact_pick(chooser, jnp.concatenate(contribs, axis=0), transposed=True)
 
 
 def boundary_backward(total, grad_agg, chooser, coupling):
-    picks = jnp.dot(chooser, grad_agg, precision=PRECISE, preferred_element_type=jnp.float32)
+    picks = exact_pick(chooser, grad_agg)
     arrived = []
     for round_index in range(ROUNDS):
         outgoing = picks[round_index * BLOCK : (round_index + 1) * BLOCK]
@@ -101,7 +101,7 @@
             preferred_element_type=jnp.float32,
         )
         arrived.append(swapped(carried, "col", round_index))
-    return total + spread(chooser, jnp.concatenate(arrived, axis=0))
+    return total + exact_pick(chooser, jnp.concatenate(arrived, axis=0), transposed=True)
 
 
 def exact_pick(chooser, values, transposed=False):

time: 114 us -> 116 us (1.018)
  blocking collectives: 0 us -> 35.5 us
  waiting for transfers between devices: 67.5 us -> 35.7 us
  starting transfers between devices: 16.8 us -> 14.1 us
  local copies, waits for them, and re-layouts: 6.84 us -> 4.74 us
  other arithmetic: 6.6 us -> 7.99 us
  matrix products: 15 us -> 16.2 us
    all_to_all x0 -> x1, blocking collectives: none -> 35.5 us  [on_device(): back = lax.all_to_all(payload, ('row', 'col'), 0, 0, tiled=True)]
    all_to_all x1 -> x0, waiting for transfers between devices: 30.9 us -> none  [on_device(): back = lax.all_to_all(payload, ('row', 'col'), 0, 0, tiled=True)]
    dot_general x4 -> x8, matrix products: 5.76 us -> 9.1 us  [exact_pick(): lax.dot_general(wide, parts, dims, preferred_element_type=jnp.float32)]
    all_to_all x1 -> x0, starting transfers between devices: 2.67 us -> none  [on_device(): back = lax.all_to_all(payload, ('row', 'col'), 0, 0, tiled=True)]
    dot_general x2 -> x0, matrix products: 1.45 us -> none  [the longest x1 0.74 us: boundary_backward(): jnp.dot(chooser, grad_agg, precision=PRECISE, preferred_element_type=jnp....]
    another operation x5 -> x10, other arithmetic: 3.14 us -> 4.52 us
    dot_general x3 -> x1, matrix products: 2.38 us -> 1.01 us  [spread(): lax.dot_general(chooser, values, (((0,), (0,)), ((), ())), precision=prec...]
    all_to_all x1, waiting for transfers between devices: 26.2 us -> 25 us  [on_device(): lax.all_to_all(jnp.concatenate([outbox, tags], axis=1), ('row', 'col'), 0...]
  transfers between devices with their start and end apart: 7 -> 6, of which waited for: 4 -> 3; matrix products, arithmetic and copies ran while one was open for 5% -> 5% of each run, Pallas kernels for 0% -> 0%
where the time goes in v16:
time: 116 us; the launch traced here: 115 us
  waiting for transfers between devices  35.7 us (31%)
  blocking collectives  35.5 us (31%)
  matrix products  16.2 us (14%)
  starting transfers between devices  14.1 us (12%)
  other arithmetic  7.99 us (7%)
  local copies, waits for them, and re-layouts  4.74 us (4%)
    all_to_all x1, blocking collectives, on_device(): back = lax.all_to_all(payload, ('row', 'col'), 0, 0, tiled=True)  35.5 us
    all_to_all x1, waiting for transfers between devices, on_device(): lax.all_to_all(jnp.concatenate([outbox, tags], axis=1), ('row', 'col'), 0...  25 us
    dot_general x8, matrix products, exact_pick(): lax.dot_general(wide, parts, dims, preferred_element_type=jnp.float32)  9.1 us
    all_to_all x1, waiting for transfers between devices, on_device(): lax.all_to_all(moment.reshape(devices, -1, feat_count), ('row', 'col'), 0...  7.79 us
    all_to_all x1, starting transfers between devices, on_device(): lax.all_to_all(jnp.concatenate([outbox, tags], axis=1), ('row', 'col'), 0...  7.48 us
    another operation x10, other arithmetic  4.52 us
    ppermute x4, starting transfers between devices, swapped(): lax.ppermute(array, axis, [(i, i ^ 1 << apart) for i in range(lax.axis_si...  3.35 us
    all_to_all x1, starting transfers between devices, on_device(): lax.all_to_all(moment.reshape(devices, -1, feat_count), ('row', 'col'), 0...  3.26 us
  transfers between devices with their start and end apart: 6, of which 3 were waited for; matrix products, arithmetic and copies ran while one was open for 5% of the time, Pallas kernels for 0%

profile of v16, /device:TPU:0, one launch (start us, length us, event | category | flops | bytes accessed | tf_op | source)
XLA Modules:
  0.0 115.3 jit_solution(7253903508873509449)
XLA Ops:
  0.6 0.6 compare_reduce_fusion
  1.3 0.7 add_select_fusion.1
  2.0 0.3 fusion.34
  2.3 0.4 iota_compare_fusion.1
  2.6 1.4 %reduce-precision_convert_fusion.11 = (bf16[512,256]{1,0:T(8,128)(2,1)S(1)}, bf16[512,256]{1,0:T(8,128)(2,1)S(1)}, bf16[512,256]{1,0:T(8,128)(2,1)S(1)}) fusion(f32[512,256]{1,0:T(8,128)} %param.12), kind=kLoop, calls=%fused_computation.108 | loop fusion | flops 917504 | bytes 1310720 | tf_op jit(solution)/shard_map/convert.27
  4.0 1.0 fusion
  5.0 0.2 reshape.176
  5.2 0.3 select_reduce_fusion
  5.5 0.7 convert_select_fusion
  6.2 0.1 reshape.177
  6.2 0.1 select_maximum_fusion
  6.3 1.7 %all_to_all.19 = f32[32,1,8320]{2,1,0:T(1,128)} reshape(f32[32,8320]{1,0:T(8,128)S(1)} %select_maximum_fusion) | data formatting | bytes 2129920 | tf_op jit(solution)/shard_map/all_to_all | solution.py:152
  8.0 7.5 %all-to-all-start = ((f32[32,1,8320]{2,1,0:T(1,128)}), f32[32,1,8320]{2,1,0:T(1,128)S(1)}, u32[]{:S(2)}, u32[]{:S(2)}) async-start(f32[32,1,8320]{2,1,0:T(1,128)} %all_to_all.19), calls=%async_computation | async-start | bytes 2129920 | tf_op jit(solution)/shard_map/all_to_all | solution.py:152
  15.6 0.1 slice_bitcast_fusion
  15.7 0.1 compare_bitcast_fusion
  15.8 0.2 select_convert_fusion
  15.9 1.0 fusion.67
  16.9 25.0 %all-to-all-done = f32[32,1,8320]{2,1,0:T(1,128)S(1)} async-done(((f32[32,1,8320]{2,1,0:T(1,128)}), f32[32,1,8320]{2,1,0:T(1,128)S(1)}, u32[]{:S(2)}, u32[]{:S(2)}) %all-to-all-start) | async-done | bytes 1064992 | tf_op jit(solution)/shard_map/all_to_all | solution.py:152
  41.9 0.1 copy.35
  42.0 0.1 slice.78
  42.1 0.2 reshape.178
  42.3 1.0 reduce-precision_convert_fusion.3
  43.3 0.1 eq.100
  43.4 0.3 iota_compare_fusion
  43.7 2.0 %reduce-precision_convert_fusion.9 = (bf16[512,256]{1,0:T(8,128)(2,1)S(1)}, bf16[512,256]{1,0:T(8,128)(2,1)S(1)}, bf16[512,256]{1,0:T(8,128)(2,1)S(1)}, f32[512,256]{1,0:T(8,128)S(1)}) fusion(bf16[1024,256]{1,0:T(8,128)(2,1)S(1)} %get-tuple-element.22, bf16[1024,256]{1,0:T(8,128)(2,1)} %get-tuple-element.23, bf16[1024,256]{1,0:T(8,128)(2,1)S(1)} %get-tuple-element.21, ...), kind=kOutput, calls=%fused_computation.104 | convolution fusion | flops 814088192 | bytes 3407872 | tf_op jit(solution)/shard_map/dot_general | solution.py:115
  45.7 0.4 fusion.46
  46.1 0.0 copy-start.1
  46.2 1.5 %collective-permute-start.1 = (f32[128,256]{1,0:T(8,128)S(1)}, f32[128,256]{1,0:T(8,128)S(1)}, u32[]{:S(2)}, u32[]{:S(2)}) collective-permute-start(f32[128,256]{1,0:T(8,128)S(1)} %get-tuple-element.44), channel_id=1, source_target_pairs={{0,2},{1,3},{2,0},{3,1},{4,6},{5,7},{6,4},{7,5},{8,10},{9,11},{10,... | collective-permute-start | bytes 393224 | tf_op jit(solution)/shard_map/ppermute | solution.py:18
  47.7 0.6 convolution_add_fusion
  48.3 2.9 %collective-permute-done.1 = f32[128,256]{1,0:T(8,128)S(1)} collective-permute-done((f32[128,256]{1,0:T(8,128)S(1)}, f32[128,256]{1,0:T(8,128)S(1)}, u32[]{:S(2)}, u32[]{:S(2)}) %collective-permute-start.1) | collective-permute-done | bytes 131104 | tf_op jit(solution)/shard_map/ppermute | solution.py:18
  51.2 0.2 convolution_bitcast_fusion.3
  51.4 0.2 convolution_bitcast_fusion.4
  51.6 0.1 reduce-precision_convert_fusion.15
  51.7 0.0 copy-start.5
  51.7 0.0 copy-start.7
  51.7 0.5 multiply_reduce_fusion.1
  52.2 0.4 copy-done.5
  52.6 1.3 %multiply_add_fusion = (f32[512,256]{1,0:T(8,128)}, f32[512,256]{1,0:T(8,128)S(1)}) fusion(f32[512,256]{1,0:T(8,128)S(1)} %get-tuple-element.49, f32[256,256]{1,0:T(8,128)S(1)} %copy-done.5, f32[512,256]{1,0:T(8,128)S(1)} %get-tuple-element.51, f32[256]{0:T(256)S(1)} %copy-done.7, f32[512]{0:T(512)S(1)} %add_rsqrt_fusion), kind=kOutput, calls=%fused_computation.119 | convolution fusion | flops 202244096 | bytes 2362368 | tf_op jit(solution)/shard_map/dot_general | solution.py:24
  53.9 0.6 multiply_reduce_fusion
  54.5 0.2 reduce-precision_convert_fusion.7
  54.7 0.1 reduce-precision_convert_fusion.6
  54.8 0.4 fusion.52
  55.2 0.3 convolution_bitcast_fusion.2
  55.5 0.3 convolution_bitcast_fusion.1
  55.8 1.0 convolution_add_fusion.3
  56.8 0.1 collective-permute-start.2
  56.9 1.8 %collective-permute-start.3 = (f32[128,256]{0,1:T(8,128)S(1)}, f32[128,256]{0,1:T(8,128)S(1)}, u32[]{:S(2)}, u32[]{:S(2)}) collective-permute-start(f32[128,256]{0,1:T(8,128)S(1)} %convolution_bitcast_fusion.1), channel_id=1, source_target_pairs={{0,2},{1,3},{2,0},{3,1},{4,6},{5,7},{6,4},{7,5},{8,10},{9,11},{10,... | collective-permute-start | bytes 393224 | tf_op jit(solution)/shard_map/ppermute | solution.py:18
  58.6 1.4 %convolution_bitcast_fusion = f32[32,8,256]{2,1,0:T(8,128)} fusion(f32[512,256]{1,0:T(8,128)S(1)} %get-tuple-element.51, f32[512]{0:T(512)S(1)} %add_rsqrt_fusion, f32[512,256]{1,0:T(8,128)S(1)} %copy-done, f32[512,256]{1,0:T(8,128)S(1)} %get-tuple-element.53), kind=kOutput, calls=%fused_computation.52 | convolution fusion | flops 202506240 | bytes 1837056 | tf_op jit(solution)/shard_map/dot_general | solution.py:34
  60.1 3.3 %all-to-all-start.1 = ((f32[32,8,256]{2,1,0:T(8,128)}), f32[32,8,256]{2,1,0:T(8,128)S(1)}, u32[]{:S(2)}, u32[]{:S(2)}) async-start(f32[32,8,256]{2,1,0:T(8,128)} %convolution_bitcast_fusion), calls=%async_computation.1 | async-start | bytes 524288 | tf_op jit(solution)/shard_map/all_to_all | solution.py:169
  63.4 0.1 reduce-precision_convert_fusion.13
  63.5 0.4 reduce-precision_convert_fusion.5
  63.9 1.8 %fusion.18 = f32[1024,256]{1,0:T(8,128)S(1)} fusion(pred[512,1024]{1,0:T(32,128)(4,1)S(1)} %iota_compare_fusion, bf16[512,256]{1,0:T(8,128)(2,1)S(1)} %get-tuple-element.25, bf16[512,256]{1,0:T(8,128)(2,1)S(1)} %get-tuple-element.26, bf16[512,256]{1,0:T(8,128)(2,1)S(1)} %get-tuple-element.24), kind=kOutput, calls=%fused_computation.18 | convolution fusion | flops 810811392 | bytes 2359296 | tf_op jit(solution)/shard_map/dot_general | solution.py:115
  65.7 0.2 reshape.180
  65.9 7.8 %all-to-all-done.1 = f32[32,8,256]{2,1,0:T(8,128)S(1)} async-done(((f32[32,8,256]{2,1,0:T(8,128)}), f32[32,8,256]{2,1,0:T(8,128)S(1)}, u32[]{:S(2)}, u32[]{:S(2)}) %all-to-all-start.1) | async-done | bytes 262176 | tf_op jit(solution)/shard_map/all_to_all | solution.py:169
  73.8 0.1 pad_maximum_fusion
  73.9 0.9 all_to_all.23
  74.8 35.5 %all_to_all.29 = f32[32,1,10240]{2,1,0:T(1,128)S(1)} all-to-all(f32[32,1,10240]{2,1,0:T(1,128)S(1)} %all_to_all.23), channel_id=1, replica_groups=mesh['row'=8,'col'=4] {'row','col'}, dimensions={0} | all-to-all | bytes 2621440 | tf_op jit(solution)/shard_map/all_to_all | solution.py:181
  110.2 0.4 copy.34
  110.7 0.1 slice.83
  110.8 0.2 reshape.182
  110.9 0.2 reduce-precision_convert_fusion.1
  111.2 0.9 multiply_reduce_fusion.2
  112.1 0.6 broadcast_multiply_fusion.1
  112.7 2.6 %fusion.12 = f32[512,256]{1,0:T(8,128)} fusion(pred[1024,512]{1,0:T(32,128)(4,1)S(1)} %copy-done.3, bf16[1024,256]{1,0:T(8,128)(2,1)S(1)} %get-tuple-element.19, bf16[1024,256]{1,0:T(8,128)(2,1)S(1)} %get-tuple-element.20, bf16[1024,256]{1,0:T(8,128)(2,1)S(1)} %get-tuple-element.18), kind=kOutput, calls=%fused_computation.12 | convolution fusion | flops 813170688 | bytes 2621440 | tf_op jit(solution)/shard_map/dot_general | solution.py:115
  (35 shorter events, 0.3 us)
Async XLA Ops:
  2.6 1.4 %copy-start.2 = (pred[1024,512]{1,0:T(32,128)(4,1)}, pred[1024,512]{1,0:T(32,128)(4,1)S(1)}, u32[]{:S(2)}) copy-start(pred[1024,512]{1,0:T(32,128)(4,1)S(1)} %iota_compare_fusion.1) | copy-start | bytes 1572868
  8.0 7.5 %copy-start.9 = (s32[1,3]{1,0:T(1,128)S(1)}, s32[1,3]{1,0:T(1,128)}, u32[]{:S(2)}) copy-start(s32[1,3]{1,0:T(1,128)} %param.18) | copy-start | bytes 40
  8.0 7.7 %copy-start.8 = (s32[1,8,2]{1,2,0:T(2,128)S(1)}, s32[1,8,2]{1,2,0:T(2,128)}, u32[]{:S(2)}) copy-start(s32[1,8,2]{1,2,0:T(2,128)} %param.17) | copy-start | bytes 196
  8.0 7.7 %copy-start.6 = (s32[1,2,128]{2,1,0:T(2,128)S(1)}, s32[1,2,128]{2,1,0:T(2,128)}, u32[]{:S(2)}) copy-start(s32[1,2,128]{2,1,0:T(2,128)} %param.19) | copy-start | bytes 3076
  8.0 7.9 %copy-start.4 = (f32[1,8,128,128]{3,2,1,0:T(8,128)S(1)}, f32[1,8,128,128]{3,2,1,0:T(8,128)}, u32[]{:S(2)}) copy-start(f32[1,8,128,128]{3,2,1,0:T(8,128)} %param.16) | copy-start | bytes 1572868
  8.0 33.9 %all-to-all-start = ((f32[32,1,8320]{2,1,0:T(1,128)}), f32[32,1,8320]{2,1,0:T(1,128)S(1)}, u32[]{:S(2)}, u32[]{:S(2)}) async-start(f32[32,1,8320]{2,1,0:T(1,128)} %all_to_all.19), calls=%async_computation | async-start | bytes 2129920 | tf_op jit(solution)/shard_map/all_to_all | solution.py:152
  46.1 5.1 %copy-start.1 = (f32[1,2,128,128]{3,2,1,0:T(8,128)S(1)}, f32[1,2,128,128]{3,2,1,0:T(8,128)}, u32[]{:S(2)}) copy-start(f32[1,2,128,128]{3,2,1,0:T(8,128)} %param.20) | copy-start | bytes 393220
  46.2 5.0 %collective-permute-start.1 = (f32[128,256]{1,0:T(8,128)S(1)}, f32[128,256]{1,0:T(8,128)S(1)}, u32[]{:S(2)}, u32[]{:S(2)}) collective-permute-start(f32[128,256]{1,0:T(8,128)S(1)} %get-tuple-element.44), channel_id=1, source_target_pairs={{0,2},{1,3},{2,0},{3,1},{4,6},{5,7},{6,4},{7,5},{8,10},{9,11},{10,... | collective-permute-start | bytes 393224 | tf_op jit(solution)/shard_map/ppermute | solution.py:18
  47.7 3.7 %collective-permute-start = (f32[128,256]{1,0:T(8,128)S(1)}, f32[128,256]{1,0:T(8,128)S(1)}, u32[]{:S(2)}, u32[]{:S(2)}) collective-permute-start(f32[128,256]{1,0:T(8,128)S(1)} %get-tuple-element.43), channel_id=1, source_target_pairs={{0,1},{1,0},{2,3},{3,2},{4,5},{5,4},{6,7},{7,6},{8,9},{9,8},{10,11... | collective-permute-start | bytes 393224 | tf_op jit(solution)/shard_map/ppermute | solution.py:18
  51.7 1.0 copy-start.5
  51.7 0.9 copy-start.7
  52.6 1.3 %copy-start = (f32[512,256]{1,0:T(8,128)S(1)}, f32[512,256]{1,0:T(8,128)}, u32[]{:S(2)}) copy-start(f32[512,256]{1,0:T(8,128)} %param.21) | copy-start | bytes 1572868
  56.8 6.5 %collective-permute-start.2 = (f32[128,256]{0,1:T(8,128)S(1)}, f32[128,256]{0,1:T(8,128)S(1)}, u32[]{:S(2)}, u32[]{:S(2)}) collective-permute-start(f32[128,256]{0,1:T(8,128)S(1)} %convolution_bitcast_fusion.2), channel_id=1, source_target_pairs={{0,1},{1,0},{2,3},{3,2},{4,5},{5,4},{6,7},{7,6},{8,9},{9,8},{10,11... | collective-permute-start | bytes 393224 | tf_op jit(solution)/shard_map/ppermute | solution.py:18
  56.9 6.5 %collective-permute-start.3 = (f32[128,256]{0,1:T(8,128)S(1)}, f32[128,256]{0,1:T(8,128)S(1)}, u32[]{:S(2)}, u32[]{:S(2)}) collective-permute-start(f32[128,256]{0,1:T(8,128)S(1)} %convolution_bitcast_fusion.1), channel_id=1, source_target_pairs={{0,2},{1,3},{2,0},{3,1},{4,6},{5,7},{6,4},{7,5},{8,10},{9,11},{10,... | collective-permute-start | bytes 393224 | tf_op jit(solution)/shard_map/ppermute | solution.py:18
  60.1 13.6 %all-to-all-start.1 = ((f32[32,8,256]{2,1,0:T(8,128)}), f32[32,8,256]{2,1,0:T(8,128)S(1)}, u32[]{:S(2)}, u32[]{:S(2)}) async-start(f32[32,8,256]{2,1,0:T(8,128)} %convolution_bitcast_fusion), calls=%async_computation.1 | async-start | bytes 524288 | tf_op jit(solution)/shard_map/all_to_all | solution.py:169
  111.2 1.5 %copy-start.3 = (pred[1024,512]{1,0:T(32,128)(4,1)S(1)}, pred[1024,512]{1,0:T(32,128)(4,1)}, u32[]{:S(2)}) copy-start(pred[1024,512]{1,0:T(32,128)(4,1)} %copy-done.2) | copy-start | bytes 1572868

commit v17 on v15

--- a/solution.py
+++ b/solution.py
@@ -71,8 +71,10 @@
     )
 
 
-def boundary_forward(total, hidden, chooser, coupling):
-    picks = jnp.dot(chooser, hidden, precision=PRECISE, preferred_element_type=jnp.float32)
+def boundary_forward(total, source, source_chooser, chooser, coupling):
+    picks = jnp.dot(
+        source_chooser, source, precision=PRECISE, preferred_element_type=jnp.float32
+    )
     contribs = []
     for round_index in range(ROUNDS):
         outgoing = picks[round_index * BLOCK : (round_index + 1) * BLOCK]
@@ -162,7 +164,11 @@
     aggregate = hidden + jnp.dot(
         tiles, hidden, precision=DENSE, preferred_element_type=jnp.float32
     )
-    aggregate = boundary_forward(aggregate, hidden, chooser, coupling)
+    arrival = jnp.sum(jnp.where(landing, slots[None, :], 0), axis=1)
+    slot_of = jnp.sum(jnp.where(chooser > 0, arrival[None, :], 0), axis=1)
+    live = jnp.sum(chooser, axis=1) > 0
+    far = jnp.where((slot_of[:, None] == slots[None, :]) & live[:, None], 1.0, 0.0)
+    aggregate = boundary_forward(aggregate, inbox, far, chooser, coupling)
     activation, grad_agg, moment = layer_both(aggregate, weight, norm_gain, cotangent)
     output = hidden + activation
     node_scale = 1.0 / math.sqrt(row_count * devices)

time: 114 us -> 115 us (level)
  waiting for transfers between devices: 67.5 us -> 65.3 us
  other arithmetic: 6.6 us -> 8.22 us
  local copies, waits for them, and re-layouts: 6.84 us -> 8.04 us
    all_to_all x1, waiting for transfers between devices: 26.2 us -> 23.9 us  [on_device(): lax.all_to_all(jnp.concatenate([outbox, tags], axis=1), ('row', 'col'), 0...]
    unnamed x29 -> x31, local copies, waits for them, and re-layouts: 1.99 us -> 3.21 us
  transfers between devices with their start and end apart: 7 -> 7, of which waited for: 4 -> 4; matrix products, arithmetic and copies ran while one was open for 5% -> 7% of each run, Pallas kernels for 0% -> 0%
where the time goes in v17:
time: 115 us
  waiting for transfers between devices  65.3 us (57%)
  starting transfers between devices  16.8 us (15%)
  matrix products  15.5 us (13%)
  other arithmetic  8.22 us (7%)
  local copies, waits for them, and re-layouts  8.04 us (7%)
    all_to_all x1, waiting for transfers between devices, on_device(): back = lax.all_to_all(payload, ('row', 'col'), 0, 0, tiled=True)  30.9 us
    all_to_all x1, waiting for transfers between devices, on_device(): lax.all_to_all(jnp.concatenate([outbox, tags], axis=1), ('row', 'col'), 0...  23.9 us
    all_to_all x1, waiting for transfers between devices, on_device(): lax.all_to_all(moment.reshape(devices, -1, feat_count), ('row', 'col'), 0...  8.21 us
    all_to_all x1, starting transfers between devices, on_device(): lax.all_to_all(jnp.concatenate([outbox, tags], axis=1), ('row', 'col'), 0...  7.48 us
    dot_general x4, matrix products, exact_pick(): lax.dot_general(wide, parts, dims, preferred_element_type=jnp.float32)  5.76 us
    ppermute x4, starting transfers between devices, swapped(): lax.ppermute(array, axis, [(i, i ^ 1 << apart) for i in range(lax.axis_si...  3.36 us
    all_to_all x1, starting transfers between devices, on_device(): lax.all_to_all(moment.reshape(devices, -1, feat_count), ('row', 'col'), 0...  3.26 us
    unnamed x31, local copies, waits for them, and re-layouts  3.21 us
  transfers between devices with their start and end apart: 7, of which 4 were waited for; matrix products, arithmetic and copies ran while one was open for 7% of the time, Pallas kernels for 0%

profile of v17, /device:TPU:0, one launch (start us, length us, event | category | flops | bytes accessed | tf_op | source)
XLA Modules:
  0.0 115.0 jit_solution(7222612519207811456)
XLA Ops:
  0.6 0.6 compare_reduce_fusion
  1.3 0.7 add_select_fusion.1
  2.0 0.3 fusion.35
  2.3 0.4 iota_compare_fusion.1
  2.6 1.4 %reduce-precision_convert_fusion.7 = (bf16[512,256]{1,0:T(8,128)(2,1)S(1)}, bf16[512,256]{1,0:T(8,128)(2,1)S(1)}, bf16[512,256]{1,0:T(8,128)(2,1)S(1)}) fusion(f32[512,256]{1,0:T(8,128)} %param.12), kind=kLoop, calls=%fused_computation.94 | loop fusion | flops 917504 | bytes 1310720 | tf_op jit(solution)/shard_map/convert.9
  4.0 1.0 fusion
  5.0 0.2 reshape.181
  5.2 0.3 select_reduce_fusion.1
  5.5 0.7 convert_select_fusion
  6.2 0.1 reshape.182
  6.2 0.1 select_maximum_fusion
  6.3 1.7 %all_to_all.19 = f32[32,1,8320]{2,1,0:T(1,128)} reshape(f32[32,8320]{1,0:T(8,128)S(1)} %select_maximum_fusion) | data formatting | bytes 2129920 | tf_op jit(solution)/shard_map/all_to_all | solution.py:154
  8.0 7.5 %all-to-all-start = ((f32[32,1,8320]{2,1,0:T(1,128)}), f32[32,1,8320]{2,1,0:T(1,128)S(1)}, u32[]{:S(2)}, u32[]{:S(2)}) async-start(f32[32,1,8320]{2,1,0:T(1,128)} %all_to_all.19), calls=%async_computation | async-start | bytes 2129920 | tf_op jit(solution)/shard_map/all_to_all | solution.py:154
  15.5 1.0 copy.37
  16.6 0.1 slice_bitcast_fusion
  16.7 0.1 compare_bitcast_fusion
  16.7 0.2 select_reduce_fusion.2
  17.0 1.0 fusion.58
  18.0 23.9 %all-to-all-done = f32[32,1,8320]{2,1,0:T(1,128)S(1)} async-done(((f32[32,1,8320]{2,1,0:T(1,128)}), f32[32,1,8320]{2,1,0:T(1,128)S(1)}, u32[]{:S(2)}, u32[]{:S(2)}) %all-to-all-start) | async-done | bytes 1064992 | tf_op jit(solution)/shard_map/all_to_all | solution.py:154
  41.9 0.1 copy.68
  42.0 0.1 slice.78
  42.1 0.1 eq.113
  42.2 0.3 select_reduce_fusion
  42.5 1.1 iota_compare_fusion
  43.6 0.3 select_reduce_fusion.3
  43.9 0.2 reshape.183
  44.0 0.2 reduce-precision_convert_fusion.3
  44.3 0.0 copy-start.5
  44.3 1.3 %fusion.40 = f32[256,256]{1,0:T(8,128)S(1)} fusion(f32[1024,256]{1,0:T(8,128)S(1)} %reshape.183, s32[256]{0:T(256)S(1)} %select_reduce_fusion.3, pred[256]{0:T(512)(128)(4,1)S(1)} %broadcast_compare_fusion.1), kind=kOutput, calls=%fused_computation.70 | convolution fusion | flops 806092800 | bytes 1312000 | tf_op jit(solution)/shard_map/dot_general | solution.py:75
  45.6 1.5 %collective-permute-start.1 = (f32[128,256]{1,0:T(8,128)S(1)}, f32[128,256]{1,0:T(8,128)S(1)}, u32[]{:S(2)}, u32[]{:S(2)}) collective-permute-start(f32[128,256]{1,0:T(8,128)S(1)} %get-tuple-element.43), channel_id=1, source_target_pairs={{0,2},{1,3},{2,0},{3,1},{4,6},{5,7},{6,4},{7,5},{8,10},{9,11},{10,... | collective-permute-start | bytes 393224 | tf_op jit(solution)/shard_map/ppermute | solution.py:18
  47.1 1.2 %fusion.6 = f32[512,256]{0,1:T(8,128)S(1)} fusion(pred[512,1024]{1,0:T(32,128)(4,1)S(1)} %copy-done.5, bf16[1024,256]{1,0:T(8,128)(2,1)S(1)} %get-tuple-element.32, bf16[1024,256]{1,0:T(8,128)(2,1)S(1)} %get-tuple-element.33, bf16[1024,256]{1,0:T(8,128)(2,1)S(1)} %get-tuple-element.31), kind=kOutput, calls=%fused_computation.6 | convolution fusion | flops 813170688 | bytes 2621440 | tf_op jit(solution)/shard_map/dot_general | solution.py:117
  48.3 2.3 %collective-permute-done.1 = f32[128,256]{1,0:T(8,128)S(1)} collective-permute-done((f32[128,256]{1,0:T(8,128)S(1)}, f32[128,256]{1,0:T(8,128)S(1)}, u32[]{:S(2)}, u32[]{:S(2)}) %collective-permute-start.1) | collective-permute-done | bytes 131104 | tf_op jit(solution)/shard_map/ppermute | solution.py:18
  50.6 0.2 convolution_bitcast_fusion.3
  50.8 0.2 convolution_bitcast_fusion.4
  51.0 0.9 fusion.33
  51.9 0.7 multiply_reduce_fusion.1
  52.6 0.3 copy-done.8
  52.9 0.6 multiply_add_fusion
  53.5 0.4 copy-done
  53.9 0.6 multiply_reduce_fusion
  54.5 0.7 fusion.31
  55.3 0.3 convolution_bitcast_fusion.2
  55.6 0.3 convolution_bitcast_fusion.1
  55.9 0.6 convolution_add_fusion.1
  56.5 0.1 collective-permute-start.2
  56.6 1.8 %collective-permute-start.3 = (f32[128,256]{0,1:T(8,128)S(1)}, f32[128,256]{0,1:T(8,128)S(1)}, u32[]{:S(2)}, u32[]{:S(2)}) collective-permute-start(f32[128,256]{0,1:T(8,128)S(1)} %convolution_bitcast_fusion.1), channel_id=1, source_target_pairs={{0,2},{1,3},{2,0},{3,1},{4,6},{5,7},{6,4},{7,5},{8,10},{9,11},{10,... | collective-permute-start | bytes 393224 | tf_op jit(solution)/shard_map/ppermute | solution.py:18
  58.4 1.3 %convolution_bitcast_fusion = f32[32,8,256]{2,1,0:T(8,128)} fusion(f32[512,256]{0,1:T(8,128)S(1)} %get-tuple-element.49, f32[512]{0:T(512)S(1)} %add_rsqrt_fusion, f32[512,256]{0,1:T(8,128)S(1)} %copy-done, f32[512,256]{0,1:T(8,128)S(1)} %get-tuple-element.51), kind=kOutput, calls=%fused_computation.56 | convolution fusion | flops 202506240 | bytes 1837056 | tf_op jit(solution)/shard_map/dot_general | solution.py:34
  59.6 3.3 %all-to-all-start.1 = ((f32[32,8,256]{2,1,0:T(8,128)}), f32[32,8,256]{2,1,0:T(8,128)S(1)}, u32[]{:S(2)}, u32[]{:S(2)}) async-start(f32[32,8,256]{2,1,0:T(8,128)} %convolution_bitcast_fusion), calls=%async_computation.1 | async-start | bytes 524288 | tf_op jit(solution)/shard_map/all_to_all | solution.py:175
  62.9 0.9 reduce-precision_convert_fusion.5
  63.8 1.0 fusion.18
  64.9 0.2 reshape.185
  65.1 8.2 %all-to-all-done.1 = f32[32,8,256]{2,1,0:T(8,128)S(1)} async-done(((f32[32,8,256]{2,1,0:T(8,128)}), f32[32,8,256]{2,1,0:T(8,128)S(1)}, u32[]{:S(2)}, u32[]{:S(2)}) %all-to-all-start.1) | async-done | bytes 262176 | tf_op jit(solution)/shard_map/all_to_all | solution.py:175
  73.3 0.1 pad_maximum_fusion
  73.4 2.0 %all_to_all.23 = f32[32,1,10240]{2,1,0:T(1,128)} reshape(f32[32,10240]{1,0:T(8,128)S(1)} %pad_maximum_fusion) | data formatting | bytes 2621440 | tf_op jit(solution)/shard_map/all_to_all | solution.py:187
  75.4 2.7 %all-to-all-start.2 = ((f32[32,1,10240]{2,1,0:T(1,128)}), f32[32,1,10240]{2,1,0:T(1,128)S(1)}, u32[]{:S(2)}, u32[]{:S(2)}) async-start(f32[32,1,10240]{2,1,0:T(1,128)} %all_to_all.23), calls=%async_computation.2 | async-start | bytes 2621440 | tf_op jit(solution)/shard_map/all_to_all | solution.py:187
  78.1 1.0 copy.40
  79.1 30.9 %all-to-all-done.2 = f32[32,1,10240]{2,1,0:T(1,128)S(1)} async-done(((f32[32,1,10240]{2,1,0:T(1,128)}), f32[32,1,10240]{2,1,0:T(1,128)S(1)}, u32[]{:S(2)}, u32[]{:S(2)}) %all-to-all-start.2) | async-done | bytes 1310752 | tf_op jit(solution)/shard_map/all_to_all | solution.py:187
  110.0 0.4 copy.67
  110.4 0.1 slice.83
  110.5 0.2 reshape.187
  110.6 0.2 reduce-precision_convert_fusion.1
  111.0 0.9 multiply_reduce_fusion.2
  111.8 0.6 broadcast_multiply_fusion.1
  112.4 2.6 %fusion.12 = f32[512,256]{1,0:T(8,128)} fusion(pred[1024,512]{1,0:T(32,128)(4,1)S(1)} %copy-done.4, bf16[1024,256]{1,0:T(8,128)(2,1)S(1)} %get-tuple-element.29, bf16[1024,256]{1,0:T(8,128)(2,1)S(1)} %get-tuple-element.30, bf16[1024,256]{1,0:T(8,128)(2,1)S(1)} %get-tuple-element.28), kind=kOutput, calls=%fused_computation.12 | convolution fusion | flops 813170688 | bytes 2621440 | tf_op jit(solution)/shard_map/dot_general | solution.py:117
  (41 shorter events, 0.3 us)
Async XLA Ops:
  2.6 1.4 %copy-start.3 = (pred[1024,512]{1,0:T(32,128)(4,1)}, pred[1024,512]{1,0:T(32,128)(4,1)S(1)}, u32[]{:S(2)}) copy-start(pred[1024,512]{1,0:T(32,128)(4,1)S(1)} %iota_compare_fusion.1) | copy-start | bytes 1572868
  8.0 7.5 %copy-start.2 = (f32[512,256]{1,0:T(8,128)S(1)}, f32[512,256]{1,0:T(8,128)}, u32[]{:S(2)}) copy-start(f32[512,256]{1,0:T(8,128)} %param.21) | copy-start | bytes 1572868
  8.0 8.5 %copy-start.12 = (s32[1,3]{1,0:T(1,128)S(1)}, s32[1,3]{1,0:T(1,128)}, u32[]{:S(2)}) copy-start(s32[1,3]{1,0:T(1,128)} %param.18) | copy-start | bytes 40
  8.0 8.7 %copy-start.9 = (s32[1,2,128]{2,1,0:T(2,128)S(1)}, s32[1,2,128]{2,1,0:T(2,128)}, u32[]{:S(2)}) copy-start(s32[1,2,128]{2,1,0:T(2,128)} %param.19) | copy-start | bytes 3076
  8.0 9.0 %copy-start.11 = (s32[1,8,2]{1,2,0:T(2,128)S(1)}, s32[1,8,2]{1,2,0:T(2,128)}, u32[]{:S(2)}) copy-start(s32[1,8,2]{1,2,0:T(2,128)} %param.17) | copy-start | bytes 196
  8.0 9.0 %copy-start.7 = (f32[1,8,128,128]{3,2,1,0:T(8,128)S(1)}, f32[1,8,128,128]{3,2,1,0:T(8,128)}, u32[]{:S(2)}) copy-start(f32[1,8,128,128]{3,2,1,0:T(8,128)} %param.16) | copy-start | bytes 1572868
  8.0 33.9 %all-to-all-start = ((f32[32,1,8320]{2,1,0:T(1,128)}), f32[32,1,8320]{2,1,0:T(1,128)S(1)}, u32[]{:S(2)}, u32[]{:S(2)}) async-start(f32[32,1,8320]{2,1,0:T(1,128)} %all_to_all.19), calls=%async_computation | async-start | bytes 2129920 | tf_op jit(solution)/shard_map/all_to_all | solution.py:154
  44.3 2.8 %copy-start.5 = (pred[512,1024]{1,0:T(32,128)(4,1)S(1)}, pred[512,1024]{1,0:T(32,128)(4,1)}, u32[]{:S(2)}) copy-start(pred[512,1024]{1,0:T(32,128)(4,1)} %iota_compare_fusion) | copy-start | bytes 1572868
  45.6 5.0 %collective-permute-start.1 = (f32[128,256]{1,0:T(8,128)S(1)}, f32[128,256]{1,0:T(8,128)S(1)}, u32[]{:S(2)}, u32[]{:S(2)}) collective-permute-start(f32[128,256]{1,0:T(8,128)S(1)} %get-tuple-element.43), channel_id=1, source_target_pairs={{0,2},{1,3},{2,0},{3,1},{4,6},{5,7},{6,4},{7,5},{8,10},{9,11},{10,... | collective-permute-start | bytes 393224 | tf_op jit(solution)/shard_map/ppermute | solution.py:18
  47.1 3.7 %collective-permute-start = (f32[128,256]{1,0:T(8,128)S(1)}, f32[128,256]{1,0:T(8,128)S(1)}, u32[]{:S(2)}, u32[]{:S(2)}) collective-permute-start(f32[128,256]{1,0:T(8,128)S(1)} %get-tuple-element.42), channel_id=1, source_target_pairs={{0,1},{1,0},{2,3},{3,2},{4,5},{5,4},{6,7},{7,6},{8,9},{9,8},{10,11... | collective-permute-start | bytes 393224 | tf_op jit(solution)/shard_map/ppermute | solution.py:18
  47.1 3.5 %copy-start.1 = (f32[1,2,128,128]{3,2,1,0:T(8,128)S(1)}, f32[1,2,128,128]{3,2,1,0:T(8,128)}, u32[]{:S(2)}) copy-start(f32[1,2,128,128]{3,2,1,0:T(8,128)} %param.20) | copy-start | bytes 393220
  51.9 1.0 copy-start.8
  51.9 0.9 copy-start.10
  52.9 1.0 copy-start
  56.5 6.4 %collective-permute-start.2 = (f32[128,256]{0,1:T(8,128)S(1)}, f32[128,256]{0,1:T(8,128)S(1)}, u32[]{:S(2)}, u32[]{:S(2)}) collective-permute-start(f32[128,256]{0,1:T(8,128)S(1)} %convolution_bitcast_fusion.2), channel_id=1, source_target_pairs={{0,1},{1,0},{2,3},{3,2},{4,5},{5,4},{6,7},{7,6},{8,9},{9,8},{10,11... | collective-permute-start | bytes 393224 | tf_op jit(solution)/shard_map/ppermute | solution.py:18
  56.6 6.3 %collective-permute-start.3 = (f32[128,256]{0,1:T(8,128)S(1)}, f32[128,256]{0,1:T(8,128)S(1)}, u32[]{:S(2)}, u32[]{:S(2)}) collective-permute-start(f32[128,256]{0,1:T(8,128)S(1)} %convolution_bitcast_fusion.1), channel_id=1, source_target_pairs={{0,2},{1,3},{2,0},{3,1},{4,6},{5,7},{6,4},{7,5},{8,10},{9,11},{10,... | collective-permute-start | bytes 393224 | tf_op jit(solution)/shard_map/ppermute | solution.py:18
  59.6 4.2 %copy-start.6 = (pred[512,1024]{1,0:T(32,128)(4,1)S(1)}, pred[512,1024]{1,0:T(32,128)(4,1)}, u32[]{:S(2)}) copy-start(pred[512,1024]{1,0:T(32,128)(4,1)} %iota_compare_fusion) | copy-start | bytes 1572868
  59.6 13.6 %all-to-all-start.1 = ((f32[32,8,256]{2,1,0:T(8,128)}), f32[32,8,256]{2,1,0:T(8,128)S(1)}, u32[]{:S(2)}, u32[]{:S(2)}) async-start(f32[32,8,256]{2,1,0:T(8,128)} %convolution_bitcast_fusion), calls=%async_computation.1 | async-start | bytes 524288 | tf_op jit(solution)/shard_map/all_to_all | solution.py:175
  75.4 34.6 %all-to-all-start.2 = ((f32[32,1,10240]{2,1,0:T(1,128)}), f32[32,1,10240]{2,1,0:T(1,128)S(1)}, u32[]{:S(2)}, u32[]{:S(2)}) async-start(f32[32,1,10240]{2,1,0:T(1,128)} %all_to_all.23), calls=%async_computation.2 | async-start | bytes 2621440 | tf_op jit(solution)/shard_map/all_to_all | solution.py:187
  110.9 1.5 %copy-start.4 = (pred[1024,512]{1,0:T(32,128)(4,1)S(1)}, pred[1024,512]{1,0:T(32,128)(4,1)}, u32[]{:S(2)}) copy-start(pred[1024,512]{1,0:T(32,128)(4,1)} %copy-done.3) | copy-start | bytes 1572868

commit v18 on v15

--- a/solution.py
+++ b/solution.py
@@ -146,8 +146,8 @@
     places = jnp.where(tag > 0, tag - 1, row_count)
     outbox = exact_pick(chosen, x_scan).reshape(devices, capacity * feat_count)
     lanes = 128 * (-(-capacity // 128))
-    tags = jnp.zeros((devices, lanes), jnp.float32).at[:, :capacity].set(
-        places.reshape(devices, capacity).astype(jnp.float32)
+    tags = jnp.pad(
+        places.reshape(devices, capacity).astype(jnp.float32), ((0, 0), (0, lanes - capacity))
     )
     got = lax.all_to_all(
         jnp.concatenate([outbox, tags], axis=1), ("row", "col"), 0, 0, tiled=True
@@ -169,7 +169,14 @@
     gathered = lax.all_to_all(
         moment.reshape(devices, -1, feat_count), ("row", "col"), 0, 0, tiled=True
     )
-    share = jnp.sum(gathered, axis=0).reshape(1, -1)
+    chunk = jnp.sum(gathered, axis=0)
+    band = chunk.shape[0]
+    first = lax.axis_index(("row", "col")) * band
+    gains = lax.dynamic_slice_in_dim(norm_gain, first, band)
+    weights = lax.dynamic_slice_in_dim(weight, first, band, axis=0)
+    weight_part = (chunk * gains[:, None] * node_scale).reshape(1, -1)
+    gain_part = (jnp.sum(chunk * weights, axis=1) * node_scale).reshape(1, -1)
+    share = jnp.concatenate([weight_part, gain_part], axis=1)
     grad_nodes = cotangent + grad_agg + spread(tiles, grad_agg, DENSE)
     grad_nodes = boundary_backward(grad_nodes, grad_agg, chooser, coupling)
     reply = exact_pick(landing, grad_nodes, transposed=True)
@@ -180,9 +187,9 @@
     )
     back = lax.all_to_all(payload, ("row", "col"), 0, 0, tiled=True)
     returned = back[:, :flat].reshape(devices * capacity, feat_count)
-    moment_sum = back[:, flat:].reshape(feat_count, feat_count)
-    weight_sum = moment_sum * norm_gain[:, None] * node_scale
-    gain_sum = jnp.sum(moment_sum * weight, axis=1) * node_scale
+    width = band * feat_count
+    weight_sum = back[:, flat : flat + width].reshape(feat_count, feat_count)
+    gain_sum = back[:, flat + width :].reshape(feat_count)
     x_grad = exact_pick(chosen, returned, transposed=True)
     return (output, x_grad, weight_sum, gain_sum)
 

time: 114 us -> 118 us (1.035)
  waiting for transfers between devices: 67.5 us -> 69.8 us
  other arithmetic: 6.6 us -> 4.62 us
  local copies, waits for them, and re-layouts: 6.84 us -> 8.59 us
  matrix products: 15 us -> 16.7 us
    ppermute x4, waiting for transfers between devices: 2.22 us -> 4.33 us  [swapped(): lax.ppermute(array, axis, [(i, i ^ 1 << apart) for i in range(lax.axis_si...]
    another operation x5 -> x3, other arithmetic: 3.14 us -> 1.66 us
    reshape x1 -> x2, local copies, waits for them, and re-layouts: 0.05 us -> 1.4 us  [the longest x1 0.75 us: on_device(): weight_sum = back[:, flat:flat + width].reshape(feat_count, feat_count)]
  transfers between devices with their start and end apart: 7 -> 7, of which waited for: 4 -> 5; matrix products, arithmetic and copies ran while one was open for 5% -> 5% of each run, Pallas kernels for 0% -> 0%
where the time goes in v18:
time: 118 us; the launch traced here: 117 us
  waiting for transfers between devices  69.8 us (59%)
  matrix products  16.7 us (14%)
  starting transfers between devices  16.3 us (14%)
  local copies, waits for them, and re-layouts  8.59 us (7%)
  other arithmetic  4.62 us (4%)
    all_to_all x1, waiting for transfers between devices, on_device(): back = lax.all_to_all(payload, ('row', 'col'), 0, 0, tiled=True)  31.2 us
    all_to_all x1, waiting for transfers between devices, on_device(): lax.all_to_all(jnp.concatenate([outbox, tags], axis=1), ('row', 'col'), 0...  26.2 us
    all_to_all x1, waiting for transfers between devices, on_device(): lax.all_to_all(moment.reshape(devices, -1, feat_count), ('row', 'col'), 0...  8.09 us
    all_to_all x1, starting transfers between devices, on_device(): lax.all_to_all(jnp.concatenate([outbox, tags], axis=1), ('row', 'col'), 0...  7.47 us
    dot_general x4, matrix products, exact_pick(): lax.dot_general(wide, parts, dims, preferred_element_type=jnp.float32)  5.8 us
    ppermute x4, waiting for transfers between devices, swapped(): lax.ppermute(array, axis, [(i, i ^ 1 << apart) for i in range(lax.axis_si...  4.33 us
    dot_general x3, matrix products, spread(): lax.dot_general(chooser, values, (((0,), (0,)), ((), ())), precision=prec...  3.23 us
    ppermute x4, starting transfers between devices, swapped(): lax.ppermute(array, axis, [(i, i ^ 1 << apart) for i in range(lax.axis_si...  3.08 us
  transfers between devices with their start and end apart: 7, of which 5 were waited for; matrix products, arithmetic and copies ran while one was open for 5% of the time, Pallas kernels for 0%

profile of v18, /device:TPU:0, one launch (start us, length us, event | category | flops | bytes accessed | tf_op | source)
XLA Modules:
  0.0 117.2 jit_solution(8734378724547498452)
XLA Ops:
  0.6 0.7 add_select_fusion.1
  1.3 0.3 fusion.30
  1.6 0.4 iota_compare_fusion.1
  2.0 0.3 select_reduce_fusion
  2.3 0.1 convert_element_type.13
  2.4 1.2 reduce-precision_convert_fusion.7
  3.5 1.0 fusion
  4.5 0.2 reshape.182
  4.7 0.1 select_maximum_fusion
  4.8 1.7 %all_to_all.19 = f32[32,1,8320]{2,1,0:T(1,128)} reshape(f32[32,8320]{1,0:T(8,128)S(1)} %select_maximum_fusion) | data formatting | bytes 2129920 | tf_op jit(solution)/shard_map/all_to_all | solution.py:152
  6.6 7.5 %all-to-all-start = ((f32[32,1,8320]{2,1,0:T(1,128)}), f32[32,1,8320]{2,1,0:T(1,128)S(1)}, u32[]{:S(2)}, u32[]{:S(2)}) async-start(f32[32,1,8320]{2,1,0:T(1,128)} %all_to_all.19), calls=%async_computation | async-start | bytes 2129920 | tf_op jit(solution)/shard_map/all_to_all | solution.py:152
  14.1 0.1 slice_bitcast_fusion
  14.2 0.1 compare_bitcast_fusion
  14.2 26.2 %all-to-all-done = f32[32,1,8320]{2,1,0:T(1,128)S(1)} async-done(((f32[32,1,8320]{2,1,0:T(1,128)}), f32[32,1,8320]{2,1,0:T(1,128)S(1)}, u32[]{:S(2)}, u32[]{:S(2)}) %all-to-all-start) | async-done | bytes 1064992 | tf_op jit(solution)/shard_map/all_to_all | solution.py:152
  40.4 0.1 copy.77
  40.5 0.1 slice.66
  40.6 0.1 eq.100
  40.7 0.2 reshape.183
  40.8 0.3 iota_compare_fusion
  41.2 0.0 copy-start.2
  41.2 0.2 reduce-precision_convert_fusion.3
  41.4 0.0 copy-start.7
  41.4 1.2 fusion.6
  42.6 0.0 copy-start.5
  42.6 0.7 fusion.40
  43.3 0.7 fusion.128
  44.0 1.0 fusion.56
  45.0 0.2 copy.46
  45.3 0.1 dynamic_slice.6
  45.3 1.5 %collective-permute-start.1 = (f32[128,256]{1,0:T(8,128)S(1)}, f32[128,256]{1,0:T(8,128)S(1)}, u32[]{:S(2)}, u32[]{:S(2)}) collective-permute-start(f32[128,256]{1,0:T(8,128)S(1)} %get-tuple-element.33), channel_id=1, source_target_pairs={{0,2},{1,3},{2,0},{3,1},{4,6},{5,7},{6,4},{7,5},{8,10},{9,11},{10,... | collective-permute-start | bytes 393224 | tf_op jit(solution)/shard_map/ppermute | solution.py:18
  46.8 0.2 convolution_bitcast_fusion.4
  47.0 4.2 %collective-permute-done.1 = f32[128,256]{1,0:T(8,128)S(1)} collective-permute-done((f32[128,256]{1,0:T(8,128)S(1)}, f32[128,256]{1,0:T(8,128)S(1)}, u32[]{:S(2)}, u32[]{:S(2)}) %collective-permute-start.1) | collective-permute-done | bytes 131104 | tf_op jit(solution)/shard_map/ppermute | solution.py:18
  51.2 0.2 convolution_bitcast_fusion.3
  51.5 0.9 fusion.38
  52.3 0.7 multiply_reduce_fusion.1
  53.0 0.2 copy-done.9
  53.3 1.4 %multiply_add_fusion = (f32[512,256]{0,1:T(8,128)}, f32[512,256]{0,1:T(8,128)S(1)}) fusion(f32[512,256]{0,1:T(8,128)S(1)} %fusion.6, f32[256,256]{1,0:T(8,128)S(1)} %copy-done.9, f32[512,256]{0,1:T(8,128)S(1)} %get-tuple-element.41, f32[256]{0:T(256)S(1)} %copy-done.10, f32[512]{0:T(512)S(1)} %add_rsqrt_fusion), kind=kOutput, calls=%fused_computation.98 | convolution fusion | flops 202244096 | bytes 2362368 | tf_op jit(solution)/shard_map/dot_general | solution.py:24
  54.7 0.6 multiply_reduce_fusion
  55.3 1.5 %convolution_add_fusion.1 = f32[512,256]{0,1:T(8,128)} fusion(f32[64,8,4,128]{3,2,1,0:T(4,128)S(1)} %bitcast.84, f32[512,256]{0,1:T(8,128)S(1)} %copy.46, f32[512,256]{0,1:T(8,128)S(1)} %get-tuple-element.45, f32[512]{0:T(512)S(1)} %broadcast_multiply_fusion, f32[512,256]{0,1:T(8,128)S(1)} %get-tuple-element.41, f32[512]{0:T(512)S(1)} %add_rsqrt_fusion), kind=kOutput, calls=%fused_computation.45 | convolution fusion | flops 403963904 | bytes 3149824 | tf_op jit(solution)/shard_map/dot_general | solution.py:68
  56.8 0.8 fusion.36
  57.6 0.3 convolution_bitcast_fusion.1
  57.9 0.3 convolution_bitcast_fusion.2
  58.2 0.1 collective-permute-start.2
  58.2 1.5 %collective-permute-start.3 = (f32[128,256]{0,1:T(8,128)S(1)}, f32[128,256]{0,1:T(8,128)S(1)}, u32[]{:S(2)}, u32[]{:S(2)}) collective-permute-start(f32[128,256]{0,1:T(8,128)S(1)} %convolution_bitcast_fusion.1), channel_id=1, source_target_pairs={{0,2},{1,3},{2,0},{3,1},{4,6},{5,7},{6,4},{7,5},{8,10},{9,11},{10,... | collective-permute-start | bytes 393224 | tf_op jit(solution)/shard_map/ppermute | solution.py:18
  59.8 1.3 %convolution_bitcast_fusion = f32[32,8,256]{2,1,0:T(8,128)} fusion(f32[512,256]{0,1:T(8,128)S(1)} %get-tuple-element.41, f32[512]{0:T(512)S(1)} %add_rsqrt_fusion, f32[512,256]{0,1:T(8,128)S(1)} %copy.46, f32[512,256]{0,1:T(8,128)S(1)} %get-tuple-element.43), kind=kOutput, calls=%fused_computation.48 | convolution fusion | flops 202506240 | bytes 1837056 | tf_op jit(solution)/shard_map/dot_general | solution.py:34
  61.0 3.0 %all-to-all-start.1 = ((f32[32,8,256]{2,1,0:T(8,128)}), f32[32,8,256]{2,1,0:T(8,128)S(1)}, u32[]{:S(2)}, u32[]{:S(2)}) async-start(f32[32,8,256]{2,1,0:T(8,128)} %convolution_bitcast_fusion), calls=%async_computation.1 | async-start | bytes 524288 | tf_op jit(solution)/shard_map/all_to_all | solution.py:169
  64.0 0.1 collective-permute-done.3
  64.2 0.9 reduce-precision_convert_fusion.5
  65.1 1.0 fusion.18
  66.1 0.2 reshape.185
  66.3 8.1 %all-to-all-done.1 = f32[32,8,256]{2,1,0:T(8,128)S(1)} async-done(((f32[32,8,256]{2,1,0:T(8,128)}), f32[32,8,256]{2,1,0:T(8,128)S(1)}, u32[]{:S(2)}, u32[]{:S(2)}) %all-to-all-start.1) | async-done | bytes 262176 | tf_op jit(solution)/shard_map/all_to_all | solution.py:169
  74.5 0.9 multiply_bitcast_fusion
  75.4 0.1 pad_maximum_fusion
  75.5 2.0 %all_to_all.23 = f32[32,1,10248]{2,1,0:T(1,128)} reshape(f32[32,10248]{1,0:T(8,128)S(1)} %pad_maximum_fusion) | data formatting | bytes 2623488 | tf_op jit(solution)/shard_map/all_to_all | solution.py:188
  77.5 2.8 %all-to-all-start.2 = ((f32[32,1,10248]{2,1,0:T(1,128)}), f32[32,1,10248]{2,1,0:T(1,128)S(1)}, u32[]{:S(2)}, u32[]{:S(2)}) async-start(f32[32,1,10248]{2,1,0:T(1,128)} %all_to_all.23), calls=%async_computation.2 | async-start | bytes 2654208 | tf_op jit(solution)/shard_map/all_to_all | solution.py:188
  80.3 1.0 copy.49
  81.3 31.2 %all-to-all-done.2 = f32[32,1,10248]{2,1,0:T(1,128)S(1)} async-done(((f32[32,1,10248]{2,1,0:T(1,128)}), f32[32,1,10248]{2,1,0:T(1,128)S(1)}, u32[]{:S(2)}, u32[]{:S(2)}) %all-to-all-start.2) | async-done | bytes 1311776 | tf_op jit(solution)/shard_map/all_to_all | solution.py:188
  112.6 0.1 copy.76
  112.7 0.1 slice.71
  112.8 0.7 reshape.189
  113.4 0.2 reshape.187
  113.6 0.7 reshape.188
  114.3 0.2 reduce-precision_convert_fusion.1
  114.6 2.6 %fusion.12 = f32[512,256]{1,0:T(8,128)} fusion(pred[1024,512]{1,0:T(32,128)(4,1)S(1)} %iota_compare_fusion.1, bf16[1024,256]{1,0:T(8,128)(2,1)S(1)} %get-tuple-element.21, bf16[1024,256]{1,0:T(8,128)(2,1)S(1)} %get-tuple-element.22, bf16[1024,256]{1,0:T(8,128)(2,1)S(1)} %get-tuple-element.20), kind=kOutput, calls=%fused_computation.12 | convolution fusion | flops 813170688 | bytes 2621440 | tf_op jit(solution)/shard_map/dot_general | solution.py:115
  (38 shorter events, 0.2 us)
Async XLA Ops:
  6.5 7.5 %copy-start.11 = (s32[1,3]{1,0:T(1,128)S(1)}, s32[1,3]{1,0:T(1,128)}, u32[]{:S(2)}) copy-start(s32[1,3]{1,0:T(1,128)} %param.16) | copy-start | bytes 40
  6.5 7.7 %copy-start.8 = (s32[1,8,2]{1,2,0:T(2,128)S(1)}, s32[1,8,2]{1,2,0:T(2,128)}, u32[]{:S(2)}) copy-start(s32[1,8,2]{1,2,0:T(2,128)} %param.15) | copy-start | bytes 196
  6.6 33.9 %all-to-all-start = ((f32[32,1,8320]{2,1,0:T(1,128)}), f32[32,1,8320]{2,1,0:T(1,128)S(1)}, u32[]{:S(2)}, u32[]{:S(2)}) async-start(f32[32,1,8320]{2,1,0:T(1,128)} %all_to_all.19), calls=%async_computation | async-start | bytes 2129920 | tf_op jit(solution)/shard_map/all_to_all | solution.py:152
  41.2 1.4 %copy-start.2 = (pred[512,1024]{1,0:T(32,128)(4,1)}, pred[512,1024]{1,0:T(32,128)(4,1)S(1)}, u32[]{:S(2)}) copy-start(pred[512,1024]{1,0:T(32,128)(4,1)S(1)} %iota_compare_fusion) | copy-start | bytes 1572868
  41.4 1.2 %copy-start.7 = (s32[1,2,128]{2,1,0:T(2,128)S(1)}, s32[1,2,128]{2,1,0:T(2,128)}, u32[]{:S(2)}) copy-start(s32[1,2,128]{2,1,0:T(2,128)} %param.17) | copy-start | bytes 3076
  42.6 1.4 %copy-start.5 = (f32[1,8,128,128]{3,2,1,0:T(8,128)S(1)}, f32[1,8,128,128]{3,2,1,0:T(8,128)}, u32[]{:S(2)}) copy-start(f32[1,8,128,128]{3,2,1,0:T(8,128)} %param.14) | copy-start | bytes 1572868
  42.6 2.4 %copy-start.1 = (f32[512,256]{1,0:T(8,128)S(1)}, f32[512,256]{1,0:T(8,128)}, u32[]{:S(2)}) copy-start(f32[512,256]{1,0:T(8,128)} %param.19) | copy-start | bytes 1572868
  44.0 1.2 %copy-start.10 = (f32[256]{0:T(256)S(1)}, f32[256]{0:T(256)}, u32[]{:S(2)}) copy-start(f32[256]{0:T(256)} %param.13) | copy-start | bytes 3076
  44.0 2.8 %copy-start = (f32[1,2,128,128]{3,2,1,0:T(8,128)S(1)}, f32[1,2,128,128]{3,2,1,0:T(8,128)}, u32[]{:S(2)}) copy-start(f32[1,2,128,128]{3,2,1,0:T(8,128)} %param.18) | copy-start | bytes 393220
  44.0 2.8 %collective-permute-start = (f32[128,256]{1,0:T(8,128)}, f32[128,256]{1,0:T(8,128)S(1)}, u32[]{:S(2)}, u32[]{:S(2)}) collective-permute-start(f32[128,256]{1,0:T(8,128)} %get-tuple-element.32), channel_id=1, source_target_pairs={{0,1},{1,0},{2,3},{3,2},{4,5},{5,4},{6,7},{7,6},{8,9},{9,8},{10,11... | collective-permute-start | bytes 393224 | tf_op jit(solution)/shard_map/ppermute | solution.py:18
  45.3 5.9 %collective-permute-start.1 = (f32[128,256]{1,0:T(8,128)S(1)}, f32[128,256]{1,0:T(8,128)S(1)}, u32[]{:S(2)}, u32[]{:S(2)}) collective-permute-start(f32[128,256]{1,0:T(8,128)S(1)} %get-tuple-element.33), channel_id=1, source_target_pairs={{0,2},{1,3},{2,0},{3,1},{4,6},{5,7},{6,4},{7,5},{8,10},{9,11},{10,... | collective-permute-start | bytes 393224 | tf_op jit(solution)/shard_map/ppermute | solution.py:18
  52.3 1.0 copy-start.9
  58.2 6.0 %copy-start.6 = (f32[512,256]{0,1:T(8,128)S(1)}, f32[512,256]{0,1:T(8,128)}, u32[]{:S(2)}) copy-start(f32[512,256]{0,1:T(8,128)} %convolution_add_fusion.1) | copy-start | bytes 1572868
  58.2 5.9 %collective-permute-start.2 = (f32[128,256]{0,1:T(8,128)S(1)}, f32[128,256]{0,1:T(8,128)S(1)}, u32[]{:S(2)}, u32[]{:S(2)}) collective-permute-start(f32[128,256]{0,1:T(8,128)S(1)} %convolution_bitcast_fusion.2), channel_id=1, source_target_pairs={{0,1},{1,0},{2,3},{3,2},{4,5},{5,4},{6,7},{7,6},{8,9},{9,8},{10,11... | collective-permute-start | bytes 393224 | tf_op jit(solution)/shard_map/ppermute | solution.py:18
  58.2 5.9 %collective-permute-start.3 = (f32[128,256]{0,1:T(8,128)S(1)}, f32[128,256]{0,1:T(8,128)S(1)}, u32[]{:S(2)}, u32[]{:S(2)}) collective-permute-start(f32[128,256]{0,1:T(8,128)S(1)} %convolution_bitcast_fusion.1), channel_id=1, source_target_pairs={{0,2},{1,3},{2,0},{3,1},{4,6},{5,7},{6,4},{7,5},{8,10},{9,11},{10,... | collective-permute-start | bytes 393224 | tf_op jit(solution)/shard_map/ppermute | solution.py:18
  61.0 4.0 %copy-start.3 = (pred[512,1024]{1,0:T(32,128)(4,1)S(1)}, pred[512,1024]{1,0:T(32,128)(4,1)}, u32[]{:S(2)}) copy-start(pred[512,1024]{1,0:T(32,128)(4,1)} %copy-done.2) | copy-start | bytes 1572868
  61.0 13.4 %all-to-all-start.1 = ((f32[32,8,256]{2,1,0:T(8,128)}), f32[32,8,256]{2,1,0:T(8,128)S(1)}, u32[]{:S(2)}, u32[]{:S(2)}) async-start(f32[32,8,256]{2,1,0:T(8,128)} %convolution_bitcast_fusion), calls=%async_computation.1 | async-start | bytes 524288 | tf_op jit(solution)/shard_map/all_to_all | solution.py:169
  77.5 2.8 %copy-start.4 = (f32[512,256]{0,1:T(8,128)S(1)}, f32[512,256]{0,1:T(8,128)}, u32[]{:S(2)}) copy-start(f32[512,256]{0,1:T(8,128)} %get-tuple-element.42) | copy-start | bytes 1572868
  77.5 35.0 %all-to-all-start.2 = ((f32[32,1,10248]{2,1,0:T(1,128)}), f32[32,1,10248]{2,1,0:T(1,128)S(1)}, u32[]{:S(2)}, u32[]{:S(2)}) async-start(f32[32,1,10248]{2,1,0:T(1,128)} %all_to_all.23), calls=%async_computation.2 | async-start | bytes 2654208 | tf_op jit(solution)/shard_map/all_to_all | solution.py:188

commit v19 on v15

--- a/solution.py
+++ b/solution.py
@@ -50,7 +50,7 @@
         where_to.astype(jnp.float32),
         tile_values.reshape(slots, block * block),
         (((0,), (0,)), ((), ())),
-        precision=PRECISE,
+        precision=DENSE,
         preferred_element_type=jnp.float32,
     )
     placed = placed.reshape(grid, grid, block, block).transpose(0, 2, 1, 3)

time: 114 us -> 114 us (level)
  no operation moved by 1% of the time
where the time goes in v19:
time: 114 us
  waiting for transfers between devices  67.8 us (59%)
  starting transfers between devices  16.8 us (15%)
  matrix products  14.7 us (13%)
  local copies, waits for them, and re-layouts  6.84 us (6%)
  other arithmetic  6.6 us (6%)
    all_to_all x1, waiting for transfers between devices, on_device(): back = lax.all_to_all(payload, ('row', 'col'), 0, 0, tiled=True)  30.9 us
    all_to_all x1, waiting for transfers between devices, on_device(): lax.all_to_all(jnp.concatenate([outbox, tags], axis=1), ('row', 'col'), 0...  26.2 us
    all_to_all x1, waiting for transfers between devices, on_device(): lax.all_to_all(moment.reshape(devices, -1, feat_count), ('row', 'col'), 0...  8.22 us
    all_to_all x1, starting transfers between devices, on_device(): lax.all_to_all(jnp.concatenate([outbox, tags], axis=1), ('row', 'col'), 0...  7.47 us
    dot_general x4, matrix products, exact_pick(): lax.dot_general(wide, parts, dims, preferred_element_type=jnp.float32)  5.76 us
    ppermute x4, starting transfers between devices, swapped(): lax.ppermute(array, axis, [(i, i ^ 1 << apart) for i in range(lax.axis_si...  3.43 us
    all_to_all x1, starting transfers between devices, on_device(): lax.all_to_all(moment.reshape(devices, -1, feat_count), ('row', 'col'), 0...  3.26 us
    another operation x5, other arithmetic  3.14 us
  transfers between devices with their start and end apart: 7, of which 4 were waited for; matrix products, arithmetic and copies ran while one was open for 5% of the time, Pallas kernels for 0%

profile of v19, /device:TPU:0, one launch (start us, length us, event | category | flops | bytes accessed | tf_op | source)
XLA Modules:
  0.0 113.9 jit_solution(3630879201989856291)
XLA Ops:
  0.6 0.6 compare_reduce_fusion
  1.3 0.7 add_select_fusion.1
  2.0 0.3 fusion.30
  2.3 0.4 iota_compare_fusion.1
  2.6 0.0 copy-start.2
  2.7 1.4 %reduce-precision_convert_fusion.7 = (bf16[512,256]{1,0:T(8,128)(2,1)S(1)}, bf16[512,256]{1,0:T(8,128)(2,1)S(1)}, bf16[512,256]{1,0:T(8,128)(2,1)S(1)}) fusion(f32[512,256]{1,0:T(8,128)} %param.12), kind=kLoop, calls=%fused_computation.89 | loop fusion | flops 917504 | bytes 1310720 | tf_op jit(solution)/shard_map/convert.9
  4.0 1.0 fusion
  5.0 0.2 reshape.176
  5.2 0.3 select_reduce_fusion
  5.5 0.7 convert_select_fusion
  6.2 0.1 reshape.177
  6.2 0.1 select_maximum_fusion
  6.3 1.7 %all_to_all.19 = f32[32,1,8320]{2,1,0:T(1,128)} reshape(f32[32,8320]{1,0:T(8,128)S(1)} %select_maximum_fusion) | data formatting | bytes 2129920 | tf_op jit(solution)/shard_map/all_to_all | solution.py:152
  8.0 7.5 %all-to-all-start = ((f32[32,1,8320]{2,1,0:T(1,128)}), f32[32,1,8320]{2,1,0:T(1,128)S(1)}, u32[]{:S(2)}, u32[]{:S(2)}) async-start(f32[32,1,8320]{2,1,0:T(1,128)} %all_to_all.19), calls=%async_computation | async-start | bytes 2129920 | tf_op jit(solution)/shard_map/all_to_all | solution.py:152
  15.6 0.1 slice_bitcast_fusion
  15.6 0.1 compare_bitcast_fusion
  15.7 26.2 %all-to-all-done = f32[32,1,8320]{2,1,0:T(1,128)S(1)} async-done(((f32[32,1,8320]{2,1,0:T(1,128)}), f32[32,1,8320]{2,1,0:T(1,128)S(1)}, u32[]{:S(2)}, u32[]{:S(2)}) %all-to-all-start) | async-done | bytes 1064992 | tf_op jit(solution)/shard_map/all_to_all | solution.py:152
  41.9 0.1 copy.68
  42.0 0.1 slice.78
  42.1 0.2 reshape.178
  42.3 0.2 reduce-precision_convert_fusion.3
  42.5 0.1 eq.100
  42.6 0.3 iota_compare_fusion
  42.9 0.0 copy-start.4
  42.9 1.2 %fusion.6 = f32[512,256]{0,1:T(8,128)S(1)} fusion(pred[512,1024]{1,0:T(32,128)(4,1)S(1)} %iota_compare_fusion, bf16[1024,256]{1,0:T(8,128)(2,1)S(1)} %get-tuple-element.32, bf16[1024,256]{1,0:T(8,128)(2,1)S(1)} %get-tuple-element.33, bf16[1024,256]{1,0:T(8,128)(2,1)S(1)} %get-tuple-element.31), kind=kOutput, calls=%fused_computation.6 | convolution fusion | flops 813170688 | bytes 2621440 | tf_op jit(solution)/shard_map/dot_general | solution.py:115
  44.1 0.0 copy-start.1
  44.1 0.7 fusion.40
  44.9 1.5 %collective-permute-start.1 = (f32[128,256]{1,0:T(8,128)S(1)}, f32[128,256]{1,0:T(8,128)S(1)}, u32[]{:S(2)}, u32[]{:S(2)}) collective-permute-start(f32[128,256]{1,0:T(8,128)S(1)} %get-tuple-element.43), channel_id=1, source_target_pairs={{0,2},{1,3},{2,0},{3,1},{4,6},{5,7},{6,4},{7,5},{8,10},{9,11},{10,... | collective-permute-start | bytes 393224 | tf_op jit(solution)/shard_map/ppermute | solution.py:18
  46.4 0.7 fusion.56
  47.1 0.2 copy.37
  47.3 0.1 collective-permute-start
  47.4 2.5 %collective-permute-done.1 = f32[128,256]{1,0:T(8,128)S(1)} collective-permute-done((f32[128,256]{1,0:T(8,128)S(1)}, f32[128,256]{1,0:T(8,128)S(1)}, u32[]{:S(2)}, u32[]{:S(2)}) %collective-permute-start.1) | collective-permute-done | bytes 131104 | tf_op jit(solution)/shard_map/ppermute | solution.py:18
  49.9 0.2 convolution_bitcast_fusion.3
  50.1 0.2 convolution_bitcast_fusion.4
  50.3 0.8 fusion.38
  51.2 0.0 copy-start.9
  51.2 0.7 multiply_reduce_fusion.1
  51.9 0.3 copy-done.7
  52.1 0.6 multiply_add_fusion
  52.7 0.6 multiply_reduce_fusion
  53.4 0.7 fusion.36
  54.1 0.3 convolution_bitcast_fusion.2
  54.4 0.3 convolution_bitcast_fusion.1
  54.7 0.6 convolution_add_fusion.1
  55.4 0.1 collective-permute-start.2
  55.4 1.8 %collective-permute-start.3 = (f32[128,256]{0,1:T(8,128)S(1)}, f32[128,256]{0,1:T(8,128)S(1)}, u32[]{:S(2)}, u32[]{:S(2)}) collective-permute-start(f32[128,256]{0,1:T(8,128)S(1)} %convolution_bitcast_fusion.1), channel_id=1, source_target_pairs={{0,2},{1,3},{2,0},{3,1},{4,6},{5,7},{6,4},{7,5},{8,10},{9,11},{10,... | collective-permute-start | bytes 393224 | tf_op jit(solution)/shard_map/ppermute | solution.py:18
  57.2 1.3 %convolution_bitcast_fusion = f32[32,8,256]{2,1,0:T(8,128)} fusion(f32[512,256]{0,1:T(8,128)S(1)} %get-tuple-element.49, f32[512]{0:T(512)S(1)} %add_rsqrt_fusion, f32[512,256]{0,1:T(8,128)S(1)} %copy.37, f32[512,256]{0,1:T(8,128)S(1)} %get-tuple-element.51), kind=kOutput, calls=%fused_computation.48 | convolution fusion | flops 202506240 | bytes 1837056 | tf_op jit(solution)/shard_map/dot_general | solution.py:34
  58.5 3.3 %all-to-all-start.1 = ((f32[32,8,256]{2,1,0:T(8,128)}), f32[32,8,256]{2,1,0:T(8,128)S(1)}, u32[]{:S(2)}, u32[]{:S(2)}) async-start(f32[32,8,256]{2,1,0:T(8,128)} %convolution_bitcast_fusion), calls=%async_computation.1 | async-start | bytes 524288 | tf_op jit(solution)/shard_map/all_to_all | solution.py:169
  61.8 0.9 reduce-precision_convert_fusion.5
  62.7 1.0 fusion.18
  63.7 0.2 reshape.180
  63.9 8.2 %all-to-all-done.1 = f32[32,8,256]{2,1,0:T(8,128)S(1)} async-done(((f32[32,8,256]{2,1,0:T(8,128)}), f32[32,8,256]{2,1,0:T(8,128)S(1)}, u32[]{:S(2)}, u32[]{:S(2)}) %all-to-all-start.1) | async-done | bytes 262176 | tf_op jit(solution)/shard_map/all_to_all | solution.py:169
  72.2 0.1 pad_maximum_fusion
  72.3 2.0 %all_to_all.23 = f32[32,1,10240]{2,1,0:T(1,128)} reshape(f32[32,10240]{1,0:T(8,128)S(1)} %pad_maximum_fusion) | data formatting | bytes 2621440 | tf_op jit(solution)/shard_map/all_to_all | solution.py:181
  74.3 2.7 %all-to-all-start.2 = ((f32[32,1,10240]{2,1,0:T(1,128)}), f32[32,1,10240]{2,1,0:T(1,128)S(1)}, u32[]{:S(2)}, u32[]{:S(2)}) async-start(f32[32,1,10240]{2,1,0:T(1,128)} %all_to_all.23), calls=%async_computation.2 | async-start | bytes 2621440 | tf_op jit(solution)/shard_map/all_to_all | solution.py:181
  76.9 1.0 copy.40
  77.9 30.9 %all-to-all-done.2 = f32[32,1,10240]{2,1,0:T(1,128)S(1)} async-done(((f32[32,1,10240]{2,1,0:T(1,128)}), f32[32,1,10240]{2,1,0:T(1,128)S(1)}, u32[]{:S(2)}, u32[]{:S(2)}) %all-to-all-start.2) | async-done | bytes 1310752 | tf_op jit(solution)/shard_map/all_to_all | solution.py:181
  108.8 0.4 copy.67
  109.2 0.1 slice.83
  109.3 0.2 reshape.182
  109.5 0.2 reduce-precision_convert_fusion.1
  109.8 0.9 multiply_reduce_fusion.2
  110.7 0.6 broadcast_multiply_fusion.1
  111.3 2.6 %fusion.12 = f32[512,256]{1,0:T(8,128)} fusion(pred[1024,512]{1,0:T(32,128)(4,1)S(1)} %copy-done.3, bf16[1024,256]{1,0:T(8,128)(2,1)S(1)} %get-tuple-element.29, bf16[1024,256]{1,0:T(8,128)(2,1)S(1)} %get-tuple-element.30, bf16[1024,256]{1,0:T(8,128)(2,1)S(1)} %get-tuple-element.28), kind=kOutput, calls=%fused_computation.12 | convolution fusion | flops 813170688 | bytes 2621440 | tf_op jit(solution)/shard_map/dot_general | solution.py:115
  (35 shorter events, 0.3 us)
Async XLA Ops:
  2.6 1.4 %copy-start.2 = (pred[1024,512]{1,0:T(32,128)(4,1)}, pred[1024,512]{1,0:T(32,128)(4,1)S(1)}, u32[]{:S(2)}) copy-start(pred[1024,512]{1,0:T(32,128)(4,1)S(1)} %iota_compare_fusion.1) | copy-start | bytes 1572868
  8.0 7.5 %copy-start.11 = (s32[1,3]{1,0:T(1,128)S(1)}, s32[1,3]{1,0:T(1,128)}, u32[]{:S(2)}) copy-start(s32[1,3]{1,0:T(1,128)} %param.18) | copy-start | bytes 40
  8.0 7.7 %copy-start.10 = (s32[1,8,2]{1,2,0:T(2,128)S(1)}, s32[1,8,2]{1,2,0:T(2,128)}, u32[]{:S(2)}) copy-start(s32[1,8,2]{1,2,0:T(2,128)} %param.17) | copy-start | bytes 196
  8.0 33.9 %all-to-all-start = ((f32[32,1,8320]{2,1,0:T(1,128)}), f32[32,1,8320]{2,1,0:T(1,128)S(1)}, u32[]{:S(2)}, u32[]{:S(2)}) async-start(f32[32,1,8320]{2,1,0:T(1,128)} %all_to_all.19), calls=%async_computation | async-start | bytes 2129920 | tf_op jit(solution)/shard_map/all_to_all | solution.py:152
  42.9 1.2 %copy-start.4 = (pred[512,1024]{1,0:T(32,128)(4,1)}, pred[512,1024]{1,0:T(32,128)(4,1)S(1)}, u32[]{:S(2)}) copy-start(pred[512,1024]{1,0:T(32,128)(4,1)S(1)} %iota_compare_fusion) | copy-start | bytes 1572868
  42.9 1.2 %copy-start.8 = (s32[1,2,128]{2,1,0:T(2,128)S(1)}, s32[1,2,128]{2,1,0:T(2,128)}, u32[]{:S(2)}) copy-start(s32[1,2,128]{2,1,0:T(2,128)} %param.19) | copy-start | bytes 3076
  44.1 2.3 %copy-start.6 = (f32[1,8,128,128]{3,2,1,0:T(8,128)S(1)}, f32[1,8,128,128]{3,2,1,0:T(8,128)}, u32[]{:S(2)}) copy-start(f32[1,8,128,128]{3,2,1,0:T(8,128)} %param.16) | copy-start | bytes 1572868
  44.1 3.0 %copy-start.1 = (f32[512,256]{1,0:T(8,128)S(1)}, f32[512,256]{1,0:T(8,128)}, u32[]{:S(2)}) copy-start(f32[512,256]{1,0:T(8,128)} %param.21) | copy-start | bytes 1572868
  44.9 5.0 %collective-permute-start.1 = (f32[128,256]{1,0:T(8,128)S(1)}, f32[128,256]{1,0:T(8,128)S(1)}, u32[]{:S(2)}, u32[]{:S(2)}) collective-permute-start(f32[128,256]{1,0:T(8,128)S(1)} %get-tuple-element.43), channel_id=1, source_target_pairs={{0,2},{1,3},{2,0},{3,1},{4,6},{5,7},{6,4},{7,5},{8,10},{9,11},{10,... | collective-permute-start | bytes 393224 | tf_op jit(solution)/shard_map/ppermute | solution.py:18
  46.4 3.5 %copy-start = (f32[1,2,128,128]{3,2,1,0:T(8,128)S(1)}, f32[1,2,128,128]{3,2,1,0:T(8,128)}, u32[]{:S(2)}) copy-start(f32[1,2,128,128]{3,2,1,0:T(8,128)} %param.20) | copy-start | bytes 393220
  47.3 2.8 %collective-permute-start = (f32[128,256]{1,0:T(8,128)S(1)}, f32[128,256]{1,0:T(8,128)S(1)}, u32[]{:S(2)}, u32[]{:S(2)}) collective-permute-start(f32[128,256]{1,0:T(8,128)S(1)} %get-tuple-element.42), channel_id=1, source_target_pairs={{0,1},{1,0},{2,3},{3,2},{4,5},{5,4},{6,7},{7,6},{8,9},{9,8},{10,11... | collective-permute-start | bytes 393224 | tf_op jit(solution)/shard_map/ppermute | solution.py:18
  51.2 1.0 copy-start.7
  51.2 0.9 copy-start.9
  55.4 6.4 %collective-permute-start.2 = (f32[128,256]{0,1:T(8,128)S(1)}, f32[128,256]{0,1:T(8,128)S(1)}, u32[]{:S(2)}, u32[]{:S(2)}) collective-permute-start(f32[128,256]{0,1:T(8,128)S(1)} %convolution_bitcast_fusion.2), channel_id=1, source_target_pairs={{0,1},{1,0},{2,3},{3,2},{4,5},{5,4},{6,7},{7,6},{8,9},{9,8},{10,11... | collective-permute-start | bytes 393224 | tf_op jit(solution)/shard_map/ppermute | solution.py:18
  55.4 6.3 %collective-permute-start.3 = (f32[128,256]{0,1:T(8,128)S(1)}, f32[128,256]{0,1:T(8,128)S(1)}, u32[]{:S(2)}, u32[]{:S(2)}) collective-permute-start(f32[128,256]{0,1:T(8,128)S(1)} %convolution_bitcast_fusion.1), channel_id=1, source_target_pairs={{0,2},{1,3},{2,0},{3,1},{4,6},{5,7},{6,4},{7,5},{8,10},{9,11},{10,... | collective-permute-start | bytes 393224 | tf_op jit(solution)/shard_map/ppermute | solution.py:18
  58.5 4.2 %copy-start.5 = (pred[512,1024]{1,0:T(32,128)(4,1)S(1)}, pred[512,1024]{1,0:T(32,128)(4,1)}, u32[]{:S(2)}) copy-start(pred[512,1024]{1,0:T(32,128)(4,1)} %copy-done.4) | copy-start | bytes 1572868
  58.5 13.6 %all-to-all-start.1 = ((f32[32,8,256]{2,1,0:T(8,128)}), f32[32,8,256]{2,1,0:T(8,128)S(1)}, u32[]{:S(2)}, u32[]{:S(2)}) async-start(f32[32,8,256]{2,1,0:T(8,128)} %convolution_bitcast_fusion), calls=%async_computation.1 | async-start | bytes 524288 | tf_op jit(solution)/shard_map/all_to_all | solution.py:169
  74.3 34.6 %all-to-all-start.2 = ((f32[32,1,10240]{2,1,0:T(1,128)}), f32[32,1,10240]{2,1,0:T(1,128)S(1)}, u32[]{:S(2)}, u32[]{:S(2)}) async-start(f32[32,1,10240]{2,1,0:T(1,128)} %all_to_all.23), calls=%async_computation.2 | async-start | bytes 2621440 | tf_op jit(solution)/shard_map/all_to_all | solution.py:181
  109.8 1.5 %copy-start.3 = (pred[1024,512]{1,0:T(32,128)(4,1)S(1)}, pred[1024,512]{1,0:T(32,128)(4,1)}, u32[]{:S(2)}) copy-start(pred[1024,512]{1,0:T(32,128)(4,1)} %copy-done.2) | copy-start | bytes 1572868

commit v20 on v15

--- a/solution.py
+++ b/solution.py
@@ -146,8 +146,8 @@
     places = jnp.where(tag > 0, tag - 1, row_count)
     outbox = exact_pick(chosen, x_scan).reshape(devices, capacity * feat_count)
     lanes = 128 * (-(-capacity // 128))
-    tags = jnp.zeros((devices, lanes), jnp.float32).at[:, :capacity].set(
-        places.reshape(devices, capacity).astype(jnp.float32)
+    tags = jnp.pad(
+        places.reshape(devices, capacity).astype(jnp.float32), ((0, 0), (0, lanes - capacity))
     )
     got = lax.all_to_all(
         jnp.concatenate([outbox, tags], axis=1), ("row", "col"), 0, 0, tiled=True

time: 114 us -> 113 us (level)
  other arithmetic: 6.6 us -> 5.32 us
    another operation x5 -> x3, other arithmetic: 3.14 us -> 1.85 us
where the time goes in v20:
time: 113 us
  waiting for transfers between devices  67.5 us (60%)
  starting transfers between devices  16.8 us (15%)
  matrix products  15 us (13%)
  local copies, waits for them, and re-layouts  6.83 us (6%)
  other arithmetic  5.32 us (5%)
    all_to_all x1, waiting for transfers between devices, on_device(): back = lax.all_to_all(payload, ('row', 'col'), 0, 0, tiled=True)  30.9 us
    all_to_all x1, waiting for transfers between devices, on_device(): lax.all_to_all(jnp.concatenate([outbox, tags], axis=1), ('row', 'col'), 0...  26.2 us
    all_to_all x1, waiting for transfers between devices, on_device(): lax.all_to_all(moment.reshape(devices, -1, feat_count), ('row', 'col'), 0...  8.22 us
    all_to_all x1, starting transfers between devices, on_device(): lax.all_to_all(jnp.concatenate([outbox, tags], axis=1), ('row', 'col'), 0...  7.48 us
    dot_general x4, matrix products, exact_pick(): lax.dot_general(wide, parts, dims, preferred_element_type=jnp.float32)  5.76 us
    ppermute x4, starting transfers between devices, swapped(): lax.ppermute(array, axis, [(i, i ^ 1 << apart) for i in range(lax.axis_si...  3.43 us
    all_to_all x1, starting transfers between devices, on_device(): lax.all_to_all(moment.reshape(devices, -1, feat_count), ('row', 'col'), 0...  3.25 us
    all_to_all x1, starting transfers between devices, on_device(): back = lax.all_to_all(payload, ('row', 'col'), 0, 0, tiled=True)  2.67 us
  transfers between devices with their start and end apart: 7, of which 4 were waited for; matrix products, arithmetic and copies ran while one was open for 5% of the time, Pallas kernels for 0%

profile of v20, /device:TPU:0, one launch (start us, length us, event | category | flops | bytes accessed | tf_op | source)
XLA Modules:
  0.0 112.6 jit_solution(16152510153557711327)
XLA Ops:
  0.6 0.7 add_select_fusion.1
  1.3 0.3 fusion.30
  1.6 0.4 iota_compare_fusion.1
  2.0 0.0 copy-start.2
  2.0 1.4 %reduce-precision_convert_fusion.7 = (bf16[512,256]{1,0:T(8,128)(2,1)S(1)}, bf16[512,256]{1,0:T(8,128)(2,1)S(1)}, bf16[512,256]{1,0:T(8,128)(2,1)S(1)}) fusion(f32[512,256]{1,0:T(8,128)} %param.10), kind=kLoop, calls=%fused_computation.89 | loop fusion | flops 917504 | bytes 1310720 | tf_op jit(solution)/shard_map/convert.9
  3.4 1.0 fusion
  4.4 0.2 reshape.145
  4.6 0.3 select_reduce_fusion
  4.9 0.1 convert_element_type.13
  5.0 0.1 select_maximum_fusion
  5.0 1.7 %all_to_all.19 = f32[32,1,8320]{2,1,0:T(1,128)} reshape(f32[32,8320]{1,0:T(8,128)S(1)} %select_maximum_fusion) | data formatting | bytes 2129920 | tf_op jit(solution)/shard_map/all_to_all | solution.py:152
  6.8 7.5 %all-to-all-start = ((f32[32,1,8320]{2,1,0:T(1,128)}), f32[32,1,8320]{2,1,0:T(1,128)S(1)}, u32[]{:S(2)}, u32[]{:S(2)}) async-start(f32[32,1,8320]{2,1,0:T(1,128)} %all_to_all.19), calls=%async_computation | async-start | bytes 2129920 | tf_op jit(solution)/shard_map/all_to_all | solution.py:152
  14.3 0.1 slice_bitcast_fusion
  14.4 0.1 compare_bitcast_fusion
  14.5 26.2 %all-to-all-done = f32[32,1,8320]{2,1,0:T(1,128)S(1)} async-done(((f32[32,1,8320]{2,1,0:T(1,128)}), f32[32,1,8320]{2,1,0:T(1,128)S(1)}, u32[]{:S(2)}, u32[]{:S(2)}) %all-to-all-start) | async-done | bytes 1064992 | tf_op jit(solution)/shard_map/all_to_all | solution.py:152
  40.6 0.1 copy.68
  40.7 0.1 slice.62
  40.8 0.2 reshape.146
  41.0 0.2 reduce-precision_convert_fusion.3
  41.2 0.1 eq.100
  41.3 0.3 iota_compare_fusion
  41.6 0.0 copy-start.4
  41.6 0.0 copy-start.8
  41.7 1.2 %fusion.6 = f32[512,256]{0,1:T(8,128)S(1)} fusion(pred[512,1024]{1,0:T(32,128)(4,1)S(1)} %iota_compare_fusion, bf16[1024,256]{1,0:T(8,128)(2,1)S(1)} %get-tuple-element.20, bf16[1024,256]{1,0:T(8,128)(2,1)S(1)} %get-tuple-element.21, bf16[1024,256]{1,0:T(8,128)(2,1)S(1)} %get-tuple-element.19), kind=kOutput, calls=%fused_computation.6 | convolution fusion | flops 813170688 | bytes 2621440 | tf_op jit(solution)/shard_map/dot_general | solution.py:115
  42.8 0.0 copy-start.1
  42.9 0.7 fusion.40
  43.6 1.5 %collective-permute-start.1 = (f32[128,256]{1,0:T(8,128)S(1)}, f32[128,256]{1,0:T(8,128)S(1)}, u32[]{:S(2)}, u32[]{:S(2)}) collective-permute-start(f32[128,256]{1,0:T(8,128)S(1)} %get-tuple-element.31), channel_id=1, source_target_pairs={{0,2},{1,3},{2,0},{3,1},{4,6},{5,7},{6,4},{7,5},{8,10},{9,11},{10,... | collective-permute-start | bytes 393224 | tf_op jit(solution)/shard_map/ppermute | solution.py:18
  45.1 1.0 fusion.56
  46.1 0.2 copy.37
  46.3 0.1 collective-permute-start
  46.4 2.2 %collective-permute-done.1 = f32[128,256]{1,0:T(8,128)S(1)} collective-permute-done((f32[128,256]{1,0:T(8,128)S(1)}, f32[128,256]{1,0:T(8,128)S(1)}, u32[]{:S(2)}, u32[]{:S(2)}) %collective-permute-start.1) | collective-permute-done | bytes 131104 | tf_op jit(solution)/shard_map/ppermute | solution.py:18
  48.6 0.2 convolution_bitcast_fusion.3
  48.9 0.2 convolution_bitcast_fusion.4
  49.1 0.8 fusion.38
  49.9 0.0 copy-start.7
  49.9 0.7 multiply_reduce_fusion.1
  50.6 0.3 copy-done.7
  50.9 0.6 multiply_add_fusion
  51.5 0.6 multiply_reduce_fusion
  52.1 0.7 fusion.36
  52.9 0.3 convolution_bitcast_fusion.2
  53.2 0.3 convolution_bitcast_fusion.1
  53.5 0.6 convolution_add_fusion.1
  54.1 0.1 collective-permute-start.2
  54.2 1.8 %collective-permute-start.3 = (f32[128,256]{0,1:T(8,128)S(1)}, f32[128,256]{0,1:T(8,128)S(1)}, u32[]{:S(2)}, u32[]{:S(2)}) collective-permute-start(f32[128,256]{0,1:T(8,128)S(1)} %convolution_bitcast_fusion.1), channel_id=1, source_target_pairs={{0,2},{1,3},{2,0},{3,1},{4,6},{5,7},{6,4},{7,5},{8,10},{9,11},{10,... | collective-permute-start | bytes 393224 | tf_op jit(solution)/shard_map/ppermute | solution.py:18
  55.9 1.3 %convolution_bitcast_fusion = f32[32,8,256]{2,1,0:T(8,128)} fusion(f32[512,256]{0,1:T(8,128)S(1)} %get-tuple-element.37, f32[512]{0:T(512)S(1)} %add_rsqrt_fusion, f32[512,256]{0,1:T(8,128)S(1)} %copy.37, f32[512,256]{0,1:T(8,128)S(1)} %get-tuple-element.39), kind=kOutput, calls=%fused_computation.48 | convolution fusion | flops 202506240 | bytes 1837056 | tf_op jit(solution)/shard_map/dot_general | solution.py:34
  57.2 3.2 %all-to-all-start.1 = ((f32[32,8,256]{2,1,0:T(8,128)}), f32[32,8,256]{2,1,0:T(8,128)S(1)}, u32[]{:S(2)}, u32[]{:S(2)}) async-start(f32[32,8,256]{2,1,0:T(8,128)} %convolution_bitcast_fusion), calls=%async_computation.1 | async-start | bytes 524288 | tf_op jit(solution)/shard_map/all_to_all | solution.py:169
  60.5 0.9 reduce-precision_convert_fusion.5
  61.4 1.0 fusion.18
  62.4 0.2 reshape.148
  62.6 8.2 %all-to-all-done.1 = f32[32,8,256]{2,1,0:T(8,128)S(1)} async-done(((f32[32,8,256]{2,1,0:T(8,128)}), f32[32,8,256]{2,1,0:T(8,128)S(1)}, u32[]{:S(2)}, u32[]{:S(2)}) %all-to-all-start.1) | async-done | bytes 262176 | tf_op jit(solution)/shard_map/all_to_all | solution.py:169
  70.9 0.1 pad_maximum_fusion
  71.0 2.0 %all_to_all.23 = f32[32,1,10240]{2,1,0:T(1,128)} reshape(f32[32,10240]{1,0:T(8,128)S(1)} %pad_maximum_fusion) | data formatting | bytes 2621440 | tf_op jit(solution)/shard_map/all_to_all | solution.py:181
  73.0 2.7 %all-to-all-start.2 = ((f32[32,1,10240]{2,1,0:T(1,128)}), f32[32,1,10240]{2,1,0:T(1,128)S(1)}, u32[]{:S(2)}, u32[]{:S(2)}) async-start(f32[32,1,10240]{2,1,0:T(1,128)} %all_to_all.23), calls=%async_computation.2 | async-start | bytes 2621440 | tf_op jit(solution)/shard_map/all_to_all | solution.py:181
  75.7 1.0 copy.40
  76.7 30.9 %all-to-all-done.2 = f32[32,1,10240]{2,1,0:T(1,128)S(1)} async-done(((f32[32,1,10240]{2,1,0:T(1,128)}), f32[32,1,10240]{2,1,0:T(1,128)S(1)}, u32[]{:S(2)}, u32[]{:S(2)}) %all-to-all-start.2) | async-done | bytes 1310752 | tf_op jit(solution)/shard_map/all_to_all | solution.py:181
  107.5 0.4 copy.67
  108.0 0.1 slice.67
  108.1 0.2 reshape.150
  108.2 0.2 reduce-precision_convert_fusion.1
  108.5 0.0 copy-start.3
  108.5 0.9 multiply_reduce_fusion.2
  109.4 0.6 broadcast_multiply_fusion.1
  110.0 2.6 %fusion.12 = f32[512,256]{1,0:T(8,128)} fusion(pred[1024,512]{1,0:T(32,128)(4,1)S(1)} %copy-done.3, bf16[1024,256]{1,0:T(8,128)(2,1)S(1)} %get-tuple-element.17, bf16[1024,256]{1,0:T(8,128)(2,1)S(1)} %get-tuple-element.18, bf16[1024,256]{1,0:T(8,128)(2,1)S(1)} %get-tuple-element.16), kind=kOutput, calls=%fused_computation.12 | convolution fusion | flops 813170688 | bytes 2621440 | tf_op jit(solution)/shard_map/dot_general | solution.py:115
  (34 shorter events, 0.3 us)
Async XLA Ops:
  2.0 1.4 %copy-start.2 = (pred[1024,512]{1,0:T(32,128)(4,1)}, pred[1024,512]{1,0:T(32,128)(4,1)S(1)}, u32[]{:S(2)}) copy-start(pred[1024,512]{1,0:T(32,128)(4,1)S(1)} %iota_compare_fusion.1) | copy-start | bytes 1572868
  6.8 7.5 %copy-start.11 = (s32[1,3]{1,0:T(1,128)S(1)}, s32[1,3]{1,0:T(1,128)}, u32[]{:S(2)}) copy-start(s32[1,3]{1,0:T(1,128)} %param.16) | copy-start | bytes 40
  6.8 7.7 %copy-start.10 = (s32[1,8,2]{1,2,0:T(2,128)S(1)}, s32[1,8,2]{1,2,0:T(2,128)}, u32[]{:S(2)}) copy-start(s32[1,8,2]{1,2,0:T(2,128)} %param.15) | copy-start | bytes 196
  6.8 33.9 %all-to-all-start = ((f32[32,1,8320]{2,1,0:T(1,128)}), f32[32,1,8320]{2,1,0:T(1,128)S(1)}, u32[]{:S(2)}, u32[]{:S(2)}) async-start(f32[32,1,8320]{2,1,0:T(1,128)} %all_to_all.19), calls=%async_computation | async-start | bytes 2129920 | tf_op jit(solution)/shard_map/all_to_all | solution.py:152
  41.6 1.2 %copy-start.4 = (pred[512,1024]{1,0:T(32,128)(4,1)}, pred[512,1024]{1,0:T(32,128)(4,1)S(1)}, u32[]{:S(2)}) copy-start(pred[512,1024]{1,0:T(32,128)(4,1)S(1)} %iota_compare_fusion) | copy-start | bytes 1572868
  41.6 1.2 %copy-start.8 = (s32[1,2,128]{2,1,0:T(2,128)S(1)}, s32[1,2,128]{2,1,0:T(2,128)}, u32[]{:S(2)}) copy-start(s32[1,2,128]{2,1,0:T(2,128)} %param.17) | copy-start | bytes 3076
  42.8 2.3 %copy-start.6 = (f32[1,8,128,128]{3,2,1,0:T(8,128)S(1)}, f32[1,8,128,128]{3,2,1,0:T(8,128)}, u32[]{:S(2)}) copy-start(f32[1,8,128,128]{3,2,1,0:T(8,128)} %param.14) | copy-start | bytes 1572868
  42.8 3.3 %copy-start.1 = (f32[512,256]{1,0:T(8,128)S(1)}, f32[512,256]{1,0:T(8,128)}, u32[]{:S(2)}) copy-start(f32[512,256]{1,0:T(8,128)} %param.19) | copy-start | bytes 1572868
  43.6 5.0 %collective-permute-start.1 = (f32[128,256]{1,0:T(8,128)S(1)}, f32[128,256]{1,0:T(8,128)S(1)}, u32[]{:S(2)}, u32[]{:S(2)}) collective-permute-start(f32[128,256]{1,0:T(8,128)S(1)} %get-tuple-element.31), channel_id=1, source_target_pairs={{0,2},{1,3},{2,0},{3,1},{4,6},{5,7},{6,4},{7,5},{8,10},{9,11},{10,... | collective-permute-start | bytes 393224 | tf_op jit(solution)/shard_map/ppermute | solution.py:18
  45.1 3.5 %copy-start = (f32[1,2,128,128]{3,2,1,0:T(8,128)S(1)}, f32[1,2,128,128]{3,2,1,0:T(8,128)}, u32[]{:S(2)}) copy-start(f32[1,2,128,128]{3,2,1,0:T(8,128)} %param.18) | copy-start | bytes 393220
  46.3 2.5 %collective-permute-start = (f32[128,256]{1,0:T(8,128)S(1)}, f32[128,256]{1,0:T(8,128)S(1)}, u32[]{:S(2)}, u32[]{:S(2)}) collective-permute-start(f32[128,256]{1,0:T(8,128)S(1)} %get-tuple-element.30), channel_id=1, source_target_pairs={{0,1},{1,0},{2,3},{3,2},{4,5},{5,4},{6,7},{7,6},{8,9},{9,8},{10,11... | collective-permute-start | bytes 393224 | tf_op jit(solution)/shard_map/ppermute | solution.py:18
  49.9 1.0 copy-start.7
  49.9 0.9 copy-start.9
  54.1 6.4 %collective-permute-start.2 = (f32[128,256]{0,1:T(8,128)S(1)}, f32[128,256]{0,1:T(8,128)S(1)}, u32[]{:S(2)}, u32[]{:S(2)}) collective-permute-start(f32[128,256]{0,1:T(8,128)S(1)} %convolution_bitcast_fusion.2), channel_id=1, source_target_pairs={{0,1},{1,0},{2,3},{3,2},{4,5},{5,4},{6,7},{7,6},{8,9},{9,8},{10,11... | collective-permute-start | bytes 393224 | tf_op jit(solution)/shard_map/ppermute | solution.py:18
  54.2 6.3 %collective-permute-start.3 = (f32[128,256]{0,1:T(8,128)S(1)}, f32[128,256]{0,1:T(8,128)S(1)}, u32[]{:S(2)}, u32[]{:S(2)}) collective-permute-start(f32[128,256]{0,1:T(8,128)S(1)} %convolution_bitcast_fusion.1), channel_id=1, source_target_pairs={{0,2},{1,3},{2,0},{3,1},{4,6},{5,7},{6,4},{7,5},{8,10},{9,11},{10,... | collective-permute-start | bytes 393224 | tf_op jit(solution)/shard_map/ppermute | solution.py:18
  57.2 4.2 %copy-start.5 = (pred[512,1024]{1,0:T(32,128)(4,1)S(1)}, pred[512,1024]{1,0:T(32,128)(4,1)}, u32[]{:S(2)}) copy-start(pred[512,1024]{1,0:T(32,128)(4,1)} %copy-done.4) | copy-start | bytes 1572868
  57.2 13.6 %all-to-all-start.1 = ((f32[32,8,256]{2,1,0:T(8,128)}), f32[32,8,256]{2,1,0:T(8,128)S(1)}, u32[]{:S(2)}, u32[]{:S(2)}) async-start(f32[32,8,256]{2,1,0:T(8,128)} %convolution_bitcast_fusion), calls=%async_computation.1 | async-start | bytes 524288 | tf_op jit(solution)/shard_map/all_to_all | solution.py:169
  73.0 34.6 %all-to-all-start.2 = ((f32[32,1,10240]{2,1,0:T(1,128)}), f32[32,1,10240]{2,1,0:T(1,128)S(1)}, u32[]{:S(2)}, u32[]{:S(2)}) async-start(f32[32,1,10240]{2,1,0:T(1,128)} %all_to_all.23), calls=%async_computation.2 | async-start | bytes 2621440 | tf_op jit(solution)/shard_map/all_to_all | solution.py:181
  108.5 1.5 %copy-start.3 = (pred[1024,512]{1,0:T(32,128)(4,1)S(1)}, pred[1024,512]{1,0:T(32,128)(4,1)}, u32[]{:S(2)}) copy-start(pred[1024,512]{1,0:T(32,128)(4,1)} %copy-done.2) | copy-start | bytes 1572868

commit v21 on v20

--- a/solution.py
+++ b/solution.py
@@ -1,6 +1,7 @@
 import math
 
 import jax
+import numpy as np
 import jax.numpy as jnp
 from jax import lax
 from jax.sharding import PartitionSpec as P
@@ -136,7 +137,7 @@
     within = owner_slot % row_count
     hit = target[:, None] == jnp.arange(devices, dtype=jnp.int32)[None, :]
     order = jnp.arange(row_count, dtype=jnp.int32)
-    earlier = (order[:, None] > order[None, :]).astype(jnp.bfloat16)
+    earlier = jnp.asarray(np.tril(np.ones((row_count, row_count), np.float32), -1), jnp.bfloat16)
     before = jnp.dot(earlier, hit.astype(jnp.bfloat16), preferred_element_type=jnp.float32)
     ranked = jnp.sum(jnp.where(hit, before, 0.0), axis=1).astype(jnp.int32)
     bucket = target * capacity + ranked

time: 113 us -> 114 us (level)
  other arithmetic: 5.32 us -> 4.15 us
    another operation x3, other arithmetic: 1.85 us -> 0.62 us
    unnamed x29 -> x31, local copies, waits for them, and re-layouts: 1.99 us -> 2.65 us
where the time goes in v21:
time: 114 us; the launch traced here: 113 us
  waiting for transfers between devices  67.5 us (59%)
  starting transfers between devices  16.8 us (15%)
  matrix products  16 us (14%)
  local copies, waits for them, and re-layouts  7.5 us (7%)
  other arithmetic  4.15 us (4%)
    all_to_all x1, waiting for transfers between devices, on_device(): back = lax.all_to_all(payload, ('row', 'col'), 0, 0, tiled=True)  30.9 us
    all_to_all x1, waiting for transfers between devices, on_device(): lax.all_to_all(jnp.concatenate([outbox, tags], axis=1), ('row', 'col'), 0...  26.2 us
    all_to_all x1, waiting for transfers between devices, on_device(): lax.all_to_all(moment.reshape(devices, -1, feat_count), ('row', 'col'), 0...  8.22 us
    all_to_all x1, starting transfers between devices, on_device(): lax.all_to_all(jnp.concatenate([outbox, tags], axis=1), ('row', 'col'), 0...  7.48 us
    dot_general x4, matrix products, exact_pick(): lax.dot_general(wide, parts, dims, preferred_element_type=jnp.float32)  5.75 us
    ppermute x4, starting transfers between devices, swapped(): lax.ppermute(array, axis, [(i, i ^ 1 << apart) for i in range(lax.axis_si...  3.43 us
    all_to_all x1, starting transfers between devices, on_device(): lax.all_to_all(moment.reshape(devices, -1, feat_count), ('row', 'col'), 0...  3.26 us
    all_to_all x1, starting transfers between devices, on_device(): back = lax.all_to_all(payload, ('row', 'col'), 0, 0, tiled=True)  2.67 us
  transfers between devices with their start and end apart: 7, of which 4 were waited for; matrix products, arithmetic and copies ran while one was open for 5% of the time, Pallas kernels for 0%

profile of v21, /device:TPU:0, one launch (start us, length us, event | category | flops | bytes accessed | tf_op | source)
XLA Modules:
  0.0 113.1 jit_solution(15238885815131675663)
XLA Ops:
  0.6 0.7 add_select_fusion.1
  1.4 1.3 %fusion.30 = f32[512]{0:T(512)S(1)} fusion(bf16[512,512]{1,0:T(8,128)(2,1)} %constant.52.clone, s32[512]{0:T(512)S(1)} %get-tuple-element.32), kind=kOutput, calls=%fused_computation.54 | convolution fusion | flops 16842240 | bytes 528384 | tf_op jit(solution)/shard_map/dot_general | solution.py:141
  2.7 0.4 iota_compare_fusion.1
  3.1 0.0 copy-start.3
  3.1 0.1 reduce-precision_convert_fusion.7
  3.3 0.7 copy-done.3
  3.9 1.0 fusion
  4.9 0.2 reshape.145
  5.1 0.3 select_reduce_fusion
  5.4 0.1 convert_element_type.13
  5.5 0.1 select_maximum_fusion
  5.6 1.7 %all_to_all.19 = f32[32,1,8320]{2,1,0:T(1,128)} reshape(f32[32,8320]{1,0:T(8,128)S(1)} %select_maximum_fusion) | data formatting | bytes 2129920 | tf_op jit(solution)/shard_map/all_to_all | solution.py:153
  7.3 7.5 %all-to-all-start = ((f32[32,1,8320]{2,1,0:T(1,128)}), f32[32,1,8320]{2,1,0:T(1,128)S(1)}, u32[]{:S(2)}, u32[]{:S(2)}) async-start(f32[32,1,8320]{2,1,0:T(1,128)} %all_to_all.19), calls=%async_computation | async-start | bytes 2129920 | tf_op jit(solution)/shard_map/all_to_all | solution.py:153
  14.8 0.1 slice_bitcast_fusion
  14.9 0.1 compare_bitcast_fusion
  15.0 26.2 %all-to-all-done = f32[32,1,8320]{2,1,0:T(1,128)S(1)} async-done(((f32[32,1,8320]{2,1,0:T(1,128)}), f32[32,1,8320]{2,1,0:T(1,128)S(1)}, u32[]{:S(2)}, u32[]{:S(2)}) %all-to-all-start) | async-done | bytes 1064992 | tf_op jit(solution)/shard_map/all_to_all | solution.py:153
  41.2 0.1 copy.69
  41.2 0.1 slice.62
  41.3 0.2 reshape.146
  41.5 0.2 reduce-precision_convert_fusion.3
  41.8 0.1 eq.100
  41.8 0.3 iota_compare_fusion
  42.2 1.2 %fusion.6 = f32[512,256]{0,1:T(8,128)S(1)} fusion(pred[512,1024]{1,0:T(32,128)(4,1)S(1)} %iota_compare_fusion, bf16[1024,256]{1,0:T(8,128)(2,1)S(1)} %get-tuple-element.20, bf16[1024,256]{1,0:T(8,128)(2,1)S(1)} %get-tuple-element.21, bf16[1024,256]{1,0:T(8,128)(2,1)S(1)} %get-tuple-element.19), kind=kOutput, calls=%fused_computation.6 | convolution fusion | flops 813170688 | bytes 2621440 | tf_op jit(solution)/shard_map/dot_general | solution.py:116
  43.3 0.0 copy-start.7
  43.4 0.0 copy-start.2
  43.4 0.7 fusion.40
  44.1 1.5 %collective-permute-start.1 = (f32[128,256]{1,0:T(8,128)S(1)}, f32[128,256]{1,0:T(8,128)S(1)}, u32[]{:S(2)}, u32[]{:S(2)}) collective-permute-start(f32[128,256]{1,0:T(8,128)S(1)} %get-tuple-element.31), channel_id=1, source_target_pairs={{0,2},{1,3},{2,0},{3,1},{4,6},{5,7},{6,4},{7,5},{8,10},{9,11},{10,... | collective-permute-start | bytes 393224 | tf_op jit(solution)/shard_map/ppermute | solution.py:19
  45.7 1.0 fusion.56
  46.7 0.2 copy.38
  46.9 0.1 collective-permute-start
  46.9 2.2 %collective-permute-done.1 = f32[128,256]{1,0:T(8,128)S(1)} collective-permute-done((f32[128,256]{1,0:T(8,128)S(1)}, f32[128,256]{1,0:T(8,128)S(1)}, u32[]{:S(2)}, u32[]{:S(2)}) %collective-permute-start.1) | collective-permute-done | bytes 131104 | tf_op jit(solution)/shard_map/ppermute | solution.py:19
  49.2 0.2 convolution_bitcast_fusion.3
  49.4 0.2 convolution_bitcast_fusion.4
  49.6 0.8 fusion.38
  50.4 0.0 copy-start.8
  50.4 0.0 copy-start.10
  50.5 0.7 multiply_reduce_fusion.1
  51.1 0.3 copy-done.8
  51.4 0.6 multiply_add_fusion
  52.0 0.6 multiply_reduce_fusion
  52.6 0.7 fusion.36
  53.4 0.3 convolution_bitcast_fusion.2
  53.7 0.3 convolution_bitcast_fusion.1
  54.0 0.6 convolution_add_fusion.1
  54.6 0.1 collective-permute-start.2
  54.7 1.8 %collective-permute-start.3 = (f32[128,256]{0,1:T(8,128)S(1)}, f32[128,256]{0,1:T(8,128)S(1)}, u32[]{:S(2)}, u32[]{:S(2)}) collective-permute-start(f32[128,256]{0,1:T(8,128)S(1)} %convolution_bitcast_fusion.1), channel_id=1, source_target_pairs={{0,2},{1,3},{2,0},{3,1},{4,6},{5,7},{6,4},{7,5},{8,10},{9,11},{10,... | collective-permute-start | bytes 393224 | tf_op jit(solution)/shard_map/ppermute | solution.py:19
  56.5 1.3 %convolution_bitcast_fusion = f32[32,8,256]{2,1,0:T(8,128)} fusion(f32[512,256]{0,1:T(8,128)S(1)} %get-tuple-element.37, f32[512]{0:T(512)S(1)} %add_rsqrt_fusion, f32[512,256]{0,1:T(8,128)S(1)} %copy.38, f32[512,256]{0,1:T(8,128)S(1)} %get-tuple-element.39), kind=kOutput, calls=%fused_computation.48 | convolution fusion | flops 202506240 | bytes 1837056 | tf_op jit(solution)/shard_map/dot_general | solution.py:35
  57.7 3.3 %all-to-all-start.1 = ((f32[32,8,256]{2,1,0:T(8,128)}), f32[32,8,256]{2,1,0:T(8,128)S(1)}, u32[]{:S(2)}, u32[]{:S(2)}) async-start(f32[32,8,256]{2,1,0:T(8,128)} %convolution_bitcast_fusion), calls=%async_computation.1 | async-start | bytes 524288 | tf_op jit(solution)/shard_map/all_to_all | solution.py:170
  61.0 0.9 reduce-precision_convert_fusion.5
  61.9 1.0 fusion.18
  63.0 0.2 reshape.148
  63.2 8.2 %all-to-all-done.1 = f32[32,8,256]{2,1,0:T(8,128)S(1)} async-done(((f32[32,8,256]{2,1,0:T(8,128)}), f32[32,8,256]{2,1,0:T(8,128)S(1)}, u32[]{:S(2)}, u32[]{:S(2)}) %all-to-all-start.1) | async-done | bytes 262176 | tf_op jit(solution)/shard_map/all_to_all | solution.py:170
  71.4 0.1 pad_maximum_fusion
  71.6 2.0 %all_to_all.23 = f32[32,1,10240]{2,1,0:T(1,128)} reshape(f32[32,10240]{1,0:T(8,128)S(1)} %pad_maximum_fusion) | data formatting | bytes 2621440 | tf_op jit(solution)/shard_map/all_to_all | solution.py:182
  73.5 2.7 %all-to-all-start.2 = ((f32[32,1,10240]{2,1,0:T(1,128)}), f32[32,1,10240]{2,1,0:T(1,128)S(1)}, u32[]{:S(2)}, u32[]{:S(2)}) async-start(f32[32,1,10240]{2,1,0:T(1,128)} %all_to_all.23), calls=%async_computation.2 | async-start | bytes 2621440 | tf_op jit(solution)/shard_map/all_to_all | solution.py:182
  76.2 1.0 copy.41
  77.2 30.9 %all-to-all-done.2 = f32[32,1,10240]{2,1,0:T(1,128)S(1)} async-done(((f32[32,1,10240]{2,1,0:T(1,128)}), f32[32,1,10240]{2,1,0:T(1,128)S(1)}, u32[]{:S(2)}, u32[]{:S(2)}) %all-to-all-start.2) | async-done | bytes 1310752 | tf_op jit(solution)/shard_map/all_to_all | solution.py:182
  108.1 0.4 copy.68
  108.5 0.1 slice.67
  108.6 0.2 reshape.150
  108.8 0.2 reduce-precision_convert_fusion.1
  109.1 0.9 multiply_reduce_fusion.2
  110.0 0.6 broadcast_multiply_fusion.1
  110.5 2.6 %fusion.12 = f32[512,256]{1,0:T(8,128)} fusion(pred[1024,512]{1,0:T(32,128)(4,1)S(1)} %copy-done.4, bf16[1024,256]{1,0:T(8,128)(2,1)S(1)} %get-tuple-element.17, bf16[1024,256]{1,0:T(8,128)(2,1)S(1)} %get-tuple-element.18, bf16[1024,256]{1,0:T(8,128)(2,1)S(1)} %get-tuple-element.16), kind=kOutput, calls=%fused_computation.12 | convolution fusion | flops 813170688 | bytes 2621440 | tf_op jit(solution)/shard_map/dot_general | solution.py:116
  (36 shorter events, 0.3 us)
Async XLA Ops:
  0.6 2.5 %copy-start.1 = (f32[512,256]{1,0:T(8,128)S(1)}, f32[512,256]{1,0:T(8,128)}, u32[]{:S(2)}) copy-start(f32[512,256]{1,0:T(8,128)} %param.11) | copy-start | bytes 1572868
  3.1 0.8 copy-start.3
  7.3 7.5 %copy-start.12 = (s32[1,3]{1,0:T(1,128)S(1)}, s32[1,3]{1,0:T(1,128)}, u32[]{:S(2)}) copy-start(s32[1,3]{1,0:T(1,128)} %param.17) | copy-start | bytes 40
  7.3 7.7 %copy-start.11 = (s32[1,8,2]{1,2,0:T(2,128)S(1)}, s32[1,8,2]{1,2,0:T(2,128)}, u32[]{:S(2)}) copy-start(s32[1,8,2]{1,2,0:T(2,128)} %param.16) | copy-start | bytes 196
  7.3 33.9 %all-to-all-start = ((f32[32,1,8320]{2,1,0:T(1,128)}), f32[32,1,8320]{2,1,0:T(1,128)S(1)}, u32[]{:S(2)}, u32[]{:S(2)}) async-start(f32[32,1,8320]{2,1,0:T(1,128)} %all_to_all.19), calls=%async_computation | async-start | bytes 2129920 | tf_op jit(solution)/shard_map/all_to_all | solution.py:153
  42.2 1.2 %copy-start.5 = (pred[512,1024]{1,0:T(32,128)(4,1)}, pred[512,1024]{1,0:T(32,128)(4,1)S(1)}, u32[]{:S(2)}) copy-start(pred[512,1024]{1,0:T(32,128)(4,1)S(1)} %iota_compare_fusion) | copy-start | bytes 1572868
  42.2 1.2 %copy-start.9 = (s32[1,2,128]{2,1,0:T(2,128)S(1)}, s32[1,2,128]{2,1,0:T(2,128)}, u32[]{:S(2)}) copy-start(s32[1,2,128]{2,1,0:T(2,128)} %param.18) | copy-start | bytes 3076
  43.3 2.3 %copy-start.7 = (f32[1,8,128,128]{3,2,1,0:T(8,128)S(1)}, f32[1,8,128,128]{3,2,1,0:T(8,128)}, u32[]{:S(2)}) copy-start(f32[1,8,128,128]{3,2,1,0:T(8,128)} %param.15) | copy-start | bytes 1572868
  43.4 3.3 %copy-start.2 = (f32[512,256]{1,0:T(8,128)S(1)}, f32[512,256]{1,0:T(8,128)}, u32[]{:S(2)}) copy-start(f32[512,256]{1,0:T(8,128)} %param.20) | copy-start | bytes 1572868
  44.1 5.0 %collective-permute-start.1 = (f32[128,256]{1,0:T(8,128)S(1)}, f32[128,256]{1,0:T(8,128)S(1)}, u32[]{:S(2)}, u32[]{:S(2)}) collective-permute-start(f32[128,256]{1,0:T(8,128)S(1)} %get-tuple-element.31), channel_id=1, source_target_pairs={{0,2},{1,3},{2,0},{3,1},{4,6},{5,7},{6,4},{7,5},{8,10},{9,11},{10,... | collective-permute-start | bytes 393224 | tf_op jit(solution)/shard_map/ppermute | solution.py:19
  45.6 3.5 %copy-start = (f32[1,2,128,128]{3,2,1,0:T(8,128)S(1)}, f32[1,2,128,128]{3,2,1,0:T(8,128)}, u32[]{:S(2)}) copy-start(f32[1,2,128,128]{3,2,1,0:T(8,128)} %param.19) | copy-start | bytes 393220
  46.9 2.5 %collective-permute-start = (f32[128,256]{1,0:T(8,128)S(1)}, f32[128,256]{1,0:T(8,128)S(1)}, u32[]{:S(2)}, u32[]{:S(2)}) collective-permute-start(f32[128,256]{1,0:T(8,128)S(1)} %get-tuple-element.30), channel_id=1, source_target_pairs={{0,1},{1,0},{2,3},{3,2},{4,5},{5,4},{6,7},{7,6},{8,9},{9,8},{10,11... | collective-permute-start | bytes 393224 | tf_op jit(solution)/shard_map/ppermute | solution.py:19
  50.4 1.0 copy-start.8
  50.4 0.9 copy-start.10
  54.6 6.4 %collective-permute-start.2 = (f32[128,256]{0,1:T(8,128)S(1)}, f32[128,256]{0,1:T(8,128)S(1)}, u32[]{:S(2)}, u32[]{:S(2)}) collective-permute-start(f32[128,256]{0,1:T(8,128)S(1)} %convolution_bitcast_fusion.2), channel_id=1, source_target_pairs={{0,1},{1,0},{2,3},{3,2},{4,5},{5,4},{6,7},{7,6},{8,9},{9,8},{10,11... | collective-permute-start | bytes 393224 | tf_op jit(solution)/shard_map/ppermute | solution.py:19
  54.7 6.3 %collective-permute-start.3 = (f32[128,256]{0,1:T(8,128)S(1)}, f32[128,256]{0,1:T(8,128)S(1)}, u32[]{:S(2)}, u32[]{:S(2)}) collective-permute-start(f32[128,256]{0,1:T(8,128)S(1)} %convolution_bitcast_fusion.1), channel_id=1, source_target_pairs={{0,2},{1,3},{2,0},{3,1},{4,6},{5,7},{6,4},{7,5},{8,10},{9,11},{10,... | collective-permute-start | bytes 393224 | tf_op jit(solution)/shard_map/ppermute | solution.py:19
  57.7 4.2 %copy-start.6 = (pred[512,1024]{1,0:T(32,128)(4,1)S(1)}, pred[512,1024]{1,0:T(32,128)(4,1)}, u32[]{:S(2)}) copy-start(pred[512,1024]{1,0:T(32,128)(4,1)} %copy-done.5) | copy-start | bytes 1572868
  57.7 13.7 %all-to-all-start.1 = ((f32[32,8,256]{2,1,0:T(8,128)}), f32[32,8,256]{2,1,0:T(8,128)S(1)}, u32[]{:S(2)}, u32[]{:S(2)}) async-start(f32[32,8,256]{2,1,0:T(8,128)} %convolution_bitcast_fusion), calls=%async_computation.1 | async-start | bytes 524288 | tf_op jit(solution)/shard_map/all_to_all | solution.py:170
  73.5 34.6 %all-to-all-start.2 = ((f32[32,1,10240]{2,1,0:T(1,128)}), f32[32,1,10240]{2,1,0:T(1,128)S(1)}, u32[]{:S(2)}, u32[]{:S(2)}) async-start(f32[32,1,10240]{2,1,0:T(1,128)} %all_to_all.23), calls=%async_computation.2 | async-start | bytes 2621440 | tf_op jit(solution)/shard_map/all_to_all | solution.py:182
  109.0 1.5 %copy-start.4 = (pred[1024,512]{1,0:T(32,128)(4,1)S(1)}, pred[1024,512]{1,0:T(32,128)(4,1)}, u32[]{:S(2)}) copy-start(pred[1024,512]{1,0:T(32,128)(4,1)} %copy-done.3) | copy-start | bytes 1572868

commit v22 on v20

--- a/solution.py
+++ b/solution.py
@@ -50,7 +50,7 @@
         where_to.astype(jnp.float32),
         tile_values.reshape(slots, block * block),
         (((0,), (0,)), ((), ())),
-        precision=PRECISE,
+        precision=DENSE,
         preferred_element_type=jnp.float32,
     )
     placed = placed.reshape(grid, grid, block, block).transpose(0, 2, 1, 3)

time: 113 us -> 113 us (level)
  no operation moved by 1% of the time
where the time goes in v22:
time: 113 us
  waiting for transfers between devices  67.8 us (60%)
  starting transfers between devices  16.8 us (15%)
  matrix products  14.7 us (13%)
  local copies, waits for them, and re-layouts  6.83 us (6%)
  other arithmetic  5.32 us (5%)
    all_to_all x1, waiting for transfers between devices, on_device(): back = lax.all_to_all(payload, ('row', 'col'), 0, 0, tiled=True)  30.9 us
    all_to_all x1, waiting for transfers between devices, on_device(): lax.all_to_all(jnp.concatenate([outbox, tags], axis=1), ('row', 'col'), 0...  26.2 us
    all_to_all x1, waiting for transfers between devices, on_device(): lax.all_to_all(moment.reshape(devices, -1, feat_count), ('row', 'col'), 0...  8.22 us
    all_to_all x1, starting transfers between devices, on_device(): lax.all_to_all(jnp.concatenate([outbox, tags], axis=1), ('row', 'col'), 0...  7.48 us
    dot_general x4, matrix products, exact_pick(): lax.dot_general(wide, parts, dims, preferred_element_type=jnp.float32)  5.76 us
    ppermute x4, starting transfers between devices, swapped(): lax.ppermute(array, axis, [(i, i ^ 1 << apart) for i in range(lax.axis_si...  3.43 us
    all_to_all x1, starting transfers between devices, on_device(): lax.all_to_all(moment.reshape(devices, -1, feat_count), ('row', 'col'), 0...  3.25 us
    all_to_all x1, starting transfers between devices, on_device(): back = lax.all_to_all(payload, ('row', 'col'), 0, 0, tiled=True)  2.67 us
  transfers between devices with their start and end apart: 7, of which 4 were waited for; matrix products, arithmetic and copies ran while one was open for 5% of the time, Pallas kernels for 0%

profile of v22, /device:TPU:0, one launch (start us, length us, event | category | flops | bytes accessed | tf_op | source)
XLA Modules:
  0.0 112.6 jit_solution(14541274670167361164)
XLA Ops:
  0.6 0.7 add_select_fusion.1
  1.3 0.3 fusion.30
  1.6 0.4 iota_compare_fusion.1
  2.0 0.0 copy-start.2
  2.0 1.4 %reduce-precision_convert_fusion.7 = (bf16[512,256]{1,0:T(8,128)(2,1)S(1)}, bf16[512,256]{1,0:T(8,128)(2,1)S(1)}, bf16[512,256]{1,0:T(8,128)(2,1)S(1)}) fusion(f32[512,256]{1,0:T(8,128)} %param.10), kind=kLoop, calls=%fused_computation.89 | loop fusion | flops 917504 | bytes 1310720 | tf_op jit(solution)/shard_map/convert.9
  3.4 1.0 fusion
  4.4 0.2 reshape.145
  4.6 0.3 select_reduce_fusion
  4.9 0.1 convert_element_type.13
  5.0 0.1 select_maximum_fusion
  5.0 1.7 %all_to_all.19 = f32[32,1,8320]{2,1,0:T(1,128)} reshape(f32[32,8320]{1,0:T(8,128)S(1)} %select_maximum_fusion) | data formatting | bytes 2129920 | tf_op jit(solution)/shard_map/all_to_all | solution.py:152
  6.8 7.5 %all-to-all-start = ((f32[32,1,8320]{2,1,0:T(1,128)}), f32[32,1,8320]{2,1,0:T(1,128)S(1)}, u32[]{:S(2)}, u32[]{:S(2)}) async-start(f32[32,1,8320]{2,1,0:T(1,128)} %all_to_all.19), calls=%async_computation | async-start | bytes 2129920 | tf_op jit(solution)/shard_map/all_to_all | solution.py:152
  14.3 0.1 slice_bitcast_fusion
  14.4 0.1 compare_bitcast_fusion
  14.5 26.2 %all-to-all-done = f32[32,1,8320]{2,1,0:T(1,128)S(1)} async-done(((f32[32,1,8320]{2,1,0:T(1,128)}), f32[32,1,8320]{2,1,0:T(1,128)S(1)}, u32[]{:S(2)}, u32[]{:S(2)}) %all-to-all-start) | async-done | bytes 1064992 | tf_op jit(solution)/shard_map/all_to_all | solution.py:152
  40.6 0.1 copy.68
  40.7 0.1 slice.62
  40.8 0.2 reshape.146
  41.0 0.2 reduce-precision_convert_fusion.3
  41.2 0.1 eq.100
  41.3 0.3 iota_compare_fusion
  41.6 0.0 copy-start.4
  41.6 0.0 copy-start.8
  41.7 1.2 %fusion.6 = f32[512,256]{0,1:T(8,128)S(1)} fusion(pred[512,1024]{1,0:T(32,128)(4,1)S(1)} %iota_compare_fusion, bf16[1024,256]{1,0:T(8,128)(2,1)S(1)} %get-tuple-element.20, bf16[1024,256]{1,0:T(8,128)(2,1)S(1)} %get-tuple-element.21, bf16[1024,256]{1,0:T(8,128)(2,1)S(1)} %get-tuple-element.19), kind=kOutput, calls=%fused_computation.6 | convolution fusion | flops 813170688 | bytes 2621440 | tf_op jit(solution)/shard_map/dot_general | solution.py:115
  42.8 0.0 copy-start.1
  42.9 0.7 fusion.40
  43.6 1.5 %collective-permute-start.1 = (f32[128,256]{1,0:T(8,128)S(1)}, f32[128,256]{1,0:T(8,128)S(1)}, u32[]{:S(2)}, u32[]{:S(2)}) collective-permute-start(f32[128,256]{1,0:T(8,128)S(1)} %get-tuple-element.31), channel_id=1, source_target_pairs={{0,2},{1,3},{2,0},{3,1},{4,6},{5,7},{6,4},{7,5},{8,10},{9,11},{10,... | collective-permute-start | bytes 393224 | tf_op jit(solution)/shard_map/ppermute | solution.py:18
  45.1 0.7 fusion.56
  45.9 0.2 copy.37
  46.1 0.1 collective-permute-start
  46.1 2.5 %collective-permute-done.1 = f32[128,256]{1,0:T(8,128)S(1)} collective-permute-done((f32[128,256]{1,0:T(8,128)S(1)}, f32[128,256]{1,0:T(8,128)S(1)}, u32[]{:S(2)}, u32[]{:S(2)}) %collective-permute-start.1) | collective-permute-done | bytes 131104 | tf_op jit(solution)/shard_map/ppermute | solution.py:18
  48.6 0.2 convolution_bitcast_fusion.3
  48.9 0.2 convolution_bitcast_fusion.4
  49.1 0.8 fusion.38
  49.9 0.0 copy-start.7
  49.9 0.7 multiply_reduce_fusion.1
  50.6 0.3 copy-done.7
  50.9 0.6 multiply_add_fusion
  51.5 0.6 multiply_reduce_fusion
  52.1 0.7 fusion.36
  52.9 0.3 convolution_bitcast_fusion.2
  53.2 0.3 convolution_bitcast_fusion.1
  53.5 0.6 convolution_add_fusion.1
  54.1 0.1 collective-permute-start.2
  54.2 1.8 %collective-permute-start.3 = (f32[128,256]{0,1:T(8,128)S(1)}, f32[128,256]{0,1:T(8,128)S(1)}, u32[]{:S(2)}, u32[]{:S(2)}) collective-permute-start(f32[128,256]{0,1:T(8,128)S(1)} %convolution_bitcast_fusion.1), channel_id=1, source_target_pairs={{0,2},{1,3},{2,0},{3,1},{4,6},{5,7},{6,4},{7,5},{8,10},{9,11},{10,... | collective-permute-start | bytes 393224 | tf_op jit(solution)/shard_map/ppermute | solution.py:18
  55.9 1.3 %convolution_bitcast_fusion = f32[32,8,256]{2,1,0:T(8,128)} fusion(f32[512,256]{0,1:T(8,128)S(1)} %get-tuple-element.37, f32[512]{0:T(512)S(1)} %add_rsqrt_fusion, f32[512,256]{0,1:T(8,128)S(1)} %copy.37, f32[512,256]{0,1:T(8,128)S(1)} %get-tuple-element.39), kind=kOutput, calls=%fused_computation.48 | convolution fusion | flops 202506240 | bytes 1837056 | tf_op jit(solution)/shard_map/dot_general | solution.py:34
  57.2 3.2 %all-to-all-start.1 = ((f32[32,8,256]{2,1,0:T(8,128)}), f32[32,8,256]{2,1,0:T(8,128)S(1)}, u32[]{:S(2)}, u32[]{:S(2)}) async-start(f32[32,8,256]{2,1,0:T(8,128)} %convolution_bitcast_fusion), calls=%async_computation.1 | async-start | bytes 524288 | tf_op jit(solution)/shard_map/all_to_all | solution.py:169
  60.5 0.9 reduce-precision_convert_fusion.5
  61.4 1.0 fusion.18
  62.4 0.2 reshape.148
  62.6 8.2 %all-to-all-done.1 = f32[32,8,256]{2,1,0:T(8,128)S(1)} async-done(((f32[32,8,256]{2,1,0:T(8,128)}), f32[32,8,256]{2,1,0:T(8,128)S(1)}, u32[]{:S(2)}, u32[]{:S(2)}) %all-to-all-start.1) | async-done | bytes 262176 | tf_op jit(solution)/shard_map/all_to_all | solution.py:169
  70.9 0.1 pad_maximum_fusion
  71.0 2.0 %all_to_all.23 = f32[32,1,10240]{2,1,0:T(1,128)} reshape(f32[32,10240]{1,0:T(8,128)S(1)} %pad_maximum_fusion) | data formatting | bytes 2621440 | tf_op jit(solution)/shard_map/all_to_all | solution.py:181
  73.0 2.7 %all-to-all-start.2 = ((f32[32,1,10240]{2,1,0:T(1,128)}), f32[32,1,10240]{2,1,0:T(1,128)S(1)}, u32[]{:S(2)}, u32[]{:S(2)}) async-start(f32[32,1,10240]{2,1,0:T(1,128)} %all_to_all.23), calls=%async_computation.2 | async-start | bytes 2621440 | tf_op jit(solution)/shard_map/all_to_all | solution.py:181
  75.7 1.0 copy.40
  76.7 30.9 %all-to-all-done.2 = f32[32,1,10240]{2,1,0:T(1,128)S(1)} async-done(((f32[32,1,10240]{2,1,0:T(1,128)}), f32[32,1,10240]{2,1,0:T(1,128)S(1)}, u32[]{:S(2)}, u32[]{:S(2)}) %all-to-all-start.2) | async-done | bytes 1310752 | tf_op jit(solution)/shard_map/all_to_all | solution.py:181
  107.5 0.4 copy.67
  108.0 0.1 slice.67
  108.1 0.2 reshape.150
  108.2 0.2 reduce-precision_convert_fusion.1
  108.5 0.0 copy-start.3
  108.5 0.9 multiply_reduce_fusion.2
  109.4 0.6 broadcast_multiply_fusion.1
  110.0 2.6 %fusion.12 = f32[512,256]{1,0:T(8,128)} fusion(pred[1024,512]{1,0:T(32,128)(4,1)S(1)} %copy-done.3, bf16[1024,256]{1,0:T(8,128)(2,1)S(1)} %get-tuple-element.17, bf16[1024,256]{1,0:T(8,128)(2,1)S(1)} %get-tuple-element.18, bf16[1024,256]{1,0:T(8,128)(2,1)S(1)} %get-tuple-element.16), kind=kOutput, calls=%fused_computation.12 | convolution fusion | flops 813170688 | bytes 2621440 | tf_op jit(solution)/shard_map/dot_general | solution.py:115
  (34 shorter events, 0.3 us)
Async XLA Ops:
  2.0 1.4 %copy-start.2 = (pred[1024,512]{1,0:T(32,128)(4,1)}, pred[1024,512]{1,0:T(32,128)(4,1)S(1)}, u32[]{:S(2)}) copy-start(pred[1024,512]{1,0:T(32,128)(4,1)S(1)} %iota_compare_fusion.1) | copy-start | bytes 1572868
  6.8 7.5 %copy-start.11 = (s32[1,3]{1,0:T(1,128)S(1)}, s32[1,3]{1,0:T(1,128)}, u32[]{:S(2)}) copy-start(s32[1,3]{1,0:T(1,128)} %param.16) | copy-start | bytes 40
  6.8 7.7 %copy-start.10 = (s32[1,8,2]{1,2,0:T(2,128)S(1)}, s32[1,8,2]{1,2,0:T(2,128)}, u32[]{:S(2)}) copy-start(s32[1,8,2]{1,2,0:T(2,128)} %param.15) | copy-start | bytes 196
  6.8 33.9 %all-to-all-start = ((f32[32,1,8320]{2,1,0:T(1,128)}), f32[32,1,8320]{2,1,0:T(1,128)S(1)}, u32[]{:S(2)}, u32[]{:S(2)}) async-start(f32[32,1,8320]{2,1,0:T(1,128)} %all_to_all.19), calls=%async_computation | async-start | bytes 2129920 | tf_op jit(solution)/shard_map/all_to_all | solution.py:152
  41.6 1.2 %copy-start.4 = (pred[512,1024]{1,0:T(32,128)(4,1)}, pred[512,1024]{1,0:T(32,128)(4,1)S(1)}, u32[]{:S(2)}) copy-start(pred[512,1024]{1,0:T(32,128)(4,1)S(1)} %iota_compare_fusion) | copy-start | bytes 1572868
  41.6 1.2 %copy-start.8 = (s32[1,2,128]{2,1,0:T(2,128)S(1)}, s32[1,2,128]{2,1,0:T(2,128)}, u32[]{:S(2)}) copy-start(s32[1,2,128]{2,1,0:T(2,128)} %param.17) | copy-start | bytes 3076
  42.8 2.3 %copy-start.6 = (f32[1,8,128,128]{3,2,1,0:T(8,128)S(1)}, f32[1,8,128,128]{3,2,1,0:T(8,128)}, u32[]{:S(2)}) copy-start(f32[1,8,128,128]{3,2,1,0:T(8,128)} %param.14) | copy-start | bytes 1572868
  42.8 3.0 %copy-start.1 = (f32[512,256]{1,0:T(8,128)S(1)}, f32[512,256]{1,0:T(8,128)}, u32[]{:S(2)}) copy-start(f32[512,256]{1,0:T(8,128)} %param.19) | copy-start | bytes 1572868
  43.6 5.0 %collective-permute-start.1 = (f32[128,256]{1,0:T(8,128)S(1)}, f32[128,256]{1,0:T(8,128)S(1)}, u32[]{:S(2)}, u32[]{:S(2)}) collective-permute-start(f32[128,256]{1,0:T(8,128)S(1)} %get-tuple-element.31), channel_id=1, source_target_pairs={{0,2},{1,3},{2,0},{3,1},{4,6},{5,7},{6,4},{7,5},{8,10},{9,11},{10,... | collective-permute-start | bytes 393224 | tf_op jit(solution)/shard_map/ppermute | solution.py:18
  45.1 3.5 %copy-start = (f32[1,2,128,128]{3,2,1,0:T(8,128)S(1)}, f32[1,2,128,128]{3,2,1,0:T(8,128)}, u32[]{:S(2)}) copy-start(f32[1,2,128,128]{3,2,1,0:T(8,128)} %param.18) | copy-start | bytes 393220
  46.1 2.8 %collective-permute-start = (f32[128,256]{1,0:T(8,128)S(1)}, f32[128,256]{1,0:T(8,128)S(1)}, u32[]{:S(2)}, u32[]{:S(2)}) collective-permute-start(f32[128,256]{1,0:T(8,128)S(1)} %get-tuple-element.30), channel_id=1, source_target_pairs={{0,1},{1,0},{2,3},{3,2},{4,5},{5,4},{6,7},{7,6},{8,9},{9,8},{10,11... | collective-permute-start | bytes 393224 | tf_op jit(solution)/shard_map/ppermute | solution.py:18
  49.9 1.0 copy-start.7
  49.9 0.9 copy-start.9
  54.1 6.4 %collective-permute-start.2 = (f32[128,256]{0,1:T(8,128)S(1)}, f32[128,256]{0,1:T(8,128)S(1)}, u32[]{:S(2)}, u32[]{:S(2)}) collective-permute-start(f32[128,256]{0,1:T(8,128)S(1)} %convolution_bitcast_fusion.2), channel_id=1, source_target_pairs={{0,1},{1,0},{2,3},{3,2},{4,5},{5,4},{6,7},{7,6},{8,9},{9,8},{10,11... | collective-permute-start | bytes 393224 | tf_op jit(solution)/shard_map/ppermute | solution.py:18
  54.2 6.3 %collective-permute-start.3 = (f32[128,256]{0,1:T(8,128)S(1)}, f32[128,256]{0,1:T(8,128)S(1)}, u32[]{:S(2)}, u32[]{:S(2)}) collective-permute-start(f32[128,256]{0,1:T(8,128)S(1)} %convolution_bitcast_fusion.1), channel_id=1, source_target_pairs={{0,2},{1,3},{2,0},{3,1},{4,6},{5,7},{6,4},{7,5},{8,10},{9,11},{10,... | collective-permute-start | bytes 393224 | tf_op jit(solution)/shard_map/ppermute | solution.py:18
  57.2 4.2 %copy-start.5 = (pred[512,1024]{1,0:T(32,128)(4,1)S(1)}, pred[512,1024]{1,0:T(32,128)(4,1)}, u32[]{:S(2)}) copy-start(pred[512,1024]{1,0:T(32,128)(4,1)} %copy-done.4) | copy-start | bytes 1572868
  57.2 13.6 %all-to-all-start.1 = ((f32[32,8,256]{2,1,0:T(8,128)}), f32[32,8,256]{2,1,0:T(8,128)S(1)}, u32[]{:S(2)}, u32[]{:S(2)}) async-start(f32[32,8,256]{2,1,0:T(8,128)} %convolution_bitcast_fusion), calls=%async_computation.1 | async-start | bytes 524288 | tf_op jit(solution)/shard_map/all_to_all | solution.py:169
  73.0 34.6 %all-to-all-start.2 = ((f32[32,1,10240]{2,1,0:T(1,128)}), f32[32,1,10240]{2,1,0:T(1,128)S(1)}, u32[]{:S(2)}, u32[]{:S(2)}) async-start(f32[32,1,10240]{2,1,0:T(1,128)} %all_to_all.23), calls=%async_computation.2 | async-start | bytes 2621440 | tf_op jit(solution)/shard_map/all_to_all | solution.py:181
  108.5 1.5 %copy-start.3 = (pred[1024,512]{1,0:T(32,128)(4,1)S(1)}, pred[1024,512]{1,0:T(32,128)(4,1)}, u32[]{:S(2)}) copy-start(pred[1024,512]{1,0:T(32,128)(4,1)} %copy-done.2) | copy-start | bytes 1572868
